TPU v7x, 128 devices: a whole 4x4x4 slice. The times are simulated.
128 devices in a mesh: slab: 32 (over z, y, x_lo), px: 2 (over x_hi), py: 2 (over core).
Axes of the slice: x: 4 (x_hi: 2, x_lo: 2; x = x_hi * 2 + x_lo), y: 4, z: 4, core: 2. Of those that a mesh axis runs over, the one named last changes fastest.
Arguments:
- source: float32 [128, 4, 256, 256], P('slab', None, 'px', 'py'), may hold values from -6 to 6
- phase: float32 [128, 256, 256], P('slab', 'px', 'py'), may hold values from 0.3 to 2.8
- attenuation: float32 [128, 256, 256], P('slab', 'px', 'py'), may hold values from 0.00078125 to 0.08
- pml_level: int32 [256, 256], P('px', 'py'), may hold values from 0 to 3
- recv_values: float32 [2, 2, 4, 16384], P('px', 'py', None, 'slab'), may hold values from -8 to 8
- recv_slab: int32 [2, 2, 16384, 1], P('px', 'py', 'slab'), may hold values from 0 to 31; in each aligned block of 512 rows (0 to 511, 512 to 1023, ..., all dimensions but the last counted through in order) at most 64 rows name the same one
- recv_lateral: int32 [2, 2, 16384], P('px', 'py', 'slab'), may hold values from 0 to 16383
- recv_layer: int32 [2, 2, 16384], P('px', 'py', 'slab'), may hold values from 0 to 3
Outputs:
- correction: float32 [128, 4, 256, 256], P('slab', None, 'px', 'py')
Inputs may be any that keep to these rules, and one draw needn't show every extreme that they name: `recv_slab`: among the rows of one device, at most 64 receivers name the same slab, a bound that some block reaches of them.
All inputs are finite; a program needn't handle non-finite values.
Results may differ from a plain program's by a relative error of at most 0.000034.
Values sent between devices are 32-bit elements; how exact they have to be, the bound alone decides.
No kernel may reach another device: no remote copies, remote signals or barrier semaphores. Data moves between devices by JAX's collectives and lax.ppermute only.
A program may use at most 128 MiB of HBM per device.

v0:
```python
import jax
import jax.numpy as jnp
from jax import lax
from jax.sharding import PartitionSpec as P


def from_behind(array, axis, by):
    count = lax.axis_size(axis)
    pairs = [(i, i + by) for i in range(count) if 0 <= i + by < count]
    return lax.ppermute(array, axis, pairs)


def padded_2(block, sides, width):
    for axis, dim in sides:
        count = lax.axis_size(axis)
        forward = [(i, i + 1) for i in range(count - 1)]
        backward = [(target, source) for source, target in forward]
        low = lax.ppermute(
            lax.slice_in_dim(block, block.shape[dim] - width, None, axis=dim), axis, forward
        )
        high = lax.ppermute(lax.slice_in_dim(block, 0, width, axis=dim), axis, backward)
        block = jnp.concatenate([low, block, high], axis=dim)
    return block


def advance(state, layer):
    real_part, imag_part, prod_real, prod_imag = state
    rate_real, rate_imag, force_layer = layer
    new_real = rate_real * real_part - rate_imag * imag_part + force_layer[:, 0]
    new_imag = rate_real * imag_part + rate_imag * real_part + force_layer[:, 1]
    next_real = rate_real * prod_real - rate_imag * prod_imag
    next_imag = rate_real * prod_imag + rate_imag * prod_real
    return (
        (new_real, new_imag, next_real, next_imag),
        (jnp.stack([new_real, new_imag], axis=1), next_real, next_imag),
    )


def shards(source, phase, attenuation, pml_level, recv_values, recv_slab, recv_lateral, recv_layer):
    layers, components, width_x, width_y = source.shape
    shot_count = components // 2
    slab_count = lax.axis_size("slab")
    depth_total = layers * slab_count
    plane_size = width_x * width_y
    rows_here = recv_values.shape[3]
    capacity = rows_here // min(8, slab_count)
    values = recv_values[0, 0]
    target_slab = recv_slab[0, 0, :, 0]
    position = recv_layer[0, 0] * (components * plane_size) + recv_lateral[0, 0]
    one_hot = (target_slab[:, None] == jnp.arange(slab_count, dtype=jnp.int32)[None, :]).astype(
        jnp.int32
    )
    ranking = jnp.sum((jnp.cumsum(one_hot, axis=0) - one_hot) * one_hot, axis=1)
    target_slot = target_slab * capacity + ranking
    send_values = (
        jnp.zeros((components, slab_count * capacity), jnp.float32).at[:, target_slot].set(values)
    )
    send_places = jnp.zeros((slab_count * capacity,), jnp.int32).at[target_slot].set(position)
    got_values, got_places = (
        lax.all_to_all(
            send_values.reshape(components, slab_count, capacity),
            "slab",
            split_axis=1,
            concat_axis=1,
            tiled=True,
        ),
        lax.all_to_all(
            send_places.reshape(1, slab_count, capacity),
            "slab",
            split_axis=1,
            concat_axis=1,
            tiled=True,
        ),
    )
    inject_values = got_values.reshape(components, slab_count * capacity)
    inject_places = got_places.reshape(slab_count * capacity)
    offsets = (jnp.arange(components, dtype=jnp.int32) * plane_size)[:, None]
    flat_index = (inject_places[None, :] + offsets).reshape(-1)
    forcing = source.reshape(-1).at[flat_index].add(inject_values.reshape(-1))
    fields = forcing.reshape(layers, shot_count, 2, width_x, width_y)
    damping = attenuation + 0.5 / depth_total * pml_level.astype(jnp.float32)[None, :, :]
    amplitude = jnp.exp(-damping)
    real_mult = amplitude * jnp.cos(phase)
    imag_mult = amplitude * jnp.sin(phase)
    zeros = jnp.zeros((shot_count, width_x, width_y), jnp.float32)
    ones_plane = jnp.ones((width_x, width_y), jnp.float32)
    zero_plane = jnp.zeros((width_x, width_y), jnp.float32)
    start_state = (zeros, zeros, ones_plane, zero_plane)
    final_down, down_parts = lax.scan(advance, start_state, (real_mult, imag_mult, fields))
    final_up, up_parts = lax.scan(
        advance, start_state, (real_mult, imag_mult, fields), reverse=True
    )
    local_down, down_real, down_imag = down_parts
    local_up, up_real, up_imag = up_parts
    total_down = (down_real[-1], down_imag[-1], local_down[-1][:, 0], local_down[-1][:, 1])
    total_up = (up_real[0], up_imag[0], local_up[0][:, 0], local_up[0][:, 1])

    def relay_turn(turn_index, carry):
        enter_real, enter_imag, below_real, below_imag = carry
        send_real = total_down[0] * enter_real - total_down[1] * enter_imag + total_down[2]
        send_imag = total_down[0] * enter_imag + total_down[1] * enter_real + total_down[3]
        rise_real = total_up[0] * below_real - total_up[1] * below_imag + total_up[2]
        rise_imag = total_up[0] * below_imag + total_up[1] * below_real + total_up[3]
        got_down = from_behind((send_real, send_imag), "slab", 1)
        got_up = from_behind((rise_real, rise_imag), "slab", -1)
        return (got_down[0], got_down[1], got_up[0], got_up[1])

    enter_real, enter_imag, below_real, below_imag = lax.fori_loop(
        0, slab_count - 1, relay_turn, (zeros, zeros, zeros, zeros)
    )
    full_down_real = (
        local_down[:, :, 0]
        + down_real[:, None] * enter_real[None]
        - down_imag[:, None] * enter_imag[None]
    )
    full_down_imag = (
        local_down[:, :, 1]
        + down_real[:, None] * enter_imag[None]
        + down_imag[:, None] * enter_real[None]
    )
    full_up_real = (
        local_up[:, :, 0]
        + up_real[:, None] * below_real[None]
        - up_imag[:, None] * below_imag[None]
    )
    full_up_imag = (
        local_up[:, :, 1]
        + up_real[:, None] * below_imag[None]
        + up_imag[:, None] * below_real[None]
    )
    downward = jnp.stack([full_down_real, full_down_imag], axis=2)
    upward = jnp.stack([full_up_real, full_up_imag], axis=2)
    combined = (downward + upward - fields).reshape(layers, components, width_x, width_y)
    padded = padded_2(combined, (("px", 2), ("py", 3)), 1)
    neighbours = (
        padded[:, :, 2:, 1:-1]
        + padded[:, :, :-2, 1:-1]
        + padded[:, :, 1:-1, 2:]
        + padded[:, :, 1:-1, :-2]
    )
    return combined - 0.2 * (4.0 * combined - neighbours)


def solution(mesh):
    in_specs = (
        P("slab", None, "px", "py"),
        P("slab", "px", "py"),
        P("slab", "px", "py"),
        P("px", "py"),
        P("px", "py", None, "slab"),
        P("px", "py", "slab", None),
        P("px", "py", "slab"),
        P("px", "py", "slab"),
    )
    out_specs = P("slab", None, "px", "py")
    return jax.shard_map(shards, mesh=mesh, in_specs=in_specs, out_specs=out_specs, check_vma=False)
```

profile of v0, /device:TPU:1, one launch (start us, length us, event | category | flops | bytes accessed | tf_op | source)
XLA Modules:
  0.0 772.8 jit_solution(7170309236231397554)
XLA Ops:
  5.4 9.8 %all-to-all-start = ((s32[1,32,64]{2,0,1:T(1,128)}), s32[1,32,64]{2,0,1:T(1,128)S(1)}, u32[]{:S(2)}, u32[]{:S(2)}) async-start(s32[1,32,64]{2,0,1:T(1,128)} %reshape.138), calls=%async_computation | async-start | bytes 32768 | tf_op jit(solution)/shard_map/all_to_all | solution.py:67
  22.3 5.0 all-to-all-start.1
  28.6 5.8 all-to-all-done.1
  35.9 53.6 %scatter_fusion = f32[262144]{0:T(1024)S(1)} fusion(f32[262144]{0:T(1024)S(1)} %bitcast.151, s32[8192]{0:T(1024)S(1)} %bitcast.160, f32[8192]{0:T(1024)S(1)} %reshape.162), kind=kCustom, calls=%fused_computation.2 | custom fusion | flops 8192 | bytes 131072 | tf_op jit(solution)/shard_map/scatter-add | solution.py:79
  105.5 591.5 %while.66 = (s32[]{:T(128)}, f32[2,128,128]{2,1,0:T(8,128)S(1)}, f32[2,128,128]{2,1,0:T(8,128)S(1)}, f32[2,128,128]{2,1,0:T(8,128)S(1)}, f32[2,128,128]{2,1,0:T(...) while((s32[]{:T(128)}, f32[2,128,128]{2,1,0:T(8,128)S(1)}, ...), condition=%wide.region_11.12_spmd, body=%wide.region_10.11_spmd.sunk | while | flops 524290 | bytes 3932453 | solution.py:108
  113.2 7.2 collective-permute-done.2
  159.5 5.0 collective-permute-start
  171.9 4.8 collective-permute-done.2
  183.6 4.7 collective-permute-start.1
  235.0 4.4 collective-permute-start
  247.1 4.6 collective-permute-done.2
  266.2 4.3 collective-permute-done.2
  277.3 5.1 collective-permute-start.1
  286.5 5.2 collective-permute-done.2
  305.9 4.6 collective-permute-done.2
  369.1 5.1 collective-permute-start
  411.7 4.3 collective-permute-start.1
  420.2 5.5 collective-permute-done.2
  428.4 4.3 collective-permute-start
  445.4 4.3 collective-permute-start
  464.2 4.3 collective-permute-start
  476.4 5.5 collective-permute-done.2
  484.2 4.5 collective-permute-start
  496.6 5.2 collective-permute-done.2
  516.7 4.7 collective-permute-done.2
  547.3 5.5 collective-permute-start.1
  575.5 4.6 collective-permute-done.2
  638.6 4.8 collective-permute-start
  651.1 4.3 collective-permute-done.2
  689.7 5.5 collective-permute-done.2
  700.4 5.7 collective-permute-start.5
  710.2 54.3 %collective-permute-start.6 = (f32[4,4,130,1]{2,1,3,0:T(4,128)S(1)}, f32[4,4,130,1]{2,1,3,0:T(4,128)S(1)}, u32[]{:S(2)}, u32[]{:S(2)}) collective-permute-start(f32[4,4,130,1]{2,1,3,0:T(4,128)S(1)} %copy.32), channel_id=1, source_target_pairs={{1,0},{3,2},{5,4},{7,6},{9,8},{11,10},{13,12},{15,14},{17,16},{19,... | collective-permute-start | bytes 24968 | tf_op jit(solution)/shard_map/ppermute | solution.py:21
  (436 shorter events, 520.9 us)
Async XLA Ops:
  5.4 16.9 %all-to-all-start = ((s32[1,32,64]{2,0,1:T(1,128)}), s32[1,32,64]{2,0,1:T(1,128)S(1)}, u32[]{:S(2)}, u32[]{:S(2)}) async-start(s32[1,32,64]{2,0,1:T(1,128)} %reshape.138), calls=%async_computation | async-start | bytes 32768 | tf_op jit(solution)/shard_map/all_to_all | solution.py:67
  22.3 12.1 %all-to-all-start.1 = ((f32[32,1,256]{2,1,0:T(1,128)}), f32[32,1,256]{2,1,0:T(1,128)S(1)}, u32[]{:S(2)}, u32[]{:S(2)}) async-start(f32[32,1,256]{2,1,0:T(1,128)} %reshape.180), calls=%async_computation.1 | async-start | bytes 65536 | tf_op jit(solution)/shard_map/all_to_all | solution.py:60
  111.8 10.6 %collective-permute-start.3 = (f32[2,128,128]{2,1,0:T(8,128)S(1)}, f32[2,128,128]{2,1,0:T(8,128)S(1)}, u32[]{:S(2)}, u32[]{:S(2)}) collective-permute-start(f32[2,128,128]{2,1,0:T(8,128)S(1)} %get-tuple-element.787), channel_id=1, source_target_pairs={{4,0},{8,4},{12,8},{16,12},{20,16},{24,20},{28,24},{32,28},{36,32}... | collective-permute-start | bytes 393224 | tf_op jit(solution)/shard_map/while/body/eval_jaxpr/ppermute | solution.py:10
  123.4 11.3 %collective-permute-start = (f32[2,128,128]{2,1,0:T(8,128)S(1)}, f32[2,128,128]{2,1,0:T(8,128)S(1)}, u32[]{:S(2)}, u32[]{:S(2)}) collective-permute-start(f32[2,128,128]{2,1,0:T(8,128)S(1)} %get-tuple-element.784), channel_id=1, source_target_pairs={{0,4},{4,8},{8,12},{12,16},{16,20},{20,24},{24,28},{28,32},{32,36}... | collective-permute-start | bytes 393224 | tf_op jit(solution)/shard_map/while/body/eval_jaxpr/ppermute | solution.py:10
  140.9 11.6 %collective-permute-start = (f32[2,128,128]{2,1,0:T(8,128)S(1)}, f32[2,128,128]{2,1,0:T(8,128)S(1)}, u32[]{:S(2)}, u32[]{:S(2)}) collective-permute-start(f32[2,128,128]{2,1,0:T(8,128)S(1)} %get-tuple-element.784), channel_id=1, source_target_pairs={{0,4},{4,8},{8,12},{12,16},{16,20},{20,24},{24,28},{28,32},{32,36}... | collective-permute-start | bytes 393224 | tf_op jit(solution)/shard_map/while/body/eval_jaxpr/ppermute | solution.py:10
  159.5 12.4 %collective-permute-start = (f32[2,128,128]{2,1,0:T(8,128)S(1)}, f32[2,128,128]{2,1,0:T(8,128)S(1)}, u32[]{:S(2)}, u32[]{:S(2)}) collective-permute-start(f32[2,128,128]{2,1,0:T(8,128)S(1)} %get-tuple-element.784), channel_id=1, source_target_pairs={{0,4},{4,8},{8,12},{12,16},{16,20},{20,24},{24,28},{28,32},{32,36}... | collective-permute-start | bytes 393224 | tf_op jit(solution)/shard_map/while/body/eval_jaxpr/ppermute | solution.py:10
  179.6 12.8 %collective-permute-start = (f32[2,128,128]{2,1,0:T(8,128)S(1)}, f32[2,128,128]{2,1,0:T(8,128)S(1)}, u32[]{:S(2)}, u32[]{:S(2)}) collective-permute-start(f32[2,128,128]{2,1,0:T(8,128)S(1)} %get-tuple-element.784), channel_id=1, source_target_pairs={{0,4},{4,8},{8,12},{12,16},{16,20},{20,24},{24,28},{28,32},{32,36}... | collective-permute-start | bytes 393224 | tf_op jit(solution)/shard_map/while/body/eval_jaxpr/ppermute | solution.py:10
  199.8 12.4 %collective-permute-start = (f32[2,128,128]{2,1,0:T(8,128)S(1)}, f32[2,128,128]{2,1,0:T(8,128)S(1)}, u32[]{:S(2)}, u32[]{:S(2)}) collective-permute-start(f32[2,128,128]{2,1,0:T(8,128)S(1)} %get-tuple-element.784), channel_id=1, source_target_pairs={{0,4},{4,8},{8,12},{12,16},{16,20},{20,24},{24,28},{28,32},{32,36}... | collective-permute-start | bytes 393224 | tf_op jit(solution)/shard_map/while/body/eval_jaxpr/ppermute | solution.py:10
  218.1 10.6 %collective-permute-start = (f32[2,128,128]{2,1,0:T(8,128)S(1)}, f32[2,128,128]{2,1,0:T(8,128)S(1)}, u32[]{:S(2)}, u32[]{:S(2)}) collective-permute-start(f32[2,128,128]{2,1,0:T(8,128)S(1)} %get-tuple-element.784), channel_id=1, source_target_pairs={{0,4},{4,8},{8,12},{12,16},{16,20},{20,24},{24,28},{28,32},{32,36}... | collective-permute-start | bytes 393224 | tf_op jit(solution)/shard_map/while/body/eval_jaxpr/ppermute | solution.py:10
  235.0 12.1 %collective-permute-start = (f32[2,128,128]{2,1,0:T(8,128)S(1)}, f32[2,128,128]{2,1,0:T(8,128)S(1)}, u32[]{:S(2)}, u32[]{:S(2)}) collective-permute-start(f32[2,128,128]{2,1,0:T(8,128)S(1)} %get-tuple-element.784), channel_id=1, source_target_pairs={{0,4},{4,8},{8,12},{12,16},{16,20},{20,24},{24,28},{28,32},{32,36}... | collective-permute-start | bytes 393224 | tf_op jit(solution)/shard_map/while/body/eval_jaxpr/ppermute | solution.py:10
  255.3 10.9 %collective-permute-start = (f32[2,128,128]{2,1,0:T(8,128)S(1)}, f32[2,128,128]{2,1,0:T(8,128)S(1)}, u32[]{:S(2)}, u32[]{:S(2)}) collective-permute-start(f32[2,128,128]{2,1,0:T(8,128)S(1)} %get-tuple-element.784), channel_id=1, source_target_pairs={{0,4},{4,8},{8,12},{12,16},{16,20},{20,24},{24,28},{28,32},{32,36}... | collective-permute-start | bytes 393224 | tf_op jit(solution)/shard_map/while/body/eval_jaxpr/ppermute | solution.py:10
  274.3 12.2 %collective-permute-start = (f32[2,128,128]{2,1,0:T(8,128)S(1)}, f32[2,128,128]{2,1,0:T(8,128)S(1)}, u32[]{:S(2)}, u32[]{:S(2)}) collective-permute-start(f32[2,128,128]{2,1,0:T(8,128)S(1)} %get-tuple-element.784), channel_id=1, source_target_pairs={{0,4},{4,8},{8,12},{12,16},{16,20},{20,24},{24,28},{28,32},{32,36}... | collective-permute-start | bytes 393224 | tf_op jit(solution)/shard_map/while/body/eval_jaxpr/ppermute | solution.py:10
  314.4 11.1 %collective-permute-start = (f32[2,128,128]{2,1,0:T(8,128)S(1)}, f32[2,128,128]{2,1,0:T(8,128)S(1)}, u32[]{:S(2)}, u32[]{:S(2)}) collective-permute-start(f32[2,128,128]{2,1,0:T(8,128)S(1)} %get-tuple-element.784), channel_id=1, source_target_pairs={{0,4},{4,8},{8,12},{12,16},{16,20},{20,24},{24,28},{28,32},{32,36}... | collective-permute-start | bytes 393224 | tf_op jit(solution)/shard_map/while/body/eval_jaxpr/ppermute | solution.py:10
  332.1 11.7 %collective-permute-start = (f32[2,128,128]{2,1,0:T(8,128)S(1)}, f32[2,128,128]{2,1,0:T(8,128)S(1)}, u32[]{:S(2)}, u32[]{:S(2)}) collective-permute-start(f32[2,128,128]{2,1,0:T(8,128)S(1)} %get-tuple-element.784), channel_id=1, source_target_pairs={{0,4},{4,8},{8,12},{12,16},{16,20},{20,24},{24,28},{28,32},{32,36}... | collective-permute-start | bytes 393224 | tf_op jit(solution)/shard_map/while/body/eval_jaxpr/ppermute | solution.py:10
  350.9 11.1 %collective-permute-start = (f32[2,128,128]{2,1,0:T(8,128)S(1)}, f32[2,128,128]{2,1,0:T(8,128)S(1)}, u32[]{:S(2)}, u32[]{:S(2)}) collective-permute-start(f32[2,128,128]{2,1,0:T(8,128)S(1)} %get-tuple-element.784), channel_id=1, source_target_pairs={{0,4},{4,8},{8,12},{12,16},{16,20},{20,24},{24,28},{28,32},{32,36}... | collective-permute-start | bytes 393224 | tf_op jit(solution)/shard_map/while/body/eval_jaxpr/ppermute | solution.py:10
  369.1 12.6 %collective-permute-start = (f32[2,128,128]{2,1,0:T(8,128)S(1)}, f32[2,128,128]{2,1,0:T(8,128)S(1)}, u32[]{:S(2)}, u32[]{:S(2)}) collective-permute-start(f32[2,128,128]{2,1,0:T(8,128)S(1)} %get-tuple-element.784), channel_id=1, source_target_pairs={{0,4},{4,8},{8,12},{12,16},{16,20},{20,24},{24,28},{28,32},{32,36}... | collective-permute-start | bytes 393224 | tf_op jit(solution)/shard_map/while/body/eval_jaxpr/ppermute | solution.py:10
  389.5 12.0 %collective-permute-start = (f32[2,128,128]{2,1,0:T(8,128)S(1)}, f32[2,128,128]{2,1,0:T(8,128)S(1)}, u32[]{:S(2)}, u32[]{:S(2)}) collective-permute-start(f32[2,128,128]{2,1,0:T(8,128)S(1)} %get-tuple-element.784), channel_id=1, source_target_pairs={{0,4},{4,8},{8,12},{12,16},{16,20},{20,24},{24,28},{28,32},{32,36}... | collective-permute-start | bytes 393224 | tf_op jit(solution)/shard_map/while/body/eval_jaxpr/ppermute | solution.py:10
  407.7 12.5 %collective-permute-start = (f32[2,128,128]{2,1,0:T(8,128)S(1)}, f32[2,128,128]{2,1,0:T(8,128)S(1)}, u32[]{:S(2)}, u32[]{:S(2)}) collective-permute-start(f32[2,128,128]{2,1,0:T(8,128)S(1)} %get-tuple-element.784), channel_id=1, source_target_pairs={{0,4},{4,8},{8,12},{12,16},{16,20},{20,24},{24,28},{28,32},{32,36}... | collective-permute-start | bytes 393224 | tf_op jit(solution)/shard_map/while/body/eval_jaxpr/ppermute | solution.py:10
  428.4 11.0 %collective-permute-start = (f32[2,128,128]{2,1,0:T(8,128)S(1)}, f32[2,128,128]{2,1,0:T(8,128)S(1)}, u32[]{:S(2)}, u32[]{:S(2)}) collective-permute-start(f32[2,128,128]{2,1,0:T(8,128)S(1)} %get-tuple-element.784), channel_id=1, source_target_pairs={{0,4},{4,8},{8,12},{12,16},{16,20},{20,24},{24,28},{28,32},{32,36}... | collective-permute-start | bytes 393224 | tf_op jit(solution)/shard_map/while/body/eval_jaxpr/ppermute | solution.py:10
  445.4 11.9 %collective-permute-start = (f32[2,128,128]{2,1,0:T(8,128)S(1)}, f32[2,128,128]{2,1,0:T(8,128)S(1)}, u32[]{:S(2)}, u32[]{:S(2)}) collective-permute-start(f32[2,128,128]{2,1,0:T(8,128)S(1)} %get-tuple-element.784), channel_id=1, source_target_pairs={{0,4},{4,8},{8,12},{12,16},{16,20},{20,24},{24,28},{28,32},{32,36}... | collective-permute-start | bytes 393224 | tf_op jit(solution)/shard_map/while/body/eval_jaxpr/ppermute | solution.py:10
  464.2 12.1 %collective-permute-start = (f32[2,128,128]{2,1,0:T(8,128)S(1)}, f32[2,128,128]{2,1,0:T(8,128)S(1)}, u32[]{:S(2)}, u32[]{:S(2)}) collective-permute-start(f32[2,128,128]{2,1,0:T(8,128)S(1)} %get-tuple-element.784), channel_id=1, source_target_pairs={{0,4},{4,8},{8,12},{12,16},{16,20},{20,24},{24,28},{28,32},{32,36}... | collective-permute-start | bytes 393224 | tf_op jit(solution)/shard_map/while/body/eval_jaxpr/ppermute | solution.py:10
  484.2 12.4 %collective-permute-start = (f32[2,128,128]{2,1,0:T(8,128)S(1)}, f32[2,128,128]{2,1,0:T(8,128)S(1)}, u32[]{:S(2)}, u32[]{:S(2)}) collective-permute-start(f32[2,128,128]{2,1,0:T(8,128)S(1)} %get-tuple-element.784), channel_id=1, source_target_pairs={{0,4},{4,8},{8,12},{12,16},{16,20},{20,24},{24,28},{28,32},{32,36}... | collective-permute-start | bytes 393224 | tf_op jit(solution)/shard_map/while/body/eval_jaxpr/ppermute | solution.py:10
  504.9 11.8 %collective-permute-start = (f32[2,128,128]{2,1,0:T(8,128)S(1)}, f32[2,128,128]{2,1,0:T(8,128)S(1)}, u32[]{:S(2)}, u32[]{:S(2)}) collective-permute-start(f32[2,128,128]{2,1,0:T(8,128)S(1)} %get-tuple-element.784), channel_id=1, source_target_pairs={{0,4},{4,8},{8,12},{12,16},{16,20},{20,24},{24,28},{28,32},{32,36}... | collective-permute-start | bytes 393224 | tf_op jit(solution)/shard_map/while/body/eval_jaxpr/ppermute | solution.py:10
  525.0 10.7 %collective-permute-start = (f32[2,128,128]{2,1,0:T(8,128)S(1)}, f32[2,128,128]{2,1,0:T(8,128)S(1)}, u32[]{:S(2)}, u32[]{:S(2)}) collective-permute-start(f32[2,128,128]{2,1,0:T(8,128)S(1)} %get-tuple-element.784), channel_id=1, source_target_pairs={{0,4},{4,8},{8,12},{12,16},{16,20},{20,24},{24,28},{28,32},{32,36}... | collective-permute-start | bytes 393224 | tf_op jit(solution)/shard_map/while/body/eval_jaxpr/ppermute | solution.py:10
  543.7 13.2 %collective-permute-start = (f32[2,128,128]{2,1,0:T(8,128)S(1)}, f32[2,128,128]{2,1,0:T(8,128)S(1)}, u32[]{:S(2)}, u32[]{:S(2)}) collective-permute-start(f32[2,128,128]{2,1,0:T(8,128)S(1)} %get-tuple-element.784), channel_id=1, source_target_pairs={{0,4},{4,8},{8,12},{12,16},{16,20},{20,24},{24,28},{28,32},{32,36}... | collective-permute-start | bytes 393224 | tf_op jit(solution)/shard_map/while/body/eval_jaxpr/ppermute | solution.py:10
  584.0 11.2 %collective-permute-start = (f32[2,128,128]{2,1,0:T(8,128)S(1)}, f32[2,128,128]{2,1,0:T(8,128)S(1)}, u32[]{:S(2)}, u32[]{:S(2)}) collective-permute-start(f32[2,128,128]{2,1,0:T(8,128)S(1)} %get-tuple-element.784), channel_id=1, source_target_pairs={{0,4},{4,8},{8,12},{12,16},{16,20},{20,24},{24,28},{28,32},{32,36}... | collective-permute-start | bytes 393224 | tf_op jit(solution)/shard_map/while/body/eval_jaxpr/ppermute | solution.py:10
  601.7 11.7 %collective-permute-start = (f32[2,128,128]{2,1,0:T(8,128)S(1)}, f32[2,128,128]{2,1,0:T(8,128)S(1)}, u32[]{:S(2)}, u32[]{:S(2)}) collective-permute-start(f32[2,128,128]{2,1,0:T(8,128)S(1)} %get-tuple-element.784), channel_id=1, source_target_pairs={{0,4},{4,8},{8,12},{12,16},{16,20},{20,24},{24,28},{28,32},{32,36}... | collective-permute-start | bytes 393224 | tf_op jit(solution)/shard_map/while/body/eval_jaxpr/ppermute | solution.py:10
  620.5 11.0 %collective-permute-start = (f32[2,128,128]{2,1,0:T(8,128)S(1)}, f32[2,128,128]{2,1,0:T(8,128)S(1)}, u32[]{:S(2)}, u32[]{:S(2)}) collective-permute-start(f32[2,128,128]{2,1,0:T(8,128)S(1)} %get-tuple-element.784), channel_id=1, source_target_pairs={{0,4},{4,8},{8,12},{12,16},{16,20},{20,24},{24,28},{28,32},{32,36}... | collective-permute-start | bytes 393224 | tf_op jit(solution)/shard_map/while/body/eval_jaxpr/ppermute | solution.py:10
  638.6 12.4 %collective-permute-start = (f32[2,128,128]{2,1,0:T(8,128)S(1)}, f32[2,128,128]{2,1,0:T(8,128)S(1)}, u32[]{:S(2)}, u32[]{:S(2)}) collective-permute-start(f32[2,128,128]{2,1,0:T(8,128)S(1)} %get-tuple-element.784), channel_id=1, source_target_pairs={{0,4},{4,8},{8,12},{12,16},{16,20},{20,24},{24,28},{28,32},{32,36}... | collective-permute-start | bytes 393224 | tf_op jit(solution)/shard_map/while/body/eval_jaxpr/ppermute | solution.py:10
  659.1 12.0 %collective-permute-start = (f32[2,128,128]{2,1,0:T(8,128)S(1)}, f32[2,128,128]{2,1,0:T(8,128)S(1)}, u32[]{:S(2)}, u32[]{:S(2)}) collective-permute-start(f32[2,128,128]{2,1,0:T(8,128)S(1)} %get-tuple-element.784), channel_id=1, source_target_pairs={{0,4},{4,8},{8,12},{12,16},{16,20},{20,24},{24,28},{28,32},{32,36}... | collective-permute-start | bytes 393224 | tf_op jit(solution)/shard_map/while/body/eval_jaxpr/ppermute | solution.py:10
  677.2 12.5 %collective-permute-start = (f32[2,128,128]{2,1,0:T(8,128)S(1)}, f32[2,128,128]{2,1,0:T(8,128)S(1)}, u32[]{:S(2)}, u32[]{:S(2)}) collective-permute-start(f32[2,128,128]{2,1,0:T(8,128)S(1)} %get-tuple-element.784), channel_id=1, source_target_pairs={{0,4},{4,8},{8,12},{12,16},{16,20},{20,24},{24,28},{28,32},{32,36}... | collective-permute-start | bytes 393224 | tf_op jit(solution)/shard_map/while/body/eval_jaxpr/ppermute | solution.py:10
  710.2 56.2 %collective-permute-start.6 = (f32[4,4,130,1]{2,1,3,0:T(4,128)S(1)}, f32[4,4,130,1]{2,1,3,0:T(4,128)S(1)}, u32[]{:S(2)}, u32[]{:S(2)}) collective-permute-start(f32[4,4,130,1]{2,1,3,0:T(4,128)S(1)} %copy.32), channel_id=1, source_target_pairs={{1,0},{3,2},{5,4},{7,6},{9,8},{11,10},{13,12},{15,14},{17,16},{19,... | collective-permute-start | bytes 24968 | tf_op jit(solution)/shard_map/ppermute | solution.py:21
  (112 other events, 833.7 us)
where the time goes:
time: 785 us; the launch traced here: 773 us
  starting transfers between devices  387 us (49%)
  waiting for transfers between devices  215 us (27%)
  other arithmetic  146 us (19%)
  local copies, waits for them, and re-layouts  23.2 us (3%)
    ppermute x124, starting transfers between devices, from_behind(): return lax.ppermute(array, axis, pairs)  309 us
    ppermute x124, waiting for transfers between devices, from_behind(): return lax.ppermute(array, axis, pairs)  204 us
    ppermute x2, starting transfers between devices, padded_2(): lax.ppermute(lax.slice_in_dim(block, 0, width, axis=dim), axis, backward)  55.6 us
    scatter-add x1, other arithmetic, shards(): forcing = source.reshape(-1).at[flat_index].add(inject_values.reshape(-1))  53.6 us
    add x31, other arithmetic, relay_turn(): total_up[0] * below_imag + total_up[1] * below_real + total_up[3]  48.3 us
    add x31, other arithmetic, relay_turn(): total_down[0] * enter_imag + total_down[1] * enter_real + total_down[3]  28.2 us
  transfers between devices with their start and end apart: 130, of which 66 were waited for; matrix products, arithmetic and copies ran while one was open for 7% of the time, Pallas kernels for 0%

commit v1 on v0

--- a/solution.py
+++ b/solution.py
@@ -92,21 +92,31 @@
     )
     local_down, down_real, down_imag = down_parts
     local_up, up_real, up_imag = up_parts
-    total_down = (down_real[-1], down_imag[-1], local_down[-1][:, 0], local_down[-1][:, 1])
-    total_up = (up_real[0], up_imag[0], local_up[0][:, 0], local_up[0][:, 1])
+    shots_here = shot_count
 
-    def relay_turn(turn_index, carry):
-        enter_real, enter_imag, below_real, below_imag = carry
-        send_real = total_down[0] * enter_real - total_down[1] * enter_imag + total_down[2]
-        send_imag = total_down[0] * enter_imag + total_down[1] * enter_real + total_down[3]
-        rise_real = total_up[0] * below_real - total_up[1] * below_imag + total_up[2]
-        rise_imag = total_up[0] * below_imag + total_up[1] * below_real + total_up[3]
-        got_down = from_behind((send_real, send_imag), "slab", 1)
-        got_up = from_behind((rise_real, rise_imag), "slab", -1)
-        return (got_down[0], got_down[1], got_up[0], got_up[1])
+    def prefix_pair(a_re, a_im, b_re, b_im, sign):
+        step = 1
+        while step < slab_count:
+            final = 2 * step >= slab_count
+            parts = [b_re, b_im] if final else [a_re[None], a_im[None], b_re, b_im]
+            got = from_behind(jnp.concatenate(parts, axis=0), "slab", sign * step)
+            lead = 0 if final else 2
+            g_re = got[lead : lead + shots_here]
+            g_im = got[lead + shots_here :]
+            next_re = a_re * g_re - a_im * g_im + b_re
+            next_im = a_re * g_im + a_im * g_re + b_im
+            if not final:
+                a_re, a_im = a_re * got[0] - a_im * got[1], a_re * got[1] + a_im * got[0]
+            b_re, b_im = next_re, next_im
+            step *= 2
+        got = from_behind(jnp.concatenate([b_re, b_im], axis=0), "slab", sign)
+        return got[:shots_here], got[shots_here:]
 
-    enter_real, enter_imag, below_real, below_imag = lax.fori_loop(
-        0, slab_count - 1, relay_turn, (zeros, zeros, zeros, zeros)
+    enter_real, enter_imag = prefix_pair(
+        down_real[-1], down_imag[-1], local_down[-1][:, 0], local_down[-1][:, 1], 1
+    )
+    below_real, below_imag = prefix_pair(
+        up_real[0], up_imag[0], local_up[0][:, 0], local_up[0][:, 1], -1
     )
     full_down_real = (
         local_down[:, :, 0]

time: 785 us -> 223 us (0.28)
  the two profiles are of different devices: /device:TPU:1 before, /device:TPU:65 now
where the time goes in v1:
time: 223 us
  other arithmetic  79.1 us (35%)
  starting transfers between devices  67.7 us (30%)
  waiting for transfers between devices  56.3 us (25%)
  local copies, waits for them, and re-layouts  18.2 us (8%)
    scatter-add x1, other arithmetic, shards(): forcing = source.reshape(-1).at[flat_index].add(inject_values.reshape(-1))  53.7 us
    ppermute x12, waiting for transfers between devices, from_behind(): return lax.ppermute(array, axis, pairs)  46 us
    ppermute x12, starting transfers between devices, from_behind(): return lax.ppermute(array, axis, pairs)  31.8 us
    ppermute x2, starting transfers between devices, padded_2(): lax.ppermute(lax.slice_in_dim(block, 0, width, axis=dim), axis, backward)  15 us
    dynamic_update_slice x24, other arithmetic, shards(): lax.scan(advance, start_state, (real_mult, imag_mult, fields))  12.6 us
    all_to_all x1, starting transfers between devices, shards(): lax.all_to_all(send_places.reshape(1, slab_count, capacity), 'slab', spli...  8.13 us
    all_to_all x1, starting transfers between devices, shards(): lax.all_to_all(send_values.reshape(components, slab_count, capacity), 'sl...  7.42 us
    ppermute x2, starting transfers between devices, padded_2(): lax.ppermute(lax.slice_in_dim(block, block.shape[dim] - width, None, axis...  5.38 us
  transfers between devices with their start and end apart: 18, of which 11 were waited for; matrix products, arithmetic and copies ran while one was open for 10% of the time, Pallas kernels for 0%

profile of v1, /device:TPU:65, one launch (start us, length us, event | category | flops | bytes accessed | tf_op | source)
XLA Modules:
  0.0 222.5 jit_solution(3790902149109069546)
XLA Ops:
  2.3 2.5 %scatter_custom_fusion = s32[2048]{0:T(1024)S(1)} fusion(s32[512]{0:T(512)S(1)} %bitcast.204, s32[512]{0:T(512)S(1)} %bitcast.206, s32[]{:T(128)} %copy.105), kind=kCustom, calls=%fused_computation.123 | custom fusion | bytes 8196 | tf_op jit(solution)/shard_map/scatter | solution.py:58
  5.4 8.1 %all-to-all-start = ((s32[1,32,64]{2,0,1:T(1,128)}), s32[1,32,64]{2,0,1:T(1,128)S(1)}, u32[]{:S(2)}, u32[]{:S(2)}) async-start(s32[1,32,64]{2,0,1:T(1,128)} %reshape.138), calls=%async_computation | async-start | bytes 32768 | tf_op jit(solution)/shard_map/all_to_all | solution.py:67
  13.6 1.7 sine_multiply_fusion
  15.4 2.0 scatter_custom_fusion.1
  18.8 7.4 %all-to-all-start.1 = ((f32[32,1,256]{2,1,0:T(1,128)}), f32[32,1,256]{2,1,0:T(1,128)S(1)}, u32[]{:S(2)}, u32[]{:S(2)}) async-start(f32[32,1,256]{2,1,0:T(1,128)} %reshape.180), calls=%async_computation.1 | async-start | bytes 65536 | tf_op jit(solution)/shard_map/all_to_all | solution.py:60
  27.6 4.0 %all-to-all-done.1 = f32[32,1,256]{2,1,0:T(1,128)S(1)} async-done(((f32[32,1,256]{2,1,0:T(1,128)}), f32[32,1,256]{2,1,0:T(1,128)S(1)}, u32[]{:S(2)}, u32[]{:S(2)}) %all-to-all-start.1) | async-done | bytes 32800 | tf_op jit(solution)/shard_map/all_to_all | solution.py:60
  33.0 53.7 %scatter_fusion = f32[262144]{0:T(1024)S(1)} fusion(f32[262144]{0:T(1024)S(1)} %bitcast.177, s32[8192]{0:T(1024)S(1)} %bitcast.198, f32[8192]{0:T(1024)S(1)} %reshape.162), kind=kCustom, calls=%fused_computation.2 | custom fusion | flops 8192 | bytes 131072 | tf_op jit(solution)/shard_map/scatter-add | solution.py:79
  87.0 4.5 %while.49 = (s32[]{:T(128)}, f32[2,128,128]{2,1,0:T(8,128)S(1)}, f32[2,128,128]{2,1,0:T(8,128)S(1)}, f32[128,128]{1,0:T(8,128)S(1)}, f32[128,128]{1,0:T(8,128)S(...) while((s32[]{:T(128)}, f32[2,128,128]{2,1,0:T(8,128)S(1)}, ...), condition=%wide.region_9.10_spmd, body=%wide.region_8.9_spmd.sunk | while | flops 425987 | bytes 3014809 | solution.py:90
  92.5 5.4 %collective-permute-start.6 = (f32[6,128,128]{2,1,0:T(8,128)}, f32[6,128,128]{2,1,0:T(8,128)}, u32[]{:S(2)}, u32[]{:S(2)}) collective-permute-start(f32[6,128,128]{2,1,0:T(8,128)} %pad_maximum_fusion.13), channel_id=1, source_target_pairs={{4,0},{8,4},{12,8},{16,12},{20,16},{24,20},{28,24},{32,28},{36,32}... | collective-permute-start | bytes 1179656 | tf_op jit(solution)/shard_map/ppermute | solution.py:10
  99.6 9.5 %while.48 = (s32[]{:T(128)}, f32[2,128,128]{2,1,0:T(8,128)S(1)}, f32[2,128,128]{2,1,0:T(8,128)S(1)}, f32[128,128]{1,0:T(8,128)S(1)}, f32[128,128]{1,0:T(8,128)S(...) while((s32[]{:T(128)}, f32[2,128,128]{2,1,0:T(8,128)S(1)}, ...), condition=%wide.region_7.8_spmd, body=%wide.region_6.7_spmd.sunk | while | flops 425986 | bytes 3014797 | solution.py:89
  102.0 1.5 bitcast_dynamic-update-slice_fusion.8
  111.0 2.1 collective-permute-start
  115.0 2.2 collective-permute-start.7
  117.2 7.0 %collective-permute-done = f32[6,128,128]{2,1,0:T(8,128)S(1)} collective-permute-done((f32[6,128,128]{2,1,0:T(8,128)S(1)}, f32[6,128,128]{2,1,0:T(8,128)S(1)}, u32[]{:S(2)}, u32[]{:S(2)}) %collective-permute-start) | collective-permute-done | bytes 393248 | tf_op jit(solution)/shard_map/ppermute | solution.py:10
  124.4 1.9 collective-permute-start.1
  126.4 1.9 collective-permute-start.8
  128.4 16.5 %collective-permute-done.1 = f32[6,128,128]{2,1,0:T(8,128)S(1)} collective-permute-done((f32[6,128,128]{2,1,0:T(8,128)S(1)}, f32[6,128,128]{2,1,0:T(8,128)S(1)}, u32[]{:S(2)}, u32[]{:S(2)}) %collective-permute-start.1) | collective-permute-done | bytes 393248 | tf_op jit(solution)/shard_map/ppermute | solution.py:10
  145.0 1.9 collective-permute-start.2
  147.0 3.5 %collective-permute-start.9 = (f32[6,128,128]{2,1,0:T(8,128)S(1)}, f32[6,128,128]{2,1,0:T(8,128)S(1)}, u32[]{:S(2)}, u32[]{:S(2)}) collective-permute-start(f32[6,128,128]{2,1,0:T(8,128)S(1)} %pad_maximum_fusion.16), channel_id=1, source_target_pairs={{32,0},{36,4},{40,8},{44,12},{48,16},{52,20},{56,24},{60,28},{64,3... | collective-permute-start | bytes 1179656 | tf_op jit(solution)/shard_map/ppermute | solution.py:10
  150.5 5.8 %collective-permute-done.2 = f32[6,128,128]{2,1,0:T(8,128)S(1)} collective-permute-done((f32[6,128,128]{2,1,0:T(8,128)S(1)}, f32[6,128,128]{2,1,0:T(8,128)S(1)}, u32[]{:S(2)}, u32[]{:S(2)}) %collective-permute-start.2) | collective-permute-done | bytes 393248 | tf_op jit(solution)/shard_map/ppermute | solution.py:10
  156.5 1.9 collective-permute-start.3
  158.5 5.8 %collective-permute-start.10 = (f32[4,128,128]{2,1,0:T(8,128)S(1)}, f32[4,128,128]{2,1,0:T(8,128)S(1)}, u32[]{:S(2)}, u32[]{:S(2)}) collective-permute-start(f32[4,128,128]{2,1,0:T(8,128)S(1)} %pad_maximum_fusion.19), channel_id=1, source_target_pairs={{64,0},{68,4},{72,8},{76,12},{80,16},{84,20},{88,24},{92,28},{96,3... | collective-permute-start | bytes 786440 | tf_op jit(solution)/shard_map/ppermute | solution.py:10
  164.3 2.7 %collective-permute-done.3 = f32[6,128,128]{2,1,0:T(8,128)S(1)} collective-permute-done((f32[6,128,128]{2,1,0:T(8,128)S(1)}, f32[6,128,128]{2,1,0:T(8,128)S(1)}, u32[]{:S(2)}, u32[]{:S(2)}) %collective-permute-start.3) | collective-permute-done | bytes 393248 | tf_op jit(solution)/shard_map/ppermute | solution.py:10
  170.0 1.9 collective-permute-start.11
  172.0 3.8 %collective-permute-done.4 = f32[4,128,128]{2,1,0:T(8,128)S(1)} collective-permute-done((f32[4,128,128]{2,1,0:T(8,128)S(1)}, f32[4,128,128]{2,1,0:T(8,128)S(1)}, u32[]{:S(2)}, u32[]{:S(2)}) %collective-permute-start.4) | collective-permute-done | bytes 262176 | tf_op jit(solution)/shard_map/ppermute | solution.py:10
  175.8 1.9 collective-permute-start.5
  177.8 8.6 %collective-permute-done.5 = f32[4,128,128]{2,1,0:T(8,128)S(1)} collective-permute-done((f32[4,128,128]{2,1,0:T(8,128)S(1)}, f32[4,128,128]{2,1,0:T(8,128)S(1)}, u32[]{:S(2)}, u32[]{:S(2)}) %collective-permute-start.5) | collective-permute-done | bytes 262176 | tf_op jit(solution)/shard_map/ppermute | solution.py:10
  187.3 4.1 %collective-permute-start.13 = (f32[4,4,1,128]{3,2,1,0:T(1,128)S(1)}, f32[4,4,1,128]{3,2,1,0:T(1,128)S(1)}, u32[]{:S(2)}, u32[]{:S(2)}) collective-permute-start(f32[4,4,1,128]{3,2,1,0:T(1,128)S(1)} %get-tuple-element.421), channel_id=1, source_target_pairs={{0,2},{1,3},{4,6},{5,7},{8,10},{9,11},{12,14},{13,15},{16,18},{17,... | collective-permute-start | bytes 24584 | tf_op jit(solution)/shard_map/ppermute | solution.py:18
  192.7 4.6 %collective-permute-done.12 = f32[4,4,1,128]{3,2,1,0:T(1,128)S(1)} collective-permute-done((f32[4,4,1,128]{3,2,1,0:T(1,128)S(1)}, f32[4,4,1,128]{3,2,1,0:T(1,128)S(1)}, u32[]{:S(2)}, u32[]{:S(2)}) %collective-permute-start.12) | collective-permute-done | bytes 8224 | tf_op jit(solution)/shard_map/ppermute | solution.py:21
  198.7 1.9 copy.32
  200.6 13.7 %collective-permute-start.14 = (f32[4,4,130,1]{2,1,3,0:T(4,128)S(1)}, f32[4,4,130,1]{2,1,3,0:T(4,128)S(1)}, u32[]{:S(2)}, u32[]{:S(2)}) collective-permute-start(f32[4,4,130,1]{2,1,3,0:T(4,128)S(1)} %copy.32), channel_id=1, source_target_pairs={{1,0},{3,2},{5,4},{7,6},{9,8},{11,10},{13,12},{15,14},{17,16},{19,... | collective-permute-start | bytes 24968 | tf_op jit(solution)/shard_map/ppermute | solution.py:21
  219.4 3.1 %fusion.9 = f32[4,4,128,128]{3,2,1,0:T(8,128)} fusion(f32[4,4,128,128]{3,2,1,0:T(8,128)S(1)} %sub.159, f32[4,4,130,1]{3,2,1,0:T(8,128)} %copy.35, f32[4,4,1,128]{3,2,1,0:T(1,128)S(1)} %collective-permute-done.12, f32[4,4,1,128]{3,2,1,0:T(1,128)S(1)} %collective-permute-done.13, f32[4,4,130,1]{3,2,1,0:T(8,128)S(1)} %copy.33), kind=kLoop, calls=%fused_computation.36 | loop fusion | flops 3932160 | bytes 2130176 | tf_op jit(solution)/shard_map/sub | solution.py:151
  (183 shorter events, 38.0 us)
Async XLA Ops:
  0.0 13.5 %copy-start.12 = (s32[128,128]{1,0:T(8,128)S(1)}, s32[128,128]{1,0:T(8,128)}, u32[]{:S(2)}) copy-start(s32[128,128]{1,0:T(8,128)} %param.15) | copy-start | bytes 196612
  0.0 13.6 %copy-start.11 = (f32[4,128,128]{2,1,0:T(8,128)S(1)}, f32[4,128,128]{2,1,0:T(8,128)}, u32[]{:S(2)}) copy-start(f32[4,128,128]{2,1,0:T(8,128)} %param.14) | copy-start | bytes 786436
  0.0 13.6 %copy-start.10 = (f32[4,128,128]{2,1,0:T(8,128)S(1)}, f32[4,128,128]{2,1,0:T(8,128)}, u32[]{:S(2)}) copy-start(f32[4,128,128]{2,1,0:T(8,128)} %param.13) | copy-start | bytes 786436
  0.0 15.2 %copy-start.14 = (f32[1,1,4,512]{3,2,1,0:T(4,128)S(1)}, f32[1,1,4,512]{3,2,1,0:T(4,128)}, u32[]{:S(2)}) copy-start(f32[1,1,4,512]{3,2,1,0:T(4,128)} %param.16) | copy-start | bytes 24580
  5.4 13.4 %all-to-all-start = ((s32[1,32,64]{2,0,1:T(1,128)}), s32[1,32,64]{2,0,1:T(1,128)S(1)}, u32[]{:S(2)}, u32[]{:S(2)}) async-start(s32[1,32,64]{2,0,1:T(1,128)} %reshape.138), calls=%async_computation | async-start | bytes 32768 | tf_op jit(solution)/shard_map/all_to_all | solution.py:67
  17.4 15.6 %copy-start = (f32[4,4,128,128]{3,2,1,0:T(8,128)S(1)}, f32[4,4,128,128]{3,2,1,0:T(8,128)}, u32[]{:S(2)}) copy-start(f32[4,4,128,128]{3,2,1,0:T(8,128)} %param.12) | copy-start | bytes 3145732
  18.8 12.8 %all-to-all-start.1 = ((f32[32,1,256]{2,1,0:T(1,128)}), f32[32,1,256]{2,1,0:T(1,128)S(1)}, u32[]{:S(2)}, u32[]{:S(2)}) async-start(f32[32,1,256]{2,1,0:T(1,128)} %reshape.180), calls=%async_computation.1 | async-start | bytes 65536 | tf_op jit(solution)/shard_map/all_to_all | solution.py:60
  91.5 6.5 %copy-start.1 = (f32[4,128,128]{2,1,0:T(8,128)}, f32[4,128,128]{2,1,0:T(8,128)S(1)}, u32[]{:S(2)}) copy-start(f32[4,128,128]{2,1,0:T(8,128)S(1)} %get-tuple-element.718) | copy-start | bytes 786436
  91.5 6.5 %copy-start.6 = (f32[4,128,128]{2,1,0:T(8,128)}, f32[4,128,128]{2,1,0:T(8,128)S(1)}, u32[]{:S(2)}) copy-start(f32[4,128,128]{2,1,0:T(8,128)S(1)} %get-tuple-element.288) | copy-start | bytes 786436
  91.5 6.5 %copy-start.8 = (f32[4,128,128]{2,1,0:T(8,128)}, f32[4,128,128]{2,1,0:T(8,128)S(1)}, u32[]{:S(2)}) copy-start(f32[4,128,128]{2,1,0:T(8,128)S(1)} %get-tuple-element.287) | copy-start | bytes 786436
  91.5 6.4 %copy-start.2 = (f32[2,2,128,128]{3,2,0,1:T(8,128)}, f32[2,2,128,128]{3,2,0,1:T(8,128)S(1)}, u32[]{:S(2)}) copy-start(f32[2,2,128,128]{3,2,0,1:T(8,128)S(1)} %slice_bitcast_fusion.4) | copy-start | bytes 786436
  92.5 20.5 %collective-permute-start.6 = (f32[6,128,128]{2,1,0:T(8,128)}, f32[6,128,128]{2,1,0:T(8,128)}, u32[]{:S(2)}, u32[]{:S(2)}) collective-permute-start(f32[6,128,128]{2,1,0:T(8,128)} %pad_maximum_fusion.13), channel_id=1, source_target_pairs={{4,0},{8,4},{12,8},{16,12},{20,16},{24,20},{28,24},{32,28},{36,32}... | collective-permute-start | bytes 1179656 | tf_op jit(solution)/shard_map/ppermute | solution.py:10
  109.1 4.0 %copy-start.7 = (f32[4,128,128]{2,1,0:T(8,128)S(1)}, f32[4,128,128]{2,1,0:T(8,128)}, u32[]{:S(2)}) copy-start(f32[4,128,128]{2,1,0:T(8,128)} %copy-done.6) | copy-start | bytes 786436
  109.1 4.0 %copy-start.9 = (f32[4,128,128]{2,1,0:T(8,128)S(1)}, f32[4,128,128]{2,1,0:T(8,128)}, u32[]{:S(2)}) copy-start(f32[4,128,128]{2,1,0:T(8,128)} %copy-done.8) | copy-start | bytes 786436
  109.1 4.8 %copy-start.3 = (f32[2,2,128,128]{3,2,0,1:T(8,128)S(1)}, f32[2,2,128,128]{3,2,0,1:T(8,128)}, u32[]{:S(2)}) copy-start(f32[2,2,128,128]{3,2,0,1:T(8,128)} %copy-done.2) | copy-start | bytes 786436
  111.0 13.3 %copy-start.4 = (f32[4,128,128]{2,1,0:T(8,128)S(1)}, f32[4,128,128]{2,1,0:T(8,128)}, u32[]{:S(2)}) copy-start(f32[4,128,128]{2,1,0:T(8,128)} %get-tuple-element.284) | copy-start | bytes 786436
  111.0 13.3 %copy-start.5 = (f32[4,128,128]{2,1,0:T(8,128)S(1)}, f32[4,128,128]{2,1,0:T(8,128)}, u32[]{:S(2)}) copy-start(f32[4,128,128]{2,1,0:T(8,128)} %get-tuple-element.285) | copy-start | bytes 786436
  111.0 13.3 %collective-permute-start = (f32[6,128,128]{2,1,0:T(8,128)S(1)}, f32[6,128,128]{2,1,0:T(8,128)S(1)}, u32[]{:S(2)}, u32[]{:S(2)}) collective-permute-start(f32[6,128,128]{2,1,0:T(8,128)S(1)} %pad_maximum_fusion.9), channel_id=1, source_target_pairs={{0,4},{4,8},{8,12},{12,16},{16,20},{20,24},{24,28},{28,32},{32,36}... | collective-permute-start | bytes 1179656 | tf_op jit(solution)/shard_map/ppermute | solution.py:10
  115.0 11.3 %collective-permute-start.7 = (f32[6,128,128]{2,1,0:T(8,128)S(1)}, f32[6,128,128]{2,1,0:T(8,128)S(1)}, u32[]{:S(2)}, u32[]{:S(2)}) collective-permute-start(f32[6,128,128]{2,1,0:T(8,128)S(1)} %pad_maximum_fusion.14), channel_id=1, source_target_pairs={{8,0},{12,4},{16,8},{20,12},{24,16},{28,20},{32,24},{36,28},{40,32... | collective-permute-start | bytes 1179656 | tf_op jit(solution)/shard_map/ppermute | solution.py:10
  124.4 20.5 %collective-permute-start.1 = (f32[6,128,128]{2,1,0:T(8,128)S(1)}, f32[6,128,128]{2,1,0:T(8,128)S(1)}, u32[]{:S(2)}, u32[]{:S(2)}) collective-permute-start(f32[6,128,128]{2,1,0:T(8,128)S(1)} %pad_maximum_fusion.10), channel_id=1, source_target_pairs={{0,8},{4,12},{8,16},{12,20},{16,24},{20,28},{24,32},{28,36},{32,40... | collective-permute-start | bytes 1179656 | tf_op jit(solution)/shard_map/ppermute | solution.py:10
  126.4 20.5 %collective-permute-start.8 = (f32[6,128,128]{2,1,0:T(8,128)S(1)}, f32[6,128,128]{2,1,0:T(8,128)S(1)}, u32[]{:S(2)}, u32[]{:S(2)}) collective-permute-start(f32[6,128,128]{2,1,0:T(8,128)S(1)} %pad_maximum_fusion.15), channel_id=1, source_target_pairs={{16,0},{20,4},{24,8},{28,12},{32,16},{36,20},{40,24},{44,28},{48,3... | collective-permute-start | bytes 1179656 | tf_op jit(solution)/shard_map/ppermute | solution.py:10
  145.0 11.4 %collective-permute-start.2 = (f32[6,128,128]{2,1,0:T(8,128)S(1)}, f32[6,128,128]{2,1,0:T(8,128)S(1)}, u32[]{:S(2)}, u32[]{:S(2)}) collective-permute-start(f32[6,128,128]{2,1,0:T(8,128)S(1)} %pad_maximum_fusion.11), channel_id=1, source_target_pairs={{0,16},{4,20},{8,24},{12,28},{16,32},{20,36},{24,40},{28,44},{32,4... | collective-permute-start | bytes 1179656 | tf_op jit(solution)/shard_map/ppermute | solution.py:10
  147.0 11.4 %collective-permute-start.9 = (f32[6,128,128]{2,1,0:T(8,128)S(1)}, f32[6,128,128]{2,1,0:T(8,128)S(1)}, u32[]{:S(2)}, u32[]{:S(2)}) collective-permute-start(f32[6,128,128]{2,1,0:T(8,128)S(1)} %pad_maximum_fusion.16), channel_id=1, source_target_pairs={{32,0},{36,4},{40,8},{44,12},{48,16},{52,20},{56,24},{60,28},{64,3... | collective-permute-start | bytes 1179656 | tf_op jit(solution)/shard_map/ppermute | solution.py:10
  156.5 10.6 %collective-permute-start.3 = (f32[6,128,128]{2,1,0:T(8,128)S(1)}, f32[6,128,128]{2,1,0:T(8,128)S(1)}, u32[]{:S(2)}, u32[]{:S(2)}) collective-permute-start(f32[6,128,128]{2,1,0:T(8,128)S(1)} %pad_maximum_fusion.12), channel_id=1, source_target_pairs={{0,32},{4,36},{8,40},{12,44},{16,48},{20,52},{24,56},{28,60},{32,6... | collective-permute-start | bytes 1179656 | tf_op jit(solution)/shard_map/ppermute | solution.py:10
  158.5 11.5 %collective-permute-start.10 = (f32[4,128,128]{2,1,0:T(8,128)S(1)}, f32[4,128,128]{2,1,0:T(8,128)S(1)}, u32[]{:S(2)}, u32[]{:S(2)}) collective-permute-start(f32[4,128,128]{2,1,0:T(8,128)S(1)} %pad_maximum_fusion.19), channel_id=1, source_target_pairs={{64,0},{68,4},{72,8},{76,12},{80,16},{84,20},{88,24},{92,28},{96,3... | collective-permute-start | bytes 786440 | tf_op jit(solution)/shard_map/ppermute | solution.py:10
  167.1 8.6 %collective-permute-start.4 = (f32[4,128,128]{2,1,0:T(8,128)S(1)}, f32[4,128,128]{2,1,0:T(8,128)S(1)}, u32[]{:S(2)}, u32[]{:S(2)}) collective-permute-start(f32[4,128,128]{2,1,0:T(8,128)S(1)} %pad_maximum_fusion.17), channel_id=1, source_target_pairs={{0,64},{4,68},{8,72},{12,76},{16,80},{20,84},{24,88},{28,92},{32,9... | collective-permute-start | bytes 786440 | tf_op jit(solution)/shard_map/ppermute | solution.py:10
  170.0 7.7 %collective-permute-start.11 = (f32[4,128,128]{2,1,0:T(8,128)S(1)}, f32[4,128,128]{2,1,0:T(8,128)S(1)}, u32[]{:S(2)}, u32[]{:S(2)}) collective-permute-start(f32[4,128,128]{2,1,0:T(8,128)S(1)} %pad_maximum_fusion.20), channel_id=1, source_target_pairs={{4,0},{8,4},{12,8},{16,12},{20,16},{24,20},{28,24},{32,28},{36,32}... | collective-permute-start | bytes 786440 | tf_op jit(solution)/shard_map/ppermute | solution.py:10
  175.8 10.6 %collective-permute-start.5 = (f32[4,128,128]{2,1,0:T(8,128)S(1)}, f32[4,128,128]{2,1,0:T(8,128)S(1)}, u32[]{:S(2)}, u32[]{:S(2)}) collective-permute-start(f32[4,128,128]{2,1,0:T(8,128)S(1)} %pad_maximum_fusion.18), channel_id=1, source_target_pairs={{0,4},{4,8},{8,12},{12,16},{16,20},{20,24},{24,28},{28,32},{32,36}... | collective-permute-start | bytes 786440 | tf_op jit(solution)/shard_map/ppermute | solution.py:10
  187.3 5.4 %collective-permute-start.13 = (f32[4,4,1,128]{3,2,1,0:T(1,128)S(1)}, f32[4,4,1,128]{3,2,1,0:T(1,128)S(1)}, u32[]{:S(2)}, u32[]{:S(2)}) collective-permute-start(f32[4,4,1,128]{3,2,1,0:T(1,128)S(1)} %get-tuple-element.421), channel_id=1, source_target_pairs={{0,2},{1,3},{4,6},{5,7},{8,10},{9,11},{12,14},{13,15},{16,18},{17,... | collective-permute-start | bytes 24584 | tf_op jit(solution)/shard_map/ppermute | solution.py:18
  191.4 5.9 %collective-permute-start.12 = (f32[4,4,1,128]{3,2,1,0:T(1,128)S(1)}, f32[4,4,1,128]{3,2,1,0:T(1,128)S(1)}, u32[]{:S(2)}, u32[]{:S(2)}) collective-permute-start(f32[4,4,1,128]{3,2,1,0:T(1,128)S(1)} %get-tuple-element.422), channel_id=1, source_target_pairs={{2,0},{3,1},{6,4},{7,5},{10,8},{11,9},{14,12},{15,13},{18,16},{19,... | collective-permute-start | bytes 24584 | tf_op jit(solution)/shard_map/ppermute | solution.py:21
  200.6 15.6 %collective-permute-start.14 = (f32[4,4,130,1]{2,1,3,0:T(4,128)S(1)}, f32[4,4,130,1]{2,1,3,0:T(4,128)S(1)}, u32[]{:S(2)}, u32[]{:S(2)}) collective-permute-start(f32[4,4,130,1]{2,1,3,0:T(4,128)S(1)} %copy.32), channel_id=1, source_target_pairs={{1,0},{3,2},{5,4},{7,6},{9,8},{11,10},{13,12},{15,14},{17,16},{19,... | collective-permute-start | bytes 24968 | tf_op jit(solution)/shard_map/ppermute | solution.py:21
  214.9 3.1 %collective-permute-start.15 = (f32[4,4,130,1]{2,1,3,0:T(4,128)S(1)}, f32[4,4,130,1]{2,1,3,0:T(4,128)S(1)}, u32[]{:S(2)}, u32[]{:S(2)}) collective-permute-start(f32[4,4,130,1]{2,1,3,0:T(4,128)S(1)} %copy.34), channel_id=1, source_target_pairs={{0,1},{2,3},{4,5},{6,7},{8,9},{10,11},{12,13},{14,15},{16,17},{18,... | collective-permute-start | bytes 24968 | tf_op jit(solution)/shard_map/ppermute | solution.py:18
  (3 other events, 5.2 us)

commit v2 on v1

--- a/solution.py
+++ b/solution.py
@@ -46,37 +46,41 @@
     capacity = rows_here // min(8, slab_count)
     values = recv_values[0, 0]
     target_slab = recv_slab[0, 0, :, 0]
-    position = recv_layer[0, 0] * (components * plane_size) + recv_lateral[0, 0]
+    position = recv_layer[0, 0] * plane_size + recv_lateral[0, 0]
     one_hot = (target_slab[:, None] == jnp.arange(slab_count, dtype=jnp.int32)[None, :]).astype(
         jnp.int32
     )
     ranking = jnp.sum((jnp.cumsum(one_hot, axis=0) - one_hot) * one_hot, axis=1)
     target_slot = target_slab * capacity + ranking
-    send_values = (
-        jnp.zeros((components, slab_count * capacity), jnp.float32).at[:, target_slot].set(values)
-    )
-    send_places = jnp.zeros((slab_count * capacity,), jnp.int32).at[target_slot].set(position)
-    got_values, got_places = (
-        lax.all_to_all(
-            send_values.reshape(components, slab_count, capacity),
-            "slab",
-            split_axis=1,
-            concat_axis=1,
-            tiled=True,
-        ),
-        lax.all_to_all(
-            send_places.reshape(1, slab_count, capacity),
-            "slab",
-            split_axis=1,
-            concat_axis=1,
-            tiled=True,
-        ),
-    )
-    inject_values = got_values.reshape(components, slab_count * capacity)
-    inject_places = got_places.reshape(slab_count * capacity)
-    offsets = (jnp.arange(components, dtype=jnp.int32) * plane_size)[:, None]
-    flat_index = (inject_places[None, :] + offsets).reshape(-1)
-    forcing = source.reshape(-1).at[flat_index].add(inject_values.reshape(-1))
+    rows = jnp.concatenate([values, position.astype(jnp.float32)[None, :]], axis=0)
+    send_rows = jnp.zeros((components + 1, slab_count * capacity), jnp.float32).at[:, target_slot].set(rows)
+    got_rows = lax.all_to_all(
+        send_rows.reshape(components + 1, slab_count, capacity),
+        "slab",
+        split_axis=1,
+        concat_axis=1,
+        tiled=True,
+    ).reshape(components + 1, slab_count * capacity)
+    inject_values = got_rows[:components]
+    inject_places = got_rows[components].astype(jnp.int32)
+    row_of = inject_places // width_y
+    col_of = inject_places % width_y
+    pick_rows = (
+        row_of[None, :] == jnp.arange(layers * width_x, dtype=jnp.int32)[:, None]
+    ).astype(jnp.bfloat16)
+    pick_cols = col_of[:, None] == jnp.arange(width_y, dtype=jnp.int32)[None, :]
+    high = lax.reduce_precision(inject_values, exponent_bits=8, mantissa_bits=7)
+    rest = inject_values - high
+    middle = lax.reduce_precision(rest, exponent_bits=8, mantissa_bits=7)
+    low = rest - middle
+    pieces = jnp.stack([high, middle, low], axis=0)
+    spread = jnp.where(pick_cols[None, None, :, :], pieces[:, :, :, None], 0.0)
+    spread = jnp.transpose(spread, (2, 0, 1, 3)).reshape(slab_count * capacity, 3 * components * width_y)
+    added = jnp.dot(pick_rows, spread.astype(jnp.bfloat16), preferred_element_type=jnp.float32)
+    added = added.reshape(layers * width_x, 3, components * width_y)
+    added = (added[:, 0] + added[:, 1]) + added[:, 2]
+    added = jnp.transpose(added.reshape(layers, width_x, components, width_y), (0, 2, 1, 3))
+    forcing = source + added
     fields = forcing.reshape(layers, shot_count, 2, width_x, width_y)
     damping = attenuation + 0.5 / depth_total * pml_level.astype(jnp.float32)[None, :, :]
     amplitude = jnp.exp(-damping)

time: 223 us -> 163 us (0.73)
  the two profiles are of different devices: /device:TPU:65 before, /device:TPU:63 now
where the time goes in v2:
time: 163 us; the launch traced here: 162 us
  starting transfers between devices  58.2 us (36%)
  waiting for transfers between devices  54.1 us (33%)
  other arithmetic  28.2 us (17%)
  local copies, waits for them, and re-layouts  17.1 us (10%)
  matrix products  3.53 us (2%)
    ppermute x12, waiting for transfers between devices, from_behind(): return lax.ppermute(array, axis, pairs)  45.3 us
    ppermute x12, starting transfers between devices, from_behind(): return lax.ppermute(array, axis, pairs)  31.2 us
    ppermute x2, starting transfers between devices, padded_2(): lax.ppermute(lax.slice_in_dim(block, 0, width, axis=dim), axis, backward)  16.2 us
    dynamic_update_slice x24, other arithmetic, shards(): lax.scan(advance, start_state, (real_mult, imag_mult, fields))  9.2 us
    all_to_all x1, starting transfers between devices, shards(): lax.all_to_all(send_rows.reshape(components + 1, slab_count, capacity), '...  8.21 us
    ppermute x2, waiting for transfers between devices, padded_2(): lax.ppermute(lax.slice_in_dim(block, block.shape[dim] - width, None, axis...  5.63 us
    dot_general x1, matrix products, shards(): jnp.dot(pick_rows, spread.astype(jnp.bfloat16), preferred_element_type=jn...  3.53 us
    slice x2, local copies, waits for them, and re-layouts, padded_2(): lax.slice_in_dim(block, 0, width, axis=dim)  3.47 us
  transfers between devices with their start and end apart: 17, of which 10 were waited for; matrix products, arithmetic and copies ran while one was open for 11% of the time, Pallas kernels for 0%

profile of v2, /device:TPU:63, one launch (start us, length us, event | category | flops | bytes accessed | tf_op | source)
XLA Modules:
  0.0 162.3 jit_solution(10250692008112379645)
XLA Ops:
  5.2 2.0 %scatter_custom_fusion = f32[5,2048]{0,1:T(8,128)S(1)} fusion(s32[512]{0:T(512)S(1)} %bitcast.212, f32[512,5]{1,0:T(8,128)S(1)} %copy.66, f32[]{:T(128)} %constant.96.clone.1), kind=kCustom, calls=%fused_computation.58 | custom fusion | bytes 40964 | tf_op jit(solution)/shard_map/scatter | solution.py:56
  8.3 8.2 %all-to-all-start = ((f32[32,1,320]{2,1,0:T(1,128)}), f32[32,1,320]{2,1,0:T(1,128)S(1)}, u32[]{:S(2)}, u32[]{:S(2)}) async-start(f32[32,1,320]{2,1,0:T(1,128)} %reshape.249), calls=%async_computation | async-start | bytes 98304 | tf_op jit(solution)/shard_map/all_to_all | solution.py:57
  17.6 3.1 %all-to-all-done = f32[32,1,320]{2,1,0:T(1,128)S(1)} async-done(((f32[32,1,320]{2,1,0:T(1,128)}), f32[32,1,320]{2,1,0:T(1,128)S(1)}, u32[]{:S(2)}, u32[]{:S(2)}) %all-to-all-start) | async-done | bytes 40992 | tf_op jit(solution)/shard_map/all_to_all | solution.py:57
  23.5 3.5 %fusion.7 = f32[512,3,512]{2,0,1:T(8,128)S(1)} fusion(bf16[3,512,2048]{2,1,0:T(8,128)(2,1)S(1)} %bitcast.190, s32[2048]{0:T(1024)S(1)} %get-tuple-element.542), kind=kOutput, calls=%fused_computation.32 | convolution fusion | flops 3222274048 | bytes 9445376 | tf_op jit(solution)/shard_map/dot_general | solution.py:79
  27.7 2.0 %bitcast_add_fusion = f32[4,4,128,128]{3,1,2,0:T(4,128)S(1)} fusion(f32[4,128,4,128]{3,2,1,0:T(4,128)S(1)} %add.334, f32[4,4,128,128]{3,2,1,0:T(8,128)} %param.12), kind=kLoop, calls=%fused_computation.52 | loop fusion | flops 262144 | bytes 3145728 | tf_op jit(solution)/shard_map/add | solution.py:83
  32.4 4.4 %collective-permute-start = (f32[6,128,128]{2,1,0:T(8,128)}, f32[6,128,128]{2,1,0:T(8,128)}, u32[]{:S(2)}, u32[]{:S(2)}) collective-permute-start(f32[6,128,128]{2,1,0:T(8,128)} %pad_maximum_fusion.9), channel_id=1, source_target_pairs={{0,4},{4,8},{8,12},{12,16},{16,20},{20,24},{24,28},{28,32},{32,36}... | collective-permute-start | bytes 1179656 | tf_op jit(solution)/shard_map/ppermute | solution.py:10
  38.4 9.5 %while.49 = (s32[]{:T(128)}, f32[2,128,128]{2,1,0:T(8,128)S(1)}, f32[2,128,128]{2,1,0:T(8,128)S(1)}, f32[128,128]{1,0:T(8,128)S(1)}, f32[128,128]{1,0:T(8,128)S(...) while((s32[]{:T(128)}, f32[2,128,128]{2,1,0:T(8,128)S(1)}, ...), condition=%wide.region_7.8_spmd, body=%wide.region_6.7_spmd.sunk | while | flops 425987 | bytes 3539097 | solution.py:94
  43.1 1.5 bitcast_dynamic-update-slice_fusion.10
  49.8 2.1 %collective-permute-start.6 = (f32[6,128,128]{2,1,0:T(8,128)S(1)}, f32[6,128,128]{2,1,0:T(8,128)S(1)}, u32[]{:S(2)}, u32[]{:S(2)}) collective-permute-start(f32[6,128,128]{2,1,0:T(8,128)S(1)} %pad_maximum_fusion.13), channel_id=1, source_target_pairs={{4,0},{8,4},{12,8},{16,12},{20,16},{24,20},{28,24},{32,28},{36,32}... | collective-permute-start | bytes 1179656 | tf_op jit(solution)/shard_map/ppermute | solution.py:10
  53.8 2.7 %collective-permute-start.1 = (f32[6,128,128]{2,1,0:T(8,128)S(1)}, f32[6,128,128]{2,1,0:T(8,128)S(1)}, u32[]{:S(2)}, u32[]{:S(2)}) collective-permute-start(f32[6,128,128]{2,1,0:T(8,128)S(1)} %pad_maximum_fusion.10), channel_id=1, source_target_pairs={{0,8},{4,12},{8,16},{12,20},{16,24},{20,28},{24,32},{28,36},{32,40... | collective-permute-start | bytes 1179656 | tf_op jit(solution)/shard_map/ppermute | solution.py:10
  56.5 6.6 %collective-permute-done.6 = f32[6,128,128]{2,1,0:T(8,128)S(1)} collective-permute-done((f32[6,128,128]{2,1,0:T(8,128)S(1)}, f32[6,128,128]{2,1,0:T(8,128)S(1)}, u32[]{:S(2)}, u32[]{:S(2)}) %collective-permute-start.6) | collective-permute-done | bytes 393248 | tf_op jit(solution)/shard_map/ppermute | solution.py:10
  63.3 1.9 %collective-permute-start.7 = (f32[6,128,128]{2,1,0:T(8,128)S(1)}, f32[6,128,128]{2,1,0:T(8,128)S(1)}, u32[]{:S(2)}, u32[]{:S(2)}) collective-permute-start(f32[6,128,128]{2,1,0:T(8,128)S(1)} %pad_maximum_fusion.14), channel_id=1, source_target_pairs={{8,0},{12,4},{16,8},{20,12},{24,16},{28,20},{32,24},{36,28},{40,32... | collective-permute-start | bytes 1179656 | tf_op jit(solution)/shard_map/ppermute | solution.py:10
  65.3 1.9 %collective-permute-start.2 = (f32[6,128,128]{2,1,0:T(8,128)S(1)}, f32[6,128,128]{2,1,0:T(8,128)S(1)}, u32[]{:S(2)}, u32[]{:S(2)}) collective-permute-start(f32[6,128,128]{2,1,0:T(8,128)S(1)} %pad_maximum_fusion.11), channel_id=1, source_target_pairs={{0,16},{4,20},{8,24},{12,28},{16,32},{20,36},{24,40},{28,44},{32,4... | collective-permute-start | bytes 1179656 | tf_op jit(solution)/shard_map/ppermute | solution.py:10
  67.2 16.6 %collective-permute-done.7 = f32[6,128,128]{2,1,0:T(8,128)S(1)} collective-permute-done((f32[6,128,128]{2,1,0:T(8,128)S(1)}, f32[6,128,128]{2,1,0:T(8,128)S(1)}, u32[]{:S(2)}, u32[]{:S(2)}) %collective-permute-start.7) | collective-permute-done | bytes 393248 | tf_op jit(solution)/shard_map/ppermute | solution.py:10
  84.0 2.1 %collective-permute-start.8 = (f32[6,128,128]{2,1,0:T(8,128)S(1)}, f32[6,128,128]{2,1,0:T(8,128)S(1)}, u32[]{:S(2)}, u32[]{:S(2)}) collective-permute-start(f32[6,128,128]{2,1,0:T(8,128)S(1)} %pad_maximum_fusion.15), channel_id=1, source_target_pairs={{16,0},{20,4},{24,8},{28,12},{32,16},{36,20},{40,24},{44,28},{48,3... | collective-permute-start | bytes 1179656 | tf_op jit(solution)/shard_map/ppermute | solution.py:10
  86.2 3.5 %collective-permute-start.3 = (f32[6,128,128]{2,1,0:T(8,128)S(1)}, f32[6,128,128]{2,1,0:T(8,128)S(1)}, u32[]{:S(2)}, u32[]{:S(2)}) collective-permute-start(f32[6,128,128]{2,1,0:T(8,128)S(1)} %pad_maximum_fusion.12), channel_id=1, source_target_pairs={{0,32},{4,36},{8,40},{12,44},{16,48},{20,52},{24,56},{28,60},{32,6... | collective-permute-start | bytes 1179656 | tf_op jit(solution)/shard_map/ppermute | solution.py:10
  89.8 5.8 %collective-permute-done.8 = f32[6,128,128]{2,1,0:T(8,128)S(1)} collective-permute-done((f32[6,128,128]{2,1,0:T(8,128)S(1)}, f32[6,128,128]{2,1,0:T(8,128)S(1)}, u32[]{:S(2)}, u32[]{:S(2)}) %collective-permute-start.8) | collective-permute-done | bytes 393248 | tf_op jit(solution)/shard_map/ppermute | solution.py:10
  95.7 3.1 %collective-permute-start.9 = (f32[6,128,128]{2,1,0:T(8,128)S(1)}, f32[6,128,128]{2,1,0:T(8,128)S(1)}, u32[]{:S(2)}, u32[]{:S(2)}) collective-permute-start(f32[6,128,128]{2,1,0:T(8,128)S(1)} %pad_maximum_fusion.16), channel_id=1, source_target_pairs={{32,0},{36,4},{40,8},{44,12},{48,16},{52,20},{56,24},{60,28},{64,3... | collective-permute-start | bytes 1179656 | tf_op jit(solution)/shard_map/ppermute | solution.py:10
  98.8 4.4 %collective-permute-start.4 = (f32[4,128,128]{2,1,0:T(8,128)S(1)}, f32[4,128,128]{2,1,0:T(8,128)S(1)}, u32[]{:S(2)}, u32[]{:S(2)}) collective-permute-start(f32[4,128,128]{2,1,0:T(8,128)S(1)} %pad_maximum_fusion.17), channel_id=1, source_target_pairs={{0,64},{4,68},{8,72},{12,76},{16,80},{20,84},{24,88},{28,92},{32,9... | collective-permute-start | bytes 786440 | tf_op jit(solution)/shard_map/ppermute | solution.py:10
  103.2 2.6 %collective-permute-done.9 = f32[6,128,128]{2,1,0:T(8,128)S(1)} collective-permute-done((f32[6,128,128]{2,1,0:T(8,128)S(1)}, f32[6,128,128]{2,1,0:T(8,128)S(1)}, u32[]{:S(2)}, u32[]{:S(2)}) %collective-permute-start.9) | collective-permute-done | bytes 393248 | tf_op jit(solution)/shard_map/ppermute | solution.py:10
  107.3 1.9 %collective-permute-done.4 = f32[4,128,128]{2,1,0:T(8,128)S(1)} collective-permute-done((f32[4,128,128]{2,1,0:T(8,128)S(1)}, f32[4,128,128]{2,1,0:T(8,128)S(1)}, u32[]{:S(2)}, u32[]{:S(2)}) %collective-permute-start.4) | collective-permute-done | bytes 262176 | tf_op jit(solution)/shard_map/ppermute | solution.py:10
  109.2 1.9 %collective-permute-start.5 = (f32[4,128,128]{2,1,0:T(8,128)S(1)}, f32[4,128,128]{2,1,0:T(8,128)S(1)}, u32[]{:S(2)}, u32[]{:S(2)}) collective-permute-start(f32[4,128,128]{2,1,0:T(8,128)S(1)} %pad_maximum_fusion.18), channel_id=1, source_target_pairs={{0,4},{4,8},{8,12},{12,16},{16,20},{20,24},{24,28},{28,32},{32,36}... | collective-permute-start | bytes 786440 | tf_op jit(solution)/shard_map/ppermute | solution.py:10
  111.2 3.4 %collective-permute-done.10 = f32[4,128,128]{2,1,0:T(8,128)S(1)} collective-permute-done((f32[4,128,128]{2,1,0:T(8,128)S(1)}, f32[4,128,128]{2,1,0:T(8,128)S(1)}, u32[]{:S(2)}, u32[]{:S(2)}) %collective-permute-start.10) | collective-permute-done | bytes 262176 | tf_op jit(solution)/shard_map/ppermute | solution.py:10
  114.6 1.9 %collective-permute-start.11 = (f32[4,128,128]{2,1,0:T(8,128)S(1)}, f32[4,128,128]{2,1,0:T(8,128)S(1)}, u32[]{:S(2)}, u32[]{:S(2)}) collective-permute-start(f32[4,128,128]{2,1,0:T(8,128)S(1)} %pad_maximum_fusion.20), channel_id=1, source_target_pairs={{4,0},{8,4},{12,8},{16,12},{20,16},{24,20},{28,24},{32,28},{36,32}... | collective-permute-start | bytes 786440 | tf_op jit(solution)/shard_map/ppermute | solution.py:10
  116.6 8.4 %collective-permute-done.11 = f32[4,128,128]{2,1,0:T(8,128)S(1)} collective-permute-done((f32[4,128,128]{2,1,0:T(8,128)S(1)}, f32[4,128,128]{2,1,0:T(8,128)S(1)}, u32[]{:S(2)}, u32[]{:S(2)}) %collective-permute-start.11) | collective-permute-done | bytes 262176 | tf_op jit(solution)/shard_map/ppermute | solution.py:10
  126.6 3.0 %collective-permute-start.12 = (f32[4,4,1,128]{3,1,2,0:T(4,128)S(1)}, f32[4,4,1,128]{3,1,2,0:T(4,128)S(1)}, u32[]{:S(2)}, u32[]{:S(2)}) collective-permute-start(f32[4,4,1,128]{3,1,2,0:T(4,128)S(1)} %get-tuple-element.488), channel_id=1, source_target_pairs={{2,0},{3,1},{6,4},{7,5},{10,8},{11,9},{14,12},{15,13},{18,16},{19,... | collective-permute-start | bytes 24584 | tf_op jit(solution)/shard_map/ppermute | solution.py:21
  131.0 4.6 %collective-permute-done.13 = f32[4,4,1,128]{3,1,2,0:T(4,128)S(1)} collective-permute-done((f32[4,4,1,128]{3,1,2,0:T(4,128)S(1)}, f32[4,4,1,128]{3,1,2,0:T(4,128)S(1)}, u32[]{:S(2)}, u32[]{:S(2)}) %collective-permute-start.13) | collective-permute-done | bytes 8224 | tf_op jit(solution)/shard_map/ppermute | solution.py:18
  135.8 1.6 fusion.25
  137.4 1.9 %copy.73 = f32[4,4,130,1]{2,1,3,0:T(4,128)S(1)} copy(f32[4,4,130,1]{3,1,2,0:T(4,128)} %get-tuple-element.485) | data formatting | bytes 16640 | tf_op jit(solution)/shard_map/slice | solution.py:21
  139.3 13.1 %collective-permute-start.14 = (f32[4,4,130,1]{2,1,3,0:T(4,128)S(1)}, f32[4,4,130,1]{2,1,3,0:T(4,128)S(1)}, u32[]{:S(2)}, u32[]{:S(2)}) collective-permute-start(f32[4,4,130,1]{2,1,3,0:T(4,128)S(1)} %copy.73), channel_id=1, source_target_pairs={{1,0},{3,2},{5,4},{7,6},{9,8},{11,10},{13,12},{15,14},{17,16},{19,... | collective-permute-start | bytes 24968 | tf_op jit(solution)/shard_map/ppermute | solution.py:21
  156.2 1.7 %copy.76 = f32[4,4,130,1]{3,1,2,0:T(4,128)} copy(f32[4,4,130,1]{2,1,3,0:T(4,128)S(1)} %collective-permute-done.15) | data formatting | bytes 16640 | tf_op jit(solution)/shard_map/ppermute | solution.py:18
  157.8 3.4 %fusion.13 = f32[4,4,128,128]{3,1,2,0:T(4,128)S(1)} fusion(f32[4,4,128,128]{3,1,2,0:T(4,128)S(1)} %sub.192, f32[4,4,130,1]{3,1,2,0:T(4,128)} %copy.76, f32[4,4,1,128]{3,1,2,0:T(4,128)S(1)} %collective-permute-done.12, f32[4,4,1,128]{3,1,2,0:T(4,128)S(1)} %collective-permute-done.13, f32[4,4,130,1]{3,1,2,0:T(4,128)S(1)} %copy.74), kind=kLoop, calls=%fused_computation.39 | loop fusion | flops 3932160 | bytes 2130176 | tf_op jit(solution)/shard_map/sub | solution.py:155
  (185 shorter events, 37.5 us)
Async XLA Ops:
  5.2 11.4 %copy-start.12 = (s32[128,128]{1,0:T(8,128)S(1)}, s32[128,128]{1,0:T(8,128)}, u32[]{:S(2)}) copy-start(s32[128,128]{1,0:T(8,128)} %param.15) | copy-start | bytes 196612
  5.2 11.4 %copy-start.10 = (f32[4,128,128]{2,1,0:T(8,128)S(1)}, f32[4,128,128]{2,1,0:T(8,128)}, u32[]{:S(2)}) copy-start(f32[4,128,128]{2,1,0:T(8,128)} %param.13) | copy-start | bytes 786436
  5.2 11.4 %copy-start.11 = (f32[4,128,128]{2,1,0:T(8,128)S(1)}, f32[4,128,128]{2,1,0:T(8,128)}, u32[]{:S(2)}) copy-start(f32[4,128,128]{2,1,0:T(8,128)} %param.14) | copy-start | bytes 786436
  8.3 12.4 %all-to-all-start = ((f32[32,1,320]{2,1,0:T(1,128)}), f32[32,1,320]{2,1,0:T(1,128)S(1)}, u32[]{:S(2)}, u32[]{:S(2)}) async-start(f32[32,1,320]{2,1,0:T(1,128)} %reshape.249), calls=%async_computation | async-start | bytes 98304 | tf_op jit(solution)/shard_map/all_to_all | solution.py:57
  31.2 1.1 copy-start
  31.2 1.1 copy-start.1
  31.2 1.1 copy-start.6
  31.3 5.6 %copy-start.8 = (f32[4,128,128]{2,1,0:T(8,128)}, f32[4,128,128]{2,1,0:T(8,128)S(1)}, u32[]{:S(2)}) copy-start(f32[4,128,128]{2,1,0:T(8,128)S(1)} %get-tuple-element.285) | copy-start | bytes 786436
  31.3 1.1 copy-start.2
  32.4 19.4 %collective-permute-start = (f32[6,128,128]{2,1,0:T(8,128)}, f32[6,128,128]{2,1,0:T(8,128)}, u32[]{:S(2)}, u32[]{:S(2)}) collective-permute-start(f32[6,128,128]{2,1,0:T(8,128)} %pad_maximum_fusion.9), channel_id=1, source_target_pairs={{0,4},{4,8},{8,12},{12,16},{16,20},{20,24},{24,28},{28,32},{32,36}... | collective-permute-start | bytes 1179656 | tf_op jit(solution)/shard_map/ppermute | solution.py:10
  47.9 4.0 %copy-start.7 = (f32[4,128,128]{2,1,0:T(8,128)S(1)}, f32[4,128,128]{2,1,0:T(8,128)}, u32[]{:S(2)}) copy-start(f32[4,128,128]{2,1,0:T(8,128)} %copy-done.6) | copy-start | bytes 786436
  47.9 4.0 %copy-start.9 = (f32[4,128,128]{2,1,0:T(8,128)S(1)}, f32[4,128,128]{2,1,0:T(8,128)}, u32[]{:S(2)}) copy-start(f32[4,128,128]{2,1,0:T(8,128)} %copy-done.8) | copy-start | bytes 786436
  47.9 4.8 %copy-start.3 = (f32[2,2,128,128]{3,2,0,1:T(8,128)S(1)}, f32[2,2,128,128]{3,2,0,1:T(8,128)}, u32[]{:S(2)}) copy-start(f32[2,2,128,128]{3,2,0,1:T(8,128)} %copy-done.2) | copy-start | bytes 786436
  49.7 13.4 %copy-start.4 = (f32[4,128,128]{2,1,0:T(8,128)S(1)}, f32[4,128,128]{2,1,0:T(8,128)}, u32[]{:S(2)}) copy-start(f32[4,128,128]{2,1,0:T(8,128)} %get-tuple-element.287) | copy-start | bytes 786436
  49.8 13.4 %copy-start.5 = (f32[4,128,128]{2,1,0:T(8,128)S(1)}, f32[4,128,128]{2,1,0:T(8,128)}, u32[]{:S(2)}) copy-start(f32[4,128,128]{2,1,0:T(8,128)} %get-tuple-element.288) | copy-start | bytes 786436
  49.8 13.4 %collective-permute-start.6 = (f32[6,128,128]{2,1,0:T(8,128)S(1)}, f32[6,128,128]{2,1,0:T(8,128)S(1)}, u32[]{:S(2)}, u32[]{:S(2)}) collective-permute-start(f32[6,128,128]{2,1,0:T(8,128)S(1)} %pad_maximum_fusion.13), channel_id=1, source_target_pairs={{4,0},{8,4},{12,8},{16,12},{20,16},{24,20},{28,24},{32,28},{36,32}... | collective-permute-start | bytes 1179656 | tf_op jit(solution)/shard_map/ppermute | solution.py:10
  53.8 11.3 %collective-permute-start.1 = (f32[6,128,128]{2,1,0:T(8,128)S(1)}, f32[6,128,128]{2,1,0:T(8,128)S(1)}, u32[]{:S(2)}, u32[]{:S(2)}) collective-permute-start(f32[6,128,128]{2,1,0:T(8,128)S(1)} %pad_maximum_fusion.10), channel_id=1, source_target_pairs={{0,8},{4,12},{8,16},{12,20},{16,24},{20,28},{24,32},{28,36},{32,40... | collective-permute-start | bytes 1179656 | tf_op jit(solution)/shard_map/ppermute | solution.py:10
  63.3 20.6 %collective-permute-start.7 = (f32[6,128,128]{2,1,0:T(8,128)S(1)}, f32[6,128,128]{2,1,0:T(8,128)S(1)}, u32[]{:S(2)}, u32[]{:S(2)}) collective-permute-start(f32[6,128,128]{2,1,0:T(8,128)S(1)} %pad_maximum_fusion.14), channel_id=1, source_target_pairs={{8,0},{12,4},{16,8},{20,12},{24,16},{28,20},{32,24},{36,28},{40,32... | collective-permute-start | bytes 1179656 | tf_op jit(solution)/shard_map/ppermute | solution.py:10
  65.3 20.8 %collective-permute-start.2 = (f32[6,128,128]{2,1,0:T(8,128)S(1)}, f32[6,128,128]{2,1,0:T(8,128)S(1)}, u32[]{:S(2)}, u32[]{:S(2)}) collective-permute-start(f32[6,128,128]{2,1,0:T(8,128)S(1)} %pad_maximum_fusion.11), channel_id=1, source_target_pairs={{0,16},{4,20},{8,24},{12,28},{16,32},{20,36},{24,40},{28,44},{32,4... | collective-permute-start | bytes 1179656 | tf_op jit(solution)/shard_map/ppermute | solution.py:10
  84.0 11.6 %collective-permute-start.8 = (f32[6,128,128]{2,1,0:T(8,128)S(1)}, f32[6,128,128]{2,1,0:T(8,128)S(1)}, u32[]{:S(2)}, u32[]{:S(2)}) collective-permute-start(f32[6,128,128]{2,1,0:T(8,128)S(1)} %pad_maximum_fusion.15), channel_id=1, source_target_pairs={{16,0},{20,4},{24,8},{28,12},{32,16},{36,20},{40,24},{44,28},{48,3... | collective-permute-start | bytes 1179656 | tf_op jit(solution)/shard_map/ppermute | solution.py:10
  86.2 12.5 %collective-permute-start.3 = (f32[6,128,128]{2,1,0:T(8,128)S(1)}, f32[6,128,128]{2,1,0:T(8,128)S(1)}, u32[]{:S(2)}, u32[]{:S(2)}) collective-permute-start(f32[6,128,128]{2,1,0:T(8,128)S(1)} %pad_maximum_fusion.12), channel_id=1, source_target_pairs={{0,32},{4,36},{8,40},{12,44},{16,48},{20,52},{24,56},{28,60},{32,6... | collective-permute-start | bytes 1179656 | tf_op jit(solution)/shard_map/ppermute | solution.py:10
  95.7 10.2 %collective-permute-start.9 = (f32[6,128,128]{2,1,0:T(8,128)S(1)}, f32[6,128,128]{2,1,0:T(8,128)S(1)}, u32[]{:S(2)}, u32[]{:S(2)}) collective-permute-start(f32[6,128,128]{2,1,0:T(8,128)S(1)} %pad_maximum_fusion.16), channel_id=1, source_target_pairs={{32,0},{36,4},{40,8},{44,12},{48,16},{52,20},{56,24},{60,28},{64,3... | collective-permute-start | bytes 1179656 | tf_op jit(solution)/shard_map/ppermute | solution.py:10
  98.8 10.4 %collective-permute-start.4 = (f32[4,128,128]{2,1,0:T(8,128)S(1)}, f32[4,128,128]{2,1,0:T(8,128)S(1)}, u32[]{:S(2)}, u32[]{:S(2)}) collective-permute-start(f32[4,128,128]{2,1,0:T(8,128)S(1)} %pad_maximum_fusion.17), channel_id=1, source_target_pairs={{0,64},{4,68},{8,72},{12,76},{16,80},{20,84},{24,88},{28,92},{32,9... | collective-permute-start | bytes 786440 | tf_op jit(solution)/shard_map/ppermute | solution.py:10
  105.9 8.6 %collective-permute-start.10 = (f32[4,128,128]{2,1,0:T(8,128)S(1)}, f32[4,128,128]{2,1,0:T(8,128)S(1)}, u32[]{:S(2)}, u32[]{:S(2)}) collective-permute-start(f32[4,128,128]{2,1,0:T(8,128)S(1)} %pad_maximum_fusion.19), channel_id=1, source_target_pairs={{64,0},{68,4},{72,8},{76,12},{80,16},{84,20},{88,24},{92,28},{96,3... | collective-permute-start | bytes 786440 | tf_op jit(solution)/shard_map/ppermute | solution.py:10
  109.2 7.3 %collective-permute-start.5 = (f32[4,128,128]{2,1,0:T(8,128)S(1)}, f32[4,128,128]{2,1,0:T(8,128)S(1)}, u32[]{:S(2)}, u32[]{:S(2)}) collective-permute-start(f32[4,128,128]{2,1,0:T(8,128)S(1)} %pad_maximum_fusion.18), channel_id=1, source_target_pairs={{0,4},{4,8},{8,12},{12,16},{16,20},{20,24},{24,28},{28,32},{32,36}... | collective-permute-start | bytes 786440 | tf_op jit(solution)/shard_map/ppermute | solution.py:10
  114.6 10.4 %collective-permute-start.11 = (f32[4,128,128]{2,1,0:T(8,128)S(1)}, f32[4,128,128]{2,1,0:T(8,128)S(1)}, u32[]{:S(2)}, u32[]{:S(2)}) collective-permute-start(f32[4,128,128]{2,1,0:T(8,128)S(1)} %pad_maximum_fusion.20), channel_id=1, source_target_pairs={{4,0},{8,4},{12,8},{16,12},{20,16},{24,20},{28,24},{32,28},{36,32}... | collective-permute-start | bytes 786440 | tf_op jit(solution)/shard_map/ppermute | solution.py:10
  126.6 4.3 %collective-permute-start.12 = (f32[4,4,1,128]{3,1,2,0:T(4,128)S(1)}, f32[4,4,1,128]{3,1,2,0:T(4,128)S(1)}, u32[]{:S(2)}, u32[]{:S(2)}) collective-permute-start(f32[4,4,1,128]{3,1,2,0:T(4,128)S(1)} %get-tuple-element.488), channel_id=1, source_target_pairs={{2,0},{3,1},{6,4},{7,5},{10,8},{11,9},{14,12},{15,13},{18,16},{19,... | collective-permute-start | bytes 24584 | tf_op jit(solution)/shard_map/ppermute | solution.py:21
  129.7 5.9 %collective-permute-start.13 = (f32[4,4,1,128]{3,1,2,0:T(4,128)S(1)}, f32[4,4,1,128]{3,1,2,0:T(4,128)S(1)}, u32[]{:S(2)}, u32[]{:S(2)}) collective-permute-start(f32[4,4,1,128]{3,1,2,0:T(4,128)S(1)} %get-tuple-element.487), channel_id=1, source_target_pairs={{0,2},{1,3},{4,6},{5,7},{8,10},{9,11},{12,14},{13,15},{16,18},{17,... | collective-permute-start | bytes 24584 | tf_op jit(solution)/shard_map/ppermute | solution.py:18
  139.3 15.1 %collective-permute-start.14 = (f32[4,4,130,1]{2,1,3,0:T(4,128)S(1)}, f32[4,4,130,1]{2,1,3,0:T(4,128)S(1)}, u32[]{:S(2)}, u32[]{:S(2)}) collective-permute-start(f32[4,4,130,1]{2,1,3,0:T(4,128)S(1)} %copy.73), channel_id=1, source_target_pairs={{1,0},{3,2},{5,4},{7,6},{9,8},{11,10},{13,12},{15,14},{17,16},{19,... | collective-permute-start | bytes 24968 | tf_op jit(solution)/shard_map/ppermute | solution.py:21
  153.1 3.1 %collective-permute-start.15 = (f32[4,4,130,1]{2,1,3,0:T(4,128)S(1)}, f32[4,4,130,1]{2,1,3,0:T(4,128)S(1)}, u32[]{:S(2)}, u32[]{:S(2)}) collective-permute-start(f32[4,4,130,1]{2,1,3,0:T(4,128)S(1)} %copy.75), channel_id=1, source_target_pairs={{0,1},{2,3},{4,5},{6,7},{8,9},{10,11},{12,13},{14,15},{16,17},{18,... | collective-permute-start | bytes 24968 | tf_op jit(solution)/shard_map/ppermute | solution.py:18

commit v3 on v2

v3 whole, which is shorter than its diff:
```python
import jax
import jax.numpy as jnp
from jax import lax
from jax.sharding import PartitionSpec as P


def from_behind(array, axis, by):
    count = lax.axis_size(axis)
    pairs = [(i, i + by) for i in range(count) if 0 <= i + by < count]
    return lax.ppermute(array, axis, pairs)


def complex_times(a_re, a_im, b_re, b_im):
    return a_re * b_re - a_im * b_im, a_re * b_im + a_im * b_re


def inject_receivers(source, recv_values, recv_slab, recv_lateral, recv_layer):
    layers, components, width_x, width_y = source.shape
    slab_count = lax.axis_size("slab")
    plane_size = width_x * width_y
    rows_here = recv_values.shape[3]
    capacity = rows_here // min(8, slab_count)
    values = recv_values[0, 0]
    target_slab = recv_slab[0, 0, :, 0]
    position = recv_layer[0, 0] * plane_size + recv_lateral[0, 0]
    one_hot = (target_slab[:, None] == jnp.arange(slab_count, dtype=jnp.int32)[None, :]).astype(
        jnp.int32
    )
    ranking = jnp.sum((jnp.cumsum(one_hot, axis=0) - one_hot) * one_hot, axis=1)
    target_slot = target_slab * capacity + ranking
    rows = jnp.concatenate([values, position.astype(jnp.float32)[None, :]], axis=0)
    send_rows = (
        jnp.zeros((components + 1, slab_count * capacity), jnp.float32).at[:, target_slot].set(rows)
    )
    got_rows = lax.all_to_all(
        send_rows.reshape(components + 1, slab_count, capacity),
        "slab",
        split_axis=1,
        concat_axis=1,
        tiled=True,
    ).reshape(components + 1, slab_count * capacity)
    inject_values = got_rows[:components]
    inject_places = got_rows[components].astype(jnp.int32)
    row_of = inject_places // width_y
    col_of = inject_places % width_y
    pick_rows = (
        row_of[None, :] == jnp.arange(layers * width_x, dtype=jnp.int32)[:, None]
    ).astype(jnp.bfloat16)
    pick_cols = col_of[:, None] == jnp.arange(width_y, dtype=jnp.int32)[None, :]
    high = lax.reduce_precision(inject_values, exponent_bits=8, mantissa_bits=7)
    rest = inject_values - high
    middle = lax.reduce_precision(rest, exponent_bits=8, mantissa_bits=7)
    low = rest - middle
    pieces = jnp.stack([high, middle, low], axis=0)
    spread = jnp.where(pick_cols[None, None, :, :], pieces[:, :, :, None], 0.0)
    spread = jnp.transpose(spread, (2, 0, 1, 3)).reshape(
        slab_count * capacity, 3 * components * width_y
    )
    added = jnp.dot(pick_rows, spread.astype(jnp.bfloat16), preferred_element_type=jnp.float32)
    added = added.reshape(layers * width_x, 3, components * width_y)
    added = (added[:, 0] + added[:, 1]) + added[:, 2]
    added = jnp.transpose(added.reshape(layers, width_x, components, width_y), (0, 2, 1, 3))
    return source + added


def map_powers(a_re, a_im, sign):
    slab_count = lax.axis_size("slab")
    powers = [(a_re, a_im)]
    step = 1
    while 2 * step < slab_count:
        got = from_behind(jnp.stack([a_re, a_im], axis=0), "slab", sign * step)
        a_re, a_im = complex_times(a_re, a_im, got[0], got[1])
        powers.append((a_re, a_im))
        step *= 2
    return powers


def entering_state(b_re, b_im, powers, sign):
    slab_count = lax.axis_size("slab")
    shots = b_re.shape[0]
    step = 1
    level = 0
    while step < slab_count:
        got = from_behind(jnp.concatenate([b_re, b_im], axis=0), "slab", sign * step)
        a_re, a_im = powers[level]
        t_re, t_im = complex_times(a_re[None], a_im[None], got[:shots], got[shots:])
        b_re, b_im = t_re + b_re, t_im + b_im
        step *= 2
        level += 1
    got = from_behind(jnp.concatenate([b_re, b_im], axis=0), "slab", sign)
    return got[:shots], got[shots:]


def neighbour_sum(block):
    from_low_x = from_behind(block[:, :, -1, :], "px", 1)
    from_high_x = from_behind(block[:, :, 0, :], "px", -1)
    from_low_y = from_behind(block[:, :, :, -1], "py", 1)
    from_high_y = from_behind(block[:, :, :, 0], "py", -1)
    next_x = jnp.concatenate([block[:, :, 1:, :], from_high_x[:, :, None, :]], axis=2)
    prev_x = jnp.concatenate([from_low_x[:, :, None, :], block[:, :, :-1, :]], axis=2)
    next_y = jnp.concatenate([block[:, :, :, 1:], from_high_y[:, :, :, None]], axis=3)
    prev_y = jnp.concatenate([from_low_y[:, :, :, None], block[:, :, :, :-1]], axis=3)
    return next_x + prev_x + next_y + prev_y


def shards(source, phase, attenuation, pml_level, recv_values, recv_slab, recv_lateral, recv_layer):
    layers, components, width_x, width_y = source.shape
    shot_count = components // 2
    slab_count = lax.axis_size("slab")
    depth_total = layers * slab_count

    damping = attenuation + 0.5 / depth_total * pml_level.astype(jnp.float32)[None, :, :]
    amplitude = jnp.exp(-damping)
    rate_re = amplitude * jnp.cos(phase)
    rate_im = amplitude * jnp.sin(phase)

    prod_down = [(rate_re[0], rate_im[0])]
    for k in range(1, layers):
        prod_down.append(complex_times(rate_re[k], rate_im[k], *prod_down[-1]))
    prod_up = [None] * layers
    prod_up[layers - 1] = (rate_re[layers - 1], rate_im[layers - 1])
    for k in range(layers - 2, -1, -1):
        prod_up[k] = complex_times(rate_re[k], rate_im[k], *prod_up[k + 1])
    powers_down = map_powers(*prod_down[-1], 1)
    powers_up = map_powers(*prod_up[0], -1)

    forcing = inject_receivers(source, recv_values, recv_slab, recv_lateral, recv_layer)
    fields = forcing.reshape(layers, shot_count, 2, width_x, width_y)
    f_re = fields[:, :, 0]
    f_im = fields[:, :, 1]

    down = [None] * layers
    state = (f_re[0], f_im[0])
    down[0] = state
    for k in range(1, layers):
        t_re, t_im = complex_times(rate_re[k][None], rate_im[k][None], *state)
        state = (t_re + f_re[k], t_im + f_im[k])
        down[k] = state
    up = [None] * layers
    state = (f_re[layers - 1], f_im[layers - 1])
    up[layers - 1] = state
    for k in range(layers - 2, -1, -1):
        t_re, t_im = complex_times(rate_re[k][None], rate_im[k][None], *state)
        state = (t_re + f_re[k], t_im + f_im[k])
        up[k] = state

    enter_re, enter_im = entering_state(*down[layers - 1], powers_down, 1)
    below_re, below_im = entering_state(*up[0], powers_up, -1)

    combined = []
    for k in range(layers):
        e_re, e_im = complex_times(prod_down[k][0][None], prod_down[k][1][None], enter_re, enter_im)
        u_re, u_im = complex_times(prod_up[k][0][None], prod_up[k][1][None], below_re, below_im)
        c_re = (down[k][0] + e_re) + (up[k][0] + u_re) - f_re[k]
        c_im = (down[k][1] + e_im) + (up[k][1] + u_im) - f_im[k]
        combined.append(jnp.stack([c_re, c_im], axis=1).reshape(components, width_x, width_y))
    combined = jnp.stack(combined, axis=0)
    neighbours = neighbour_sum(combined)
    return combined - 0.2 * (4.0 * combined - neighbours)


def solution(mesh):
    in_specs = (
        P("slab", None, "px", "py"),
        P("slab", "px", "py"),
        P("slab", "px", "py"),
        P("px", "py"),
        P("px", "py", None, "slab"),
        P("px", "py", "slab", None),
        P("px", "py", "slab"),
        P("px", "py", "slab"),
    )
    out_specs = P("slab", None, "px", "py")
    return jax.shard_map(shards, mesh=mesh, in_specs=in_specs, out_specs=out_specs, check_vma=False)
```

time: 163 us -> 159 us (0.975)
  the two profiles are of different devices: /device:TPU:63 before, /device:TPU:64 now
where the time goes in v3:
time: 159 us; the launch traced here: 158 us
  starting transfers between devices  88 us (55%)
  waiting for transfers between devices  32.4 us (20%)
  other arithmetic  22.4 us (14%)
  local copies, waits for them, and re-layouts  10.4 us (7%)
  matrix products  3.53 us (2%)
    ppermute x24, starting transfers between devices, from_behind(): return lax.ppermute(array, axis, pairs)  79.4 us
    ppermute x24, waiting for transfers between devices, from_behind(): return lax.ppermute(array, axis, pairs)  32.4 us
    all_to_all x1, starting transfers between devices, inject_receivers(): lax.all_to_all(send_rows.reshape(components + 1, slab_count, capacity), '...  8.68 us
    sub x1, other arithmetic, shards(): return combined - 0.2 * (4.0 * combined - neighbours)  3.99 us
    dot_general x1, matrix products, inject_receivers(): jnp.dot(pick_rows, spread.astype(jnp.bfloat16), preferred_element_type=jn...  3.53 us
  transfers between devices with their start and end apart: 25, of which 11 were waited for; matrix products, arithmetic and copies ran while one was open for 13% of the time, Pallas kernels for 0%

profile of v3, /device:TPU:64, one launch (start us, length us, event | category | flops | bytes accessed | tf_op | source)
XLA Modules:
  0.0 157.7 jit_solution(4323863724997134353)
XLA Ops:
  5.2 2.0 %scatter_custom_fusion = f32[5,2048]{0,1:T(8,128)S(1)} fusion(s32[512]{0:T(512)S(1)} %bitcast.293, f32[512,5]{1,0:T(8,128)S(1)} %copy.69, f32[]{:T(128)} %constant.36.clone.1), kind=kCustom, calls=%fused_computation.19 | custom fusion | bytes 40964 | tf_op jit(solution)/shard_map/scatter | solution.py:33
  8.2 8.7 %all-to-all-start = ((f32[32,1,320]{2,1,0:T(1,128)}), f32[32,1,320]{2,1,0:T(1,128)S(1)}, u32[]{:S(2)}, u32[]{:S(2)}) async-start(f32[32,1,320]{2,1,0:T(1,128)} %reshape.231), calls=%async_computation | async-start | bytes 98304 | tf_op jit(solution)/shard_map/all_to_all | solution.py:35
  17.8 2.0 %cosine_multiply_fusion = (f32[4,128,128]{2,1,0:T(8,128)S(1)}, f32[4,128,128]{2,1,0:T(8,128)S(1)}) fusion(f32[4,128,128]{2,1,0:T(8,128)} %param.9, f32[4,128,128]{2,1,0:T(8,128)} %param.10, f32[128,128]{1,0:T(8,128)S(1)} %convert_multiply_fusion), kind=kLoop, calls=%fused_computation.38 | loop fusion | flops 262144 | bytes 1114112 | tf_op jit(solution)/shard_map/mul | solution.py:114
  22.0 5.5 %collective-permute-start.10 = (f32[2,128,128]{2,1,0:T(8,128)}, f32[2,128,128]{2,1,0:T(8,128)}, u32[]{:S(2)}, u32[]{:S(2)}) collective-permute-start(f32[2,128,128]{2,1,0:T(8,128)} %pad_maximum_fusion.21), channel_id=1, source_target_pairs={{4,0},{8,4},{12,8},{16,12},{20,16},{24,20},{28,24},{32,28},{36,32}... | collective-permute-start | bytes 393224 | tf_op jit(solution)/shard_map/ppermute | solution.py:10
  33.0 3.5 %fusion.1 = f32[512,3,512]{2,0,1:T(8,128)S(1)} fusion(bf16[3,512,2048]{2,1,0:T(8,128)(2,1)S(1)} %bitcast.242, s32[2048]{0:T(1024)S(1)} %get-tuple-element.98), kind=kOutput, calls=%fused_computation.4 | convolution fusion | flops 3222274048 | bytes 9445376 | tf_op jit(solution)/shard_map/dot_general | solution.py:59
  40.1 6.9 %collective-permute-start.14 = (f32[4,128,128]{2,1,0:T(8,128)S(1)}, f32[4,128,128]{2,1,0:T(8,128)S(1)}, u32[]{:S(2)}, u32[]{:S(2)}) collective-permute-start(f32[4,128,128]{2,1,0:T(8,128)S(1)} %pad_maximum_fusion.7), channel_id=1, source_target_pairs={{4,0},{8,4},{12,8},{16,12},{20,16},{24,20},{28,24},{32,28},{36,32}... | collective-permute-start | bytes 786440 | tf_op jit(solution)/shard_map/ppermute | solution.py:10
  47.1 1.9 %collective-permute-start.4 = (f32[4,128,128]{2,1,0:T(8,128)S(1)}, f32[4,128,128]{2,1,0:T(8,128)S(1)}, u32[]{:S(2)}, u32[]{:S(2)}) collective-permute-start(f32[4,128,128]{2,1,0:T(8,128)S(1)} %pad_maximum_fusion.1), channel_id=1, source_target_pairs={{0,4},{4,8},{8,12},{12,16},{16,20},{20,24},{24,28},{28,32},{32,36}... | collective-permute-start | bytes 786440 | tf_op jit(solution)/shard_map/ppermute | solution.py:10
  50.0 2.5 %collective-permute-start.11 = (f32[2,128,128]{2,1,0:T(8,128)S(1)}, f32[2,128,128]{2,1,0:T(8,128)S(1)}, u32[]{:S(2)}, u32[]{:S(2)}) collective-permute-start(f32[2,128,128]{2,1,0:T(8,128)S(1)} %pad_maximum_fusion.22), channel_id=1, source_target_pairs={{8,0},{12,4},{16,8},{20,12},{24,16},{28,20},{32,24},{36,28},{40,32... | collective-permute-start | bytes 393224 | tf_op jit(solution)/shard_map/ppermute | solution.py:10
  53.4 3.4 %collective-permute-start.1 = (f32[2,128,128]{2,1,0:T(8,128)S(1)}, f32[2,128,128]{2,1,0:T(8,128)S(1)}, u32[]{:S(2)}, u32[]{:S(2)}) collective-permute-start(f32[2,128,128]{2,1,0:T(8,128)S(1)} %pad_maximum_fusion.18), channel_id=1, source_target_pairs={{0,8},{4,12},{8,16},{12,20},{16,24},{20,28},{24,32},{28,36},{32,40... | collective-permute-start | bytes 393224 | tf_op jit(solution)/shard_map/ppermute | solution.py:10
  56.9 1.9 %collective-permute-start.12 = (f32[2,128,128]{2,1,0:T(8,128)S(1)}, f32[2,128,128]{2,1,0:T(8,128)S(1)}, u32[]{:S(2)}, u32[]{:S(2)}) collective-permute-start(f32[2,128,128]{2,1,0:T(8,128)S(1)} %pad_maximum_fusion.23), channel_id=1, source_target_pairs={{16,0},{20,4},{24,8},{28,12},{32,16},{36,20},{40,24},{44,28},{48,3... | collective-permute-start | bytes 393224 | tf_op jit(solution)/shard_map/ppermute | solution.py:10
  58.8 4.7 %collective-permute-done.1 = f32[2,128,128]{2,1,0:T(8,128)S(1)} collective-permute-done((f32[2,128,128]{2,1,0:T(8,128)S(1)}, f32[2,128,128]{2,1,0:T(8,128)S(1)}, u32[]{:S(2)}, u32[]{:S(2)}) %collective-permute-start.1) | collective-permute-done | bytes 131104 | tf_op jit(solution)/shard_map/ppermute | solution.py:10
  63.5 1.9 %collective-permute-start.2 = (f32[2,128,128]{2,1,0:T(8,128)S(1)}, f32[2,128,128]{2,1,0:T(8,128)S(1)}, u32[]{:S(2)}, u32[]{:S(2)}) collective-permute-start(f32[2,128,128]{2,1,0:T(8,128)S(1)} %pad_maximum_fusion.19), channel_id=1, source_target_pairs={{0,16},{4,20},{8,24},{12,28},{16,32},{20,36},{24,40},{28,44},{32,4... | collective-permute-start | bytes 393224 | tf_op jit(solution)/shard_map/ppermute | solution.py:10
  65.6 4.3 %collective-permute-start.15 = (f32[4,128,128]{2,1,0:T(8,128)S(1)}, f32[4,128,128]{2,1,0:T(8,128)S(1)}, u32[]{:S(2)}, u32[]{:S(2)}) collective-permute-start(f32[4,128,128]{2,1,0:T(8,128)S(1)} %pad_maximum_fusion.8), channel_id=1, source_target_pairs={{8,0},{12,4},{16,8},{20,12},{24,16},{28,20},{32,24},{36,28},{40,32... | collective-permute-start | bytes 786440 | tf_op jit(solution)/shard_map/ppermute | solution.py:10
  70.0 1.9 %collective-permute-start.5 = (f32[4,128,128]{2,1,0:T(8,128)S(1)}, f32[4,128,128]{2,1,0:T(8,128)S(1)}, u32[]{:S(2)}, u32[]{:S(2)}) collective-permute-start(f32[4,128,128]{2,1,0:T(8,128)S(1)} %pad_maximum_fusion.2), channel_id=1, source_target_pairs={{0,8},{4,12},{8,16},{12,20},{16,24},{20,28},{24,32},{28,36},{32,40... | collective-permute-start | bytes 786440 | tf_op jit(solution)/shard_map/ppermute | solution.py:10
  72.0 2.9 %collective-permute-start.13 = (f32[2,128,128]{2,1,0:T(8,128)S(1)}, f32[2,128,128]{2,1,0:T(8,128)S(1)}, u32[]{:S(2)}, u32[]{:S(2)}) collective-permute-start(f32[2,128,128]{2,1,0:T(8,128)S(1)} %pad_maximum_fusion.24), channel_id=1, source_target_pairs={{32,0},{36,4},{40,8},{44,12},{48,16},{52,20},{56,24},{60,28},{64,3... | collective-permute-start | bytes 393224 | tf_op jit(solution)/shard_map/ppermute | solution.py:10
  74.9 3.1 %collective-permute-start.3 = (f32[2,128,128]{2,1,0:T(8,128)S(1)}, f32[2,128,128]{2,1,0:T(8,128)S(1)}, u32[]{:S(2)}, u32[]{:S(2)}) collective-permute-start(f32[2,128,128]{2,1,0:T(8,128)S(1)} %pad_maximum_fusion.20), channel_id=1, source_target_pairs={{0,32},{4,36},{8,40},{12,44},{16,48},{20,52},{24,56},{28,60},{32,6... | collective-permute-start | bytes 393224 | tf_op jit(solution)/shard_map/ppermute | solution.py:10
  78.8 4.3 %collective-permute-done.3 = f32[2,128,128]{2,1,0:T(8,128)S(1)} collective-permute-done((f32[2,128,128]{2,1,0:T(8,128)S(1)}, f32[2,128,128]{2,1,0:T(8,128)S(1)}, u32[]{:S(2)}, u32[]{:S(2)}) %collective-permute-start.3) | collective-permute-done | bytes 131104 | tf_op jit(solution)/shard_map/ppermute | solution.py:10
  83.3 5.1 %collective-permute-start.16 = (f32[4,128,128]{2,1,0:T(8,128)S(1)}, f32[4,128,128]{2,1,0:T(8,128)S(1)}, u32[]{:S(2)}, u32[]{:S(2)}) collective-permute-start(f32[4,128,128]{2,1,0:T(8,128)S(1)} %pad_maximum_fusion.9), channel_id=1, source_target_pairs={{16,0},{20,4},{24,8},{28,12},{32,16},{36,20},{40,24},{44,28},{48,3... | collective-permute-start | bytes 786440 | tf_op jit(solution)/shard_map/ppermute | solution.py:10
  88.5 2.4 %collective-permute-start.6 = (f32[4,128,128]{2,1,0:T(8,128)S(1)}, f32[4,128,128]{2,1,0:T(8,128)S(1)}, u32[]{:S(2)}, u32[]{:S(2)}) collective-permute-start(f32[4,128,128]{2,1,0:T(8,128)S(1)} %pad_maximum_fusion.3), channel_id=1, source_target_pairs={{0,16},{4,20},{8,24},{12,28},{16,32},{20,36},{24,40},{28,44},{32,4... | collective-permute-start | bytes 786440 | tf_op jit(solution)/shard_map/ppermute | solution.py:10
  90.9 5.0 %collective-permute-done.16 = f32[4,128,128]{2,1,0:T(8,128)S(1)} collective-permute-done((f32[4,128,128]{2,1,0:T(8,128)S(1)}, f32[4,128,128]{2,1,0:T(8,128)S(1)}, u32[]{:S(2)}, u32[]{:S(2)}) %collective-permute-start.16) | collective-permute-done | bytes 262176 | tf_op jit(solution)/shard_map/ppermute | solution.py:10
  95.9 2.8 %collective-permute-start.17 = (f32[4,128,128]{2,1,0:T(8,128)S(1)}, f32[4,128,128]{2,1,0:T(8,128)S(1)}, u32[]{:S(2)}, u32[]{:S(2)}) collective-permute-start(f32[4,128,128]{2,1,0:T(8,128)S(1)} %pad_maximum_fusion.10), channel_id=1, source_target_pairs={{32,0},{36,4},{40,8},{44,12},{48,16},{52,20},{56,24},{60,28},{64,3... | collective-permute-start | bytes 786440 | tf_op jit(solution)/shard_map/ppermute | solution.py:10
  98.8 2.1 %collective-permute-done.6 = f32[4,128,128]{2,1,0:T(8,128)S(1)} collective-permute-done((f32[4,128,128]{2,1,0:T(8,128)S(1)}, f32[4,128,128]{2,1,0:T(8,128)S(1)}, u32[]{:S(2)}, u32[]{:S(2)}) %collective-permute-start.6) | collective-permute-done | bytes 262176 | tf_op jit(solution)/shard_map/ppermute | solution.py:10
  101.0 3.0 %collective-permute-start.7 = (f32[4,128,128]{2,1,0:T(8,128)S(1)}, f32[4,128,128]{2,1,0:T(8,128)S(1)}, u32[]{:S(2)}, u32[]{:S(2)}) collective-permute-start(f32[4,128,128]{2,1,0:T(8,128)S(1)} %pad_maximum_fusion.4), channel_id=1, source_target_pairs={{0,32},{4,36},{8,40},{12,44},{16,48},{20,52},{24,56},{28,60},{32,6... | collective-permute-start | bytes 786440 | tf_op jit(solution)/shard_map/ppermute | solution.py:10
  104.3 2.6 %collective-permute-start.18 = (f32[4,128,128]{2,1,0:T(8,128)S(1)}, f32[4,128,128]{2,1,0:T(8,128)S(1)}, u32[]{:S(2)}, u32[]{:S(2)}) collective-permute-start(f32[4,128,128]{2,1,0:T(8,128)S(1)} %pad_maximum_fusion.11), channel_id=1, source_target_pairs={{64,0},{68,4},{72,8},{76,12},{80,16},{84,20},{88,24},{92,28},{96,3... | collective-permute-start | bytes 786440 | tf_op jit(solution)/shard_map/ppermute | solution.py:10
  106.9 3.9 %collective-permute-done.7 = f32[4,128,128]{2,1,0:T(8,128)S(1)} collective-permute-done((f32[4,128,128]{2,1,0:T(8,128)S(1)}, f32[4,128,128]{2,1,0:T(8,128)S(1)}, u32[]{:S(2)}, u32[]{:S(2)}) %collective-permute-start.7) | collective-permute-done | bytes 262176 | tf_op jit(solution)/shard_map/ppermute | solution.py:10
  112.4 2.1 %collective-permute-done.18 = f32[4,128,128]{2,1,0:T(8,128)S(1)} collective-permute-done((f32[4,128,128]{2,1,0:T(8,128)S(1)}, f32[4,128,128]{2,1,0:T(8,128)S(1)}, u32[]{:S(2)}, u32[]{:S(2)}) %collective-permute-start.18) | collective-permute-done | bytes 262176 | tf_op jit(solution)/shard_map/ppermute | solution.py:10
  114.5 10.2 %collective-permute-start.19 = (f32[4,128,128]{2,1,0:T(8,128)S(1)}, f32[4,128,128]{2,1,0:T(8,128)S(1)}, u32[]{:S(2)}, u32[]{:S(2)}) collective-permute-start(f32[4,128,128]{2,1,0:T(8,128)S(1)} %pad_maximum_fusion.12), channel_id=1, source_target_pairs={{4,0},{8,4},{12,8},{16,12},{20,16},{24,20},{28,24},{32,28},{36,32}... | collective-permute-start | bytes 786440 | tf_op jit(solution)/shard_map/ppermute | solution.py:10
  124.8 1.9 %collective-permute-start.9 = (f32[4,128,128]{2,1,0:T(8,128)S(1)}, f32[4,128,128]{2,1,0:T(8,128)S(1)}, u32[]{:S(2)}, u32[]{:S(2)}) collective-permute-start(f32[4,128,128]{2,1,0:T(8,128)S(1)} %pad_maximum_fusion.6), channel_id=1, source_target_pairs={{0,4},{4,8},{8,12},{12,16},{16,20},{20,24},{24,28},{28,32},{32,36}... | collective-permute-start | bytes 786440 | tf_op jit(solution)/shard_map/ppermute | solution.py:10
  128.6 7.5 %collective-permute-done.9 = f32[4,128,128]{2,1,0:T(8,128)S(1)} collective-permute-done((f32[4,128,128]{2,1,0:T(8,128)S(1)}, f32[4,128,128]{2,1,0:T(8,128)S(1)}, u32[]{:S(2)}, u32[]{:S(2)}) %collective-permute-start.9) | collective-permute-done | bytes 262176 | tf_op jit(solution)/shard_map/ppermute | solution.py:10
  140.9 6.0 %collective-permute-start.21 = (f32[4,4,128]{2,1,0:T(4,128)S(1)}, f32[4,4,128]{2,1,0:T(4,128)S(1)}, u32[]{:S(2)}, u32[]{:S(2)}) collective-permute-start(f32[4,4,128]{2,1,0:T(4,128)S(1)} %bitcast.289), channel_id=1, source_target_pairs={{0,2},{1,3},{4,6},{5,7},{8,10},{9,11},{12,14},{13,15},{16,18},{17,... | collective-permute-start | bytes 24584 | tf_op jit(solution)/shard_map/ppermute | solution.py:10
  148.3 3.0 %collective-permute-start.23 = (f32[4,4,128]{2,1,0:T(4,128)S(1)}, f32[4,4,128]{2,1,0:T(4,128)S(1)}, u32[]{:S(2)}, u32[]{:S(2)}) collective-permute-start(f32[4,4,128]{2,1,0:T(4,128)S(1)} %get-tuple-element.5), channel_id=1, source_target_pairs={{0,1},{2,3},{4,5},{6,7},{8,9},{10,11},{12,13},{14,15},{16,17},{18,... | collective-permute-start | bytes 24584 | tf_op jit(solution)/shard_map/ppermute | solution.py:10
  153.7 4.0 %fusion.8 = f32[4,4,128,128]{3,2,1,0:T(8,128)} fusion(f32[4,4,1,128]{3,2,1,0:T(1,128)S(1)} %bitcast.291, f32[4,4,127,128]{3,2,1,0:T(8,128)} %get-tuple-element.40, f32[4,4,127,128]{3,2,1,0:T(8,128)S(1)} %get-tuple-element.39, f32[4,4,1,128]{3,2,1,0:T(1,128)S(1)} %bitcast.292, f32[4,4,128,1]{3,2,1,0:T(8,128)S(1)} %copy.87, ...), kind=kLoop, calls=%fused_computation.16 | loop fusion | flops 3670016 | bytes 6291456 | tf_op jit(solution)/shard_map/sub | solution.py:159
  (148 shorter events, 33.7 us)
Async XLA Ops:
  8.2 21.9 %all-to-all-start = ((f32[32,1,320]{2,1,0:T(1,128)}), f32[32,1,320]{2,1,0:T(1,128)S(1)}, u32[]{:S(2)}, u32[]{:S(2)}) async-start(f32[32,1,320]{2,1,0:T(1,128)} %reshape.231), calls=%async_computation | async-start | bytes 98304 | tf_op jit(solution)/shard_map/all_to_all | solution.py:35
  22.0 27.0 %collective-permute-start.10 = (f32[2,128,128]{2,1,0:T(8,128)}, f32[2,128,128]{2,1,0:T(8,128)}, u32[]{:S(2)}, u32[]{:S(2)}) collective-permute-start(f32[2,128,128]{2,1,0:T(8,128)} %pad_maximum_fusion.21), channel_id=1, source_target_pairs={{4,0},{8,4},{12,8},{16,12},{20,16},{24,20},{28,24},{32,28},{36,32}... | collective-permute-start | bytes 393224 | tf_op jit(solution)/shard_map/ppermute | solution.py:10
  28.2 24.3 %collective-permute-start = (f32[2,128,128]{2,1,0:T(8,128)}, f32[2,128,128]{2,1,0:T(8,128)}, u32[]{:S(2)}, u32[]{:S(2)}) collective-permute-start(f32[2,128,128]{2,1,0:T(8,128)} %pad_maximum_fusion.17), channel_id=1, source_target_pairs={{0,4},{4,8},{8,12},{12,16},{16,20},{20,24},{24,28},{28,32},{32,36}... | collective-permute-start | bytes 393224 | tf_op jit(solution)/shard_map/ppermute | solution.py:10
  40.1 25.3 %collective-permute-start.14 = (f32[4,128,128]{2,1,0:T(8,128)S(1)}, f32[4,128,128]{2,1,0:T(8,128)S(1)}, u32[]{:S(2)}, u32[]{:S(2)}) collective-permute-start(f32[4,128,128]{2,1,0:T(8,128)S(1)} %pad_maximum_fusion.7), channel_id=1, source_target_pairs={{4,0},{8,4},{12,8},{16,12},{20,16},{24,20},{28,24},{32,28},{36,32}... | collective-permute-start | bytes 786440 | tf_op jit(solution)/shard_map/ppermute | solution.py:10
  47.1 22.8 %collective-permute-start.4 = (f32[4,128,128]{2,1,0:T(8,128)S(1)}, f32[4,128,128]{2,1,0:T(8,128)S(1)}, u32[]{:S(2)}, u32[]{:S(2)}) collective-permute-start(f32[4,128,128]{2,1,0:T(8,128)S(1)} %pad_maximum_fusion.1), channel_id=1, source_target_pairs={{0,4},{4,8},{8,12},{12,16},{16,20},{20,24},{24,28},{28,32},{32,36}... | collective-permute-start | bytes 786440 | tf_op jit(solution)/shard_map/ppermute | solution.py:10
  50.0 6.9 %collective-permute-start.11 = (f32[2,128,128]{2,1,0:T(8,128)S(1)}, f32[2,128,128]{2,1,0:T(8,128)S(1)}, u32[]{:S(2)}, u32[]{:S(2)}) collective-permute-start(f32[2,128,128]{2,1,0:T(8,128)S(1)} %pad_maximum_fusion.22), channel_id=1, source_target_pairs={{8,0},{12,4},{16,8},{20,12},{24,16},{28,20},{32,24},{36,28},{40,32... | collective-permute-start | bytes 393224 | tf_op jit(solution)/shard_map/ppermute | solution.py:10
  53.4 10.1 %collective-permute-start.1 = (f32[2,128,128]{2,1,0:T(8,128)S(1)}, f32[2,128,128]{2,1,0:T(8,128)S(1)}, u32[]{:S(2)}, u32[]{:S(2)}) collective-permute-start(f32[2,128,128]{2,1,0:T(8,128)S(1)} %pad_maximum_fusion.18), channel_id=1, source_target_pairs={{0,8},{4,12},{8,16},{12,20},{16,24},{20,28},{24,32},{28,36},{32,40... | collective-permute-start | bytes 393224 | tf_op jit(solution)/shard_map/ppermute | solution.py:10
  56.9 15.0 %collective-permute-start.12 = (f32[2,128,128]{2,1,0:T(8,128)S(1)}, f32[2,128,128]{2,1,0:T(8,128)S(1)}, u32[]{:S(2)}, u32[]{:S(2)}) collective-permute-start(f32[2,128,128]{2,1,0:T(8,128)S(1)} %pad_maximum_fusion.23), channel_id=1, source_target_pairs={{16,0},{20,4},{24,8},{28,12},{32,16},{36,20},{40,24},{44,28},{48,3... | collective-permute-start | bytes 393224 | tf_op jit(solution)/shard_map/ppermute | solution.py:10
  63.5 11.3 %collective-permute-start.2 = (f32[2,128,128]{2,1,0:T(8,128)S(1)}, f32[2,128,128]{2,1,0:T(8,128)S(1)}, u32[]{:S(2)}, u32[]{:S(2)}) collective-permute-start(f32[2,128,128]{2,1,0:T(8,128)S(1)} %pad_maximum_fusion.19), channel_id=1, source_target_pairs={{0,16},{4,20},{8,24},{12,28},{16,32},{20,36},{24,40},{28,44},{32,4... | collective-permute-start | bytes 393224 | tf_op jit(solution)/shard_map/ppermute | solution.py:10
  65.6 17.6 %collective-permute-start.15 = (f32[4,128,128]{2,1,0:T(8,128)S(1)}, f32[4,128,128]{2,1,0:T(8,128)S(1)}, u32[]{:S(2)}, u32[]{:S(2)}) collective-permute-start(f32[4,128,128]{2,1,0:T(8,128)S(1)} %pad_maximum_fusion.8), channel_id=1, source_target_pairs={{8,0},{12,4},{16,8},{20,12},{24,16},{28,20},{32,24},{36,28},{40,32... | collective-permute-start | bytes 786440 | tf_op jit(solution)/shard_map/ppermute | solution.py:10
  70.0 18.4 %collective-permute-start.5 = (f32[4,128,128]{2,1,0:T(8,128)S(1)}, f32[4,128,128]{2,1,0:T(8,128)S(1)}, u32[]{:S(2)}, u32[]{:S(2)}) collective-permute-start(f32[4,128,128]{2,1,0:T(8,128)S(1)} %pad_maximum_fusion.2), channel_id=1, source_target_pairs={{0,8},{4,12},{8,16},{12,20},{16,24},{20,28},{24,32},{28,36},{32,40... | collective-permute-start | bytes 786440 | tf_op jit(solution)/shard_map/ppermute | solution.py:10
  72.0 6.9 %collective-permute-start.13 = (f32[2,128,128]{2,1,0:T(8,128)S(1)}, f32[2,128,128]{2,1,0:T(8,128)S(1)}, u32[]{:S(2)}, u32[]{:S(2)}) collective-permute-start(f32[2,128,128]{2,1,0:T(8,128)S(1)} %pad_maximum_fusion.24), channel_id=1, source_target_pairs={{32,0},{36,4},{40,8},{44,12},{48,16},{52,20},{56,24},{60,28},{64,3... | collective-permute-start | bytes 393224 | tf_op jit(solution)/shard_map/ppermute | solution.py:10
  74.9 61.2 %copy-start.11 = (f32[1,128,128]{2,1,0:T(8,128)S(1)}, f32[1,128,128]{2,1,0:T(8,128)}, u32[]{:S(2)}) copy-start(f32[1,128,128]{2,1,0:T(8,128)} %copy-done.10) | copy-start | bytes 196612
  74.9 61.2 %copy-start.13 = (f32[1,128,128]{2,1,0:T(8,128)S(1)}, f32[1,128,128]{2,1,0:T(8,128)}, u32[]{:S(2)}) copy-start(f32[1,128,128]{2,1,0:T(8,128)} %copy-done.12) | copy-start | bytes 196612
  74.9 61.2 %copy-start.16 = (f32[1,128,128]{2,1,0:T(8,128)S(1)}, f32[1,128,128]{2,1,0:T(8,128)}, u32[]{:S(2)}) copy-start(f32[1,128,128]{2,1,0:T(8,128)} %get-tuple-element.49) | copy-start | bytes 196612
  74.9 61.2 %copy-start.17 = (f32[1,128,128]{2,1,0:T(8,128)S(1)}, f32[1,128,128]{2,1,0:T(8,128)}, u32[]{:S(2)}) copy-start(f32[1,128,128]{2,1,0:T(8,128)} %get-tuple-element.50) | copy-start | bytes 196612
  74.9 8.2 %collective-permute-start.3 = (f32[2,128,128]{2,1,0:T(8,128)S(1)}, f32[2,128,128]{2,1,0:T(8,128)S(1)}, u32[]{:S(2)}, u32[]{:S(2)}) collective-permute-start(f32[2,128,128]{2,1,0:T(8,128)S(1)} %pad_maximum_fusion.20), channel_id=1, source_target_pairs={{0,32},{4,36},{8,40},{12,44},{16,48},{20,52},{24,56},{28,60},{32,6... | collective-permute-start | bytes 393224 | tf_op jit(solution)/shard_map/ppermute | solution.py:10
  83.3 12.6 %collective-permute-start.16 = (f32[4,128,128]{2,1,0:T(8,128)S(1)}, f32[4,128,128]{2,1,0:T(8,128)S(1)}, u32[]{:S(2)}, u32[]{:S(2)}) collective-permute-start(f32[4,128,128]{2,1,0:T(8,128)S(1)} %pad_maximum_fusion.9), channel_id=1, source_target_pairs={{16,0},{20,4},{24,8},{28,12},{32,16},{36,20},{40,24},{44,28},{48,3... | collective-permute-start | bytes 786440 | tf_op jit(solution)/shard_map/ppermute | solution.py:10
  88.4 47.8 %copy-start.7 = (f32[1,128,128]{2,1,0:T(8,128)S(1)}, f32[1,128,128]{2,1,0:T(8,128)}, u32[]{:S(2)}) copy-start(f32[1,128,128]{2,1,0:T(8,128)} %copy-done.6) | copy-start | bytes 196612
  88.4 47.8 %copy-start.9 = (f32[1,128,128]{2,1,0:T(8,128)S(1)}, f32[1,128,128]{2,1,0:T(8,128)}, u32[]{:S(2)}) copy-start(f32[1,128,128]{2,1,0:T(8,128)} %copy-done.8) | copy-start | bytes 196612
  88.5 47.8 %copy-start.14 = (f32[1,128,128]{2,1,0:T(8,128)S(1)}, f32[1,128,128]{2,1,0:T(8,128)}, u32[]{:S(2)}) copy-start(f32[1,128,128]{2,1,0:T(8,128)} %get-tuple-element.10) | copy-start | bytes 196612
  88.5 12.4 %collective-permute-start.6 = (f32[4,128,128]{2,1,0:T(8,128)S(1)}, f32[4,128,128]{2,1,0:T(8,128)S(1)}, u32[]{:S(2)}, u32[]{:S(2)}) collective-permute-start(f32[4,128,128]{2,1,0:T(8,128)S(1)} %pad_maximum_fusion.3), channel_id=1, source_target_pairs={{0,16},{4,20},{8,24},{12,28},{16,32},{20,36},{24,40},{28,44},{32,4... | collective-permute-start | bytes 786440 | tf_op jit(solution)/shard_map/ppermute | solution.py:10
  95.9 8.3 %collective-permute-start.17 = (f32[4,128,128]{2,1,0:T(8,128)S(1)}, f32[4,128,128]{2,1,0:T(8,128)S(1)}, u32[]{:S(2)}, u32[]{:S(2)}) collective-permute-start(f32[4,128,128]{2,1,0:T(8,128)S(1)} %pad_maximum_fusion.10), channel_id=1, source_target_pairs={{32,0},{36,4},{40,8},{44,12},{48,16},{52,20},{56,24},{60,28},{64,3... | collective-permute-start | bytes 786440 | tf_op jit(solution)/shard_map/ppermute | solution.py:10
  101.0 9.8 %collective-permute-start.7 = (f32[4,128,128]{2,1,0:T(8,128)S(1)}, f32[4,128,128]{2,1,0:T(8,128)S(1)}, u32[]{:S(2)}, u32[]{:S(2)}) collective-permute-start(f32[4,128,128]{2,1,0:T(8,128)S(1)} %pad_maximum_fusion.4), channel_id=1, source_target_pairs={{0,32},{4,36},{8,40},{12,44},{16,48},{20,52},{24,56},{28,60},{32,6... | collective-permute-start | bytes 786440 | tf_op jit(solution)/shard_map/ppermute | solution.py:10
  104.3 10.2 %collective-permute-start.18 = (f32[4,128,128]{2,1,0:T(8,128)S(1)}, f32[4,128,128]{2,1,0:T(8,128)S(1)}, u32[]{:S(2)}, u32[]{:S(2)}) collective-permute-start(f32[4,128,128]{2,1,0:T(8,128)S(1)} %pad_maximum_fusion.11), channel_id=1, source_target_pairs={{64,0},{68,4},{72,8},{76,12},{80,16},{84,20},{88,24},{92,28},{96,3... | collective-permute-start | bytes 786440 | tf_op jit(solution)/shard_map/ppermute | solution.py:10
  110.9 13.8 %collective-permute-start.8 = (f32[4,128,128]{2,1,0:T(8,128)S(1)}, f32[4,128,128]{2,1,0:T(8,128)S(1)}, u32[]{:S(2)}, u32[]{:S(2)}) collective-permute-start(f32[4,128,128]{2,1,0:T(8,128)S(1)} %pad_maximum_fusion.5), channel_id=1, source_target_pairs={{0,64},{4,68},{8,72},{12,76},{16,80},{20,84},{24,88},{28,92},{32,9... | collective-permute-start | bytes 786440 | tf_op jit(solution)/shard_map/ppermute | solution.py:10
  114.5 14.0 %collective-permute-start.19 = (f32[4,128,128]{2,1,0:T(8,128)S(1)}, f32[4,128,128]{2,1,0:T(8,128)S(1)}, u32[]{:S(2)}, u32[]{:S(2)}) collective-permute-start(f32[4,128,128]{2,1,0:T(8,128)S(1)} %pad_maximum_fusion.12), channel_id=1, source_target_pairs={{4,0},{8,4},{12,8},{16,12},{20,16},{24,20},{28,24},{32,28},{36,32}... | collective-permute-start | bytes 786440 | tf_op jit(solution)/shard_map/ppermute | solution.py:10
  124.8 11.3 %collective-permute-start.9 = (f32[4,128,128]{2,1,0:T(8,128)S(1)}, f32[4,128,128]{2,1,0:T(8,128)S(1)}, u32[]{:S(2)}, u32[]{:S(2)}) collective-permute-start(f32[4,128,128]{2,1,0:T(8,128)S(1)} %pad_maximum_fusion.6), channel_id=1, source_target_pairs={{0,4},{4,8},{8,12},{12,16},{16,20},{20,24},{24,28},{28,32},{32,36}... | collective-permute-start | bytes 786440 | tf_op jit(solution)/shard_map/ppermute | solution.py:10
  139.6 14.1 %collective-permute-start.20 = (f32[4,4,128]{2,1,0:T(4,128)S(1)}, f32[4,4,128]{2,1,0:T(4,128)S(1)}, u32[]{:S(2)}, u32[]{:S(2)}) collective-permute-start(f32[4,4,128]{2,1,0:T(4,128)S(1)} %bitcast.290), channel_id=1, source_target_pairs={{2,0},{3,1},{6,4},{7,5},{10,8},{11,9},{14,12},{15,13},{18,16},{19,... | collective-permute-start | bytes 24584 | tf_op jit(solution)/shard_map/ppermute | solution.py:10
  140.9 12.8 %collective-permute-start.21 = (f32[4,4,128]{2,1,0:T(4,128)S(1)}, f32[4,4,128]{2,1,0:T(4,128)S(1)}, u32[]{:S(2)}, u32[]{:S(2)}) collective-permute-start(f32[4,4,128]{2,1,0:T(4,128)S(1)} %bitcast.289), channel_id=1, source_target_pairs={{0,2},{1,3},{4,6},{5,7},{8,10},{9,11},{12,14},{13,15},{16,18},{17,... | collective-permute-start | bytes 24584 | tf_op jit(solution)/shard_map/ppermute | solution.py:10
  147.0 6.0 %collective-permute-start.22 = (f32[4,4,128]{2,1,0:T(4,128)S(1)}, f32[4,4,128]{2,1,0:T(4,128)S(1)}, u32[]{:S(2)}, u32[]{:S(2)}) collective-permute-start(f32[4,4,128]{2,1,0:T(4,128)S(1)} %get-tuple-element.6), channel_id=1, source_target_pairs={{1,0},{3,2},{5,4},{7,6},{9,8},{11,10},{13,12},{15,14},{17,16},{19,... | collective-permute-start | bytes 24584 | tf_op jit(solution)/shard_map/ppermute | solution.py:10
  148.3 5.1 %collective-permute-start.23 = (f32[4,4,128]{2,1,0:T(4,128)S(1)}, f32[4,4,128]{2,1,0:T(4,128)S(1)}, u32[]{:S(2)}, u32[]{:S(2)}) collective-permute-start(f32[4,4,128]{2,1,0:T(4,128)S(1)} %get-tuple-element.5), channel_id=1, source_target_pairs={{0,1},{2,3},{4,5},{6,7},{8,9},{10,11},{12,13},{14,15},{16,17},{18,... | collective-permute-start | bytes 24584 | tf_op jit(solution)/shard_map/ppermute | solution.py:10
  (11 other events, 171.8 us)

commit v4 on v3

--- a/solution.py
+++ b/solution.py
@@ -63,32 +63,85 @@
     return source + added
 
 
-def map_powers(a_re, a_im, sign):
-    slab_count = lax.axis_size("slab")
-    powers = [(a_re, a_im)]
+def exchange(array, step):
+    count = lax.axis_size("slab")
+    return lax.ppermute(array, "slab", [(i, i ^ step) for i in range(count)])
+
+
+def block_products(a_re, a_im):
+    slab_count = lax.axis_size("slab")
+    here = lax.axis_index("slab")
+    one = jnp.ones_like(a_re)
+    zero = jnp.zeros_like(a_re)
+    total = (a_re, a_im)
+    below = (one, zero)
+    above = (one, zero)
+    levels = []
     step = 1
     while 2 * step < slab_count:
-        got = from_behind(jnp.stack([a_re, a_im], axis=0), "slab", sign * step)
-        a_re, a_im = complex_times(a_re, a_im, got[0], got[1])
-        powers.append((a_re, a_im))
+        got = exchange(jnp.stack(total, axis=0), step)
+        partner = (got[0], got[1])
+        levels.append((total, partner, below, above))
+        lower = (here & step) == 0
+        grown_below = complex_times(*below, *partner)
+        grown_above = complex_times(*above, *partner)
+        below = (jnp.where(lower, below[0], grown_below[0]), jnp.where(lower, below[1], grown_below[1]))
+        above = (jnp.where(lower, grown_above[0], above[0]), jnp.where(lower, grown_above[1], above[1]))
+        total = complex_times(*total, *partner)
         step *= 2
-    return powers
-
-
-def entering_state(b_re, b_im, powers, sign):
-    slab_count = lax.axis_size("slab")
-    shots = b_re.shape[0]
+    levels.append((None, None, below, above))
+    return levels
+
+
+def entering_states(down_b, up_b, levels):
+    slab_count = lax.axis_size("slab")
+    here = lax.axis_index("slab")
+    shots = down_b[0].shape[0]
+    before = (jnp.zeros_like(down_b[0]), jnp.zeros_like(down_b[1]))
+    after = (jnp.zeros_like(up_b[0]), jnp.zeros_like(up_b[1]))
     step = 1
     level = 0
     while step < slab_count:
-        got = from_behind(jnp.concatenate([b_re, b_im], axis=0), "slab", sign * step)
-        a_re, a_im = powers[level]
-        t_re, t_im = complex_times(a_re[None], a_im[None], got[:shots], got[shots:])
-        b_re, b_im = t_re + b_re, t_im + b_im
+        lower = (here & step) == 0
+        total, partner, below, above = levels[level]
+        if 2 * step < slab_count:
+            got = exchange(jnp.concatenate([*down_b, *up_b], axis=0), step)
+            pd = (got[:shots], got[shots : 2 * shots])
+            pu = (got[2 * shots : 3 * shots], got[3 * shots :])
+            t_re, t_im = total[0][None], total[1][None]
+            q_re, q_im = partner[0][None], partner[1][None]
+            first = (jnp.where(lower, q_re, t_re), jnp.where(lower, q_im, t_im))
+            inner = (jnp.where(lower, down_b[0], pd[0]), jnp.where(lower, down_b[1], pd[1]))
+            outer = (jnp.where(lower, pd[0], down_b[0]), jnp.where(lower, pd[1], down_b[1]))
+            m_re, m_im = complex_times(*first, *inner)
+            new_down = (m_re + outer[0], m_im + outer[1])
+            first = (jnp.where(lower, t_re, q_re), jnp.where(lower, t_im, q_im))
+            inner = (jnp.where(lower, pu[0], up_b[0]), jnp.where(lower, pu[1], up_b[1]))
+            outer = (jnp.where(lower, up_b[0], pu[0]), jnp.where(lower, up_b[1], pu[1]))
+            m_re, m_im = complex_times(*first, *inner)
+            new_up = (m_re + outer[0], m_im + outer[1])
+        else:
+            send = jnp.concatenate(
+                [jnp.where(lower, down_b[0], up_b[0]), jnp.where(lower, down_b[1], up_b[1])], axis=0
+            )
+            got = exchange(send, step)
+            pd = (got[:shots], got[shots:])
+            pu = pd
+        g_re, g_im = complex_times(below[0][None], below[1][None], *pd)
+        before = (
+            jnp.where(lower, before[0], g_re + before[0]),
+            jnp.where(lower, before[1], g_im + before[1]),
+        )
+        g_re, g_im = complex_times(above[0][None], above[1][None], *pu)
+        after = (
+            jnp.where(lower, g_re + after[0], after[0]),
+            jnp.where(lower, g_im + after[1], after[1]),
+        )
+        if 2 * step < slab_count:
+            down_b, up_b = new_down, new_up
         step *= 2
         level += 1
-    got = from_behind(jnp.concatenate([b_re, b_im], axis=0), "slab", sign)
-    return got[:shots], got[shots:]
+    return before, after
 
 
 def neighbour_sum(block):
@@ -121,8 +174,7 @@
     prod_up[layers - 1] = (rate_re[layers - 1], rate_im[layers - 1])
     for k in range(layers - 2, -1, -1):
         prod_up[k] = complex_times(rate_re[k], rate_im[k], *prod_up[k + 1])
-    powers_down = map_powers(*prod_down[-1], 1)
-    powers_up = map_powers(*prod_up[0], -1)
+    levels = block_products(*prod_down[-1])
 
     forcing = inject_receivers(source, recv_values, recv_slab, recv_lateral, recv_layer)
     fields = forcing.reshape(layers, shot_count, 2, width_x, width_y)
@@ -144,8 +196,7 @@
         state = (t_re + f_re[k], t_im + f_im[k])
         up[k] = state
 
-    enter_re, enter_im = entering_state(*down[layers - 1], powers_down, 1)
-    below_re, below_im = entering_state(*up[0], powers_up, -1)
+    (enter_re, enter_im), (below_re, below_im) = entering_states(down[layers - 1], up[0], levels)
 
     combined = []
     for k in range(layers):

time: 159 us -> 140 us (0.88)
  the two profiles are of different devices: /device:TPU:64 before, /device:TPU:1 now
where the time goes in v4:
time: 140 us; the launch traced here: 139 us
  waiting for transfers between devices  47.8 us (34%)
  other arithmetic  39.4 us (28%)
  starting transfers between devices  35.8 us (26%)
  local copies, waits for them, and re-layouts  11.4 us (8%)
  matrix products  3.53 us (3%)
    ppermute x9, waiting for transfers between devices, exchange(): return lax.ppermute(array, 'slab', [(i, i ^ step) for i in range(count)])  44.2 us
    ppermute x4, starting transfers between devices, from_behind(): return lax.ppermute(array, axis, pairs)  16.7 us
    all_to_all x1, starting transfers between devices, inject_receivers(): lax.all_to_all(send_rows.reshape(components + 1, slab_count, capacity), '...  9.81 us
    ppermute x9, starting transfers between devices, exchange(): return lax.ppermute(array, 'slab', [(i, i ^ step) for i in range(count)])  9.26 us
    mul x5, other arithmetic, complex_times(): return (a_re * b_re - a_im * b_im, a_re * b_im + a_im * b_re)  5.57 us
    sub x1, other arithmetic, shards(): return combined - 0.2 * (4.0 * combined - neighbours)  3.99 us
    all_to_all x1, waiting for transfers between devices, inject_receivers(): lax.all_to_all(send_rows.reshape(components + 1, slab_count, capacity), '...  3.53 us
    dot_general x1, matrix products, inject_receivers(): jnp.dot(pick_rows, spread.astype(jnp.bfloat16), preferred_element_type=jn...  3.53 us
  transfers between devices with their start and end apart: 14, of which 6 were waited for; matrix products, arithmetic and copies ran while one was open for 13% of the time, Pallas kernels for 0%

profile of v4, /device:TPU:1, one launch (start us, length us, event | category | flops | bytes accessed | tf_op | source)
XLA Modules:
  0.0 138.8 jit_solution(1539153138155020588)
XLA Ops:
  0.7 1.2 reduce-window.6
  5.2 2.0 %scatter_custom_fusion = f32[5,2048]{0,1:T(8,128)S(1)} fusion(s32[512]{0:T(512)S(1)} %bitcast.321, f32[512,5]{1,0:T(8,128)S(1)} %copy.69, f32[]{:T(128)} %constant.21.clone.1), kind=kCustom, calls=%fused_computation.23 | custom fusion | bytes 40964 | tf_op jit(solution)/shard_map/scatter | solution.py:33
  8.2 9.8 %all-to-all-start = ((f32[32,1,320]{2,1,0:T(1,128)}), f32[32,1,320]{2,1,0:T(1,128)S(1)}, u32[]{:S(2)}, u32[]{:S(2)}) async-start(f32[32,1,320]{2,1,0:T(1,128)} %reshape.231), calls=%async_computation | async-start | bytes 98304 | tf_op jit(solution)/shard_map/all_to_all | solution.py:35
  18.9 2.0 %cosine_multiply_fusion = (f32[4,128,128]{2,1,0:T(8,128)S(1)}, f32[4,128,128]{2,1,0:T(8,128)S(1)}) fusion(f32[4,128,128]{2,1,0:T(8,128)} %param.9, f32[4,128,128]{2,1,0:T(8,128)} %param.10, f32[128,128]{1,0:T(8,128)S(1)} %convert_multiply_fusion), kind=kLoop, calls=%fused_computation.31 | loop fusion | flops 262144 | bytes 1114112 | tf_op jit(solution)/shard_map/mul | solution.py:167
  21.7 3.5 %all-to-all-done = f32[32,1,320]{2,1,0:T(1,128)S(1)} async-done(((f32[32,1,320]{2,1,0:T(1,128)}), f32[32,1,320]{2,1,0:T(1,128)S(1)}, u32[]{:S(2)}, u32[]{:S(2)}) %all-to-all-start) | async-done | bytes 40992 | tf_op jit(solution)/shard_map/all_to_all | solution.py:35
  28.0 3.5 %fusion.1 = f32[512,3,512]{2,0,1:T(8,128)S(1)} fusion(bf16[3,512,2048]{2,1,0:T(8,128)(2,1)S(1)} %bitcast.280, s32[2048]{0:T(1024)S(1)} %get-tuple-element.138), kind=kOutput, calls=%fused_computation.4 | convolution fusion | flops 3222274048 | bytes 9445376 | tf_op jit(solution)/shard_map/dot_general | solution.py:59
  32.3 1.4 %bitcast_add_fusion = f32[4,4,128,128]{3,2,1,0:T(8,128)S(1)} fusion(f32[4,4,128,128]{3,2,1,0:T(8,128)} %param.8, f32[4,128,4,128]{3,2,1,0:T(4,128)S(1)} %add.514), kind=kLoop, calls=%fused_computation.17 | loop fusion | flops 262144 | bytes 3145728 | tf_op jit(solution)/shard_map/add | solution.py:63
  34.6 1.7 %subtract_add_fusion.3 = (f32[2,128,128]{2,1,0:T(8,128)S(1)}, f32[2,128,128]{2,1,0:T(8,128)S(1)}, f32[2,128,128]{2,1,0:T(8,128)S(1)}, f32[2,128,128]{2,1,0:T(8,128)}, f32[2,128,128]{2,1,0:T(8,128)}) fusion(f32[4,2,2,128,128]{4,3,2,1,0:T(8,128)S(1)} %bitcast.274, f32[128,128]{1,0:T(8,128)S(1)} %get-tuple-element.100, f32[128,128]{1,0:T(8,128)S(1)} %get-tuple-element.97, ...), kind=kLoop, calls=%fused_computation.90 | loop fusion | flops 655360 | bytes 1966080 | tf_op jit(solution)/shard_map/add | solution.py:189
  39.2 1.0 collective-permute-start.1
  40.2 11.4 %collective-permute-done.1 = f32[2,128,128]{2,1,0:T(8,128)} collective-permute-done((f32[2,128,128]{2,1,0:T(8,128)}, f32[2,128,128]{2,1,0:T(8,128)}, u32[]{:S(2)}, u32[]{:S(2)}) %collective-permute-start.1) | collective-permute-done | bytes 131104 | tf_op jit(solution)/shard_map/ppermute | solution.py:68
  51.7 1.6 %select_bitcast_fusion.23 = (f32[128,128]{1,0:T(8,128)}, f32[1,128,128]{2,1,0:T(8,128)}, f32[128,128]{1,0:T(8,128)S(1)}, f32[128,128]{1,0:T(8,128)S(1)}, f32[128...) fusion(pred[]{:T(512)S(6)} %eq.94, ...), kind=kLoop, calls=%fused_computation.173 | loop fusion | flops 262144 | bytes 917505 | tf_op jit(solution)/shard_map/mul | solution.py:14
  56.5 11.2 %collective-permute-done.3 = f32[2,128,128]{2,1,0:T(8,128)} collective-permute-done((f32[2,128,128]{2,1,0:T(8,128)}, f32[2,128,128]{2,1,0:T(8,128)}, u32[]{:S(2)}, u32[]{:S(2)}) %collective-permute-start.3) | collective-permute-done | bytes 131104 | tf_op jit(solution)/shard_map/ppermute | solution.py:68
  68.7 1.2 select_add_fusion.7
  71.5 1.1 collective-permute-start.4
  73.2 1.9 %collective-permute-start.5 = (f32[2,128,128]{2,1,0:T(8,128)}, f32[2,128,128]{2,1,0:T(8,128)}, u32[]{:S(2)}, u32[]{:S(2)}) collective-permute-start(f32[2,128,128]{2,1,0:T(8,128)} %pad_maximum_fusion.12), channel_id=1, source_target_pairs={{0,16},{4,20},{8,24},{12,28},{16,0},{20,4},{24,8},{28,12},{32,48},... | collective-permute-start | bytes 393224 | tf_op jit(solution)/shard_map/ppermute | solution.py:68
  75.1 10.2 %collective-permute-done.5 = f32[2,128,128]{2,1,0:T(8,128)} collective-permute-done((f32[2,128,128]{2,1,0:T(8,128)}, f32[2,128,128]{2,1,0:T(8,128)}, u32[]{:S(2)}, u32[]{:S(2)}) %collective-permute-start.5) | collective-permute-done | bytes 131104 | tf_op jit(solution)/shard_map/ppermute | solution.py:68
  87.2 1.2 select_add_fusion.3
  89.9 1.3 collective-permute-start.6
  91.4 1.3 select_bitcast_fusion.1
  93.7 7.4 %collective-permute-done.6 = f32[8,128,128]{2,1,0:T(8,128)} collective-permute-done((f32[8,128,128]{2,1,0:T(8,128)}, f32[8,128,128]{2,1,0:T(8,128)}, u32[]{:S(2)}, u32[]{:S(2)}) %collective-permute-start.6) | collective-permute-done | bytes 524320 | tf_op jit(solution)/shard_map/ppermute | solution.py:68
  101.1 1.5 %add_select_fusion.17 = (f32[2,128,128]{2,1,0:T(8,128)S(1)}, f32[2,128,128]{2,1,0:T(8,128)S(1)}) fusion(f32[2,128,128]{2,1,0:T(8,128)} %copy-done.20, f32[2,128,128]{2,1,0:T(8,128)} %copy-done.17, f32[2,128,128]{2,1,0:T(8,128)} %copy-done.19, f32[8,128,128]{2,1,0:T(8,128)} %collective-permute-done.6, f32[2,128,128]{2,1,0:T(8,128)} %copy-done.18, ...), kind=kLoop, calls=%fused_computation.70 | loop fusion | flops 851968 | bytes 1572866 | tf_op jit(solution)/shard_map/jit(_where)/select_n | solution.py:125
  102.6 1.8 %collective-permute-start.8 = (f32[4,128,128]{2,1,0:T(8,128)S(1)}, f32[4,128,128]{2,1,0:T(8,128)S(1)}, u32[]{:S(2)}, u32[]{:S(2)}) collective-permute-start(f32[4,128,128]{2,1,0:T(8,128)S(1)} %pad_maximum_fusion.5), channel_id=1, source_target_pairs={{0,64},{4,68},{8,72},{12,76},{16,80},{20,84},{24,88},{28,92},{32,9... | collective-permute-start | bytes 786440 | tf_op jit(solution)/shard_map/ppermute | solution.py:68
  105.3 4.1 %collective-permute-done.8 = f32[4,128,128]{2,1,0:T(8,128)S(1)} collective-permute-done((f32[4,128,128]{2,1,0:T(8,128)S(1)}, f32[4,128,128]{2,1,0:T(8,128)S(1)}, u32[]{:S(2)}, u32[]{:S(2)}) %collective-permute-start.8) | collective-permute-done | bytes 262176 | tf_op jit(solution)/shard_map/ppermute | solution.py:68
  109.4 1.6 %subtract_bitcast_fusion.7 = (f32[2,1,128,128]{3,2,0,1:T(8,128)S(1)}, f32[2,128,128]{2,1,0:T(8,128)S(1)}, f32[2,128,128]{2,1,0:T(8,128)S(1)}, f32[2,128,128]{2,1,0:T(8,128)S(1)}, f32[2,128,128]{2,1,0:T(8,128)S(1)}) fusion(f32[2,128,128]{2,1,0:T(8,128)S(1)} %get-tuple-element.41, f32[4,2,2,128,128]{4,3,2,1,0:T(8,128)S(1)} %bitcast.276, ...), kind=kLoop, calls=%fused_computation.68 | loop fusion | flops 3342336 | bytes 4587525 | tf_op jit(solution)/shard_map/stack | solution.py:207
  111.6 1.0 subtract_bitcast_fusion.1
  113.5 1.2 fusion.20
  115.7 1.3 collective-permute-start.9
  117.0 5.5 %collective-permute-start.10 = (f32[4,4,128]{2,1,0:T(4,128)S(1)}, f32[4,4,128]{2,1,0:T(4,128)S(1)}, u32[]{:S(2)}, u32[]{:S(2)}) collective-permute-start(f32[4,4,128]{2,1,0:T(4,128)S(1)} %bitcast.317), channel_id=1, source_target_pairs={{0,2},{1,3},{4,6},{5,7},{8,10},{9,11},{12,14},{13,15},{16,18},{17,... | collective-permute-start | bytes 24584 | tf_op jit(solution)/shard_map/ppermute | solution.py:10
  122.5 8.6 %collective-permute-start.11 = (f32[4,4,128]{2,1,0:T(4,128)S(1)}, f32[4,4,128]{2,1,0:T(4,128)S(1)}, u32[]{:S(2)}, u32[]{:S(2)}) collective-permute-start(f32[4,4,128]{2,1,0:T(4,128)S(1)} %get-tuple-element.6), channel_id=1, source_target_pairs={{1,0},{3,2},{5,4},{7,6},{9,8},{11,10},{13,12},{15,14},{17,16},{19,... | collective-permute-start | bytes 24584 | tf_op jit(solution)/shard_map/ppermute | solution.py:10
  131.1 1.3 collective-permute-start.12
  132.4 1.7 %fusion.18 = (f32[4,4,128,127]{3,2,1,0:T(8,128)}, f32[4,4,128,127]{3,2,1,0:T(8,128)}) fusion(f32[4,4,128,128]{3,2,1,0:T(8,128)S(1)} %pad_maximum_fusion), kind=kLoop, calls=%fused_computation.198 | loop fusion | bytes 4161536 | tf_op jit(solution)/shard_map/slice | solution.py:155
  134.8 4.0 %fusion.8 = f32[4,4,128,128]{3,2,1,0:T(8,128)} fusion(f32[4,4,1,128]{3,2,1,0:T(1,128)S(1)} %bitcast.319, f32[4,4,127,128]{3,2,1,0:T(8,128)} %get-tuple-element.60, f32[4,4,127,128]{3,2,1,0:T(8,128)S(1)} %get-tuple-element.59, f32[4,4,1,128]{3,2,1,0:T(1,128)S(1)} %bitcast.320, f32[4,4,128,1]{3,2,1,0:T(8,128)S(1)} %copy.87, ...), kind=kLoop, calls=%fused_computation.16 | loop fusion | flops 3670016 | bytes 6291456 | tf_op jit(solution)/shard_map/sub | solution.py:210
  (191 shorter events, 28.3 us)
Async XLA Ops:
  8.2 17.0 %all-to-all-start = ((f32[32,1,320]{2,1,0:T(1,128)}), f32[32,1,320]{2,1,0:T(1,128)S(1)}, u32[]{:S(2)}, u32[]{:S(2)}) async-start(f32[32,1,320]{2,1,0:T(1,128)} %reshape.231), calls=%async_computation | async-start | bytes 98304 | tf_op jit(solution)/shard_map/all_to_all | solution.py:35
  21.7 30.0 %copy-start.35 = (f32[1,128,128]{2,1,0:T(8,128)}, f32[1,128,128]{2,1,0:T(8,128)S(1)}, u32[]{:S(2)}) copy-start(f32[1,128,128]{2,1,0:T(8,128)S(1)} %get-tuple-element.31) | copy-start | bytes 196612
  21.7 87.7 %copy-start.7 = (f32[128,128]{1,0:T(8,128)}, f32[128,128]{1,0:T(8,128)S(1)}, u32[]{:S(2)}) copy-start(f32[128,128]{1,0:T(8,128)S(1)} %get-tuple-element.98) | copy-start | bytes 196612
  21.7 87.7 %copy-start.8 = (f32[128,128]{1,0:T(8,128)}, f32[128,128]{1,0:T(8,128)S(1)}, u32[]{:S(2)}) copy-start(f32[128,128]{1,0:T(8,128)S(1)} %get-tuple-element.99) | copy-start | bytes 196612
  36.3 33.6 %copy-start.13 = (f32[2,128,128]{2,1,0:T(8,128)}, f32[2,128,128]{2,1,0:T(8,128)S(1)}, u32[]{:S(2)}) copy-start(f32[2,128,128]{2,1,0:T(8,128)S(1)} %get-tuple-element.37) | copy-start | bytes 393220
  36.3 33.7 %copy-start.15 = (f32[2,128,128]{2,1,0:T(8,128)}, f32[2,128,128]{2,1,0:T(8,128)S(1)}, u32[]{:S(2)}) copy-start(f32[2,128,128]{2,1,0:T(8,128)S(1)} %get-tuple-element.38) | copy-start | bytes 393220
  37.3 16.0 %collective-permute-start = (f32[8,128,128]{2,1,0:T(8,128)}, f32[8,128,128]{2,1,0:T(8,128)S(1)}, u32[]{:S(2)}, u32[]{:S(2)}) collective-permute-start(f32[8,128,128]{2,1,0:T(8,128)} %pad_maximum_fusion.1), channel_id=1, source_target_pairs={{0,4},{4,0},{8,12},{12,8},{16,20},{20,16},{24,28},{28,24},{32,36},... | collective-permute-start | bytes 1572872 | tf_op jit(solution)/shard_map/ppermute | solution.py:68
  39.2 12.4 %collective-permute-start.1 = (f32[2,128,128]{2,1,0:T(8,128)}, f32[2,128,128]{2,1,0:T(8,128)}, u32[]{:S(2)}, u32[]{:S(2)}) collective-permute-start(f32[2,128,128]{2,1,0:T(8,128)} %pad_maximum_fusion.10), channel_id=1, source_target_pairs={{0,4},{4,0},{8,12},{12,8},{16,20},{20,16},{24,28},{28,24},{32,36},... | collective-permute-start | bytes 393224 | tf_op jit(solution)/shard_map/ppermute | solution.py:68
  54.4 14.3 %collective-permute-start.2 = (f32[8,128,128]{2,1,0:T(8,128)}, f32[8,128,128]{2,1,0:T(8,128)S(1)}, u32[]{:S(2)}, u32[]{:S(2)}) collective-permute-start(f32[8,128,128]{2,1,0:T(8,128)} %pad_maximum_fusion.2), channel_id=1, source_target_pairs={{0,8},{4,12},{8,0},{12,4},{16,24},{20,28},{24,16},{28,20},{32,40},... | collective-permute-start | bytes 1572872 | tf_op jit(solution)/shard_map/ppermute | solution.py:68
  55.8 11.9 %collective-permute-start.3 = (f32[2,128,128]{2,1,0:T(8,128)}, f32[2,128,128]{2,1,0:T(8,128)}, u32[]{:S(2)}, u32[]{:S(2)}) collective-permute-start(f32[2,128,128]{2,1,0:T(8,128)} %pad_maximum_fusion.11), channel_id=1, source_target_pairs={{0,8},{4,12},{8,0},{12,4},{16,24},{20,28},{24,16},{28,20},{32,40},... | collective-permute-start | bytes 393224 | tf_op jit(solution)/shard_map/ppermute | solution.py:68
  71.5 15.7 %collective-permute-start.4 = (f32[8,128,128]{2,1,0:T(8,128)}, f32[8,128,128]{2,1,0:T(8,128)S(1)}, u32[]{:S(2)}, u32[]{:S(2)}) collective-permute-start(f32[8,128,128]{2,1,0:T(8,128)} %pad_maximum_fusion.3), channel_id=1, source_target_pairs={{0,16},{4,20},{8,24},{12,28},{16,0},{20,4},{24,8},{28,12},{32,48},... | collective-permute-start | bytes 1572872 | tf_op jit(solution)/shard_map/ppermute | solution.py:68
  73.2 12.0 %collective-permute-start.5 = (f32[2,128,128]{2,1,0:T(8,128)}, f32[2,128,128]{2,1,0:T(8,128)}, u32[]{:S(2)}, u32[]{:S(2)}) collective-permute-start(f32[2,128,128]{2,1,0:T(8,128)} %pad_maximum_fusion.12), channel_id=1, source_target_pairs={{0,16},{4,20},{8,24},{12,28},{16,0},{20,4},{24,8},{28,12},{32,48},... | collective-permute-start | bytes 393224 | tf_op jit(solution)/shard_map/ppermute | solution.py:68
  87.0 4.4 %collective-permute-start.7 = (f32[2,128,128]{2,1,0:T(8,128)}, f32[2,128,128]{2,1,0:T(8,128)}, u32[]{:S(2)}, u32[]{:S(2)}) collective-permute-start(f32[2,128,128]{2,1,0:T(8,128)} %pad_maximum_fusion.13), channel_id=1, source_target_pairs={{0,32},{4,36},{8,40},{12,44},{16,48},{20,52},{24,56},{28,60},{32,0... | collective-permute-start | bytes 393224 | tf_op jit(solution)/shard_map/ppermute | solution.py:68
  89.9 11.1 %collective-permute-start.6 = (f32[8,128,128]{2,1,0:T(8,128)}, f32[8,128,128]{2,1,0:T(8,128)}, u32[]{:S(2)}, u32[]{:S(2)}) collective-permute-start(f32[8,128,128]{2,1,0:T(8,128)} %pad_maximum_fusion.4), channel_id=1, source_target_pairs={{0,32},{4,36},{8,40},{12,44},{16,48},{20,52},{24,56},{28,60},{32,0... | collective-permute-start | bytes 1572872 | tf_op jit(solution)/shard_map/ppermute | solution.py:68
  91.2 19.8 %copy-start.49 = (f32[1,128,128]{2,1,0:T(8,128)S(1)}, f32[1,128,128]{2,1,0:T(8,128)}, u32[]{:S(2)}) copy-start(f32[1,128,128]{2,1,0:T(8,128)} %get-tuple-element.33) | copy-start | bytes 196612
  91.2 19.8 %copy-start.54 = (f32[2,128,128]{2,1,0:T(8,128)S(1)}, f32[2,128,128]{2,1,0:T(8,128)}, u32[]{:S(2)}) copy-start(f32[2,128,128]{2,1,0:T(8,128)} %get-tuple-element.44) | copy-start | bytes 393220
  91.2 19.8 %copy-start.55 = (f32[2,128,128]{2,1,0:T(8,128)S(1)}, f32[2,128,128]{2,1,0:T(8,128)}, u32[]{:S(2)}) copy-start(f32[2,128,128]{2,1,0:T(8,128)} %get-tuple-element.45) | copy-start | bytes 393220
  91.3 19.8 %copy-start.56 = (f32[1,128,128]{2,1,0:T(8,128)S(1)}, f32[1,128,128]{2,1,0:T(8,128)}, u32[]{:S(2)}) copy-start(f32[1,128,128]{2,1,0:T(8,128)} %get-tuple-element.15) | copy-start | bytes 196612
  91.3 19.8 %copy-start.57 = (f32[1,128,128]{2,1,0:T(8,128)S(1)}, f32[1,128,128]{2,1,0:T(8,128)}, u32[]{:S(2)}) copy-start(f32[1,128,128]{2,1,0:T(8,128)} %get-tuple-element.16) | copy-start | bytes 196612
  91.3 20.0 %copy-start.10 = (f32[2,128,128]{2,1,0:T(8,128)S(1)}, f32[2,128,128]{2,1,0:T(8,128)}, u32[]{:S(2)}) copy-start(f32[2,128,128]{2,1,0:T(8,128)} %copy-done.9) | copy-start | bytes 393220
  91.3 20.0 %copy-start.12 = (f32[2,128,128]{2,1,0:T(8,128)S(1)}, f32[2,128,128]{2,1,0:T(8,128)}, u32[]{:S(2)}) copy-start(f32[2,128,128]{2,1,0:T(8,128)} %copy-done.11) | copy-start | bytes 393220
  91.3 20.0 %copy-start.38 = (f32[1,128,128]{2,1,0:T(8,128)S(1)}, f32[1,128,128]{2,1,0:T(8,128)}, u32[]{:S(2)}) copy-start(f32[1,128,128]{2,1,0:T(8,128)} %get-tuple-element.13) | copy-start | bytes 196612
  91.3 20.0 %copy-start.39 = (f32[1,128,128]{2,1,0:T(8,128)S(1)}, f32[1,128,128]{2,1,0:T(8,128)}, u32[]{:S(2)}) copy-start(f32[1,128,128]{2,1,0:T(8,128)} %get-tuple-element.14) | copy-start | bytes 196612
  91.3 20.0 %copy-start.52 = (f32[2,128,128]{2,1,0:T(8,128)S(1)}, f32[2,128,128]{2,1,0:T(8,128)}, u32[]{:S(2)}) copy-start(f32[2,128,128]{2,1,0:T(8,128)} %get-tuple-element.39) | copy-start | bytes 393220
  91.3 20.0 %copy-start.53 = (f32[2,128,128]{2,1,0:T(8,128)S(1)}, f32[2,128,128]{2,1,0:T(8,128)}, u32[]{:S(2)}) copy-start(f32[2,128,128]{2,1,0:T(8,128)} %get-tuple-element.40) | copy-start | bytes 393220
  91.3 20.0 %copy-start.58 = (f32[1,128,128]{2,1,0:T(8,128)S(1)}, f32[1,128,128]{2,1,0:T(8,128)}, u32[]{:S(2)}) copy-start(f32[1,128,128]{2,1,0:T(8,128)} %get-tuple-element.34) | copy-start | bytes 196612
  91.3 20.0 %copy-start.59 = (f32[1,128,128]{2,1,0:T(8,128)S(1)}, f32[1,128,128]{2,1,0:T(8,128)}, u32[]{:S(2)}) copy-start(f32[1,128,128]{2,1,0:T(8,128)} %get-tuple-element.35) | copy-start | bytes 196612
  102.6 6.8 %collective-permute-start.8 = (f32[4,128,128]{2,1,0:T(8,128)S(1)}, f32[4,128,128]{2,1,0:T(8,128)S(1)}, u32[]{:S(2)}, u32[]{:S(2)}) collective-permute-start(f32[4,128,128]{2,1,0:T(8,128)S(1)} %pad_maximum_fusion.5), channel_id=1, source_target_pairs={{0,64},{4,68},{8,72},{12,76},{16,80},{20,84},{24,88},{28,92},{32,9... | collective-permute-start | bytes 786440 | tf_op jit(solution)/shard_map/ppermute | solution.py:68
  115.7 19.1 %collective-permute-start.9 = (f32[4,4,128]{2,1,0:T(4,128)S(1)}, f32[4,4,128]{2,1,0:T(4,128)S(1)}, u32[]{:S(2)}, u32[]{:S(2)}) collective-permute-start(f32[4,4,128]{2,1,0:T(4,128)S(1)} %bitcast.318), channel_id=1, source_target_pairs={{2,0},{3,1},{6,4},{7,5},{10,8},{11,9},{14,12},{15,13},{18,16},{19,... | collective-permute-start | bytes 24584 | tf_op jit(solution)/shard_map/ppermute | solution.py:10
  117.0 17.8 %collective-permute-start.10 = (f32[4,4,128]{2,1,0:T(4,128)S(1)}, f32[4,4,128]{2,1,0:T(4,128)S(1)}, u32[]{:S(2)}, u32[]{:S(2)}) collective-permute-start(f32[4,4,128]{2,1,0:T(4,128)S(1)} %bitcast.317), channel_id=1, source_target_pairs={{0,2},{1,3},{4,6},{5,7},{8,10},{9,11},{12,14},{13,15},{16,18},{17,... | collective-permute-start | bytes 24584 | tf_op jit(solution)/shard_map/ppermute | solution.py:10
  122.5 11.6 %collective-permute-start.11 = (f32[4,4,128]{2,1,0:T(4,128)S(1)}, f32[4,4,128]{2,1,0:T(4,128)S(1)}, u32[]{:S(2)}, u32[]{:S(2)}) collective-permute-start(f32[4,4,128]{2,1,0:T(4,128)S(1)} %get-tuple-element.6), channel_id=1, source_target_pairs={{1,0},{3,2},{5,4},{7,6},{9,8},{11,10},{13,12},{15,14},{17,16},{19,... | collective-permute-start | bytes 24584 | tf_op jit(solution)/shard_map/ppermute | solution.py:10
  131.1 3.3 %collective-permute-start.12 = (f32[4,4,128]{2,1,0:T(4,128)S(1)}, f32[4,4,128]{2,1,0:T(4,128)S(1)}, u32[]{:S(2)}, u32[]{:S(2)}) collective-permute-start(f32[4,4,128]{2,1,0:T(4,128)S(1)} %get-tuple-element.5), channel_id=1, source_target_pairs={{0,1},{2,3},{4,5},{6,7},{8,9},{10,11},{12,13},{14,15},{16,17},{18,... | collective-permute-start | bytes 24584 | tf_op jit(solution)/shard_map/ppermute | solution.py:10
  (42 other events, 336.1 us)

commit v5 on v4

--- a/solution.py
+++ b/solution.py
@@ -14,7 +14,7 @@
     return a_re * b_re - a_im * b_im, a_re * b_im + a_im * b_re
 
 
-def inject_receivers(source, recv_values, recv_slab, recv_lateral, recv_layer):
+def inject_receivers(source, recv_values, recv_slab, recv_lateral, recv_layer, levels):
     layers, components, width_x, width_y = source.shape
     slab_count = lax.axis_size("slab")
     plane_size = width_x * width_y
@@ -39,6 +39,7 @@
         concat_axis=1,
         tiled=True,
     ).reshape(components + 1, slab_count * capacity)
+    got_rows, levels = lax.optimization_barrier((got_rows, levels))
     inject_values = got_rows[:components]
     inject_places = got_rows[components].astype(jnp.int32)
     row_of = inject_places // width_y
@@ -60,7 +61,7 @@
     added = added.reshape(layers * width_x, 3, components * width_y)
     added = (added[:, 0] + added[:, 1]) + added[:, 2]
     added = jnp.transpose(added.reshape(layers, width_x, components, width_y), (0, 2, 1, 3))
-    return source + added
+    return source + added, levels
 
 
 def exchange(array, step):
@@ -144,11 +145,21 @@
     return before, after
 
 
+def edge_pair(block, axis, dim):
+    count = lax.axis_size(axis)
+    last = lax.index_in_dim(block, block.shape[dim] - 1, axis=dim, keepdims=False)
+    first = lax.index_in_dim(block, 0, axis=dim, keepdims=False)
+    if count == 2:
+        here = lax.axis_index(axis)
+        got = lax.ppermute(jnp.where(here == 0, last, first), axis, [(0, 1), (1, 0)])
+        zero = jnp.zeros_like(got)
+        return jnp.where(here == 1, got, zero), jnp.where(here == 0, got, zero)
+    return from_behind(last, axis, 1), from_behind(first, axis, -1)
+
+
 def neighbour_sum(block):
-    from_low_x = from_behind(block[:, :, -1, :], "px", 1)
-    from_high_x = from_behind(block[:, :, 0, :], "px", -1)
-    from_low_y = from_behind(block[:, :, :, -1], "py", 1)
-    from_high_y = from_behind(block[:, :, :, 0], "py", -1)
+    from_low_x, from_high_x = edge_pair(block, "px", 2)
+    from_low_y, from_high_y = edge_pair(block, "py", 3)
     next_x = jnp.concatenate([block[:, :, 1:, :], from_high_x[:, :, None, :]], axis=2)
     prev_x = jnp.concatenate([from_low_x[:, :, None, :], block[:, :, :-1, :]], axis=2)
     next_y = jnp.concatenate([block[:, :, :, 1:], from_high_y[:, :, :, None]], axis=3)
@@ -176,7 +187,9 @@
         prod_up[k] = complex_times(rate_re[k], rate_im[k], *prod_up[k + 1])
     levels = block_products(*prod_down[-1])
 
-    forcing = inject_receivers(source, recv_values, recv_slab, recv_lateral, recv_layer)
+    forcing, levels = inject_receivers(
+        source, recv_values, recv_slab, recv_lateral, recv_layer, levels
+    )
     fields = forcing.reshape(layers, shot_count, 2, width_x, width_y)
     f_re = fields[:, :, 0]
     f_im = fields[:, :, 1]

time: 140 us -> 140 us (level)
  local copies, waits for them, and re-layouts: 11.4 us -> 14.1 us
  other arithmetic: 39.4 us -> 41.9 us
  waiting for transfers between devices: 47.8 us -> 45.5 us
  starting transfers between devices: 35.8 us -> 33.9 us
    mul x5 -> x1, other arithmetic: 5.57 us -> 0.71 us  [complex_times(): return (a_re * b_re - a_im * b_im, a_re * b_im + a_im * b_re)]
    select_n x0 -> x10, other arithmetic: none -> 3.95 us  [the longest x4 1.02 us: entering_states(): first = (jnp.where(lower, q_re, t_re), jnp.where(lower, q_im, t_im))]
    another operation x8 -> x7, other arithmetic: 2.97 us -> 6.15 us  [shards(): jnp.stack([c_re, c_im], axis=1).reshape(components, width_x, width_y)]
    ppermute x9, starting transfers between devices: 9.26 us -> 12.3 us  [exchange(): return lax.ppermute(array, 'slab', [(i, i ^ step) for i in range(count)])]
    ppermute x4 -> x2, starting transfers between devices: 16.7 us -> 13.9 us  [edge_pair(): lax.ppermute(jnp.where(here == 0, last, first), axis, [(0, 1), (1, 0)])]
    another operation x4, other arithmetic: 2.72 us -> 0.04 us  [block_products(): got = exchange(jnp.stack(total, axis=0), step)]
    ppermute x9, waiting for transfers between devices: 44.2 us -> 41.9 us  [exchange(): return lax.ppermute(array, 'slab', [(i, i ^ step) for i in range(count)])]
    all_to_all x1, starting transfers between devices: 9.81 us -> 7.76 us  [inject_receivers(): lax.all_to_all(send_rows.reshape(components + 1, slab_count, capacity), '...]
  transfers between devices with their start and end apart: 14 -> 12, of which waited for: 6 -> 7; matrix products, arithmetic and copies ran while one was open for 13% -> 10% of each run, Pallas kernels for 0% -> 0%
where the time goes in v5:
time: 140 us
  waiting for transfers between devices  45.5 us (32%)
  other arithmetic  41.9 us (30%)
  starting transfers between devices  33.9 us (24%)
  local copies, waits for them, and re-layouts  14.1 us (10%)
  matrix products  3.53 us (3%)
    ppermute x9, waiting for transfers between devices, exchange(): return lax.ppermute(array, 'slab', [(i, i ^ step) for i in range(count)])  41.9 us
    ppermute x2, starting transfers between devices, edge_pair(): lax.ppermute(jnp.where(here == 0, last, first), axis, [(0, 1), (1, 0)])  13.9 us
    ppermute x9, starting transfers between devices, exchange(): return lax.ppermute(array, 'slab', [(i, i ^ step) for i in range(count)])  12.3 us
    all_to_all x1, starting transfers between devices, inject_receivers(): lax.all_to_all(send_rows.reshape(components + 1, slab_count, capacity), '...  7.76 us
    another operation x7, other arithmetic, shards(): jnp.stack([c_re, c_im], axis=1).reshape(components, width_x, width_y)  6.15 us
    sub x1, other arithmetic, shards(): return combined - 0.2 * (4.0 * combined - neighbours)  4.1 us
    all_to_all x1, waiting for transfers between devices, inject_receivers(): lax.all_to_all(send_rows.reshape(components + 1, slab_count, capacity), '...  3.59 us
    add x2, other arithmetic, shards(): state = (t_re + f_re[k], t_im + f_im[k])  3.58 us
  transfers between devices with their start and end apart: 12, of which 7 were waited for; matrix products, arithmetic and copies ran while one was open for 10% of the time, Pallas kernels for 0%

profile of v5, /device:TPU:1, one launch (start us, length us, event | category | flops | bytes accessed | tf_op | source)
XLA Modules:
  0.0 139.8 jit_solution(18249006229219764185)
XLA Ops:
  0.8 2.0 %cosine_multiply_fusion = (f32[4,128,128]{2,1,0:T(8,128)S(1)}, f32[4,128,128]{2,1,0:T(8,128)S(1)}) fusion(f32[4,128,128]{2,1,0:T(8,128)} %param.9, f32[4,128,128]{2,1,0:T(8,128)} %param.10, f32[128,128]{1,0:T(8,128)S(1)} %convert_multiply_fusion), kind=kLoop, calls=%fused_computation.30 | loop fusion | flops 262144 | bytes 1114112 | tf_op jit(solution)/shard_map/mul | solution.py:178
  5.0 2.1 %collective-permute-start = (f32[2,128,128]{2,1,0:T(8,128)S(1)}, f32[2,128,128]{2,1,0:T(8,128)S(1)}, u32[]{:S(2)}, u32[]{:S(2)}) collective-permute-start(f32[2,128,128]{2,1,0:T(8,128)S(1)} %pad_maximum_fusion.10), channel_id=1, source_target_pairs={{0,4},{4,0},{8,12},{12,8},{16,20},{20,16},{24,28},{28,24},{32,36},... | collective-permute-start | bytes 393224 | tf_op jit(solution)/shard_map/ppermute | solution.py:69
  7.9 1.2 reduce-window.6
  12.3 1.4 collective-permute-start.1
  14.4 2.0 %scatter_custom_fusion = f32[5,2048]{0,1:T(8,128)S(1)} fusion(s32[512]{0:T(512)S(1)} %bitcast.408, f32[512,5]{1,0:T(8,128)S(1)} %copy.71, f32[]{:T(128)} %constant.24.clone.1), kind=kCustom, calls=%fused_computation.22 | custom fusion | bytes 40964 | tf_op jit(solution)/shard_map/scatter | solution.py:33
  17.5 7.8 %all-to-all-start = ((f32[32,1,320]{2,1,0:T(1,128)}), f32[32,1,320]{2,1,0:T(1,128)S(1)}, u32[]{:S(2)}, u32[]{:S(2)}) async-start(f32[32,1,320]{2,1,0:T(1,128)} %reshape.222), calls=%async_computation | async-start | bytes 98304 | tf_op jit(solution)/shard_map/all_to_all | solution.py:35
  25.9 2.8 %collective-permute-start.2 = (f32[2,128,128]{2,1,0:T(8,128)S(1)}, f32[2,128,128]{2,1,0:T(8,128)S(1)}, u32[]{:S(2)}, u32[]{:S(2)}) collective-permute-start(f32[2,128,128]{2,1,0:T(8,128)S(1)} %pad_maximum_fusion.12), channel_id=1, source_target_pairs={{0,16},{4,20},{8,24},{12,28},{16,0},{20,4},{24,8},{28,12},{32,48},... | collective-permute-start | bytes 393224 | tf_op jit(solution)/shard_map/ppermute | solution.py:69
  28.8 3.6 %all-to-all-done = f32[32,1,320]{2,1,0:T(1,128)S(1)} async-done(((f32[32,1,320]{2,1,0:T(1,128)}), f32[32,1,320]{2,1,0:T(1,128)S(1)}, u32[]{:S(2)}, u32[]{:S(2)}) %all-to-all-start) | async-done | bytes 40992 | tf_op jit(solution)/shard_map/all_to_all | solution.py:35
  35.9 2.7 %collective-permute-done.3 = f32[2,128,128]{2,1,0:T(8,128)S(1)} collective-permute-done((f32[2,128,128]{2,1,0:T(8,128)S(1)}, f32[2,128,128]{2,1,0:T(8,128)S(1)}, u32[]{:S(2)}, u32[]{:S(2)}) %collective-permute-start.3) | collective-permute-done | bytes 131104 | tf_op jit(solution)/shard_map/ppermute | solution.py:69
  40.1 0.9 add_select_fusion.19
  42.0 0.9 select_convert_fusion
  43.0 3.5 %fusion.1 = f32[512,3,512]{2,0,1:T(8,128)S(1)} fusion(bf16[3,512,2048]{2,1,0:T(8,128)(2,1)S(1)} %bitcast.376, s32[2048]{0:T(1024)S(1)} %bitcast.407), kind=kOutput, calls=%fused_computation.4 | convolution fusion | flops 3222274048 | bytes 9445376 | tf_op jit(solution)/shard_map/dot_general | solution.py:60
  47.3 1.5 %bitcast_add_fusion = f32[4,4,128,128]{3,2,1,0:T(8,128)S(1)} fusion(f32[4,4,128,128]{3,2,1,0:T(8,128)} %param.8, f32[4,128,4,128]{3,2,1,0:T(4,128)S(1)} %add.512), kind=kLoop, calls=%fused_computation.16 | loop fusion | flops 262144 | bytes 3145728 | tf_op jit(solution)/shard_map/add | solution.py:64
  49.0 3.2 %subtract_add_fusion.3 = (f32[2,128,128]{2,0,1:T(2,128)S(1)}, f32[2,128,128]{2,0,1:T(2,128)S(1)}, f32[2,128,128]{2,0,1:T(2,128)S(1)}, f32[2,128,128]{2,0,1:T(2,1...) fusion(f32[128,128]{1,0:T(8,128)S(1)} %get-tuple-element.175, ...), kind=kLoop, calls=%fused_computation.89 | loop fusion | flops 1310720 | bytes 2883584 | tf_op jit(solution)/shard_map/add | solution.py:202
  53.7 8.9 %collective-permute-done.4 = f32[8,128,128]{2,0,1:T(8,128)S(1)} collective-permute-done((f32[8,128,128]{2,0,1:T(8,128)S(1)}, f32[8,128,128]{2,0,1:T(8,128)S(1)}, u32[]{:S(2)}, u32[]{:S(2)}) %collective-permute-start.4) | collective-permute-done | bytes 524320 | tf_op jit(solution)/shard_map/ppermute | solution.py:69
  63.6 8.3 %collective-permute-done.5 = f32[8,128,128]{2,0,1:T(8,128)S(1)} collective-permute-done((f32[8,128,128]{2,0,1:T(8,128)S(1)}, f32[8,128,128]{2,0,1:T(8,128)S(1)}, u32[]{:S(2)}, u32[]{:S(2)}) %collective-permute-start.5) | collective-permute-done | bytes 524320 | tf_op jit(solution)/shard_map/ppermute | solution.py:69
  72.7 1.2 collective-permute-start.6
  73.9 9.3 %collective-permute-done.6 = f32[8,128,128]{2,0,1:T(8,128)S(1)} collective-permute-done((f32[8,128,128]{2,0,1:T(8,128)S(1)}, f32[8,128,128]{2,0,1:T(8,128)S(1)}, u32[]{:S(2)}, u32[]{:S(2)}) %collective-permute-start.6) | collective-permute-done | bytes 524320 | tf_op jit(solution)/shard_map/ppermute | solution.py:69
  84.5 1.0 pad_maximum_fusion.4
  86.4 1.0 broadcast_select_fusion.22
  87.3 6.4 %collective-permute-done.7 = f32[8,128,128]{2,0,1:T(8,128)S(1)} collective-permute-done((f32[8,128,128]{2,0,1:T(8,128)}, f32[8,128,128]{2,0,1:T(8,128)S(1)}, u32[]{:S(2)}, u32[]{:S(2)}) %collective-permute-start.7) | collective-permute-done | bytes 524320 | tf_op jit(solution)/shard_map/ppermute | solution.py:69
  93.8 1.7 %add_select_fusion.17 = (f32[2,128,128]{2,0,1:T(2,128)S(1)}, f32[2,128,128]{2,0,1:T(2,128)S(1)}) fusion(f32[2,128,128]{2,0,1:T(2,128)} %copy-done.13, f32[2,128,128]{2,0,1:T(2,128)} %copy-done.16, pred[]{:T(512)S(6)} %eq.103, f32[2,128,128]{2,0,1:T(2,128)} %copy-done.15, f32[2,128,128]{2,0,1:T(2,128)} %copy-done.14, pred[]{:T(512)S(6)} %eq.111, ...), kind=kLoop, calls=%fused_computation.69 | loop fusion | flops 851968 | bytes 1572866 | tf_op jit(solution)/shard_map/jit(_where)/select_n | solution.py:126
  96.3 2.6 %collective-permute-start.8 = (f32[4,128,128]{2,0,1:T(4,128)}, f32[4,128,128]{2,0,1:T(4,128)}, u32[]{:S(2)}, u32[]{:S(2)}) collective-permute-start(f32[4,128,128]{2,0,1:T(4,128)} %pad_maximum_fusion.5), channel_id=1, source_target_pairs={{0,64},{4,68},{8,72},{12,76},{16,80},{20,84},{24,88},{28,92},{32,9... | collective-permute-start | bytes 786440 | tf_op jit(solution)/shard_map/ppermute | solution.py:69
  99.0 6.2 %collective-permute-done.8 = f32[4,128,128]{2,0,1:T(4,128)} collective-permute-done((f32[4,128,128]{2,0,1:T(4,128)}, f32[4,128,128]{2,0,1:T(4,128)}, u32[]{:S(2)}, u32[]{:S(2)}) %collective-permute-start.8) | collective-permute-done | bytes 262176 | tf_op jit(solution)/shard_map/ppermute | solution.py:69
  105.2 4.5 %subtract_bitcast_fusion.5 = (f32[2,1,128,128]{3,0,2,1:T(2,128)S(1)}, f32[2,128,128]{2,0,1:T(2,128)S(1)}, f32[2,128,128]{2,0,1:T(2,128)S(1)}, f32[2,128,128]{2,0,1:T(2,128)S(1)}, f32[2,128,128]{2,0,1:T(2,128)S(1)}) fusion(f32[2,128,128]{2,0,1:T(2,128)S(1)} %get-tuple-element.132, f32[128,128]{1,0:T(8,128)} %get-tuple-element.172, ...), kind=kLoop, calls=%fused_computation.67 | loop fusion | flops 3473408 | bytes 4849669 | tf_op jit(solution)/shard_map/stack | solution.py:220
  109.8 1.8 %add_subtract_fusion.1 = (f32[2,128,128]{2,0,1:T(2,128)S(1)}, f32[2,128,128]{2,0,1:T(2,128)S(1)}, f32[2,1,128,128]{3,0,2,1:T(2,128)S(1)}) fusion(f32[2,128,128]{2,0,1:T(2,128)S(1)} %get-tuple-element.82, f32[2,128,128]{2,0,1:T(2,128)S(1)} %get-tuple-element.83, f32[2,128,128]{2,0,1:T(2,128)S(1)} %get-tuple-element.89, ...), kind=kLoop, calls=%fused_computation.61 | loop fusion | flops 983040 | bytes 2228224 | tf_op jit(solution)/shard_map/sub | solution.py:218
  114.9 1.6 %fusion.18 = (f32[4,4,128,127]{3,1,0,2:T(4,128)S(1)}, f32[4,4,128,127]{3,1,0,2:T(4,128)}) fusion(f32[4,4,128,128]{3,1,0,2:T(4,128)S(1)} %pad_maximum_fusion), kind=kLoop, calls=%fused_computation.225 | loop fusion | bytes 4161536 | tf_op jit(solution)/shard_map/slice | solution.py:166
  116.5 1.6 %fusion.19 = (f32[4,4,127,128]{3,1,0,2:T(4,128)}, f32[4,4,127,128]{3,1,0,2:T(4,128)}) fusion(f32[4,4,128,128]{3,1,0,2:T(4,128)S(1)} %pad_maximum_fusion), kind=kLoop, calls=%fused_computation.226 | loop fusion | bytes 4161536 | tf_op jit(solution)/shard_map/slice | solution.py:164
  119.3 10.1 %collective-permute-start.10 = (f32[4,4,128]{2,1,0:T(4,128)S(1)}, f32[4,4,128]{2,1,0:T(4,128)S(1)}, u32[]{:S(2)}, u32[]{:S(2)}) collective-permute-start(f32[4,4,128]{2,1,0:T(4,128)S(1)} %bitcast.404), channel_id=1, source_target_pairs={{0,1},{1,0},{2,3},{3,2},{4,5},{5,4},{6,7},{7,6},{8,9},{9,8},{10,11... | collective-permute-start | bytes 24584 | tf_op jit(solution)/shard_map/ppermute | solution.py:154
  129.4 3.8 %collective-permute-start.9 = (f32[4,4,128]{2,1,0:T(4,128)S(1)}, f32[4,4,128]{2,1,0:T(4,128)S(1)}, u32[]{:S(2)}, u32[]{:S(2)}) collective-permute-start(f32[4,4,128]{2,1,0:T(4,128)S(1)} %fusion.17), channel_id=1, source_target_pairs={{0,2},{2,0},{1,3},{3,1},{4,6},{6,4},{5,7},{7,5},{8,10},{10,8},{9,1... | collective-permute-start | bytes 24584 | tf_op jit(solution)/shard_map/ppermute | solution.py:154
  134.4 4.1 %fusion.8 = f32[4,4,128,128]{3,1,0,2:T(4,128)S(1)} fusion(f32[4,4,1,128]{3,1,0,2:T(4,128)S(1)} %get-tuple-element.224, f32[4,4,127,128]{3,1,0,2:T(4,128)} %get-tuple-element.131, f32[4,4,127,128]{3,1,0,2:T(4,128)} %get-tuple-element.130, f32[4,4,1,128]{3,1,0,2:T(4,128)S(1)} %get-tuple-element.223, f32[4,4,128,1]{3,1,0,2:T(4,128)S(1)} %copy.88, ...), kind=kLoop, calls=%fused_computation.15 | loop fusion | flops 3670016 | bytes 6291456 | tf_op jit(solution)/shard_map/sub | solution.py:223
  138.5 1.3 copy.90
  (190 shorter events, 28.1 us)
Async XLA Ops:
  4.3 35.1 %copy-start.25 = (f32[1,128,128]{2,1,0:T(8,128)}, f32[1,128,128]{2,1,0:T(8,128)S(1)}, u32[]{:S(2)}) copy-start(f32[1,128,128]{2,1,0:T(8,128)S(1)} %get-tuple-element.119) | copy-start | bytes 196612
  4.3 35.1 %copy-start.27 = (f32[1,128,128]{2,1,0:T(8,128)}, f32[1,128,128]{2,1,0:T(8,128)S(1)}, u32[]{:S(2)}) copy-start(f32[1,128,128]{2,1,0:T(8,128)S(1)} %get-tuple-element.120) | copy-start | bytes 196612
  4.3 37.4 %copy-start.19 = (f32[1,128,128]{2,1,0:T(8,128)}, f32[1,128,128]{2,1,0:T(8,128)S(1)}, u32[]{:S(2)}) copy-start(f32[1,128,128]{2,1,0:T(8,128)S(1)} %get-tuple-element.118) | copy-start | bytes 196612
  5.0 37.9 %copy-start.20 = (f32[1,128,128]{2,1,0:T(8,128)}, f32[1,128,128]{2,1,0:T(8,128)S(1)}, u32[]{:S(2)}) copy-start(f32[1,128,128]{2,1,0:T(8,128)S(1)} %get-tuple-element.174) | copy-start | bytes 196612
  5.0 47.2 %copy-start.17 = (f32[128,128]{1,0:T(8,128)}, f32[128,128]{1,0:T(8,128)S(1)}, u32[]{:S(2)}) copy-start(f32[128,128]{1,0:T(8,128)S(1)} %get-tuple-element.173) | copy-start | bytes 196612
  5.0 47.2 %copy-start.18 = (f32[128,128]{1,0:T(8,128)}, f32[128,128]{1,0:T(8,128)S(1)}, u32[]{:S(2)}) copy-start(f32[128,128]{1,0:T(8,128)S(1)} %get-tuple-element.175) | copy-start | bytes 196612
  5.0 6.6 %collective-permute-start = (f32[2,128,128]{2,1,0:T(8,128)S(1)}, f32[2,128,128]{2,1,0:T(8,128)S(1)}, u32[]{:S(2)}, u32[]{:S(2)}) collective-permute-start(f32[2,128,128]{2,1,0:T(8,128)S(1)} %pad_maximum_fusion.10), channel_id=1, source_target_pairs={{0,4},{4,0},{8,12},{12,8},{16,20},{20,16},{24,28},{28,24},{32,36},... | collective-permute-start | bytes 393224 | tf_op jit(solution)/shard_map/ppermute | solution.py:69
  12.3 12.9 %collective-permute-start.1 = (f32[2,128,128]{2,1,0:T(8,128)S(1)}, f32[2,128,128]{2,1,0:T(8,128)S(1)}, u32[]{:S(2)}, u32[]{:S(2)}) collective-permute-start(f32[2,128,128]{2,1,0:T(8,128)S(1)} %pad_maximum_fusion.11), channel_id=1, source_target_pairs={{0,8},{4,12},{8,0},{12,4},{16,24},{20,28},{24,16},{28,20},{32,40},... | collective-permute-start | bytes 393224 | tf_op jit(solution)/shard_map/ppermute | solution.py:69
  17.5 14.9 %all-to-all-start = ((f32[32,1,320]{2,1,0:T(1,128)}), f32[32,1,320]{2,1,0:T(1,128)S(1)}, u32[]{:S(2)}, u32[]{:S(2)}) async-start(f32[32,1,320]{2,1,0:T(1,128)} %reshape.222), calls=%async_computation | async-start | bytes 98304 | tf_op jit(solution)/shard_map/all_to_all | solution.py:35
  25.9 8.0 %collective-permute-start.2 = (f32[2,128,128]{2,1,0:T(8,128)S(1)}, f32[2,128,128]{2,1,0:T(8,128)S(1)}, u32[]{:S(2)}, u32[]{:S(2)}) collective-permute-start(f32[2,128,128]{2,1,0:T(8,128)S(1)} %pad_maximum_fusion.12), channel_id=1, source_target_pairs={{0,16},{4,20},{8,24},{12,28},{16,0},{20,4},{24,8},{28,12},{32,48},... | collective-permute-start | bytes 393224 | tf_op jit(solution)/shard_map/ppermute | solution.py:69
  34.6 4.1 %collective-permute-start.3 = (f32[2,128,128]{2,1,0:T(8,128)S(1)}, f32[2,128,128]{2,1,0:T(8,128)S(1)}, u32[]{:S(2)}, u32[]{:S(2)}) collective-permute-start(f32[2,128,128]{2,1,0:T(8,128)S(1)} %pad_maximum_fusion.13), channel_id=1, source_target_pairs={{0,32},{4,36},{8,40},{12,44},{16,48},{20,52},{24,56},{28,60},{32,0... | collective-permute-start | bytes 393224 | tf_op jit(solution)/shard_map/ppermute | solution.py:69
  47.3 16.3 %copy-start.43 = (f32[128,128]{1,0:T(8,128)S(1)}, f32[128,128]{1,0:T(8,128)}, u32[]{:S(2)}) copy-start(f32[128,128]{1,0:T(8,128)} %get-tuple-element.55) | copy-start | bytes 196612
  47.3 16.3 %copy-start.44 = (f32[128,128]{1,0:T(8,128)S(1)}, f32[128,128]{1,0:T(8,128)}, u32[]{:S(2)}) copy-start(f32[128,128]{1,0:T(8,128)} %get-tuple-element.53) | copy-start | bytes 196612
  47.3 16.3 %copy-start.49 = (f32[128,128]{1,0:T(8,128)S(1)}, f32[128,128]{1,0:T(8,128)}, u32[]{:S(2)}) copy-start(f32[128,128]{1,0:T(8,128)} %get-tuple-element.54) | copy-start | bytes 196612
  47.3 16.3 %copy-start.50 = (f32[128,128]{1,0:T(8,128)S(1)}, f32[128,128]{1,0:T(8,128)}, u32[]{:S(2)}) copy-start(f32[128,128]{1,0:T(8,128)} %get-tuple-element.52) | copy-start | bytes 196612
  48.9 24.9 %copy-start.30 = (f32[128,128]{1,0:T(8,128)S(1)}, f32[128,128]{1,0:T(8,128)}, u32[]{:S(2)}) copy-start(f32[128,128]{1,0:T(8,128)} %copy-done.29) | copy-start | bytes 196612
  49.0 24.9 %copy-start.32 = (f32[128,128]{1,0:T(8,128)S(1)}, f32[128,128]{1,0:T(8,128)}, u32[]{:S(2)}) copy-start(f32[128,128]{1,0:T(8,128)} %copy-done.31) | copy-start | bytes 196612
  49.0 24.9 %copy-start.53 = (f32[128,128]{1,0:T(8,128)S(1)}, f32[128,128]{1,0:T(8,128)}, u32[]{:S(2)}) copy-start(f32[128,128]{1,0:T(8,128)} %get-tuple-element.60) | copy-start | bytes 196612
  49.0 24.9 %copy-start.54 = (f32[128,128]{1,0:T(8,128)S(1)}, f32[128,128]{1,0:T(8,128)}, u32[]{:S(2)}) copy-start(f32[128,128]{1,0:T(8,128)} %get-tuple-element.58) | copy-start | bytes 196612
  53.1 9.5 %collective-permute-start.4 = (f32[8,128,128]{2,0,1:T(8,128)S(1)}, f32[8,128,128]{2,0,1:T(8,128)S(1)}, u32[]{:S(2)}, u32[]{:S(2)}) collective-permute-start(f32[8,128,128]{2,0,1:T(8,128)S(1)} %pad_maximum_fusion.1), channel_id=1, source_target_pairs={{0,4},{4,0},{8,12},{12,8},{16,20},{20,16},{24,28},{28,24},{32,36},... | collective-permute-start | bytes 1572872 | tf_op jit(solution)/shard_map/ppermute | solution.py:69
  63.3 8.6 %collective-permute-start.5 = (f32[8,128,128]{2,0,1:T(8,128)S(1)}, f32[8,128,128]{2,0,1:T(8,128)S(1)}, u32[]{:S(2)}, u32[]{:S(2)}) collective-permute-start(f32[8,128,128]{2,0,1:T(8,128)S(1)} %pad_maximum_fusion.2), channel_id=1, source_target_pairs={{0,8},{4,12},{8,0},{12,4},{16,24},{20,28},{24,16},{28,20},{32,40},... | collective-permute-start | bytes 1572872 | tf_op jit(solution)/shard_map/ppermute | solution.py:69
  72.7 10.5 %collective-permute-start.6 = (f32[8,128,128]{2,0,1:T(8,128)S(1)}, f32[8,128,128]{2,0,1:T(8,128)S(1)}, u32[]{:S(2)}, u32[]{:S(2)}) collective-permute-start(f32[8,128,128]{2,0,1:T(8,128)S(1)} %pad_maximum_fusion.3), channel_id=1, source_target_pairs={{0,16},{4,20},{8,24},{12,28},{16,0},{20,4},{24,8},{28,12},{32,48},... | collective-permute-start | bytes 1572872 | tf_op jit(solution)/shard_map/ppermute | solution.py:69
  85.5 8.2 %collective-permute-start.7 = (f32[8,128,128]{2,0,1:T(8,128)}, f32[8,128,128]{2,0,1:T(8,128)S(1)}, u32[]{:S(2)}, u32[]{:S(2)}) collective-permute-start(f32[8,128,128]{2,0,1:T(8,128)} %pad_maximum_fusion.4), channel_id=1, source_target_pairs={{0,32},{4,36},{8,40},{12,44},{16,48},{20,52},{24,56},{28,60},{32,0... | collective-permute-start | bytes 1572872 | tf_op jit(solution)/shard_map/ppermute | solution.py:69
  96.3 8.9 %collective-permute-start.8 = (f32[4,128,128]{2,0,1:T(4,128)}, f32[4,128,128]{2,0,1:T(4,128)}, u32[]{:S(2)}, u32[]{:S(2)}) collective-permute-start(f32[4,128,128]{2,0,1:T(4,128)} %pad_maximum_fusion.5), channel_id=1, source_target_pairs={{0,64},{4,68},{8,72},{12,76},{16,80},{20,84},{24,88},{28,92},{32,9... | collective-permute-start | bytes 786440 | tf_op jit(solution)/shard_map/ppermute | solution.py:69
  98.9 13.9 %copy-start.26 = (f32[1,128,128]{2,1,0:T(8,128)S(1)}, f32[1,128,128]{2,1,0:T(8,128)}, u32[]{:S(2)}) copy-start(f32[1,128,128]{2,1,0:T(8,128)} %copy-done.25) | copy-start | bytes 196612
  98.9 13.9 %copy-start.28 = (f32[1,128,128]{2,1,0:T(8,128)S(1)}, f32[1,128,128]{2,1,0:T(8,128)}, u32[]{:S(2)}) copy-start(f32[1,128,128]{2,1,0:T(8,128)} %copy-done.27) | copy-start | bytes 196612
  99.0 13.9 %copy-start.37 = (f32[2,128,128]{2,0,1:T(2,128)S(1)}, f32[2,128,128]{2,0,1:T(2,128)}, u32[]{:S(2)}) copy-start(f32[2,128,128]{2,0,1:T(2,128)} %get-tuple-element.135) | copy-start | bytes 393220
  99.0 13.9 %copy-start.38 = (f32[2,128,128]{2,0,1:T(2,128)S(1)}, f32[2,128,128]{2,0,1:T(2,128)}, u32[]{:S(2)}) copy-start(f32[2,128,128]{2,0,1:T(2,128)} %get-tuple-element.136) | copy-start | bytes 393220
  99.0 13.9 %copy-start.47 = (f32[1,128,128]{2,1,0:T(8,128)S(1)}, f32[1,128,128]{2,1,0:T(8,128)}, u32[]{:S(2)}) copy-start(f32[1,128,128]{2,1,0:T(8,128)} %get-tuple-element.87) | copy-start | bytes 196612
  99.0 13.9 %copy-start.48 = (f32[1,128,128]{2,1,0:T(8,128)S(1)}, f32[1,128,128]{2,1,0:T(8,128)}, u32[]{:S(2)}) copy-start(f32[1,128,128]{2,1,0:T(8,128)} %get-tuple-element.88) | copy-start | bytes 196612
  119.3 13.9 %collective-permute-start.10 = (f32[4,4,128]{2,1,0:T(4,128)S(1)}, f32[4,4,128]{2,1,0:T(4,128)S(1)}, u32[]{:S(2)}, u32[]{:S(2)}) collective-permute-start(f32[4,4,128]{2,1,0:T(4,128)S(1)} %bitcast.404), channel_id=1, source_target_pairs={{0,1},{1,0},{2,3},{3,2},{4,5},{5,4},{6,7},{7,6},{8,9},{9,8},{10,11... | collective-permute-start | bytes 24584 | tf_op jit(solution)/shard_map/ppermute | solution.py:154
  129.4 5.0 %collective-permute-start.9 = (f32[4,4,128]{2,1,0:T(4,128)S(1)}, f32[4,4,128]{2,1,0:T(4,128)S(1)}, u32[]{:S(2)}, u32[]{:S(2)}) collective-permute-start(f32[4,4,128]{2,1,0:T(4,128)S(1)} %fusion.17), channel_id=1, source_target_pairs={{0,2},{2,0},{1,3},{3,1},{4,6},{6,4},{5,7},{7,5},{8,10},{10,8},{9,1... | collective-permute-start | bytes 24584 | tf_op jit(solution)/shard_map/ppermute | solution.py:154
  (35 other events, 209.4 us)

commit v6 on v5

--- a/solution.py
+++ b/solution.py
@@ -2,6 +2,8 @@
 import jax.numpy as jnp
 from jax import lax
 from jax.sharding import PartitionSpec as P
+from jax.experimental import pallas as pl
+from jax.experimental.pallas import tpu as pltpu
 
 
 def from_behind(array, axis, by):
@@ -145,10 +147,8 @@
     return before, after
 
 
-def edge_pair(block, axis, dim):
+def edge_pair(last, first, axis):
     count = lax.axis_size(axis)
-    last = lax.index_in_dim(block, block.shape[dim] - 1, axis=dim, keepdims=False)
-    first = lax.index_in_dim(block, 0, axis=dim, keepdims=False)
     if count == 2:
         here = lax.axis_index(axis)
         got = lax.ppermute(jnp.where(here == 0, last, first), axis, [(0, 1), (1, 0)])
@@ -157,14 +157,69 @@
     return from_behind(last, axis, 1), from_behind(first, axis, -1)
 
 
-def neighbour_sum(block):
-    from_low_x, from_high_x = edge_pair(block, "px", 2)
-    from_low_y, from_high_y = edge_pair(block, "py", 3)
-    next_x = jnp.concatenate([block[:, :, 1:, :], from_high_x[:, :, None, :]], axis=2)
-    prev_x = jnp.concatenate([from_low_x[:, :, None, :], block[:, :, :-1, :]], axis=2)
-    next_y = jnp.concatenate([block[:, :, :, 1:], from_high_y[:, :, :, None]], axis=3)
-    prev_y = jnp.concatenate([from_low_y[:, :, :, None], block[:, :, :, :-1]], axis=3)
-    return next_x + prev_x + next_y + prev_y
+def sweep_kernel(f_ref, rr_ref, ri_ref, er_ref, ei_ref, br_ref, bi_ref,
+                 c_ref, x0_ref, x1_ref, y0_ref, y1_ref):
+    layers = f_ref.shape[0]
+    shots = er_ref.shape[0]
+    downs = []
+    for s in range(shots):
+        w_re, w_im = er_ref[s], ei_ref[s]
+        per_layer = []
+        for k in range(layers):
+            t_re, t_im = complex_times(rr_ref[k], ri_ref[k], w_re, w_im)
+            w_re, w_im = t_re + f_ref[k, 2 * s], t_im + f_ref[k, 2 * s + 1]
+            per_layer.append((w_re, w_im))
+        downs.append(per_layer)
+    for s in range(shots):
+        v_re, v_im = br_ref[s], bi_ref[s]
+        for k in range(layers - 1, -1, -1):
+            t_re, t_im = complex_times(rr_ref[k], ri_ref[k], v_re, v_im)
+            f_re, f_im = f_ref[k, 2 * s], f_ref[k, 2 * s + 1]
+            v_re, v_im = t_re + f_re, t_im + f_im
+            d_re, d_im = downs[s][k]
+            for part, plane in ((0, d_re + v_re - f_re), (1, d_im + v_im - f_im)):
+                c = 2 * s + part
+                c_ref[k, c] = plane
+                x0_ref[k, pl.ds(c, 1), :] = plane[0:1, :]
+                x1_ref[k, pl.ds(c, 1), :] = plane[-1:, :]
+                flipped = jnp.transpose(plane)
+                y0_ref[k, pl.ds(c, 1), :] = flipped[0:1, :]
+                y1_ref[k, pl.ds(c, 1), :] = flipped[-1:, :]
+
+
+def stencil_kernel(c_ref, lx_ref, hx_ref, ly_ref, hy_ref, o_ref):
+    layers, components, width_x, width_y = c_ref.shape
+    rows = lax.broadcasted_iota(jnp.int32, (width_x, width_y), 0)
+    cols = lax.broadcasted_iota(jnp.int32, (width_x, width_y), 1)
+    for k in range(layers):
+        for c in range(components):
+            plane = c_ref[k, c]
+            low_x = jnp.broadcast_to(lx_ref[k, pl.ds(c, 1), :], (width_x, width_y))
+            high_x = jnp.broadcast_to(hx_ref[k, pl.ds(c, 1), :], (width_x, width_y))
+            low_y = jnp.transpose(jnp.broadcast_to(ly_ref[k, pl.ds(c, 1), :], (width_y, width_x)))
+            high_y = jnp.transpose(jnp.broadcast_to(hy_ref[k, pl.ds(c, 1), :], (width_y, width_x)))
+            next_x = jnp.where(rows == width_x - 1, high_x, pltpu.roll(plane, width_x - 1, 0))
+            prev_x = jnp.where(rows == 0, low_x, pltpu.roll(plane, 1, 0))
+            next_y = jnp.where(cols == width_y - 1, high_y, pltpu.roll(plane, width_y - 1, 1))
+            prev_y = jnp.where(cols == 0, low_y, pltpu.roll(plane, 1, 1))
+            neighbours = next_x + prev_x + next_y + prev_y
+            o_ref[k, c] = plane - 0.2 * (4.0 * plane - neighbours)
+
+
+def finish(fields, rate_re, rate_im, enter_re, enter_im, below_re, below_im):
+    layers, components, width_x, width_y = fields.shape
+    edge_x = jax.ShapeDtypeStruct((layers, components, width_y), jnp.float32)
+    edge_y = jax.ShapeDtypeStruct((layers, components, width_x), jnp.float32)
+    combined, x0, x1, y0, y1 = pl.pallas_call(
+        sweep_kernel,
+        out_shape=(jax.ShapeDtypeStruct(fields.shape, jnp.float32), edge_x, edge_x, edge_y, edge_y),
+    )(fields, rate_re, rate_im, enter_re, enter_im, below_re, below_im)
+    from_low_x, from_high_x = edge_pair(x1, x0, "px")
+    from_low_y, from_high_y = edge_pair(y1, y0, "py")
+    return pl.pallas_call(
+        stencil_kernel,
+        out_shape=jax.ShapeDtypeStruct(fields.shape, jnp.float32),
+    )(combined, from_low_x, from_high_x, from_low_y, from_high_y)
 
 
 def shards(source, phase, attenuation, pml_level, recv_values, recv_slab, recv_lateral, recv_layer):
@@ -181,10 +236,6 @@
     prod_down = [(rate_re[0], rate_im[0])]
     for k in range(1, layers):
         prod_down.append(complex_times(rate_re[k], rate_im[k], *prod_down[-1]))
-    prod_up = [None] * layers
-    prod_up[layers - 1] = (rate_re[layers - 1], rate_im[layers - 1])
-    for k in range(layers - 2, -1, -1):
-        prod_up[k] = complex_times(rate_re[k], rate_im[k], *prod_up[k + 1])
     levels = block_products(*prod_down[-1])
 
     forcing, levels = inject_receivers(
@@ -211,16 +262,7 @@
 
     (enter_re, enter_im), (below_re, below_im) = entering_states(down[layers - 1], up[0], levels)
 
-    combined = []
-    for k in range(layers):
-        e_re, e_im = complex_times(prod_down[k][0][None], prod_down[k][1][None], enter_re, enter_im)
-        u_re, u_im = complex_times(prod_up[k][0][None], prod_up[k][1][None], below_re, below_im)
-        c_re = (down[k][0] + e_re) + (up[k][0] + u_re) - f_re[k]
-        c_im = (down[k][1] + e_im) + (up[k][1] + u_im) - f_im[k]
-        combined.append(jnp.stack([c_re, c_im], axis=1).reshape(components, width_x, width_y))
-    combined = jnp.stack(combined, axis=0)
-    neighbours = neighbour_sum(combined)
-    return combined - 0.2 * (4.0 * combined - neighbours)
+    return finish(forcing, rate_re, rate_im, enter_re, enter_im, below_re, below_im)
 
 
 def solution(mesh):

time: 140 us -> 127 us (0.907)
  other arithmetic: 41.9 us -> 29.3 us
  local copies, waits for them, and re-layouts: 14.1 us -> 5.79 us
  Pallas kernels: 0 us -> 6.33 us
  waiting for transfers between devices: 45.5 us -> 47.2 us
    another operation x10 -> x2, other arithmetic: 7.56 us -> 1.19 us  [the longest x7 6.15 us: shards(): jnp.stack([c_re, c_im], axis=1).reshape(components, width_x, width_y)]
    pallas_call x0 -> x2, Pallas kernels: none -> 6.33 us  [the longest x1 3.4 us: finish(): pl.pallas_call(stencil_kernel, out_shape=jax.ShapeDtypeStruct(fields.shap...]
    select_n x0 -> x6, other arithmetic: none -> 6.06 us  [the longest x1 1.66 us: entering_states(): jnp.where(lower, g_im + after[1], after[1])]
    sub x2 -> x0, other arithmetic: 5.86 us -> none  [the longest x1 4.1 us: shards(): return combined - 0.2 * (4.0 * combined - neighbours)]
    slice x4 -> x1, local copies, waits for them, and re-layouts: 3.47 us -> 0.22 us  [the longest x1 1.58 us: neighbour_sum(): block[:, :, :, :-1]]
    select_n x1, other arithmetic: 1.66 us -> 0.12 us  [entering_states(): jnp.where(lower, down_b[0], up_b[0])]
    add x2 -> x4, other arithmetic: 3.58 us -> 3.39 us  [shards(): state = (t_re + f_re[k], t_im + f_im[k])]
  transfers between devices with their start and end apart: 12 -> 12, of which waited for: 7 -> 8; matrix products, arithmetic and copies ran while one was open for 10% -> 11% of each run, Pallas kernels for 0% -> 0%
where the time goes in v6:
time: 127 us; the launch traced here: 126 us
  waiting for transfers between devices  47.2 us (37%)
  starting transfers between devices  33.5 us (26%)
  other arithmetic  29.3 us (23%)
  Pallas kernels  6.33 us (5%)
  local copies, waits for them, and re-layouts  5.79 us (5%)
  matrix products  3.52 us (3%)
    ppermute x9, waiting for transfers between devices, exchange(): return lax.ppermute(array, 'slab', [(i, i ^ step) for i in range(count)])  42.9 us
    ppermute x2, starting transfers between devices, edge_pair(): lax.ppermute(jnp.where(here == 0, last, first), axis, [(0, 1), (1, 0)])  13.2 us
    ppermute x9, starting transfers between devices, exchange(): return lax.ppermute(array, 'slab', [(i, i ^ step) for i in range(count)])  12.6 us
    all_to_all x1, starting transfers between devices, inject_receivers(): lax.all_to_all(send_rows.reshape(components + 1, slab_count, capacity), '...  7.76 us
    all_to_all x1, waiting for transfers between devices, inject_receivers(): lax.all_to_all(send_rows.reshape(components + 1, slab_count, capacity), '...  3.59 us
    dot_general x1, matrix products, inject_receivers(): jnp.dot(pick_rows, spread.astype(jnp.bfloat16), preferred_element_type=jn...  3.52 us
    pallas_call x1, Pallas kernels, finish(): pl.pallas_call(stencil_kernel, out_shape=jax.ShapeDtypeStruct(fields.shap...  3.4 us
    add x4, other arithmetic, shards(): state = (t_re + f_re[k], t_im + f_im[k])  3.39 us
  transfers between devices with their start and end apart: 12, of which 8 were waited for; matrix products, arithmetic and copies ran while one was open for 11% of the time, Pallas kernels for 0%

profile of v6, /device:TPU:1, one launch (start us, length us, event | category | flops | bytes accessed | tf_op | source)
XLA Modules:
  0.0 126.2 jit_solution(3679763822726647886)
XLA Ops:
  0.0 0.8 convert_multiply_fusion
  0.8 2.0 %cosine_multiply_fusion = (f32[4,128,128]{2,1,0:T(8,128)S(1)}, f32[4,128,128]{2,1,0:T(8,128)S(1)}) fusion(f32[4,128,128]{2,1,0:T(8,128)} %param.9, f32[4,128,128]{2,1,0:T(8,128)} %param.10, f32[128,128]{1,0:T(8,128)S(1)} %convert_multiply_fusion), kind=kLoop, calls=%fused_computation.18 | loop fusion | flops 262144 | bytes 1114112 | tf_op jit(solution)/shard_map/mul | solution.py:233
  2.9 0.9 multiply_subtract_fusion.7
  3.8 2.1 %collective-permute-start = (f32[2,128,128]{2,1,0:T(8,128)S(1)}, f32[2,128,128]{2,1,0:T(8,128)S(1)}, u32[]{:S(2)}, u32[]{:S(2)}) collective-permute-start(f32[2,128,128]{2,1,0:T(8,128)S(1)} %pad_maximum_fusion.5), channel_id=1, source_target_pairs={{0,4},{4,0},{8,12},{12,8},{16,20},{20,16},{24,28},{28,24},{32,36},... | collective-permute-start | bytes 393224 | tf_op jit(solution)/shard_map/ppermute | solution.py:71
  6.6 1.2 reduce-window.6
  11.1 1.4 %collective-permute-start.1 = (f32[2,128,128]{2,1,0:T(8,128)S(1)}, f32[2,128,128]{2,1,0:T(8,128)S(1)}, u32[]{:S(2)}, u32[]{:S(2)}) collective-permute-start(f32[2,128,128]{2,1,0:T(8,128)S(1)} %pad_maximum_fusion.6), channel_id=1, source_target_pairs={{0,8},{4,12},{8,0},{12,4},{16,24},{20,28},{24,16},{28,20},{32,40},... | collective-permute-start | bytes 393224 | tf_op jit(solution)/shard_map/ppermute | solution.py:71
  13.1 2.0 %scatter_custom_fusion = f32[5,2048]{0,1:T(8,128)S(1)} fusion(s32[512]{0:T(512)S(1)} %bitcast.345, f32[512,5]{1,0:T(8,128)S(1)} %copy.36, f32[]{:T(128)} %constant.25.clone.1), kind=kCustom, calls=%fused_computation.14 | custom fusion | bytes 40964 | tf_op jit(solution)/shard_map/scatter | solution.py:35
  16.2 7.8 %all-to-all-start = ((f32[32,1,320]{2,1,0:T(1,128)}), f32[32,1,320]{2,1,0:T(1,128)S(1)}, u32[]{:S(2)}, u32[]{:S(2)}) async-start(f32[32,1,320]{2,1,0:T(1,128)} %reshape.218), calls=%async_computation | async-start | bytes 98304 | tf_op jit(solution)/shard_map/all_to_all | solution.py:37
  24.7 2.8 %collective-permute-start.2 = (f32[2,128,128]{2,1,0:T(8,128)S(1)}, f32[2,128,128]{2,1,0:T(8,128)S(1)}, u32[]{:S(2)}, u32[]{:S(2)}) collective-permute-start(f32[2,128,128]{2,1,0:T(8,128)S(1)} %pad_maximum_fusion.7), channel_id=1, source_target_pairs={{0,16},{4,20},{8,24},{12,28},{16,0},{20,4},{24,8},{28,12},{32,48},... | collective-permute-start | bytes 393224 | tf_op jit(solution)/shard_map/ppermute | solution.py:71
  27.5 3.6 %all-to-all-done = f32[32,1,320]{2,1,0:T(1,128)S(1)} async-done(((f32[32,1,320]{2,1,0:T(1,128)}), f32[32,1,320]{2,1,0:T(1,128)S(1)}, u32[]{:S(2)}, u32[]{:S(2)}) %all-to-all-start) | async-done | bytes 40992 | tf_op jit(solution)/shard_map/all_to_all | solution.py:37
  34.5 2.7 %collective-permute-done.3 = f32[2,128,128]{2,1,0:T(8,128)S(1)} collective-permute-done((f32[2,128,128]{2,1,0:T(8,128)S(1)}, f32[2,128,128]{2,1,0:T(8,128)S(1)}, u32[]{:S(2)}, u32[]{:S(2)}) %collective-permute-start.3) | collective-permute-done | bytes 131104 | tf_op jit(solution)/shard_map/ppermute | solution.py:71
  40.3 0.9 select_convert_fusion
  41.3 3.5 %fusion.1 = f32[512,3,512]{2,0,1:T(8,128)S(1)} fusion(bf16[3,512,2048]{2,1,0:T(8,128)(2,1)S(1)} %bitcast.329, s32[2048]{0:T(1024)S(1)} %bitcast.344), kind=kOutput, calls=%fused_computation.4 | convolution fusion | flops 3222274048 | bytes 9445376 | tf_op jit(solution)/shard_map/dot_general | solution.py:62
  46.3 1.2 add_add_fusion.5
  47.6 1.1 subtract_add_fusion.3
  48.7 1.0 subtract_add_fusion
  50.5 8.8 %collective-permute-done.4 = f32[8,128,128]{2,1,0:T(8,128)S(1)} collective-permute-done((f32[8,128,128]{2,1,0:T(8,128)S(1)}, f32[8,128,128]{2,1,0:T(8,128)S(1)}, u32[]{:S(2)}, u32[]{:S(2)}) %collective-permute-start.4) | collective-permute-done | bytes 524320 | tf_op jit(solution)/shard_map/ppermute | solution.py:71
  59.9 8.3 %collective-permute-done.5 = f32[8,128,128]{2,1,0:T(8,128)S(1)} collective-permute-done((f32[8,128,128]{2,1,0:T(8,128)S(1)}, f32[8,128,128]{2,1,0:T(8,128)S(1)}, u32[]{:S(2)}, u32[]{:S(2)}) %collective-permute-start.5) | collective-permute-done | bytes 524320 | tf_op jit(solution)/shard_map/ppermute | solution.py:71
  68.4 1.2 collective-permute-start.6
  69.6 9.9 %collective-permute-done.6 = f32[8,128,128]{2,1,0:T(8,128)S(1)} collective-permute-done((f32[8,128,128]{2,1,0:T(8,128)S(1)}, f32[8,128,128]{2,1,0:T(8,128)S(1)}, u32[]{:S(2)}, u32[]{:S(2)}) %collective-permute-start.6) | collective-permute-done | bytes 524320 | tf_op jit(solution)/shard_map/ppermute | solution.py:71
  79.6 0.8 pad_maximum_fusion.3
  80.4 0.9 collective-permute-start.7
  81.3 1.0 broadcast_select_fusion.6
  82.3 6.4 %collective-permute-done.7 = f32[8,128,128]{2,1,0:T(8,128)S(1)} collective-permute-done((f32[8,128,128]{2,1,0:T(8,128)}, f32[8,128,128]{2,1,0:T(8,128)S(1)}, u32[]{:S(2)}, u32[]{:S(2)}) %collective-permute-start.7) | collective-permute-done | bytes 524320 | tf_op jit(solution)/shard_map/ppermute | solution.py:71
  88.8 2.8 %collective-permute-start.8 = (f32[4,128,128]{2,1,0:T(8,128)S(1)}, f32[4,128,128]{2,1,0:T(8,128)S(1)}, u32[]{:S(2)}, u32[]{:S(2)}) collective-permute-start(f32[4,128,128]{2,1,0:T(8,128)S(1)} %pad_maximum_fusion.4), channel_id=1, source_target_pairs={{0,64},{4,68},{8,72},{12,76},{16,80},{20,84},{24,88},{28,92},{32,9... | collective-permute-start | bytes 786440 | tf_op jit(solution)/shard_map/ppermute | solution.py:71
  91.6 6.8 %collective-permute-done.8 = f32[4,128,128]{2,1,0:T(8,128)S(1)} collective-permute-done((f32[4,128,128]{2,1,0:T(8,128)S(1)}, f32[4,128,128]{2,1,0:T(8,128)S(1)}, u32[]{:S(2)}, u32[]{:S(2)}) %collective-permute-start.8) | collective-permute-done | bytes 262176 | tf_op jit(solution)/shard_map/ppermute | solution.py:71
  98.5 1.7 %add_select_fusion.bi_ref = f32[2,128,128]{2,1,0:T(8,128)} fusion(f32[4,128,128]{2,1,0:T(8,128)S(1)} %collective-permute-done.8, f32[8,128,128]{2,1,0:T(8,128)S(1)} %collective-permute-done.7, f32[8,128,128]{2,1,0:T(8,128)S(1)} %collective-permute-done.6, f32[8,128,128]{2,1,0:T(8,128)S(1)} %collective-permute-done.5, ...), kind=kLoop, calls=%fused_computation.20 | loop fusion | flops 786432 | bytes 2097157 | tf_op jit(solution)/shard_map/jit(_where)/select_n | solution.py:141
  100.2 1.7 %add_select_fusion.4.br_ref = f32[2,128,128]{2,1,0:T(8,128)} fusion(f32[4,128,128]{2,1,0:T(8,128)S(1)} %collective-permute-done.8, f32[8,128,128]{2,1,0:T(8,128)S(1)} %collective-permute-done.7, f32[8,128,128]{2,1,0:T(8,128)S(1)} %collective-permute-done.6, f32[8,128,128]{2,1,0:T(8,128)S(1)} %collective-permute-done.5, ...), kind=kLoop, calls=%fused_computation.24 | loop fusion | flops 786432 | bytes 2097157 | tf_op jit(solution)/shard_map/jit(_where)/select_n | solution.py:140
  103.4 2.9 %shard_map.82 = (f32[4,4,128,128]{3,2,1,0:T(8,128)}, f32[4,4,128]{2,1,0:T(4,128)}, f32[4,4,128]{2,1,0:T(4,128)}, f32[4,4,128]{2,1,0:T(4,128)}, f32[4,4,128]{2,1,0:T(4,128)}) custom-call(f32[4,4,128,128]{3,2,1,0:T(8,128)} %copy-done, f32[4,128,128]{2,1,0:T(8,128)} %copy-done.1, f32[4,128,128]{2,1,0:T(8,128)} %copy-done.2, ...), custom_call_target="tpu_custom_call" | custom-call | tf_op jit(solution)/shard_map/pallas_call | solution.py:213
  107.0 10.4 %collective-permute-start.10 = (f32[4,4,128]{2,1,0:T(4,128)S(1)}, f32[4,4,128]{2,1,0:T(4,128)S(1)}, u32[]{:S(2)}, u32[]{:S(2)}) collective-permute-start(f32[4,4,128]{2,1,0:T(4,128)S(1)} %bitcast.341), channel_id=1, source_target_pairs={{0,1},{1,0},{2,3},{3,2},{4,5},{5,4},{6,7},{7,6},{8,9},{9,8},{10,11... | collective-permute-start | bytes 24584 | tf_op jit(solution)/shard_map/ppermute | solution.py:154
  118.2 2.7 %collective-permute-start.9 = (f32[4,4,128]{2,1,0:T(4,128)S(1)}, f32[4,4,128]{2,1,0:T(4,128)S(1)}, u32[]{:S(2)}, u32[]{:S(2)}) collective-permute-start(f32[4,4,128]{2,1,0:T(4,128)S(1)} %bitcast.338), channel_id=1, source_target_pairs={{0,2},{2,0},{1,3},{3,1},{4,6},{6,4},{5,7},{7,5},{8,10},{10,8},{9,1... | collective-permute-start | bytes 24584 | tf_op jit(solution)/shard_map/ppermute | solution.py:154
  122.8 3.4 %shard_map.83 = f32[4,4,128,128]{3,2,1,0:T(8,128)} custom-call(f32[4,4,128,128]{3,2,1,0:T(8,128)} %get-tuple-element.84.c_ref, f32[4,4,128]{2,1,0:T(4,128)} %get-tuple-element.200.lx_ref, f32[4,4,128]{2,1,0:T(4,128)} %get-tuple-element.199.hx_ref, f32[4,4,128]{2,1,0:T(4,128)} %get-tuple-element.198.ly_ref, f32[4,4,128]{2,1,0:T(4,128)} %get-tuple-element.197.hy_ref), custom_call_target="tpu_custom_call" | custom-call | tf_op jit(solution)/shard_map/pallas_call | solution.py:219
  (128 shorter events, 20.9 us)
Async XLA Ops:
  2.8 36.5 %copy-start.1 = (f32[4,128,128]{2,1,0:T(8,128)}, f32[4,128,128]{2,1,0:T(8,128)S(1)}, u32[]{:S(2)}) copy-start(f32[4,128,128]{2,1,0:T(8,128)S(1)} %get-tuple-element.140.rr_ref) | copy-start | bytes 786436
  2.8 36.5 %copy-start.2 = (f32[4,128,128]{2,1,0:T(8,128)}, f32[4,128,128]{2,1,0:T(8,128)S(1)}, u32[]{:S(2)}) copy-start(f32[4,128,128]{2,1,0:T(8,128)S(1)} %get-tuple-element.141.ri_ref) | copy-start | bytes 786436
  3.8 6.6 %collective-permute-start = (f32[2,128,128]{2,1,0:T(8,128)S(1)}, f32[2,128,128]{2,1,0:T(8,128)S(1)}, u32[]{:S(2)}, u32[]{:S(2)}) collective-permute-start(f32[2,128,128]{2,1,0:T(8,128)S(1)} %pad_maximum_fusion.5), channel_id=1, source_target_pairs={{0,4},{4,0},{8,12},{12,8},{16,20},{20,16},{24,28},{28,24},{32,36},... | collective-permute-start | bytes 393224 | tf_op jit(solution)/shard_map/ppermute | solution.py:71
  11.1 12.9 %collective-permute-start.1 = (f32[2,128,128]{2,1,0:T(8,128)S(1)}, f32[2,128,128]{2,1,0:T(8,128)S(1)}, u32[]{:S(2)}, u32[]{:S(2)}) collective-permute-start(f32[2,128,128]{2,1,0:T(8,128)S(1)} %pad_maximum_fusion.6), channel_id=1, source_target_pairs={{0,8},{4,12},{8,0},{12,4},{16,24},{20,28},{24,16},{28,20},{32,40},... | collective-permute-start | bytes 393224 | tf_op jit(solution)/shard_map/ppermute | solution.py:71
  16.2 14.9 %all-to-all-start = ((f32[32,1,320]{2,1,0:T(1,128)}), f32[32,1,320]{2,1,0:T(1,128)S(1)}, u32[]{:S(2)}, u32[]{:S(2)}) async-start(f32[32,1,320]{2,1,0:T(1,128)} %reshape.218), calls=%async_computation | async-start | bytes 98304 | tf_op jit(solution)/shard_map/all_to_all | solution.py:37
  24.7 7.9 %collective-permute-start.2 = (f32[2,128,128]{2,1,0:T(8,128)S(1)}, f32[2,128,128]{2,1,0:T(8,128)S(1)}, u32[]{:S(2)}, u32[]{:S(2)}) collective-permute-start(f32[2,128,128]{2,1,0:T(8,128)S(1)} %pad_maximum_fusion.7), channel_id=1, source_target_pairs={{0,16},{4,20},{8,24},{12,28},{16,0},{20,4},{24,8},{28,12},{32,48},... | collective-permute-start | bytes 393224 | tf_op jit(solution)/shard_map/ppermute | solution.py:71
  33.3 3.9 %collective-permute-start.3 = (f32[2,128,128]{2,1,0:T(8,128)S(1)}, f32[2,128,128]{2,1,0:T(8,128)S(1)}, u32[]{:S(2)}, u32[]{:S(2)}) collective-permute-start(f32[2,128,128]{2,1,0:T(8,128)S(1)} %pad_maximum_fusion.8), channel_id=1, source_target_pairs={{0,32},{4,36},{8,40},{12,44},{16,48},{20,52},{24,56},{28,60},{32,0... | collective-permute-start | bytes 393224 | tf_op jit(solution)/shard_map/ppermute | solution.py:71
  46.0 4.3 %copy-start.22 = (f32[128,128]{1,0:T(8,128)S(1)}, f32[128,128]{1,0:T(8,128)}, u32[]{:S(2)}) copy-start(f32[128,128]{1,0:T(8,128)} %get-tuple-element.54) | copy-start | bytes 196612
  46.1 13.8 %copy-start.20 = (f32[128,128]{1,0:T(8,128)S(1)}, f32[128,128]{1,0:T(8,128)}, u32[]{:S(2)}) copy-start(f32[128,128]{1,0:T(8,128)} %get-tuple-element.60) | copy-start | bytes 196612
  46.1 13.8 %copy-start.21 = (f32[128,128]{1,0:T(8,128)S(1)}, f32[128,128]{1,0:T(8,128)}, u32[]{:S(2)}) copy-start(f32[128,128]{1,0:T(8,128)} %get-tuple-element.58) | copy-start | bytes 196612
  46.1 13.8 %copy-start.24 = (f32[128,128]{1,0:T(8,128)S(1)}, f32[128,128]{1,0:T(8,128)}, u32[]{:S(2)}) copy-start(f32[128,128]{1,0:T(8,128)} %get-tuple-element.59) | copy-start | bytes 196612
  46.1 13.8 %copy-start.25 = (f32[128,128]{1,0:T(8,128)S(1)}, f32[128,128]{1,0:T(8,128)}, u32[]{:S(2)}) copy-start(f32[128,128]{1,0:T(8,128)} %get-tuple-element.57) | copy-start | bytes 196612
  46.3 22.1 %copy-start = (f32[4,4,128,128]{3,2,1,0:T(8,128)}, f32[4,4,128,128]{3,2,1,0:T(8,128)S(1)}, u32[]{:S(2)}) copy-start(f32[4,4,128,128]{3,2,1,0:T(8,128)S(1)} %bitcast_add_fusion.f_ref) | copy-start | bytes 3145732
  47.6 22.0 %copy-start.13 = (f32[128,128]{1,0:T(8,128)S(1)}, f32[128,128]{1,0:T(8,128)}, u32[]{:S(2)}) copy-start(f32[128,128]{1,0:T(8,128)} %copy-done.12) | copy-start | bytes 196612
  47.6 22.0 %copy-start.15 = (f32[128,128]{1,0:T(8,128)S(1)}, f32[128,128]{1,0:T(8,128)}, u32[]{:S(2)}) copy-start(f32[128,128]{1,0:T(8,128)} %copy-done.14) | copy-start | bytes 196612
  47.6 22.0 %copy-start.28 = (f32[128,128]{1,0:T(8,128)S(1)}, f32[128,128]{1,0:T(8,128)}, u32[]{:S(2)}) copy-start(f32[128,128]{1,0:T(8,128)} %get-tuple-element.65) | copy-start | bytes 196612
  47.6 22.0 %copy-start.29 = (f32[128,128]{1,0:T(8,128)S(1)}, f32[128,128]{1,0:T(8,128)}, u32[]{:S(2)}) copy-start(f32[128,128]{1,0:T(8,128)} %get-tuple-element.63) | copy-start | bytes 196612
  49.8 9.5 %collective-permute-start.4 = (f32[8,128,128]{2,1,0:T(8,128)S(1)}, f32[8,128,128]{2,1,0:T(8,128)S(1)}, u32[]{:S(2)}, u32[]{:S(2)}) collective-permute-start(f32[8,128,128]{2,1,0:T(8,128)S(1)} %pad_maximum_fusion), channel_id=1, source_target_pairs={{0,4},{4,0},{8,12},{12,8},{16,20},{20,16},{24,28},{28,24},{32,36},... | collective-permute-start | bytes 1572872 | tf_op jit(solution)/shard_map/ppermute | solution.py:71
  50.4 48.1 %copy-start.7 = (f32[128,128]{1,0:T(8,128)S(1)}, f32[128,128]{1,0:T(8,128)}, u32[]{:S(2)}) copy-start(f32[128,128]{1,0:T(8,128)} %get-tuple-element.75) | copy-start | bytes 196612
  50.4 48.1 %copy-start.8 = (f32[128,128]{1,0:T(8,128)S(1)}, f32[128,128]{1,0:T(8,128)}, u32[]{:S(2)}) copy-start(f32[128,128]{1,0:T(8,128)} %get-tuple-element.79) | copy-start | bytes 196612
  50.4 48.1 %copy-start.9 = (f32[128,128]{1,0:T(8,128)S(1)}, f32[128,128]{1,0:T(8,128)}, u32[]{:S(2)}) copy-start(f32[128,128]{1,0:T(8,128)} %get-tuple-element.78) | copy-start | bytes 196612
  50.5 48.1 %copy-start.11 = (f32[128,128]{1,0:T(8,128)S(1)}, f32[128,128]{1,0:T(8,128)}, u32[]{:S(2)}) copy-start(f32[128,128]{1,0:T(8,128)} %get-tuple-element.74) | copy-start | bytes 196612
  59.5 8.7 %collective-permute-start.5 = (f32[8,128,128]{2,1,0:T(8,128)S(1)}, f32[8,128,128]{2,1,0:T(8,128)S(1)}, u32[]{:S(2)}, u32[]{:S(2)}) collective-permute-start(f32[8,128,128]{2,1,0:T(8,128)S(1)} %pad_maximum_fusion.1), channel_id=1, source_target_pairs={{0,8},{4,12},{8,0},{12,4},{16,24},{20,28},{24,16},{28,20},{32,40},... | collective-permute-start | bytes 1572872 | tf_op jit(solution)/shard_map/ppermute | solution.py:71
  68.2 33.6 %copy-start.4 = (f32[128,128]{1,0:T(8,128)S(1)}, f32[128,128]{1,0:T(8,128)}, u32[]{:S(2)}) copy-start(f32[128,128]{1,0:T(8,128)} %get-tuple-element.56) | copy-start | bytes 196612
  68.2 33.6 %copy-start.5 = (f32[128,128]{1,0:T(8,128)S(1)}, f32[128,128]{1,0:T(8,128)}, u32[]{:S(2)}) copy-start(f32[128,128]{1,0:T(8,128)} %get-tuple-element.55) | copy-start | bytes 196612
  68.2 33.6 %copy-start.6 = (f32[128,128]{1,0:T(8,128)S(1)}, f32[128,128]{1,0:T(8,128)}, u32[]{:S(2)}) copy-start(f32[128,128]{1,0:T(8,128)} %get-tuple-element.50) | copy-start | bytes 196612
  68.2 33.6 %copy-start.10 = (f32[128,128]{1,0:T(8,128)S(1)}, f32[128,128]{1,0:T(8,128)}, u32[]{:S(2)}) copy-start(f32[128,128]{1,0:T(8,128)} %subtract_select_fusion.1) | copy-start | bytes 196612
  68.4 11.1 %collective-permute-start.6 = (f32[8,128,128]{2,1,0:T(8,128)S(1)}, f32[8,128,128]{2,1,0:T(8,128)S(1)}, u32[]{:S(2)}, u32[]{:S(2)}) collective-permute-start(f32[8,128,128]{2,1,0:T(8,128)S(1)} %pad_maximum_fusion.2), channel_id=1, source_target_pairs={{0,16},{4,20},{8,24},{12,28},{16,0},{20,4},{24,8},{28,12},{32,48},... | collective-permute-start | bytes 1572872 | tf_op jit(solution)/shard_map/ppermute | solution.py:71
  80.4 8.2 %collective-permute-start.7 = (f32[8,128,128]{2,1,0:T(8,128)}, f32[8,128,128]{2,1,0:T(8,128)S(1)}, u32[]{:S(2)}, u32[]{:S(2)}) collective-permute-start(f32[8,128,128]{2,1,0:T(8,128)} %pad_maximum_fusion.3), channel_id=1, source_target_pairs={{0,32},{4,36},{8,40},{12,44},{16,48},{20,52},{24,56},{28,60},{32,0... | collective-permute-start | bytes 1572872 | tf_op jit(solution)/shard_map/ppermute | solution.py:71
  88.8 9.6 %collective-permute-start.8 = (f32[4,128,128]{2,1,0:T(8,128)S(1)}, f32[4,128,128]{2,1,0:T(8,128)S(1)}, u32[]{:S(2)}, u32[]{:S(2)}) collective-permute-start(f32[4,128,128]{2,1,0:T(8,128)S(1)} %pad_maximum_fusion.4), channel_id=1, source_target_pairs={{0,64},{4,68},{8,72},{12,76},{16,80},{20,84},{24,88},{28,92},{32,9... | collective-permute-start | bytes 786440 | tf_op jit(solution)/shard_map/ppermute | solution.py:71
  107.0 13.9 %collective-permute-start.10 = (f32[4,4,128]{2,1,0:T(4,128)S(1)}, f32[4,4,128]{2,1,0:T(4,128)S(1)}, u32[]{:S(2)}, u32[]{:S(2)}) collective-permute-start(f32[4,4,128]{2,1,0:T(4,128)S(1)} %bitcast.341), channel_id=1, source_target_pairs={{0,1},{1,0},{2,3},{3,2},{4,5},{5,4},{6,7},{7,6},{8,9},{9,8},{10,11... | collective-permute-start | bytes 24584 | tf_op jit(solution)/shard_map/ppermute | solution.py:154
  118.2 4.0 %collective-permute-start.9 = (f32[4,4,128]{2,1,0:T(4,128)S(1)}, f32[4,4,128]{2,1,0:T(4,128)S(1)}, u32[]{:S(2)}, u32[]{:S(2)}) collective-permute-start(f32[4,4,128]{2,1,0:T(4,128)S(1)} %bitcast.338), channel_id=1, source_target_pairs={{0,2},{2,0},{1,3},{3,1},{4,6},{6,4},{5,7},{7,5},{8,10},{10,8},{9,1... | collective-permute-start | bytes 24584 | tf_op jit(solution)/shard_map/ppermute | solution.py:154
  (10 other events, 37.1 us)

commit v7 on v6

--- a/solution.py
+++ b/solution.py
@@ -16,26 +16,52 @@
     return a_re * b_re - a_im * b_im, a_re * b_im + a_im * b_re
 
 
+def exact_pieces(values):
+    high = lax.reduce_precision(values, exponent_bits=8, mantissa_bits=7)
+    rest = values - high
+    middle = lax.reduce_precision(rest, exponent_bits=8, mantissa_bits=7)
+    return high, middle, rest - middle
+
+
+def route_kernel(rows_ref, slab_ref, out_ref):
+    rows_here = slab_ref.shape[0]
+    slab_count = out_ref.shape[1]
+    capacity = out_ref.shape[2]
+    slab = slab_ref[...]
+    picked = (slab == lax.broadcasted_iota(jnp.int32, (rows_here, slab_count), 1)).astype(jnp.float32)
+    earlier = (
+        lax.broadcasted_iota(jnp.int32, (rows_here, rows_here), 1)
+        < lax.broadcasted_iota(jnp.int32, (rows_here, rows_here), 0)
+    ).astype(jnp.bfloat16)
+    counts = jnp.dot(earlier, picked.astype(jnp.bfloat16), preferred_element_type=jnp.float32)
+    rank = jnp.sum(counts * picked, axis=1, keepdims=True).astype(jnp.int32)
+    slot = slab * capacity + rank
+    spots = (
+        slot == lax.broadcasted_iota(jnp.int32, (rows_here, slab_count * capacity), 1)
+    ).astype(jnp.bfloat16)
+    rows = rows_ref[...]
+    total = None
+    for piece in exact_pieces(rows):
+        part = jnp.dot(piece.astype(jnp.bfloat16), spots, preferred_element_type=jnp.float32)
+        total = part if total is None else total + part
+    for s in range(slab_count):
+        out_ref[:, s, :] = total[:, s * capacity : (s + 1) * capacity]
+
+
 def inject_receivers(source, recv_values, recv_slab, recv_lateral, recv_layer, levels):
     layers, components, width_x, width_y = source.shape
     slab_count = lax.axis_size("slab")
     plane_size = width_x * width_y
     rows_here = recv_values.shape[3]
     capacity = rows_here // min(8, slab_count)
-    values = recv_values[0, 0]
-    target_slab = recv_slab[0, 0, :, 0]
     position = recv_layer[0, 0] * plane_size + recv_lateral[0, 0]
-    one_hot = (target_slab[:, None] == jnp.arange(slab_count, dtype=jnp.int32)[None, :]).astype(
-        jnp.int32
-    )
-    ranking = jnp.sum((jnp.cumsum(one_hot, axis=0) - one_hot) * one_hot, axis=1)
-    target_slot = target_slab * capacity + ranking
-    rows = jnp.concatenate([values, position.astype(jnp.float32)[None, :]], axis=0)
-    send_rows = (
-        jnp.zeros((components + 1, slab_count * capacity), jnp.float32).at[:, target_slot].set(rows)
-    )
+    rows = jnp.concatenate([recv_values[0, 0], position.astype(jnp.float32)[None, :]], axis=0)
+    send_rows = pl.pallas_call(
+        route_kernel,
+        out_shape=jax.ShapeDtypeStruct((components + 1, slab_count, capacity), jnp.float32),
+    )(rows, recv_slab[0, 0])
     got_rows = lax.all_to_all(
-        send_rows.reshape(components + 1, slab_count, capacity),
+        send_rows,
         "slab",
         split_axis=1,
         concat_axis=1,
@@ -50,11 +76,7 @@
         row_of[None, :] == jnp.arange(layers * width_x, dtype=jnp.int32)[:, None]
     ).astype(jnp.bfloat16)
     pick_cols = col_of[:, None] == jnp.arange(width_y, dtype=jnp.int32)[None, :]
-    high = lax.reduce_precision(inject_values, exponent_bits=8, mantissa_bits=7)
-    rest = inject_values - high
-    middle = lax.reduce_precision(rest, exponent_bits=8, mantissa_bits=7)
-    low = rest - middle
-    pieces = jnp.stack([high, middle, low], axis=0)
+    pieces = jnp.stack(exact_pieces(inject_values), axis=0)
     spread = jnp.where(pick_cols[None, None, :, :], pieces[:, :, :, None], 0.0)
     spread = jnp.transpose(spread, (2, 0, 1, 3)).reshape(
         slab_count * capacity, 3 * components * width_y

time: 127 us -> 132 us (1.039)
  Pallas kernels: 6.33 us -> 9.96 us
  other arithmetic: 29.3 us -> 26.6 us
  waiting for transfers between devices: 47.2 us -> 49.6 us
  starting transfers between devices: 33.5 us -> 35.3 us
    pallas_call x0 -> x1, Pallas kernels: none -> 3.65 us  [inject_receivers(): pl.pallas_call(route_kernel, out_shape=jax.ShapeDtypeStruct((components +...]
    ppermute x9, waiting for transfers between devices: 42.9 us -> 45 us  [exchange(): return lax.ppermute(array, 'slab', [(i, i ^ step) for i in range(count)])]
    scatter x1 -> x0, local copies, waits for them, and re-layouts: 1.96 us -> none  [inject_receivers(): jnp.zeros((components + 1, slab_count * capacity), jnp.float32)]
    squeeze x0 -> x1, local copies, waits for them, and re-layouts: none -> 1.53 us  [inject_receivers(): recv_slab[0, 0]]
  transfers between devices with their start and end apart: 12 -> 12, of which waited for: 8 -> 9; matrix products, arithmetic and copies ran while one was open for 11% -> 8% of each run, Pallas kernels for 0% -> 3%
where the time goes in v7:
time: 132 us; the launch traced here: 131 us
  waiting for transfers between devices  49.6 us (38%)
  starting transfers between devices  35.3 us (27%)
  other arithmetic  26.6 us (20%)
  Pallas kernels  9.96 us (8%)
  local copies, waits for them, and re-layouts  5.53 us (4%)
  matrix products  3.53 us (3%)
    ppermute x9, waiting for transfers between devices, exchange(): return lax.ppermute(array, 'slab', [(i, i ^ step) for i in range(count)])  45 us
    ppermute x9, starting transfers between devices, exchange(): return lax.ppermute(array, 'slab', [(i, i ^ step) for i in range(count)])  13.7 us
    ppermute x2, starting transfers between devices, edge_pair(): lax.ppermute(jnp.where(here == 0, last, first), axis, [(0, 1), (1, 0)])  12.9 us
    all_to_all x1, starting transfers between devices, inject_receivers(): lax.all_to_all(send_rows, 'slab', split_axis=1, concat_axis=1, tiled=True)  8.69 us
    pallas_call x1, Pallas kernels, inject_receivers(): pl.pallas_call(route_kernel, out_shape=jax.ShapeDtypeStruct((components +...  3.65 us
    all_to_all x1, waiting for transfers between devices, inject_receivers(): lax.all_to_all(send_rows, 'slab', split_axis=1, concat_axis=1, tiled=True)  3.6 us
    dot_general x1, matrix products, inject_receivers(): jnp.dot(pick_rows, spread.astype(jnp.bfloat16), preferred_element_type=jn...  3.53 us
    pallas_call x1, Pallas kernels, finish(): pl.pallas_call(stencil_kernel, out_shape=jax.ShapeDtypeStruct(fields.shap...  3.4 us
  transfers between devices with their start and end apart: 12, of which 9 were waited for; matrix products, arithmetic and copies ran while one was open for 8% of the time, Pallas kernels for 3%

profile of v7, /device:TPU:1, one launch (start us, length us, event | category | flops | bytes accessed | tf_op | source)
XLA Modules:
  0.0 131.1 jit_solution(16498443083767010568)
XLA Ops:
  0.8 2.0 %cosine_multiply_fusion = (f32[4,128,128]{2,1,0:T(8,128)S(1)}, f32[4,128,128]{2,1,0:T(8,128)S(1)}) fusion(f32[4,128,128]{2,1,0:T(8,128)} %param.9, f32[4,128,128]{2,1,0:T(8,128)} %param.10, f32[128,128]{1,0:T(8,128)S(1)} %convert_multiply_fusion), kind=kLoop, calls=%fused_computation.15 | loop fusion | flops 262144 | bytes 1114112 | tf_op jit(solution)/shard_map/mul | solution.py:255
  3.8 2.1 %collective-permute-start = (f32[2,128,128]{2,1,0:T(8,128)S(1)}, f32[2,128,128]{2,1,0:T(8,128)S(1)}, u32[]{:S(2)}, u32[]{:S(2)}) collective-permute-start(f32[2,128,128]{2,1,0:T(8,128)S(1)} %pad_maximum_fusion.5), channel_id=1, source_target_pairs={{0,4},{4,0},{8,12},{12,8},{16,20},{20,16},{24,28},{28,24},{32,36},... | collective-permute-start | bytes 393224 | tf_op jit(solution)/shard_map/ppermute | solution.py:93
  5.9 2.7 %collective-permute-done = f32[2,128,128]{2,1,0:T(8,128)S(1)} collective-permute-done((f32[2,128,128]{2,1,0:T(8,128)S(1)}, f32[2,128,128]{2,1,0:T(8,128)S(1)}, u32[]{:S(2)}, u32[]{:S(2)}) %collective-permute-start) | collective-permute-done | bytes 131104 | tf_op jit(solution)/shard_map/ppermute | solution.py:93
  9.3 1.8 %collective-permute-start.1 = (f32[2,128,128]{2,1,0:T(8,128)S(1)}, f32[2,128,128]{2,1,0:T(8,128)S(1)}, u32[]{:S(2)}, u32[]{:S(2)}) collective-permute-start(f32[2,128,128]{2,1,0:T(8,128)S(1)} %pad_maximum_fusion.6), channel_id=1, source_target_pairs={{0,8},{4,12},{8,0},{12,4},{16,24},{20,28},{24,16},{28,20},{32,40},... | collective-permute-start | bytes 393224 | tf_op jit(solution)/shard_map/ppermute | solution.py:93
  11.9 1.5 %copy.30.slab_ref = s32[512,1]{1,0:T(8,128)} copy(s32[512,1]{0,1:T(1,128)} %bitcast.314) | data formatting | bytes 4096 | tf_op jit(solution)/shard_map/squeeze | solution.py:62
  13.4 1.3 pad_maximum_fusion.9.rows_ref
  14.7 3.6 %shard_map.82 = f32[5,32,64]{2,1,0:T(8,128)} custom-call(f32[5,512]{1,0:T(8,128)} %pad_maximum_fusion.9.rows_ref, s32[512,1]{1,0:T(8,128)} %copy.30.slab_ref), custom_call_target="tpu_custom_call" | custom-call | tf_op jit(solution)/shard_map/pallas_call | solution.py:59
  18.3 0.9 copy.52
  20.0 8.7 %all-to-all-start = ((f32[32,1,320]{2,1,0:T(1,128)}), f32[32,1,320]{2,1,0:T(1,128)S(1)}, u32[]{:S(2)}, u32[]{:S(2)}) async-start(f32[32,1,320]{2,1,0:T(1,128)} %reshape.157), calls=%async_computation | async-start | bytes 98304 | tf_op jit(solution)/shard_map/all_to_all | solution.py:63
  29.4 2.8 %collective-permute-start.2 = (f32[2,128,128]{2,1,0:T(8,128)S(1)}, f32[2,128,128]{2,1,0:T(8,128)S(1)}, u32[]{:S(2)}, u32[]{:S(2)}) collective-permute-start(f32[2,128,128]{2,1,0:T(8,128)S(1)} %pad_maximum_fusion.7), channel_id=1, source_target_pairs={{0,16},{4,20},{8,24},{12,28},{16,0},{20,4},{24,8},{28,12},{32,48},... | collective-permute-start | bytes 393224 | tf_op jit(solution)/shard_map/ppermute | solution.py:93
  32.2 3.6 %all-to-all-done = f32[32,1,320]{2,1,0:T(1,128)S(1)} async-done(((f32[32,1,320]{2,1,0:T(1,128)}), f32[32,1,320]{2,1,0:T(1,128)S(1)}, u32[]{:S(2)}, u32[]{:S(2)}) %all-to-all-start) | async-done | bytes 40992 | tf_op jit(solution)/shard_map/all_to_all | solution.py:63
  39.2 2.7 %collective-permute-done.3 = f32[2,128,128]{2,1,0:T(8,128)S(1)} collective-permute-done((f32[2,128,128]{2,1,0:T(8,128)S(1)}, f32[2,128,128]{2,1,0:T(8,128)S(1)}, u32[]{:S(2)}, u32[]{:S(2)}) %collective-permute-start.3) | collective-permute-done | bytes 131104 | tf_op jit(solution)/shard_map/ppermute | solution.py:93
  45.0 0.9 select_convert_fusion
  46.0 3.5 %fusion.1 = f32[512,3,512]{2,0,1:T(8,128)S(1)} fusion(bf16[3,512,2048]{2,1,0:T(8,128)(2,1)S(1)} %bitcast.302, s32[2048]{0:T(1024)S(1)} %bitcast.313), kind=kOutput, calls=%fused_computation.3 | convolution fusion | flops 3222274048 | bytes 9445376 | tf_op jit(solution)/shard_map/dot_general | solution.py:84
  51.0 1.2 add_add_fusion.5
  52.3 1.1 subtract_add_fusion.3
  53.4 1.0 subtract_add_fusion
  55.2 8.5 %collective-permute-done.4 = f32[8,128,128]{2,1,0:T(8,128)S(1)} collective-permute-done((f32[8,128,128]{2,1,0:T(8,128)S(1)}, f32[8,128,128]{2,1,0:T(8,128)S(1)}, u32[]{:S(2)}, u32[]{:S(2)}) %collective-permute-start.4) | collective-permute-done | bytes 524320 | tf_op jit(solution)/shard_map/ppermute | solution.py:93
  64.2 7.7 %collective-permute-done.5 = f32[8,128,128]{2,1,0:T(8,128)S(1)} collective-permute-done((f32[8,128,128]{2,1,0:T(8,128)S(1)}, f32[8,128,128]{2,1,0:T(8,128)S(1)}, u32[]{:S(2)}, u32[]{:S(2)}) %collective-permute-start.5) | collective-permute-done | bytes 524320 | tf_op jit(solution)/shard_map/ppermute | solution.py:93
  72.1 1.3 %collective-permute-start.6 = (f32[8,128,128]{2,1,0:T(8,128)S(1)}, f32[8,128,128]{2,1,0:T(8,128)S(1)}, u32[]{:S(2)}, u32[]{:S(2)}) collective-permute-start(f32[8,128,128]{2,1,0:T(8,128)S(1)} %pad_maximum_fusion.2), channel_id=1, source_target_pairs={{0,16},{4,20},{8,24},{12,28},{16,0},{20,4},{24,8},{28,12},{32,48},... | collective-permute-start | bytes 1572872 | tf_op jit(solution)/shard_map/ppermute | solution.py:93
  73.5 10.4 %collective-permute-done.6 = f32[8,128,128]{2,1,0:T(8,128)S(1)} collective-permute-done((f32[8,128,128]{2,1,0:T(8,128)S(1)}, f32[8,128,128]{2,1,0:T(8,128)S(1)}, u32[]{:S(2)}, u32[]{:S(2)}) %collective-permute-start.6) | collective-permute-done | bytes 524320 | tf_op jit(solution)/shard_map/ppermute | solution.py:93
  85.7 1.0 broadcast_select_fusion.6
  86.7 6.4 %collective-permute-done.7 = f32[8,128,128]{2,1,0:T(8,128)S(1)} collective-permute-done((f32[8,128,128]{2,1,0:T(8,128)}, f32[8,128,128]{2,1,0:T(8,128)S(1)}, u32[]{:S(2)}, u32[]{:S(2)}) %collective-permute-start.7) | collective-permute-done | bytes 524320 | tf_op jit(solution)/shard_map/ppermute | solution.py:93
  93.2 3.4 %collective-permute-start.8 = (f32[4,128,128]{2,1,0:T(8,128)S(1)}, f32[4,128,128]{2,1,0:T(8,128)S(1)}, u32[]{:S(2)}, u32[]{:S(2)}) collective-permute-start(f32[4,128,128]{2,1,0:T(8,128)S(1)} %pad_maximum_fusion.4), channel_id=1, source_target_pairs={{0,64},{4,68},{8,72},{12,76},{16,80},{20,84},{24,88},{28,92},{32,9... | collective-permute-start | bytes 786440 | tf_op jit(solution)/shard_map/ppermute | solution.py:93
  96.6 6.6 %collective-permute-done.8 = f32[4,128,128]{2,1,0:T(8,128)S(1)} collective-permute-done((f32[4,128,128]{2,1,0:T(8,128)S(1)}, f32[4,128,128]{2,1,0:T(8,128)S(1)}, u32[]{:S(2)}, u32[]{:S(2)}) %collective-permute-start.8) | collective-permute-done | bytes 262176 | tf_op jit(solution)/shard_map/ppermute | solution.py:93
  103.3 1.7 %add_select_fusion.bi_ref = f32[2,128,128]{2,1,0:T(8,128)} fusion(f32[4,128,128]{2,1,0:T(8,128)S(1)} %collective-permute-done.8, f32[8,128,128]{2,1,0:T(8,128)S(1)} %collective-permute-done.7, f32[8,128,128]{2,1,0:T(8,128)S(1)} %collective-permute-done.6, f32[8,128,128]{2,1,0:T(8,128)S(1)} %collective-permute-done.5, ...), kind=kLoop, calls=%fused_computation.17 | loop fusion | flops 786432 | bytes 2097157 | tf_op jit(solution)/shard_map/jit(_where)/select_n | solution.py:163
  105.0 1.7 %add_select_fusion.4.br_ref = f32[2,128,128]{2,1,0:T(8,128)} fusion(f32[4,128,128]{2,1,0:T(8,128)S(1)} %collective-permute-done.8, f32[8,128,128]{2,1,0:T(8,128)S(1)} %collective-permute-done.7, f32[8,128,128]{2,1,0:T(8,128)S(1)} %collective-permute-done.6, f32[8,128,128]{2,1,0:T(8,128)S(1)} %collective-permute-done.5, ...), kind=kLoop, calls=%fused_computation.21 | loop fusion | flops 786432 | bytes 2097157 | tf_op jit(solution)/shard_map/jit(_where)/select_n | solution.py:162
  108.2 2.9 %shard_map.83 = (f32[4,4,128,128]{3,2,1,0:T(8,128)}, f32[4,4,128]{2,1,0:T(4,128)}, f32[4,4,128]{2,1,0:T(4,128)}, f32[4,4,128]{2,1,0:T(4,128)}, f32[4,4,128]{2,1,0:T(4,128)}) custom-call(f32[4,4,128,128]{3,2,1,0:T(8,128)} %copy-done, f32[4,128,128]{2,1,0:T(8,128)} %copy-done.1, f32[4,128,128]{2,1,0:T(8,128)} %copy-done.2, ...), custom_call_target="tpu_custom_call" | custom-call | tf_op jit(solution)/shard_map/pallas_call | solution.py:235
  111.9 10.5 %collective-permute-start.10 = (f32[4,4,128]{2,1,0:T(4,128)S(1)}, f32[4,4,128]{2,1,0:T(4,128)S(1)}, u32[]{:S(2)}, u32[]{:S(2)}) collective-permute-start(f32[4,4,128]{2,1,0:T(4,128)S(1)} %bitcast.311), channel_id=1, source_target_pairs={{0,1},{1,0},{2,3},{3,2},{4,5},{5,4},{6,7},{7,6},{8,9},{9,8},{10,11... | collective-permute-start | bytes 24584 | tf_op jit(solution)/shard_map/ppermute | solution.py:176
  123.0 2.5 %collective-permute-start.9 = (f32[4,4,128]{2,1,0:T(4,128)S(1)}, f32[4,4,128]{2,1,0:T(4,128)S(1)}, u32[]{:S(2)}, u32[]{:S(2)}) collective-permute-start(f32[4,4,128]{2,1,0:T(4,128)S(1)} %bitcast.308), channel_id=1, source_target_pairs={{0,2},{2,0},{1,3},{3,1},{4,6},{6,4},{5,7},{7,5},{8,10},{10,8},{9,1... | collective-permute-start | bytes 24584 | tf_op jit(solution)/shard_map/ppermute | solution.py:176
  126.1 0.9 collective-permute-done.9
  127.7 3.4 %shard_map.84 = f32[4,4,128,128]{3,2,1,0:T(8,128)} custom-call(f32[4,4,128,128]{3,2,1,0:T(8,128)} %get-tuple-element.84.c_ref, f32[4,4,128]{2,1,0:T(4,128)} %get-tuple-element.200.lx_ref, f32[4,4,128]{2,1,0:T(4,128)} %get-tuple-element.199.hx_ref, f32[4,4,128]{2,1,0:T(4,128)} %get-tuple-element.198.ly_ref, f32[4,4,128]{2,1,0:T(4,128)} %get-tuple-element.197.hy_ref), custom_call_target="tpu_custom_call" | custom-call | tf_op jit(solution)/shard_map/pallas_call | solution.py:241
  (121 shorter events, 20.0 us)
Async XLA Ops:
  2.8 43.1 %copy-start.1 = (f32[4,128,128]{2,1,0:T(8,128)}, f32[4,128,128]{2,1,0:T(8,128)S(1)}, u32[]{:S(2)}) copy-start(f32[4,128,128]{2,1,0:T(8,128)S(1)} %get-tuple-element.140.rr_ref) | copy-start | bytes 786436
  2.8 43.1 %copy-start.2 = (f32[4,128,128]{2,1,0:T(8,128)}, f32[4,128,128]{2,1,0:T(8,128)S(1)}, u32[]{:S(2)}) copy-start(f32[4,128,128]{2,1,0:T(8,128)S(1)} %get-tuple-element.141.ri_ref) | copy-start | bytes 786436
  3.8 4.8 %collective-permute-start = (f32[2,128,128]{2,1,0:T(8,128)S(1)}, f32[2,128,128]{2,1,0:T(8,128)S(1)}, u32[]{:S(2)}, u32[]{:S(2)}) collective-permute-start(f32[2,128,128]{2,1,0:T(8,128)S(1)} %pad_maximum_fusion.5), channel_id=1, source_target_pairs={{0,4},{4,0},{8,12},{12,8},{16,20},{20,16},{24,28},{28,24},{32,36},... | collective-permute-start | bytes 393224 | tf_op jit(solution)/shard_map/ppermute | solution.py:93
  9.3 19.4 %collective-permute-start.1 = (f32[2,128,128]{2,1,0:T(8,128)S(1)}, f32[2,128,128]{2,1,0:T(8,128)S(1)}, u32[]{:S(2)}, u32[]{:S(2)}) collective-permute-start(f32[2,128,128]{2,1,0:T(8,128)S(1)} %pad_maximum_fusion.6), channel_id=1, source_target_pairs={{0,8},{4,12},{8,0},{12,4},{16,24},{20,28},{24,16},{28,20},{32,40},... | collective-permute-start | bytes 393224 | tf_op jit(solution)/shard_map/ppermute | solution.py:93
  20.0 15.8 %all-to-all-start = ((f32[32,1,320]{2,1,0:T(1,128)}), f32[32,1,320]{2,1,0:T(1,128)S(1)}, u32[]{:S(2)}, u32[]{:S(2)}) async-start(f32[32,1,320]{2,1,0:T(1,128)} %reshape.157), calls=%async_computation | async-start | bytes 98304 | tf_op jit(solution)/shard_map/all_to_all | solution.py:63
  29.4 7.9 %collective-permute-start.2 = (f32[2,128,128]{2,1,0:T(8,128)S(1)}, f32[2,128,128]{2,1,0:T(8,128)S(1)}, u32[]{:S(2)}, u32[]{:S(2)}) collective-permute-start(f32[2,128,128]{2,1,0:T(8,128)S(1)} %pad_maximum_fusion.7), channel_id=1, source_target_pairs={{0,16},{4,20},{8,24},{12,28},{16,0},{20,4},{24,8},{28,12},{32,48},... | collective-permute-start | bytes 393224 | tf_op jit(solution)/shard_map/ppermute | solution.py:93
  38.0 3.9 %collective-permute-start.3 = (f32[2,128,128]{2,1,0:T(8,128)S(1)}, f32[2,128,128]{2,1,0:T(8,128)S(1)}, u32[]{:S(2)}, u32[]{:S(2)}) collective-permute-start(f32[2,128,128]{2,1,0:T(8,128)S(1)} %pad_maximum_fusion.8), channel_id=1, source_target_pairs={{0,32},{4,36},{8,40},{12,44},{16,48},{20,52},{24,56},{28,60},{32,0... | collective-permute-start | bytes 393224 | tf_op jit(solution)/shard_map/ppermute | solution.py:93
  50.8 4.3 %copy-start.22 = (f32[128,128]{1,0:T(8,128)S(1)}, f32[128,128]{1,0:T(8,128)}, u32[]{:S(2)}) copy-start(f32[128,128]{1,0:T(8,128)} %get-tuple-element.54) | copy-start | bytes 196612
  50.8 13.4 %copy-start.20 = (f32[128,128]{1,0:T(8,128)S(1)}, f32[128,128]{1,0:T(8,128)}, u32[]{:S(2)}) copy-start(f32[128,128]{1,0:T(8,128)} %get-tuple-element.60) | copy-start | bytes 196612
  50.8 13.4 %copy-start.21 = (f32[128,128]{1,0:T(8,128)S(1)}, f32[128,128]{1,0:T(8,128)}, u32[]{:S(2)}) copy-start(f32[128,128]{1,0:T(8,128)} %get-tuple-element.58) | copy-start | bytes 196612
  50.8 13.4 %copy-start.24 = (f32[128,128]{1,0:T(8,128)S(1)}, f32[128,128]{1,0:T(8,128)}, u32[]{:S(2)}) copy-start(f32[128,128]{1,0:T(8,128)} %get-tuple-element.59) | copy-start | bytes 196612
  50.8 13.4 %copy-start.25 = (f32[128,128]{1,0:T(8,128)S(1)}, f32[128,128]{1,0:T(8,128)}, u32[]{:S(2)}) copy-start(f32[128,128]{1,0:T(8,128)} %get-tuple-element.57) | copy-start | bytes 196612
  51.0 21.1 %copy-start = (f32[4,4,128,128]{3,2,1,0:T(8,128)}, f32[4,4,128,128]{3,2,1,0:T(8,128)S(1)}, u32[]{:S(2)}) copy-start(f32[4,4,128,128]{3,2,1,0:T(8,128)S(1)} %bitcast_add_fusion.f_ref) | copy-start | bytes 3145732
  52.3 21.2 %copy-start.13 = (f32[128,128]{1,0:T(8,128)S(1)}, f32[128,128]{1,0:T(8,128)}, u32[]{:S(2)}) copy-start(f32[128,128]{1,0:T(8,128)} %copy-done.12) | copy-start | bytes 196612
  52.3 21.2 %copy-start.15 = (f32[128,128]{1,0:T(8,128)S(1)}, f32[128,128]{1,0:T(8,128)}, u32[]{:S(2)}) copy-start(f32[128,128]{1,0:T(8,128)} %copy-done.14) | copy-start | bytes 196612
  52.3 21.2 %copy-start.28 = (f32[128,128]{1,0:T(8,128)S(1)}, f32[128,128]{1,0:T(8,128)}, u32[]{:S(2)}) copy-start(f32[128,128]{1,0:T(8,128)} %get-tuple-element.65) | copy-start | bytes 196612
  52.3 21.2 %copy-start.29 = (f32[128,128]{1,0:T(8,128)S(1)}, f32[128,128]{1,0:T(8,128)}, u32[]{:S(2)}) copy-start(f32[128,128]{1,0:T(8,128)} %get-tuple-element.63) | copy-start | bytes 196612
  54.5 9.1 %collective-permute-start.4 = (f32[8,128,128]{2,1,0:T(8,128)S(1)}, f32[8,128,128]{2,1,0:T(8,128)S(1)}, u32[]{:S(2)}, u32[]{:S(2)}) collective-permute-start(f32[8,128,128]{2,1,0:T(8,128)S(1)} %pad_maximum_fusion), channel_id=1, source_target_pairs={{0,4},{4,0},{8,12},{12,8},{16,20},{20,16},{24,28},{28,24},{32,36},... | collective-permute-start | bytes 1572872 | tf_op jit(solution)/shard_map/ppermute | solution.py:93
  55.1 48.2 %copy-start.7 = (f32[128,128]{1,0:T(8,128)S(1)}, f32[128,128]{1,0:T(8,128)}, u32[]{:S(2)}) copy-start(f32[128,128]{1,0:T(8,128)} %get-tuple-element.75) | copy-start | bytes 196612
  55.1 48.2 %copy-start.8 = (f32[128,128]{1,0:T(8,128)S(1)}, f32[128,128]{1,0:T(8,128)}, u32[]{:S(2)}) copy-start(f32[128,128]{1,0:T(8,128)} %get-tuple-element.79) | copy-start | bytes 196612
  55.2 48.2 %copy-start.9 = (f32[128,128]{1,0:T(8,128)S(1)}, f32[128,128]{1,0:T(8,128)}, u32[]{:S(2)}) copy-start(f32[128,128]{1,0:T(8,128)} %get-tuple-element.78) | copy-start | bytes 196612
  55.2 48.2 %copy-start.11 = (f32[128,128]{1,0:T(8,128)S(1)}, f32[128,128]{1,0:T(8,128)}, u32[]{:S(2)}) copy-start(f32[128,128]{1,0:T(8,128)} %get-tuple-element.74) | copy-start | bytes 196612
  63.8 8.1 %collective-permute-start.5 = (f32[8,128,128]{2,1,0:T(8,128)S(1)}, f32[8,128,128]{2,1,0:T(8,128)S(1)}, u32[]{:S(2)}, u32[]{:S(2)}) collective-permute-start(f32[8,128,128]{2,1,0:T(8,128)S(1)} %pad_maximum_fusion.1), channel_id=1, source_target_pairs={{0,8},{4,12},{8,0},{12,4},{16,24},{20,28},{24,16},{28,20},{32,40},... | collective-permute-start | bytes 1572872 | tf_op jit(solution)/shard_map/ppermute | solution.py:93
  71.9 34.8 %copy-start.4 = (f32[128,128]{1,0:T(8,128)S(1)}, f32[128,128]{1,0:T(8,128)}, u32[]{:S(2)}) copy-start(f32[128,128]{1,0:T(8,128)} %get-tuple-element.56) | copy-start | bytes 196612
  71.9 34.8 %copy-start.5 = (f32[128,128]{1,0:T(8,128)S(1)}, f32[128,128]{1,0:T(8,128)}, u32[]{:S(2)}) copy-start(f32[128,128]{1,0:T(8,128)} %get-tuple-element.55) | copy-start | bytes 196612
  71.9 34.8 %copy-start.6 = (f32[128,128]{1,0:T(8,128)S(1)}, f32[128,128]{1,0:T(8,128)}, u32[]{:S(2)}) copy-start(f32[128,128]{1,0:T(8,128)} %get-tuple-element.50) | copy-start | bytes 196612
  71.9 34.8 %copy-start.10 = (f32[128,128]{1,0:T(8,128)S(1)}, f32[128,128]{1,0:T(8,128)}, u32[]{:S(2)}) copy-start(f32[128,128]{1,0:T(8,128)} %subtract_select_fusion.1) | copy-start | bytes 196612
  72.1 11.8 %collective-permute-start.6 = (f32[8,128,128]{2,1,0:T(8,128)S(1)}, f32[8,128,128]{2,1,0:T(8,128)S(1)}, u32[]{:S(2)}, u32[]{:S(2)}) collective-permute-start(f32[8,128,128]{2,1,0:T(8,128)S(1)} %pad_maximum_fusion.2), channel_id=1, source_target_pairs={{0,16},{4,20},{8,24},{12,28},{16,0},{20,4},{24,8},{28,12},{32,48},... | collective-permute-start | bytes 1572872 | tf_op jit(solution)/shard_map/ppermute | solution.py:93
  84.8 8.2 %collective-permute-start.7 = (f32[8,128,128]{2,1,0:T(8,128)}, f32[8,128,128]{2,1,0:T(8,128)S(1)}, u32[]{:S(2)}, u32[]{:S(2)}) collective-permute-start(f32[8,128,128]{2,1,0:T(8,128)} %pad_maximum_fusion.3), channel_id=1, source_target_pairs={{0,32},{4,36},{8,40},{12,44},{16,48},{20,52},{24,56},{28,60},{32,0... | collective-permute-start | bytes 1572872 | tf_op jit(solution)/shard_map/ppermute | solution.py:93
  93.2 10.0 %collective-permute-start.8 = (f32[4,128,128]{2,1,0:T(8,128)S(1)}, f32[4,128,128]{2,1,0:T(8,128)S(1)}, u32[]{:S(2)}, u32[]{:S(2)}) collective-permute-start(f32[4,128,128]{2,1,0:T(8,128)S(1)} %pad_maximum_fusion.4), channel_id=1, source_target_pairs={{0,64},{4,68},{8,72},{12,76},{16,80},{20,84},{24,88},{28,92},{32,9... | collective-permute-start | bytes 786440 | tf_op jit(solution)/shard_map/ppermute | solution.py:93
  111.9 13.6 %collective-permute-start.10 = (f32[4,4,128]{2,1,0:T(4,128)S(1)}, f32[4,4,128]{2,1,0:T(4,128)S(1)}, u32[]{:S(2)}, u32[]{:S(2)}) collective-permute-start(f32[4,4,128]{2,1,0:T(4,128)S(1)} %bitcast.311), channel_id=1, source_target_pairs={{0,1},{1,0},{2,3},{3,2},{4,5},{5,4},{6,7},{7,6},{8,9},{9,8},{10,11... | collective-permute-start | bytes 24584 | tf_op jit(solution)/shard_map/ppermute | solution.py:176
  123.0 4.0 %collective-permute-start.9 = (f32[4,4,128]{2,1,0:T(4,128)S(1)}, f32[4,4,128]{2,1,0:T(4,128)S(1)}, u32[]{:S(2)}, u32[]{:S(2)}) collective-permute-start(f32[4,4,128]{2,1,0:T(4,128)S(1)} %bitcast.308), channel_id=1, source_target_pairs={{0,2},{2,0},{1,3},{3,1},{4,6},{6,4},{5,7},{7,5},{8,10},{10,8},{9,1... | collective-permute-start | bytes 24584 | tf_op jit(solution)/shard_map/ppermute | solution.py:176
  (10 other events, 37.1 us)

commit v8 on v6

--- a/solution.py
+++ b/solution.py
@@ -16,7 +16,7 @@
     return a_re * b_re - a_im * b_im, a_re * b_im + a_im * b_re
 
 
-def inject_receivers(source, recv_values, recv_slab, recv_lateral, recv_layer, levels):
+def route_rows(source, recv_values, recv_slab, recv_lateral, recv_layer):
     layers, components, width_x, width_y = source.shape
     slab_count = lax.axis_size("slab")
     plane_size = width_x * width_y
@@ -34,14 +34,20 @@
     send_rows = (
         jnp.zeros((components + 1, slab_count * capacity), jnp.float32).at[:, target_slot].set(rows)
     )
+    return send_rows.reshape(components + 1, slab_count, capacity)
+
+
+def inject_receivers(source, send_rows):
+    layers, components, width_x, width_y = source.shape
+    slab_count = lax.axis_size("slab")
+    capacity = send_rows.shape[2]
     got_rows = lax.all_to_all(
-        send_rows.reshape(components + 1, slab_count, capacity),
+        send_rows,
         "slab",
         split_axis=1,
         concat_axis=1,
         tiled=True,
     ).reshape(components + 1, slab_count * capacity)
-    got_rows, levels = lax.optimization_barrier((got_rows, levels))
     inject_values = got_rows[:components]
     inject_places = got_rows[components].astype(jnp.int32)
     row_of = inject_places // width_y
@@ -63,7 +69,7 @@
     added = added.reshape(layers * width_x, 3, components * width_y)
     added = (added[:, 0] + added[:, 1]) + added[:, 2]
     added = jnp.transpose(added.reshape(layers, width_x, components, width_y), (0, 2, 1, 3))
-    return source + added, levels
+    return source + added
 
 
 def exchange(array, step):
@@ -71,44 +77,26 @@
     return lax.ppermute(array, "slab", [(i, i ^ step) for i in range(count)])
 
 
-def block_products(a_re, a_im):
+def entering_states(down_b, up_b, a_re, a_im):
     slab_count = lax.axis_size("slab")
     here = lax.axis_index("slab")
+    shots = down_b[0].shape[0]
+    before = (jnp.zeros_like(down_b[0]), jnp.zeros_like(down_b[1]))
+    after = (jnp.zeros_like(up_b[0]), jnp.zeros_like(up_b[1]))
     one = jnp.ones_like(a_re)
     zero = jnp.zeros_like(a_re)
     total = (a_re, a_im)
     below = (one, zero)
     above = (one, zero)
-    levels = []
     step = 1
-    while 2 * step < slab_count:
-        got = exchange(jnp.stack(total, axis=0), step)
-        partner = (got[0], got[1])
-        levels.append((total, partner, below, above))
-        lower = (here & step) == 0
-        grown_below = complex_times(*below, *partner)
-        grown_above = complex_times(*above, *partner)
-        below = (jnp.where(lower, below[0], grown_below[0]), jnp.where(lower, below[1], grown_below[1]))
-        above = (jnp.where(lower, grown_above[0], above[0]), jnp.where(lower, grown_above[1], above[1]))
-        total = complex_times(*total, *partner)
-        step *= 2
-    levels.append((None, None, below, above))
-    return levels
-
-
-def entering_states(down_b, up_b, levels):
-    slab_count = lax.axis_size("slab")
-    here = lax.axis_index("slab")
-    shots = down_b[0].shape[0]
-    before = (jnp.zeros_like(down_b[0]), jnp.zeros_like(down_b[1]))
-    after = (jnp.zeros_like(up_b[0]), jnp.zeros_like(up_b[1]))
-    step = 1
-    level = 0
     while step < slab_count:
         lower = (here & step) == 0
-        total, partner, below, above = levels[level]
         if 2 * step < slab_count:
-            got = exchange(jnp.concatenate([*down_b, *up_b], axis=0), step)
+            got = exchange(
+                jnp.concatenate([total[0][None], total[1][None], *down_b, *up_b], axis=0), step
+            )
+            partner = (got[0], got[1])
+            got = got[2:]
             pd = (got[:shots], got[shots : 2 * shots])
             pu = (got[2 * shots : 3 * shots], got[3 * shots :])
             t_re, t_im = total[0][None], total[1][None]
@@ -142,8 +130,18 @@
         )
         if 2 * step < slab_count:
             down_b, up_b = new_down, new_up
+            grown_below = complex_times(*below, *partner)
+            grown_above = complex_times(*above, *partner)
+            below = (
+                jnp.where(lower, below[0], grown_below[0]),
+                jnp.where(lower, below[1], grown_below[1]),
+            )
+            above = (
+                jnp.where(lower, grown_above[0], above[0]),
+                jnp.where(lower, grown_above[1], above[1]),
+            )
+            total = complex_times(*total, *partner)
         step *= 2
-        level += 1
     return before, after
 
 
@@ -228,6 +226,7 @@
     slab_count = lax.axis_size("slab")
     depth_total = layers * slab_count
 
+    send_rows = route_rows(source, recv_values, recv_slab, recv_lateral, recv_layer)
     damping = attenuation + 0.5 / depth_total * pml_level.astype(jnp.float32)[None, :, :]
     amplitude = jnp.exp(-damping)
     rate_re = amplitude * jnp.cos(phase)
@@ -236,11 +235,8 @@
     prod_down = [(rate_re[0], rate_im[0])]
     for k in range(1, layers):
         prod_down.append(complex_times(rate_re[k], rate_im[k], *prod_down[-1]))
-    levels = block_products(*prod_down[-1])
-
-    forcing, levels = inject_receivers(
-        source, recv_values, recv_slab, recv_lateral, recv_layer, levels
-    )
+
+    forcing = inject_receivers(source, send_rows)
     fields = forcing.reshape(layers, shot_count, 2, width_x, width_y)
     f_re = fields[:, :, 0]
     f_im = fields[:, :, 1]
@@ -260,7 +256,9 @@
         state = (t_re + f_re[k], t_im + f_im[k])
         up[k] = state
 
-    (enter_re, enter_im), (below_re, below_im) = entering_states(down[layers - 1], up[0], levels)
+    (enter_re, enter_im), (below_re, below_im) = entering_states(
+        down[layers - 1], up[0], *prod_down[-1]
+    )
 
     return finish(forcing, rate_re, rate_im, enter_re, enter_im, below_re, below_im)
 

time: 127 us -> 142 us (1.12)
  other arithmetic: 29.3 us -> 44.5 us
  waiting for transfers between devices: 47.2 us -> 57.3 us
  starting transfers between devices: 33.5 us -> 24.9 us
    unnamed x0 -> x17, other arithmetic: none -> 12.7 us
    ppermute x9 -> x5, waiting for transfers between devices: 42.9 us -> 54.9 us  [exchange(): return lax.ppermute(array, 'slab', [(i, i ^ step) for i in range(count)])]
    ppermute x9 -> x5, starting transfers between devices: 12.6 us -> 6 us  [exchange(): return lax.ppermute(array, 'slab', [(i, i ^ step) for i in range(count)])]
    mul x1 -> x8, other arithmetic: 1.98 us -> 8.55 us  [the longest x7 6.56 us: complex_times(): return (a_re * b_re - a_im * b_im, a_re * b_im + a_im * b_re)]
    ppermute x2, starting transfers between devices: 13.2 us -> 9.11 us  [edge_pair(): lax.ppermute(jnp.where(here == 0, last, first), axis, [(0, 1), (1, 0)])]
    add x4 -> x1, other arithmetic: 3.39 us -> 0.04 us  [shards(): state = (t_re + f_re[k], t_im + f_im[k])]
    select_n x9 -> x1, other arithmetic: 3.88 us -> 0.69 us  [route_rows(): jnp.zeros((components + 1, slab_count * capacity), jnp.float32)]
    sub x5 -> x0, other arithmetic: 2.9 us -> none  [complex_times(): return (a_re * b_re - a_im * b_im, a_re * b_im + a_im * b_re)]
  transfers between devices with their start and end apart: 12 -> 8, of which waited for: 8 -> 7; matrix products, arithmetic and copies ran while one was open for 11% -> 4% of each run, Pallas kernels for 0% -> 0%
where the time goes in v8:
time: 142 us; the launch traced here: 141 us
  waiting for transfers between devices  57.3 us (40%)
  other arithmetic  44.5 us (31%)
  starting transfers between devices  24.9 us (18%)
  Pallas kernels  6.35 us (4%)
  local copies, waits for them, and re-layouts  4.61 us (3%)
  matrix products  3.53 us (2%)
    ppermute x5, waiting for transfers between devices, exchange(): return lax.ppermute(array, 'slab', [(i, i ^ step) for i in range(count)])  54.9 us
    unnamed x17, other arithmetic  12.7 us
    all_to_all x1, starting transfers between devices, inject_receivers(): lax.all_to_all(send_rows, 'slab', split_axis=1, concat_axis=1, tiled=True)  9.81 us
    ppermute x2, starting transfers between devices, edge_pair(): lax.ppermute(jnp.where(here == 0, last, first), axis, [(0, 1), (1, 0)])  9.11 us
    mul x7, other arithmetic, complex_times(): return (a_re * b_re - a_im * b_im, a_re * b_im + a_im * b_re)  6.56 us
    ppermute x5, starting transfers between devices, exchange(): return lax.ppermute(array, 'slab', [(i, i ^ step) for i in range(count)])  6 us
    dot_general x1, matrix products, inject_receivers(): jnp.dot(pick_rows, spread.astype(jnp.bfloat16), preferred_element_type=jn...  3.53 us
    pallas_call x1, Pallas kernels, finish(): pl.pallas_call(stencil_kernel, out_shape=jax.ShapeDtypeStruct(fields.shap...  3.4 us
  transfers between devices with their start and end apart: 8, of which 7 were waited for; matrix products, arithmetic and copies ran while one was open for 4% of the time, Pallas kernels for 0%

profile of v8, /device:TPU:1, one launch (start us, length us, event | category | flops | bytes accessed | tf_op | source)
XLA Modules:
  0.0 141.5 jit_solution(13903372264479559358)
XLA Ops:
  0.7 1.2 reduce-window.6
  2.1 0.8 fusion.8
  5.2 2.0 %scatter_custom_fusion = f32[5,2048]{0,1:T(8,128)S(1)} fusion(s32[512]{0:T(512)S(1)} %bitcast.245, f32[512,5]{1,0:T(8,128)S(1)} %copy.36, f32[]{:T(128)} %constant.25.clone.1), kind=kCustom, calls=%fused_computation.10 | custom fusion | bytes 40964 | tf_op jit(solution)/shard_map/scatter | solution.py:35
  8.3 9.8 %all-to-all-start = ((f32[32,1,320]{2,1,0:T(1,128)}), f32[32,1,320]{2,1,0:T(1,128)S(1)}, u32[]{:S(2)}, u32[]{:S(2)}) async-start(f32[32,1,320]{2,1,0:T(1,128)} %reshape.229), calls=%async_computation | async-start | bytes 98304 | tf_op jit(solution)/shard_map/all_to_all | solution.py:44
  18.1 0.8 convert_multiply_fusion
  18.9 2.0 %sine_multiply_fusion = (f32[4,128,128]{2,1,0:T(8,128)S(1)}, f32[4,128,128]{2,1,0:T(8,128)S(1)}) fusion(f32[4,128,128]{2,1,0:T(8,128)} %param.9, f32[4,128,128]{2,1,0:T(8,128)} %param.10, f32[128,128]{1,0:T(8,128)S(1)} %convert_multiply_fusion), kind=kLoop, calls=%fused_computation.13 | loop fusion | flops 262144 | bytes 1114112 | tf_op jit(solution)/shard_map/mul | solution.py:233
  20.9 0.8 slice_bitcast_fusion.12
  23.0 2.2 %all-to-all-done = f32[32,1,320]{2,1,0:T(1,128)S(1)} async-done(((f32[32,1,320]{2,1,0:T(1,128)}), f32[32,1,320]{2,1,0:T(1,128)S(1)}, u32[]{:S(2)}, u32[]{:S(2)}) %all-to-all-start) | async-done | bytes 40992 | tf_op jit(solution)/shard_map/all_to_all | solution.py:44
  25.8 0.8 reduce.6
  27.1 0.9 select_convert_fusion
  28.0 3.5 %fusion.1 = f32[512,3,512]{2,0,1:T(8,128)S(1)} fusion(bf16[3,512,2048]{2,1,0:T(8,128)(2,1)S(1)} %bitcast.214, s32[2048]{0:T(1024)S(1)} %get-tuple-element.138), kind=kOutput, calls=%fused_computation.4 | convolution fusion | flops 3222274048 | bytes 9445376 | tf_op jit(solution)/shard_map/dot_general | solution.py:68
  32.3 1.4 bitcast_add_fusion.f_ref
  33.7 1.8 %constant_dynamic-update-slice_fusion.3 = (f32[10,128,128]{2,1,0:T(8,128)}, f32[2,128,128]{2,1,0:T(8,128)S(1)}, f32[2,128,128]{2,1,0:T(8,128)S(1)}, f32[2,128,12...) fusion(f32[10,128,128]{2,1,0:T(8,128)} %get-tuple-element.75, ...), kind=kLoop, calls=%fused_computation.150 | loop fusion | flops 655360 | bytes 1835008
  38.0 13.9 %collective-permute-done = f32[10,128,128]{2,1,0:T(8,128)S(1)} collective-permute-done((f32[10,128,128]{2,1,0:T(8,128)}, f32[10,128,128]{2,1,0:T(8,128)S(1)}, u32[]{:S(2)}, u32[]{:S(2)}) %collective-permute-start) | collective-permute-done | bytes 655392 | tf_op jit(solution)/shard_map/ppermute | solution.py:77
  56.0 0.7 collective-permute-start.1
  56.8 12.7 %collective-permute-done.1 = f32[10,128,128]{2,1,0:T(8,128)S(1)} collective-permute-done((f32[10,128,128]{2,1,0:T(8,128)}, f32[10,128,128]{2,1,0:T(8,128)S(1)}, u32[]{:S(2)}, u32[]{:S(2)}) %collective-permute-start.1) | collective-permute-done | bytes 655392 | tf_op jit(solution)/shard_map/ppermute | solution.py:77
  73.6 1.1 collective-permute-start.2
  74.6 12.9 %collective-permute-done.2 = f32[10,128,128]{2,1,0:T(8,128)S(1)} collective-permute-done((f32[10,128,128]{2,1,0:T(8,128)}, f32[10,128,128]{2,1,0:T(8,128)S(1)}, u32[]{:S(2)}, u32[]{:S(2)}) %collective-permute-start.2) | collective-permute-done | bytes 655392 | tf_op jit(solution)/shard_map/ppermute | solution.py:77
  92.0 11.4 %collective-permute-done.3 = f32[10,128,128]{2,1,0:T(8,128)S(1)} collective-permute-done((f32[10,128,128]{2,1,0:T(8,128)}, f32[10,128,128]{2,1,0:T(8,128)S(1)}, u32[]{:S(2)}, u32[]{:S(2)}) %collective-permute-start.3) | collective-permute-done | bytes 655392 | tf_op jit(solution)/shard_map/ppermute | solution.py:77
  104.1 1.6 %select_bitcast_fusion.7 = (f32[128,128]{1,0:T(8,128)S(1)}, f32[1,128,128]{2,1,0:T(8,128)S(1)}, f32[1,128,128]{2,1,0:T(8,128)S(1)}, f32[1,128,128]{2,1,0:T(8,128...) fusion(f32[10,128,128]{2,1,0:T(8,128)S(1)} %collective-permute-, ...), kind=kLoop, calls=%fused_computation.99 | loop fusion | flops 425984 | bytes 1310724 | tf_op jit(solution)/shard_map/mul | solution.py:16
  105.7 1.5 %select_bitcast_fusion.5 = (f32[128,128]{1,0:T(8,128)S(1)}, f32[128,128]{1,0:T(8,128)S(1)}, f32[128,128]{1,0:T(8,128)S(1)}, f32[128,128]{1,0:T(8,128)}) fusion(f32[1,128,128]{2,1,0:T(8,128)} %get-tuple-element.94, f32[10,128,128]{2,1,0:T(8,128)S(1)} %collective-permute-done.3, pred[]{:T(512)S(6)} %eq.101, f32[1,128,128]{2,1,0:T(8,128)S(1)} %get-tuple-element.17, ...), kind=kLoop, calls=%fused_computation.97 | loop fusion | flops 163840 | bytes 720897 | tf_op jit(solution)/shard_map/mul | solution.py:16
  107.2 1.1 add_select_fusion.17
  109.0 3.5 %collective-permute-start.4 = (f32[4,128,128]{2,1,0:T(8,128)}, f32[4,128,128]{2,1,0:T(8,128)S(1)}, u32[]{:S(2)}, u32[]{:S(2)}) collective-permute-start(f32[4,128,128]{2,1,0:T(8,128)} %pad_maximum_fusion), channel_id=1, source_target_pairs={{0,64},{4,68},{8,72},{12,76},{16,80},{20,84},{24,88},{28,92},{32,9... | collective-permute-start | bytes 786440 | tf_op jit(solution)/shard_map/ppermute | solution.py:77
  112.5 4.0 %collective-permute-done.4 = f32[4,128,128]{2,1,0:T(8,128)S(1)} collective-permute-done((f32[4,128,128]{2,1,0:T(8,128)}, f32[4,128,128]{2,1,0:T(8,128)S(1)}, u32[]{:S(2)}, u32[]{:S(2)}) %collective-permute-start.4) | collective-permute-done | bytes 262176 | tf_op jit(solution)/shard_map/ppermute | solution.py:77
  116.5 1.7 %add_select_fusion.12.er_ref = f32[2,128,128]{2,1,0:T(8,128)} fusion(f32[4,128,128]{2,1,0:T(8,128)S(1)} %collective-permute-done.4, f32[10,128,128]{2,1,0:T(8,128)S(1)} %collective-permute-done.3, f32[10,128,128]{2,1,0:T(8,128)S(1)} %collective-permute-done.2, f32[10,128,128]{2,1,0:T(8,128)S(1)} %collective-permute-done.1, ...), kind=kLoop, calls=%fused_computation.28 | loop fusion | flops 753664 | bytes 1966085 | tf_op jit(solution)/shard_map/jit(_where)/select_n | solution.py:123
  118.1 1.7 %add_select_fusion.8.ei_ref = f32[2,128,128]{2,1,0:T(8,128)} fusion(f32[4,128,128]{2,1,0:T(8,128)S(1)} %collective-permute-done.4, f32[10,128,128]{2,1,0:T(8,128)S(1)} %collective-permute-done.3, f32[10,128,128]{2,1,0:T(8,128)S(1)} %collective-permute-done.2, f32[10,128,128]{2,1,0:T(8,128)S(1)} %collective-permute-done.1, ...), kind=kLoop, calls=%fused_computation.24 | loop fusion | flops 753664 | bytes 1966085 | tf_op jit(solution)/shard_map/jit(_where)/select_n | solution.py:124
  119.8 1.7 %add_select_fusion.4.br_ref = f32[2,128,128]{2,1,0:T(8,128)} fusion(f32[4,128,128]{2,1,0:T(8,128)S(1)} %collective-permute-done.4, f32[10,128,128]{2,1,0:T(8,128)S(1)} %collective-permute-done.3, f32[10,128,128]{2,1,0:T(8,128)S(1)} %collective-permute-done.2, f32[10,128,128]{2,1,0:T(8,128)S(1)} %collective-permute-done.1, ...), kind=kLoop, calls=%fused_computation.20 | loop fusion | flops 753664 | bytes 1966085 | tf_op jit(solution)/shard_map/jit(_where)/select_n | solution.py:128
  121.5 1.7 %add_select_fusion.bi_ref = f32[2,128,128]{2,1,0:T(8,128)} fusion(f32[4,128,128]{2,1,0:T(8,128)S(1)} %collective-permute-done.4, f32[10,128,128]{2,1,0:T(8,128)S(1)} %collective-permute-done.3, f32[10,128,128]{2,1,0:T(8,128)S(1)} %collective-permute-done.2, f32[10,128,128]{2,1,0:T(8,128)S(1)} %collective-permute-done.1, ...), kind=kLoop, calls=%fused_computation.16 | loop fusion | flops 753664 | bytes 1966085 | tf_op jit(solution)/shard_map/jit(_where)/select_n | solution.py:129
  123.2 3.0 %shard_map.82 = (f32[4,4,128,128]{3,2,1,0:T(8,128)}, f32[4,4,128]{2,1,0:T(4,128)}, f32[4,4,128]{2,1,0:T(4,128)}, f32[4,4,128]{2,1,0:T(4,128)}, f32[4,4,128]{2,1,0:T(4,128)}) custom-call(f32[4,4,128,128]{3,2,1,0:T(8,128)} %copy-done, f32[4,128,128]{2,1,0:T(8,128)} %copy-done.2, f32[4,128,128]{2,1,0:T(8,128)} %copy-done.1, ...), custom_call_target="tpu_custom_call" | custom-call | tf_op jit(solution)/shard_map/pallas_call | solution.py:211
  126.8 2.5 %collective-permute-start.5 = (f32[4,4,128]{2,1,0:T(4,128)S(1)}, f32[4,4,128]{2,1,0:T(4,128)S(1)}, u32[]{:S(2)}, u32[]{:S(2)}) collective-permute-start(f32[4,4,128]{2,1,0:T(4,128)S(1)} %bitcast.242), channel_id=1, source_target_pairs={{0,2},{2,0},{1,3},{3,1},{4,6},{6,4},{5,7},{7,5},{8,10},{10,8},{9,1... | collective-permute-start | bytes 24584 | tf_op jit(solution)/shard_map/ppermute | solution.py:152
  130.0 6.6 %collective-permute-start.6 = (f32[4,4,128]{2,1,0:T(4,128)S(1)}, f32[4,4,128]{2,1,0:T(4,128)S(1)}, u32[]{:S(2)}, u32[]{:S(2)}) collective-permute-start(f32[4,4,128]{2,1,0:T(4,128)S(1)} %bitcast.239), channel_id=1, source_target_pairs={{0,1},{1,0},{2,3},{3,2},{4,5},{5,4},{6,7},{7,6},{8,9},{9,8},{10,11... | collective-permute-start | bytes 24584 | tf_op jit(solution)/shard_map/ppermute | solution.py:152
  138.1 3.4 %shard_map.83 = f32[4,4,128,128]{3,2,1,0:T(8,128)} custom-call(f32[4,4,128,128]{3,2,1,0:T(8,128)} %get-tuple-element.10.c_ref, f32[4,4,128]{2,1,0:T(4,128)} %get-tuple-element.137.lx_ref, f32[4,4,128]{2,1,0:T(4,128)} %get-tuple-element.136.hx_ref, f32[4,4,128]{2,1,0:T(4,128)} %get-tuple-element.135.ly_ref, f32[4,4,128]{2,1,0:T(4,128)} %get-tuple-element.134.hy_ref), custom_call_target="tpu_custom_call" | custom-call | tf_op jit(solution)/shard_map/pallas_call | solution.py:217
  (63 shorter events, 26.8 us)
Async XLA Ops:
  8.3 17.0 %all-to-all-start = ((f32[32,1,320]{2,1,0:T(1,128)}), f32[32,1,320]{2,1,0:T(1,128)S(1)}, u32[]{:S(2)}, u32[]{:S(2)}) async-start(f32[32,1,320]{2,1,0:T(1,128)} %reshape.229), calls=%async_computation | async-start | bytes 98304 | tf_op jit(solution)/shard_map/all_to_all | solution.py:44
  20.9 10.7 %copy-start.1 = (f32[4,128,128]{2,1,0:T(8,128)}, f32[4,128,128]{2,1,0:T(8,128)S(1)}, u32[]{:S(2)}) copy-start(f32[4,128,128]{2,1,0:T(8,128)S(1)} %get-tuple-element.113.ri_ref) | copy-start | bytes 786436
  20.9 10.7 %copy-start.2 = (f32[4,128,128]{2,1,0:T(8,128)}, f32[4,128,128]{2,1,0:T(8,128)S(1)}, u32[]{:S(2)}) copy-start(f32[4,128,128]{2,1,0:T(8,128)S(1)} %get-tuple-element.114.rr_ref) | copy-start | bytes 786436
  33.7 38.5 %copy-start = (f32[4,4,128,128]{3,2,1,0:T(8,128)}, f32[4,4,128,128]{3,2,1,0:T(8,128)S(1)}, u32[]{:S(2)}) copy-start(f32[4,4,128,128]{3,2,1,0:T(8,128)S(1)} %bitcast_add_fusion.f_ref) | copy-start | bytes 3145732
  37.6 14.4 %collective-permute-start = (f32[10,128,128]{2,1,0:T(8,128)}, f32[10,128,128]{2,1,0:T(8,128)S(1)}, u32[]{:S(2)}, u32[]{:S(2)}) collective-permute-start(f32[10,128,128]{2,1,0:T(8,128)} %get-tuple-element.63), channel_id=1, source_target_pairs={{0,4},{4,0},{8,12},{12,8},{16,20},{20,16},{24,28},{28,24},{32,36},... | collective-permute-start | bytes 1966088 | tf_op jit(solution)/shard_map/ppermute | solution.py:77
  56.0 13.4 %collective-permute-start.1 = (f32[10,128,128]{2,1,0:T(8,128)}, f32[10,128,128]{2,1,0:T(8,128)S(1)}, u32[]{:S(2)}, u32[]{:S(2)}) collective-permute-start(f32[10,128,128]{2,1,0:T(8,128)} %get-tuple-element.51), channel_id=1, source_target_pairs={{0,8},{4,12},{8,0},{12,4},{16,24},{20,28},{24,16},{28,20},{32,40},... | collective-permute-start | bytes 1966088 | tf_op jit(solution)/shard_map/ppermute | solution.py:77
  73.6 14.0 %collective-permute-start.2 = (f32[10,128,128]{2,1,0:T(8,128)}, f32[10,128,128]{2,1,0:T(8,128)S(1)}, u32[]{:S(2)}, u32[]{:S(2)}) collective-permute-start(f32[10,128,128]{2,1,0:T(8,128)} %get-tuple-element.39), channel_id=1, source_target_pairs={{0,16},{4,20},{8,24},{12,28},{16,0},{20,4},{24,8},{28,12},{32,48},... | collective-permute-start | bytes 1966088 | tf_op jit(solution)/shard_map/ppermute | solution.py:77
  91.8 11.6 %collective-permute-start.3 = (f32[10,128,128]{2,1,0:T(8,128)}, f32[10,128,128]{2,1,0:T(8,128)S(1)}, u32[]{:S(2)}, u32[]{:S(2)}) collective-permute-start(f32[10,128,128]{2,1,0:T(8,128)} %get-tuple-element.27), channel_id=1, source_target_pairs={{0,32},{4,36},{8,40},{12,44},{16,48},{20,52},{24,56},{28,60},{32,0... | collective-permute-start | bytes 1966088 | tf_op jit(solution)/shard_map/ppermute | solution.py:77
  109.0 7.5 %collective-permute-start.4 = (f32[4,128,128]{2,1,0:T(8,128)}, f32[4,128,128]{2,1,0:T(8,128)S(1)}, u32[]{:S(2)}, u32[]{:S(2)}) collective-permute-start(f32[4,128,128]{2,1,0:T(8,128)} %pad_maximum_fusion), channel_id=1, source_target_pairs={{0,64},{4,68},{8,72},{12,76},{16,80},{20,84},{24,88},{28,92},{32,9... | collective-permute-start | bytes 786440 | tf_op jit(solution)/shard_map/ppermute | solution.py:77
  126.8 9.8 %collective-permute-start.5 = (f32[4,4,128]{2,1,0:T(4,128)S(1)}, f32[4,4,128]{2,1,0:T(4,128)S(1)}, u32[]{:S(2)}, u32[]{:S(2)}) collective-permute-start(f32[4,4,128]{2,1,0:T(4,128)S(1)} %bitcast.242), channel_id=1, source_target_pairs={{0,2},{2,0},{1,3},{3,1},{4,6},{6,4},{5,7},{7,5},{8,10},{10,8},{9,1... | collective-permute-start | bytes 24584 | tf_op jit(solution)/shard_map/ppermute | solution.py:152
  130.0 7.5 %collective-permute-start.6 = (f32[4,4,128]{2,1,0:T(4,128)S(1)}, f32[4,4,128]{2,1,0:T(4,128)S(1)}, u32[]{:S(2)}, u32[]{:S(2)}) collective-permute-start(f32[4,4,128]{2,1,0:T(4,128)S(1)} %bitcast.239), channel_id=1, source_target_pairs={{0,1},{1,0},{2,3},{3,2},{4,5},{5,4},{6,7},{7,6},{8,9},{9,8},{10,11... | collective-permute-start | bytes 24584 | tf_op jit(solution)/shard_map/ppermute | solution.py:152

commit v9 on v6

--- a/solution.py
+++ b/solution.py
@@ -96,7 +96,7 @@
     return levels
 
 
-def entering_states(down_b, up_b, levels):
+def entering_states(down_b, up_b, levels, defer_last=False):
     slab_count = lax.axis_size("slab")
     here = lax.axis_index("slab")
     shots = down_b[0].shape[0]
@@ -128,6 +128,8 @@
                 [jnp.where(lower, down_b[0], up_b[0]), jnp.where(lower, down_b[1], up_b[1])], axis=0
             )
             got = exchange(send, step)
+            if defer_last:
+                return before, after, got, below, above, lower
             pd = (got[:shots], got[shots:])
             pu = pd
         g_re, g_im = complex_times(below[0][None], below[1][None], *pd)
@@ -144,6 +146,8 @@
             down_b, up_b = new_down, new_up
         step *= 2
         level += 1
+    if defer_last:
+        return before, after, None, None, None, None
     return before, after
 
 
@@ -222,6 +226,93 @@
     )(combined, from_low_x, from_high_x, from_low_y, from_high_y)
 
 
+def last_sweep_kernel(flag_ref, f_ref, rr_ref, ri_ref, br_ref, bi_ref, ar_ref, ai_ref,
+                      lr_ref, li_ref, hr_ref, hi_ref, got_ref, c_ref, sx_ref, sy_ref):
+    layers = f_ref.shape[0]
+    shots = br_ref.shape[0]
+    lower = flag_ref[0] == 1
+    first_x = flag_ref[1] == 0
+    first_y = flag_ref[2] == 0
+    for s in range(shots):
+        p_re, p_im = got_ref[s], got_ref[shots + s]
+        g_re, g_im = complex_times(lr_ref[...], li_ref[...], p_re, p_im)
+        w_re = jnp.where(lower, br_ref[s], g_re + br_ref[s])
+        w_im = jnp.where(lower, bi_ref[s], g_im + bi_ref[s])
+        g_re, g_im = complex_times(hr_ref[...], hi_ref[...], p_re, p_im)
+        v_re = jnp.where(lower, g_re + ar_ref[s], ar_ref[s])
+        v_im = jnp.where(lower, g_im + ai_ref[s], ai_ref[s])
+        downs = []
+        for k in range(layers):
+            t_re, t_im = complex_times(rr_ref[k], ri_ref[k], w_re, w_im)
+            w_re, w_im = t_re + f_ref[k, 2 * s], t_im + f_ref[k, 2 * s + 1]
+            downs.append((w_re, w_im))
+        for k in range(layers - 1, -1, -1):
+            t_re, t_im = complex_times(rr_ref[k], ri_ref[k], v_re, v_im)
+            f_re, f_im = f_ref[k, 2 * s], f_ref[k, 2 * s + 1]
+            v_re, v_im = t_re + f_re, t_im + f_im
+            d_re, d_im = downs[k]
+            for part, plane in ((0, d_re + v_re - f_re), (1, d_im + v_im - f_im)):
+                c = 2 * s + part
+                c_ref[k, c] = plane
+                sx_ref[k, pl.ds(c, 1), :] = jnp.where(first_x, plane[-1:, :], plane[0:1, :])
+                flipped = jnp.transpose(plane)
+                sy_ref[k, pl.ds(c, 1), :] = jnp.where(first_y, flipped[-1:, :], flipped[0:1, :])
+
+
+def paired_stencil_kernel(flag_ref, c_ref, gx_ref, gy_ref, o_ref):
+    layers, components, width_x, width_y = c_ref.shape
+    rows = lax.broadcasted_iota(jnp.int32, (width_x, width_y), 0)
+    cols = lax.broadcasted_iota(jnp.int32, (width_x, width_y), 1)
+    first_x = flag_ref[1] == 0
+    first_y = flag_ref[2] == 0
+    for k in range(layers):
+        for c in range(components):
+            plane = c_ref[k, c]
+            edge_x = gx_ref[k, pl.ds(c, 1), :]
+            edge_y = gy_ref[k, pl.ds(c, 1), :]
+            none_x = jnp.zeros_like(edge_x)
+            none_y = jnp.zeros_like(edge_y)
+            low_x = jnp.broadcast_to(jnp.where(first_x, none_x, edge_x), (width_x, width_y))
+            high_x = jnp.broadcast_to(jnp.where(first_x, edge_x, none_x), (width_x, width_y))
+            low_y = jnp.transpose(
+                jnp.broadcast_to(jnp.where(first_y, none_y, edge_y), (width_y, width_x))
+            )
+            high_y = jnp.transpose(
+                jnp.broadcast_to(jnp.where(first_y, edge_y, none_y), (width_y, width_x))
+            )
+            next_x = jnp.where(rows == width_x - 1, high_x, pltpu.roll(plane, width_x - 1, 0))
+            prev_x = jnp.where(rows == 0, low_x, pltpu.roll(plane, 1, 0))
+            next_y = jnp.where(cols == width_y - 1, high_y, pltpu.roll(plane, width_y - 1, 1))
+            prev_y = jnp.where(cols == 0, low_y, pltpu.roll(plane, 1, 1))
+            neighbours = next_x + prev_x + next_y + prev_y
+            o_ref[k, c] = plane - 0.2 * (4.0 * plane - neighbours)
+
+
+def finish_paired(fields, rate_re, rate_im, before, after, got, below, above, lower):
+    layers, components, width_x, width_y = fields.shape
+    flags = jnp.stack(
+        [lower.astype(jnp.int32), lax.axis_index("px"), lax.axis_index("py")]
+    ).astype(jnp.int32)
+    smem = pl.BlockSpec(memory_space=pltpu.SMEM)
+    vmem = pl.BlockSpec(memory_space=pltpu.VMEM)
+    edge_x = jax.ShapeDtypeStruct((layers, components, width_y), jnp.float32)
+    edge_y = jax.ShapeDtypeStruct((layers, components, width_x), jnp.float32)
+    combined, send_x, send_y = pl.pallas_call(
+        last_sweep_kernel,
+        in_specs=[smem] + [vmem] * 12,
+        out_specs=(vmem, vmem, vmem),
+        out_shape=(jax.ShapeDtypeStruct(fields.shape, jnp.float32), edge_x, edge_y),
+    )(flags, fields, rate_re, rate_im, *before, *after, *below, *above, got)
+    got_x = lax.ppermute(send_x, "px", [(0, 1), (1, 0)])
+    got_y = lax.ppermute(send_y, "py", [(0, 1), (1, 0)])
+    return pl.pallas_call(
+        paired_stencil_kernel,
+        in_specs=[smem, vmem, vmem, vmem],
+        out_specs=vmem,
+        out_shape=jax.ShapeDtypeStruct(fields.shape, jnp.float32),
+    )(flags, combined, got_x, got_y)
+
+
 def shards(source, phase, attenuation, pml_level, recv_values, recv_slab, recv_lateral, recv_layer):
     layers, components, width_x, width_y = source.shape
     shot_count = components // 2
@@ -260,6 +351,9 @@
         state = (t_re + f_re[k], t_im + f_im[k])
         up[k] = state
 
+    if lax.axis_size("px") == 2 and lax.axis_size("py") == 2 and slab_count > 1:
+        parts = entering_states(down[layers - 1], up[0], levels, defer_last=True)
+        return finish_paired(forcing, rate_re, rate_im, *parts)
     (enter_re, enter_im), (below_re, below_im) = entering_states(down[layers - 1], up[0], levels)
 
     return finish(forcing, rate_re, rate_im, enter_re, enter_im, below_re, below_im)

time: 127 us -> 121 us (0.953)
  other arithmetic: 29.3 us -> 25.4 us
  waiting for transfers between devices: 47.2 us -> 44 us
    ppermute x9, waiting for transfers between devices: 42.9 us -> 39.3 us  [exchange(): return lax.ppermute(array, 'slab', [(i, i ^ step) for i in range(count)])]
    select_n x4 -> x0, other arithmetic: 2.61 us -> none  [the longest x2 1.4 us: edge_pair(): jnp.where(here == 0, last, first)]
  transfers between devices with their start and end apart: 12 -> 12, of which waited for: 8 -> 8; matrix products, arithmetic and copies ran while one was open for 11% -> 13% of each run, Pallas kernels for 0% -> 0%
where the time goes in v9:
time: 121 us; the launch traced here: 120 us
  waiting for transfers between devices  44 us (36%)
  starting transfers between devices  33.8 us (28%)
  other arithmetic  25.4 us (21%)
  Pallas kernels  6.59 us (5%)
  local copies, waits for them, and re-layouts  6.37 us (5%)
  matrix products  3.53 us (3%)
    ppermute x9, waiting for transfers between devices, exchange(): return lax.ppermute(array, 'slab', [(i, i ^ step) for i in range(count)])  39.3 us
    ppermute x9, starting transfers between devices, exchange(): return lax.ppermute(array, 'slab', [(i, i ^ step) for i in range(count)])  12.6 us
    ppermute x1, starting transfers between devices, finish_paired(): got_y = lax.ppermute(send_y, 'py', [(0, 1), (1, 0)])  10.5 us
    all_to_all x1, starting transfers between devices, inject_receivers(): lax.all_to_all(send_rows.reshape(components + 1, slab_count, capacity), '...  7.76 us
    all_to_all x1, waiting for transfers between devices, inject_receivers(): lax.all_to_all(send_rows.reshape(components + 1, slab_count, capacity), '...  3.6 us
    dot_general x1, matrix products, inject_receivers(): jnp.dot(pick_rows, spread.astype(jnp.bfloat16), preferred_element_type=jn...  3.53 us
    pallas_call x1, Pallas kernels, finish_paired(): pl.pallas_call(paired_stencil_kernel, in_specs=[smem, vmem, vmem, vmem],...  3.39 us
    add x4, other arithmetic, shards(): state = (t_re + f_re[k], t_im + f_im[k])  3.37 us
  transfers between devices with their start and end apart: 12, of which 8 were waited for; matrix products, arithmetic and copies ran while one was open for 13% of the time, Pallas kernels for 0%

profile of v9, /device:TPU:1, one launch (start us, length us, event | category | flops | bytes accessed | tf_op | source)
XLA Modules:
  0.0 120.3 jit_solution(2753770326354666962)
XLA Ops:
  0.0 0.8 convert_multiply_fusion
  0.8 2.0 %cosine_multiply_fusion = (f32[4,128,128]{2,1,0:T(8,128)S(1)}, f32[4,128,128]{2,1,0:T(8,128)S(1)}) fusion(f32[4,128,128]{2,1,0:T(8,128)} %param.9, f32[4,128,128]{2,1,0:T(8,128)} %param.10, f32[128,128]{1,0:T(8,128)S(1)} %convert_multiply_fusion), kind=kLoop, calls=%fused_computation.18 | loop fusion | flops 262144 | bytes 1114112 | tf_op jit(solution)/shard_map/mul | solution.py:324
  2.9 0.9 multiply_subtract_fusion.7
  3.8 2.1 %collective-permute-start = (f32[2,128,128]{2,1,0:T(8,128)S(1)}, f32[2,128,128]{2,1,0:T(8,128)S(1)}, u32[]{:S(2)}, u32[]{:S(2)}) collective-permute-start(f32[2,128,128]{2,1,0:T(8,128)S(1)} %pad_maximum_fusion.5), channel_id=1, source_target_pairs={{0,4},{4,0},{8,12},{12,8},{16,20},{20,16},{24,28},{28,24},{32,36},... | collective-permute-start | bytes 393224 | tf_op jit(solution)/shard_map/ppermute | solution.py:71
  6.6 1.2 reduce-window.6
  11.1 1.4 %collective-permute-start.1 = (f32[2,128,128]{2,1,0:T(8,128)S(1)}, f32[2,128,128]{2,1,0:T(8,128)S(1)}, u32[]{:S(2)}, u32[]{:S(2)}) collective-permute-start(f32[2,128,128]{2,1,0:T(8,128)S(1)} %pad_maximum_fusion.6), channel_id=1, source_target_pairs={{0,8},{4,12},{8,0},{12,4},{16,24},{20,28},{24,16},{28,20},{32,40},... | collective-permute-start | bytes 393224 | tf_op jit(solution)/shard_map/ppermute | solution.py:71
  13.2 2.0 %scatter_custom_fusion = f32[5,2048]{0,1:T(8,128)S(1)} fusion(s32[512]{0:T(512)S(1)} %bitcast.337, f32[512,5]{1,0:T(8,128)S(1)} %copy.36, f32[]{:T(128)} %constant.56.clone.1), kind=kCustom, calls=%fused_computation.14 | custom fusion | bytes 40964 | tf_op jit(solution)/shard_map/scatter | solution.py:35
  16.2 7.8 %all-to-all-start = ((f32[32,1,320]{2,1,0:T(1,128)}), f32[32,1,320]{2,1,0:T(1,128)S(1)}, u32[]{:S(2)}, u32[]{:S(2)}) async-start(f32[32,1,320]{2,1,0:T(1,128)} %reshape.215), calls=%async_computation | async-start | bytes 98304 | tf_op jit(solution)/shard_map/all_to_all | solution.py:37
  24.7 2.8 %collective-permute-start.2 = (f32[2,128,128]{2,1,0:T(8,128)S(1)}, f32[2,128,128]{2,1,0:T(8,128)S(1)}, u32[]{:S(2)}, u32[]{:S(2)}) collective-permute-start(f32[2,128,128]{2,1,0:T(8,128)S(1)} %pad_maximum_fusion.7), channel_id=1, source_target_pairs={{0,16},{4,20},{8,24},{12,28},{16,0},{20,4},{24,8},{28,12},{32,48},... | collective-permute-start | bytes 393224 | tf_op jit(solution)/shard_map/ppermute | solution.py:71
  27.6 3.6 %all-to-all-done = f32[32,1,320]{2,1,0:T(1,128)S(1)} async-done(((f32[32,1,320]{2,1,0:T(1,128)}), f32[32,1,320]{2,1,0:T(1,128)S(1)}, u32[]{:S(2)}, u32[]{:S(2)}) %all-to-all-start) | async-done | bytes 40992 | tf_op jit(solution)/shard_map/all_to_all | solution.py:37
  34.5 2.7 %collective-permute-done.3 = f32[2,128,128]{2,1,0:T(8,128)S(1)} collective-permute-done((f32[2,128,128]{2,1,0:T(8,128)S(1)}, f32[2,128,128]{2,1,0:T(8,128)S(1)}, u32[]{:S(2)}, u32[]{:S(2)}) %collective-permute-start.3) | collective-permute-done | bytes 131104 | tf_op jit(solution)/shard_map/ppermute | solution.py:71
  38.6 0.8 add_select_fusion.15
  40.4 0.9 select_convert_fusion
  41.4 3.5 %fusion.1 = f32[512,3,512]{2,0,1:T(8,128)S(1)} fusion(bf16[3,512,2048]{2,1,0:T(8,128)(2,1)S(1)} %bitcast.327, s32[2048]{0:T(1024)S(1)} %bitcast.336), kind=kOutput, calls=%fused_computation.4 | convolution fusion | flops 3222274048 | bytes 9445376 | tf_op jit(solution)/shard_map/dot_general | solution.py:62
  46.4 1.2 %add_add_fusion.5 = (f32[2,128,128]{2,1,0:T(8,128)S(1)}, f32[2,128,128]{2,1,0:T(8,128)S(1)}) fusion(f32[4,2,2,128,128]{4,3,2,1,0:T(8,128)S(1)} %bitcast.323, f32[128,128]{1,0:T(8,128)} %get-tuple-element.148, f32[128,128]{1,0:T(8,128)} %get-tuple-element.151), kind=kLoop, calls=%fused_computation.68 | loop fusion | flops 262144 | bytes 917504 | tf_op jit(solution)/shard_map/add | solution.py:344
  47.7 1.1 subtract_add_fusion.3
  48.7 1.0 subtract_add_fusion
  50.5 8.8 %collective-permute-done.4 = f32[8,128,128]{2,1,0:T(8,128)S(1)} collective-permute-done((f32[8,128,128]{2,1,0:T(8,128)S(1)}, f32[8,128,128]{2,1,0:T(8,128)S(1)}, u32[]{:S(2)}, u32[]{:S(2)}) %collective-permute-start.4) | collective-permute-done | bytes 524320 | tf_op jit(solution)/shard_map/ppermute | solution.py:71
  60.0 8.2 %collective-permute-done.5 = f32[8,128,128]{2,1,0:T(8,128)S(1)} collective-permute-done((f32[8,128,128]{2,1,0:T(8,128)S(1)}, f32[8,128,128]{2,1,0:T(8,128)S(1)}, u32[]{:S(2)}, u32[]{:S(2)}) %collective-permute-start.5) | collective-permute-done | bytes 524320 | tf_op jit(solution)/shard_map/ppermute | solution.py:71
  68.4 1.2 collective-permute-start.6
  69.6 9.9 %collective-permute-done.6 = f32[8,128,128]{2,1,0:T(8,128)S(1)} collective-permute-done((f32[8,128,128]{2,1,0:T(8,128)S(1)}, f32[8,128,128]{2,1,0:T(8,128)S(1)}, u32[]{:S(2)}, u32[]{:S(2)}) %collective-permute-start.6) | collective-permute-done | bytes 524320 | tf_op jit(solution)/shard_map/ppermute | solution.py:71
  79.7 0.8 pad_maximum_fusion.3
  80.5 0.9 collective-permute-start.7
  82.1 0.9 broadcast_select_fusion.6
  82.9 5.8 %collective-permute-done.7 = f32[8,128,128]{2,1,0:T(8,128)S(1)} collective-permute-done((f32[8,128,128]{2,1,0:T(8,128)}, f32[8,128,128]{2,1,0:T(8,128)S(1)}, u32[]{:S(2)}, u32[]{:S(2)}) %collective-permute-start.7) | collective-permute-done | bytes 524320 | tf_op jit(solution)/shard_map/ppermute | solution.py:71
  88.9 2.9 %collective-permute-start.8 = (f32[4,128,128]{2,1,0:T(8,128)S(1)}, f32[4,128,128]{2,1,0:T(8,128)}, u32[]{:S(2)}, u32[]{:S(2)}) collective-permute-start(f32[4,128,128]{2,1,0:T(8,128)S(1)} %pad_maximum_fusion.4), channel_id=1, source_target_pairs={{0,64},{4,68},{8,72},{12,76},{16,80},{20,84},{24,88},{28,92},{32,9... | collective-permute-start | bytes 786440 | tf_op jit(solution)/shard_map/ppermute | solution.py:71
  94.8 3.8 %collective-permute-done.8.got_ref = f32[4,128,128]{2,1,0:T(8,128)} collective-permute-done((f32[4,128,128]{2,1,0:T(8,128)S(1)}, f32[4,128,128]{2,1,0:T(8,128)}, u32[]{:S(2)}, u32[]{:S(2)}) %collective-permute-start.8) | collective-permute-done | bytes 262176 | tf_op jit(solution)/shard_map/ppermute | solution.py:71
  98.6 3.2 %shard_map.82 = (f32[4,4,128,128]{3,2,1,0:T(8,128)}, f32[4,4,128]{2,1,0:T(4,128)}, f32[4,4,128]{2,1,0:T(4,128)}) custom-call(s32[3]{0:T(128)} %pad_add_fusion.flag_ref, f32[4,4,128,128]{3,2,1,0:T(8,128)} %copy-done, f32[4,128,128]{2,1,0:T(8,128)} %copy-done.1, f32[4,128,128]{2,1,0:T(8,128)} %copy-done.2, f32[2,128,128]{2,1,0:T(8,128)} %add_select_fusion.9.br_ref, ...), custom_call_target="tpu_custom_call" | custom-call | tf_op jit(solution)/shard_map/pallas_call | solution.py:300
  101.8 3.0 %collective-permute-start.9 = (f32[4,4,128]{2,1,0:T(4,128)}, f32[4,4,128]{2,1,0:T(4,128)S(1)}, u32[]{:S(2)}, u32[]{:S(2)}) collective-permute-start(f32[4,4,128]{2,1,0:T(4,128)} %get-tuple-element.83), channel_id=1, source_target_pairs={{0,2},{2,0},{1,3},{3,1},{4,6},{6,4},{5,7},{7,5},{8,10},{10,8},{9,1... | collective-permute-start | bytes 24584 | tf_op jit(solution)/shard_map/ppermute | solution.py:306
  104.8 10.5 %collective-permute-start.10 = (f32[4,4,128]{2,1,0:T(4,128)}, f32[4,4,128]{2,1,0:T(4,128)S(1)}, u32[]{:S(2)}, u32[]{:S(2)}) collective-permute-start(f32[4,4,128]{2,1,0:T(4,128)} %get-tuple-element.84), channel_id=1, source_target_pairs={{0,1},{1,0},{2,3},{3,2},{4,5},{5,4},{6,7},{7,6},{8,9},{9,8},{10,11... | collective-permute-start | bytes 24584 | tf_op jit(solution)/shard_map/ppermute | solution.py:307
  115.3 1.0 collective-permute-done.10.gy_ref
  116.9 3.4 %shard_map.83 = f32[4,4,128,128]{3,2,1,0:T(8,128)} custom-call(s32[3]{0:T(128)} %pad_add_fusion.flag_ref, f32[4,4,128,128]{3,2,1,0:T(8,128)} %get-tuple-element.82.c_ref, f32[4,4,128]{2,1,0:T(4,128)} %copy-done.28, f32[4,4,128]{2,1,0:T(4,128)} %copy-done.29), custom_call_target="tpu_custom_call" | custom-call | tf_op jit(solution)/shard_map/pallas_call | solution.py:308
  (125 shorter events, 19.6 us)
Async XLA Ops:
  2.8 36.6 %copy-start.1 = (f32[4,128,128]{2,1,0:T(8,128)}, f32[4,128,128]{2,1,0:T(8,128)S(1)}, u32[]{:S(2)}) copy-start(f32[4,128,128]{2,1,0:T(8,128)S(1)} %get-tuple-element.136.rr_ref) | copy-start | bytes 786436
  2.8 36.6 %copy-start.2 = (f32[4,128,128]{2,1,0:T(8,128)}, f32[4,128,128]{2,1,0:T(8,128)S(1)}, u32[]{:S(2)}) copy-start(f32[4,128,128]{2,1,0:T(8,128)S(1)} %get-tuple-element.137.ri_ref) | copy-start | bytes 786436
  3.8 6.6 %collective-permute-start = (f32[2,128,128]{2,1,0:T(8,128)S(1)}, f32[2,128,128]{2,1,0:T(8,128)S(1)}, u32[]{:S(2)}, u32[]{:S(2)}) collective-permute-start(f32[2,128,128]{2,1,0:T(8,128)S(1)} %pad_maximum_fusion.5), channel_id=1, source_target_pairs={{0,4},{4,0},{8,12},{12,8},{16,20},{20,16},{24,28},{28,24},{32,36},... | collective-permute-start | bytes 393224 | tf_op jit(solution)/shard_map/ppermute | solution.py:71
  11.1 12.9 %collective-permute-start.1 = (f32[2,128,128]{2,1,0:T(8,128)S(1)}, f32[2,128,128]{2,1,0:T(8,128)S(1)}, u32[]{:S(2)}, u32[]{:S(2)}) collective-permute-start(f32[2,128,128]{2,1,0:T(8,128)S(1)} %pad_maximum_fusion.6), channel_id=1, source_target_pairs={{0,8},{4,12},{8,0},{12,4},{16,24},{20,28},{24,16},{28,20},{32,40},... | collective-permute-start | bytes 393224 | tf_op jit(solution)/shard_map/ppermute | solution.py:71
  16.2 14.9 %all-to-all-start = ((f32[32,1,320]{2,1,0:T(1,128)}), f32[32,1,320]{2,1,0:T(1,128)S(1)}, u32[]{:S(2)}, u32[]{:S(2)}) async-start(f32[32,1,320]{2,1,0:T(1,128)} %reshape.215), calls=%async_computation | async-start | bytes 98304 | tf_op jit(solution)/shard_map/all_to_all | solution.py:37
  24.7 7.9 %collective-permute-start.2 = (f32[2,128,128]{2,1,0:T(8,128)S(1)}, f32[2,128,128]{2,1,0:T(8,128)S(1)}, u32[]{:S(2)}, u32[]{:S(2)}) collective-permute-start(f32[2,128,128]{2,1,0:T(8,128)S(1)} %pad_maximum_fusion.7), channel_id=1, source_target_pairs={{0,16},{4,20},{8,24},{12,28},{16,0},{20,4},{24,8},{28,12},{32,48},... | collective-permute-start | bytes 393224 | tf_op jit(solution)/shard_map/ppermute | solution.py:71
  33.3 3.9 %collective-permute-start.3 = (f32[2,128,128]{2,1,0:T(8,128)S(1)}, f32[2,128,128]{2,1,0:T(8,128)S(1)}, u32[]{:S(2)}, u32[]{:S(2)}) collective-permute-start(f32[2,128,128]{2,1,0:T(8,128)S(1)} %pad_maximum_fusion.8), channel_id=1, source_target_pairs={{0,32},{4,36},{8,40},{12,44},{16,48},{20,52},{24,56},{28,60},{32,0... | collective-permute-start | bytes 393224 | tf_op jit(solution)/shard_map/ppermute | solution.py:71
  46.1 4.3 %copy-start.20 = (f32[128,128]{1,0:T(8,128)S(1)}, f32[128,128]{1,0:T(8,128)}, u32[]{:S(2)}) copy-start(f32[128,128]{1,0:T(8,128)} %get-tuple-element.52) | copy-start | bytes 196612
  46.2 13.8 %copy-start.18 = (f32[128,128]{1,0:T(8,128)S(1)}, f32[128,128]{1,0:T(8,128)}, u32[]{:S(2)}) copy-start(f32[128,128]{1,0:T(8,128)} %get-tuple-element.58) | copy-start | bytes 196612
  46.2 13.8 %copy-start.19 = (f32[128,128]{1,0:T(8,128)S(1)}, f32[128,128]{1,0:T(8,128)}, u32[]{:S(2)}) copy-start(f32[128,128]{1,0:T(8,128)} %get-tuple-element.56) | copy-start | bytes 196612
  46.2 13.8 %copy-start.22 = (f32[128,128]{1,0:T(8,128)S(1)}, f32[128,128]{1,0:T(8,128)}, u32[]{:S(2)}) copy-start(f32[128,128]{1,0:T(8,128)} %get-tuple-element.57) | copy-start | bytes 196612
  46.2 13.8 %copy-start.23 = (f32[128,128]{1,0:T(8,128)S(1)}, f32[128,128]{1,0:T(8,128)}, u32[]{:S(2)}) copy-start(f32[128,128]{1,0:T(8,128)} %get-tuple-element.55) | copy-start | bytes 196612
  46.4 22.0 %copy-start = (f32[4,4,128,128]{3,2,1,0:T(8,128)}, f32[4,4,128,128]{3,2,1,0:T(8,128)S(1)}, u32[]{:S(2)}) copy-start(f32[4,4,128,128]{3,2,1,0:T(8,128)S(1)} %bitcast_add_fusion.f_ref) | copy-start | bytes 3145732
  47.6 21.9 %copy-start.26 = (f32[128,128]{1,0:T(8,128)S(1)}, f32[128,128]{1,0:T(8,128)}, u32[]{:S(2)}) copy-start(f32[128,128]{1,0:T(8,128)} %get-tuple-element.63) | copy-start | bytes 196612
  47.6 21.9 %copy-start.27 = (f32[128,128]{1,0:T(8,128)S(1)}, f32[128,128]{1,0:T(8,128)}, u32[]{:S(2)}) copy-start(f32[128,128]{1,0:T(8,128)} %get-tuple-element.61) | copy-start | bytes 196612
  49.8 32.3 %copy-start.16 = (f32[128,128]{1,0:T(8,128)S(1)}, f32[128,128]{1,0:T(8,128)}, u32[]{:S(2)}) copy-start(f32[128,128]{1,0:T(8,128)} %get-tuple-element.81) | copy-start | bytes 196612
  49.8 32.3 %copy-start.17 = (f32[128,128]{1,0:T(8,128)S(1)}, f32[128,128]{1,0:T(8,128)}, u32[]{:S(2)}) copy-start(f32[128,128]{1,0:T(8,128)} %get-tuple-element.79) | copy-start | bytes 196612
  49.9 9.5 %collective-permute-start.4 = (f32[8,128,128]{2,1,0:T(8,128)S(1)}, f32[8,128,128]{2,1,0:T(8,128)S(1)}, u32[]{:S(2)}, u32[]{:S(2)}) collective-permute-start(f32[8,128,128]{2,1,0:T(8,128)S(1)} %pad_maximum_fusion), channel_id=1, source_target_pairs={{0,4},{4,0},{8,12},{12,8},{16,20},{20,16},{24,28},{28,24},{32,36},... | collective-permute-start | bytes 1572872 | tf_op jit(solution)/shard_map/ppermute | solution.py:71
  50.5 41.3 %copy-start.10 = (f32[128,128]{1,0:T(8,128)S(1)}, f32[128,128]{1,0:T(8,128)}, u32[]{:S(2)}) copy-start(f32[128,128]{1,0:T(8,128)} %get-tuple-element.69) | copy-start | bytes 196612
  50.5 41.3 %copy-start.11 = (f32[128,128]{1,0:T(8,128)S(1)}, f32[128,128]{1,0:T(8,128)}, u32[]{:S(2)}) copy-start(f32[128,128]{1,0:T(8,128)} %get-tuple-element.68) | copy-start | bytes 196612
  50.5 41.3 %copy-start.12 = (f32[128,128]{1,0:T(8,128)S(1)}, f32[128,128]{1,0:T(8,128)}, u32[]{:S(2)}) copy-start(f32[128,128]{1,0:T(8,128)} %get-tuple-element.71) | copy-start | bytes 196612
  50.5 41.3 %copy-start.13 = (f32[128,128]{1,0:T(8,128)S(1)}, f32[128,128]{1,0:T(8,128)}, u32[]{:S(2)}) copy-start(f32[128,128]{1,0:T(8,128)} %get-tuple-element.70) | copy-start | bytes 196612
  59.5 8.7 %collective-permute-start.5 = (f32[8,128,128]{2,1,0:T(8,128)S(1)}, f32[8,128,128]{2,1,0:T(8,128)S(1)}, u32[]{:S(2)}, u32[]{:S(2)}) collective-permute-start(f32[8,128,128]{2,1,0:T(8,128)S(1)} %pad_maximum_fusion.1), channel_id=1, source_target_pairs={{0,8},{4,12},{8,0},{12,4},{16,24},{20,28},{24,16},{28,20},{32,40},... | collective-permute-start | bytes 1572872 | tf_op jit(solution)/shard_map/ppermute | solution.py:71
  60.0 33.3 %copy-start.6 = (f32[128,128]{1,0:T(8,128)S(1)}, f32[128,128]{1,0:T(8,128)}, u32[]{:S(2)}) copy-start(f32[128,128]{1,0:T(8,128)} %get-tuple-element.59) | copy-start | bytes 196612
  60.0 33.3 %copy-start.7 = (f32[128,128]{1,0:T(8,128)S(1)}, f32[128,128]{1,0:T(8,128)}, u32[]{:S(2)}) copy-start(f32[128,128]{1,0:T(8,128)} %get-tuple-element.54) | copy-start | bytes 196612
  60.0 33.3 %copy-start.8 = (f32[128,128]{1,0:T(8,128)S(1)}, f32[128,128]{1,0:T(8,128)}, u32[]{:S(2)}) copy-start(f32[128,128]{1,0:T(8,128)} %get-tuple-element.53) | copy-start | bytes 196612
  60.0 33.3 %copy-start.9 = (f32[128,128]{1,0:T(8,128)S(1)}, f32[128,128]{1,0:T(8,128)}, u32[]{:S(2)}) copy-start(f32[128,128]{1,0:T(8,128)} %get-tuple-element.48) | copy-start | bytes 196612
  68.4 11.1 %collective-permute-start.6 = (f32[8,128,128]{2,1,0:T(8,128)S(1)}, f32[8,128,128]{2,1,0:T(8,128)S(1)}, u32[]{:S(2)}, u32[]{:S(2)}) collective-permute-start(f32[8,128,128]{2,1,0:T(8,128)S(1)} %pad_maximum_fusion.2), channel_id=1, source_target_pairs={{0,16},{4,20},{8,24},{12,28},{16,0},{20,4},{24,8},{28,12},{32,48},... | collective-permute-start | bytes 1572872 | tf_op jit(solution)/shard_map/ppermute | solution.py:71
  80.5 8.2 %collective-permute-start.7 = (f32[8,128,128]{2,1,0:T(8,128)}, f32[8,128,128]{2,1,0:T(8,128)S(1)}, u32[]{:S(2)}, u32[]{:S(2)}) collective-permute-start(f32[8,128,128]{2,1,0:T(8,128)} %pad_maximum_fusion.3), channel_id=1, source_target_pairs={{0,32},{4,36},{8,40},{12,44},{16,48},{20,52},{24,56},{28,60},{32,0... | collective-permute-start | bytes 1572872 | tf_op jit(solution)/shard_map/ppermute | solution.py:71
  88.9 9.7 %collective-permute-start.8 = (f32[4,128,128]{2,1,0:T(8,128)S(1)}, f32[4,128,128]{2,1,0:T(8,128)}, u32[]{:S(2)}, u32[]{:S(2)}) collective-permute-start(f32[4,128,128]{2,1,0:T(8,128)S(1)} %pad_maximum_fusion.4), channel_id=1, source_target_pairs={{0,64},{4,68},{8,72},{12,76},{16,80},{20,84},{24,88},{28,92},{32,9... | collective-permute-start | bytes 786440 | tf_op jit(solution)/shard_map/ppermute | solution.py:71
  101.8 13.4 %collective-permute-start.9 = (f32[4,4,128]{2,1,0:T(4,128)}, f32[4,4,128]{2,1,0:T(4,128)S(1)}, u32[]{:S(2)}, u32[]{:S(2)}) collective-permute-start(f32[4,4,128]{2,1,0:T(4,128)} %get-tuple-element.83), channel_id=1, source_target_pairs={{0,2},{2,0},{1,3},{3,1},{4,6},{6,4},{5,7},{7,5},{8,10},{10,8},{9,1... | collective-permute-start | bytes 24584 | tf_op jit(solution)/shard_map/ppermute | solution.py:306
  104.8 11.5 %collective-permute-start.10 = (f32[4,4,128]{2,1,0:T(4,128)}, f32[4,4,128]{2,1,0:T(4,128)S(1)}, u32[]{:S(2)}, u32[]{:S(2)}) collective-permute-start(f32[4,4,128]{2,1,0:T(4,128)} %get-tuple-element.84), channel_id=1, source_target_pairs={{0,1},{1,0},{2,3},{3,2},{4,5},{5,4},{6,7},{7,6},{8,9},{9,8},{10,11... | collective-permute-start | bytes 24584 | tf_op jit(solution)/shard_map/ppermute | solution.py:307
  (10 other events, 30.3 us)

commit v10 on v9

--- a/solution.py
+++ b/solution.py
@@ -25,23 +25,15 @@
     values = recv_values[0, 0]
     target_slab = recv_slab[0, 0, :, 0]
     position = recv_layer[0, 0] * plane_size + recv_lateral[0, 0]
-    one_hot = (target_slab[:, None] == jnp.arange(slab_count, dtype=jnp.int32)[None, :]).astype(
-        jnp.int32
-    )
-    ranking = jnp.sum((jnp.cumsum(one_hot, axis=0) - one_hot) * one_hot, axis=1)
+    order = jnp.arange(rows_here, dtype=jnp.int32)
+    same_before = (target_slab[:, None] == target_slab[None, :]) & (order[None, :] < order[:, None])
+    ranking = jnp.sum(same_before.astype(jnp.int32), axis=1)
     target_slot = target_slab * capacity + ranking
     rows = jnp.concatenate([values, position.astype(jnp.float32)[None, :]], axis=0)
     send_rows = (
         jnp.zeros((components + 1, slab_count * capacity), jnp.float32).at[:, target_slot].set(rows)
     )
-    got_rows = lax.all_to_all(
-        send_rows.reshape(components + 1, slab_count, capacity),
-        "slab",
-        split_axis=1,
-        concat_axis=1,
-        tiled=True,
-    ).reshape(components + 1, slab_count * capacity)
-    got_rows, levels = lax.optimization_barrier((got_rows, levels))
+    got_rows = lax.all_to_all(send_rows, "slab", split_axis=1, concat_axis=1, tiled=True)
     inject_values = got_rows[:components]
     inject_places = got_rows[components].astype(jnp.int32)
     row_of = inject_places // width_y

time: 121 us -> 103 us (0.85); the launches traced: 120 us -> 101 us
  other arithmetic: 25.4 us -> 15.8 us
  starting transfers between devices: 33.8 us -> 28.9 us
  waiting for transfers between devices: 44 us -> 40.2 us
    ppermute x1, starting transfers between devices: 10.5 us -> 6.53 us  [finish_paired(): got_y = lax.ppermute(send_y, 'py', [(0, 1), (1, 0)])]
    add x4, other arithmetic: 3.37 us -> 0.25 us  [shards(): state = (t_re + f_re[k], t_im + f_im[k])]
    ppermute x9, waiting for transfers between devices: 39.3 us -> 36.3 us  [exchange(): return lax.ppermute(array, 'slab', [(i, i ^ step) for i in range(count)])]
    sub x5 -> x4, other arithmetic: 2.92 us -> 0.14 us  [complex_times(): return (a_re * b_re - a_im * b_im, a_re * b_im + a_im * b_re)]
    ppermute x9, starting transfers between devices: 12.6 us -> 10.1 us  [exchange(): return lax.ppermute(array, 'slab', [(i, i ^ step) for i in range(count)])]
    all_to_all x1, starting transfers between devices: 7.76 us -> 9.81 us  [inject_receivers(): lax.all_to_all(send_rows, 'slab', split_axis=1, concat_axis=1, tiled=True)]
    select_n x7 -> x2, other arithmetic: 2.44 us -> 0.72 us  [block_products(): jnp.where(lower, grown_above[0], above[0])]
    another operation x3 -> x0, other arithmetic: 1.21 us -> none
  transfers between devices with their start and end apart: 12 -> 12, of which waited for: 8 -> 8; matrix products, arithmetic and copies ran while one was open for 13% -> 17% of each run, Pallas kernels for 0% -> 0%
where the time goes in v10:
time: 103 us; the launch traced here: 101 us
  waiting for transfers between devices  40.2 us (39%)
  starting transfers between devices  28.9 us (28%)
  other arithmetic  15.8 us (15%)
  Pallas kernels  6.56 us (6%)
  local copies, waits for them, and re-layouts  5.71 us (6%)
  matrix products  3.53 us (3%)
    ppermute x9, waiting for transfers between devices, exchange(): return lax.ppermute(array, 'slab', [(i, i ^ step) for i in range(count)])  36.3 us
    ppermute x9, starting transfers between devices, exchange(): return lax.ppermute(array, 'slab', [(i, i ^ step) for i in range(count)])  10.1 us
    all_to_all x1, starting transfers between devices, inject_receivers(): lax.all_to_all(send_rows, 'slab', split_axis=1, concat_axis=1, tiled=True)  9.81 us
    ppermute x1, starting transfers between devices, finish_paired(): got_y = lax.ppermute(send_y, 'py', [(0, 1), (1, 0)])  6.53 us
    dot_general x1, matrix products, inject_receivers(): jnp.dot(pick_rows, spread.astype(jnp.bfloat16), preferred_element_type=jn...  3.53 us
    pallas_call x1, Pallas kernels, finish_paired(): pl.pallas_call(paired_stencil_kernel, in_specs=[smem, vmem, vmem, vmem],...  3.39 us
    pallas_call x1, Pallas kernels, finish_paired(): pl.pallas_call(last_sweep_kernel, in_specs=[smem] + [vmem] * 12, out_spec...  3.16 us
    all_to_all x1, waiting for transfers between devices, inject_receivers(): lax.all_to_all(send_rows, 'slab', split_axis=1, concat_axis=1, tiled=True)  2.86 us
  transfers between devices with their start and end apart: 12, of which 8 were waited for; matrix products, arithmetic and copies ran while one was open for 17% of the time, Pallas kernels for 0%

profile of v10, /device:TPU:1, one launch (start us, length us, event | category | flops | bytes accessed | tf_op | source)
XLA Modules:
  0.0 101.1 jit_solution(5747315680661695820)
XLA Ops:
  0.0 1.0 convert_reduce_fusion
  3.3 2.0 %scatter_custom_fusion = f32[5,2048]{0,1:T(8,128)S(1)} fusion(s32[512]{0:T(512)S(1)} %bitcast.322, f32[512,5]{1,0:T(8,128)S(1)} %copy.45, f32[]{:T(128)} %constant.52.clone.1), kind=kCustom, calls=%fused_computation.17 | custom fusion | bytes 40964 | tf_op jit(solution)/shard_map/scatter | solution.py:34
  5.6 0.7 reshape.198
  6.4 9.8 %all-to-all-start = ((f32[32,1,320]{2,1,0:T(1,128)}), f32[32,1,320]{2,1,0:T(1,128)S(1)}, u32[]{:S(2)}, u32[]{:S(2)}) async-start(f32[32,1,320]{2,1,0:T(1,128)} %reshape.198), calls=%async_computation | async-start | bytes 98304 | tf_op jit(solution)/shard_map/all_to_all | solution.py:36
  16.2 0.8 convert_multiply_fusion
  17.0 2.0 %sine_multiply_fusion = (f32[4,128,128]{2,1,0:T(8,128)S(1)}, f32[4,128,128]{2,1,0:T(8,128)S(1)}) fusion(f32[4,128,128]{2,1,0:T(8,128)} %param.9, f32[4,128,128]{2,1,0:T(8,128)} %param.10, f32[128,128]{1,0:T(8,128)S(1)} %convert_multiply_fusion), kind=kLoop, calls=%fused_computation.20 | loop fusion | flops 262144 | bytes 1114112 | tf_op jit(solution)/shard_map/mul | solution.py:317
  19.2 1.3 %collective-permute-start.1 = (f32[2,128,128]{2,1,0:T(8,128)S(1)}, f32[2,128,128]{2,1,0:T(8,128)S(1)}, u32[]{:S(2)}, u32[]{:S(2)}) collective-permute-start(f32[2,128,128]{2,1,0:T(8,128)S(1)} %pad_maximum_fusion.5), channel_id=1, source_target_pairs={{0,4},{4,0},{8,12},{12,8},{16,20},{20,16},{24,28},{28,24},{32,36},... | collective-permute-start | bytes 393224 | tf_op jit(solution)/shard_map/ppermute | solution.py:63
  20.5 2.9 %all-to-all-done = f32[32,1,320]{2,1,0:T(1,128)S(1)} async-done(((f32[32,1,320]{2,1,0:T(1,128)}), f32[32,1,320]{2,1,0:T(1,128)S(1)}, u32[]{:S(2)}, u32[]{:S(2)}) %all-to-all-start) | async-done | bytes 40992 | tf_op jit(solution)/shard_map/all_to_all | solution.py:36
  23.9 0.8 reduce.4
  25.2 0.9 select_convert_fusion
  26.1 3.5 %fusion.1 = f32[512,3,512]{2,0,1:T(8,128)S(1)} fusion(bf16[3,512,2048]{2,1,0:T(8,128)(2,1)S(1)} %bitcast.306, s32[2048]{0:T(1024)S(1)} %get-tuple-element.117), kind=kOutput, calls=%fused_computation.4 | convolution fusion | flops 3222274048 | bytes 9445376 | tf_op jit(solution)/shard_map/dot_general | solution.py:54
  30.4 1.4 %bitcast_add_fusion.f_ref = f32[4,4,128,128]{3,2,1,0:T(8,128)S(1)} fusion(f32[4,4,128,128]{3,2,1,0:T(8,128)} %param.8, f32[4,128,4,128]{3,2,1,0:T(4,128)S(1)} %add.365), kind=kLoop, calls=%fused_computation.8 | loop fusion | flops 262144 | bytes 3145728 | tf_op jit(solution)/shard_map/add | solution.py:58
  33.7 2.9 %collective-permute-done.3 = f32[2,128,128]{2,1,0:T(8,128)S(1)} collective-permute-done((f32[2,128,128]{2,1,0:T(8,128)S(1)}, f32[2,128,128]{2,1,0:T(8,128)S(1)}, u32[]{:S(2)}, u32[]{:S(2)}) %collective-permute-start.3) | collective-permute-done | bytes 131104 | tf_op jit(solution)/shard_map/ppermute | solution.py:63
  36.7 0.9 collective-permute-start.5
  37.6 6.0 %collective-permute-done = f32[8,128,128]{2,1,0:T(8,128)S(1)} collective-permute-done((f32[8,128,128]{2,1,0:T(8,128)S(1)}, f32[8,128,128]{2,1,0:T(8,128)S(1)}, u32[]{:S(2)}, u32[]{:S(2)}) %collective-permute-start) | collective-permute-done | bytes 524320 | tf_op jit(solution)/shard_map/ppermute | solution.py:63
  43.7 0.8 collective-permute-start.2
  44.7 9.5 %collective-permute-done.2 = f32[8,128,128]{2,1,0:T(8,128)S(1)} collective-permute-done((f32[8,128,128]{2,1,0:T(8,128)S(1)}, f32[8,128,128]{2,1,0:T(8,128)S(1)}, u32[]{:S(2)}, u32[]{:S(2)}) %collective-permute-start.2) | collective-permute-done | bytes 524320 | tf_op jit(solution)/shard_map/ppermute | solution.py:63
  54.4 1.2 %collective-permute-start.4 = (f32[8,128,128]{2,1,0:T(8,128)S(1)}, f32[8,128,128]{2,1,0:T(8,128)S(1)}, u32[]{:S(2)}, u32[]{:S(2)}) collective-permute-start(f32[8,128,128]{2,1,0:T(8,128)S(1)} %pad_maximum_fusion.2), channel_id=1, source_target_pairs={{0,16},{4,20},{8,24},{12,28},{16,0},{20,4},{24,8},{28,12},{32,48},... | collective-permute-start | bytes 1572872 | tf_op jit(solution)/shard_map/ppermute | solution.py:63
  55.6 1.3 %collective-permute-start.7 = (f32[2,128,128]{2,1,0:T(8,128)S(1)}, f32[2,128,128]{2,1,0:T(8,128)S(1)}, u32[]{:S(2)}, u32[]{:S(2)}) collective-permute-start(f32[2,128,128]{2,1,0:T(8,128)S(1)} %pad_maximum_fusion.8), channel_id=1, source_target_pairs={{0,32},{4,36},{8,40},{12,44},{16,48},{20,52},{24,56},{28,60},{32,0... | collective-permute-start | bytes 393224 | tf_op jit(solution)/shard_map/ppermute | solution.py:63
  57.0 7.9 %collective-permute-done.4 = f32[8,128,128]{2,1,0:T(8,128)S(1)} collective-permute-done((f32[8,128,128]{2,1,0:T(8,128)S(1)}, f32[8,128,128]{2,1,0:T(8,128)S(1)}, u32[]{:S(2)}, u32[]{:S(2)}) %collective-permute-start.4) | collective-permute-done | bytes 524320 | tf_op jit(solution)/shard_map/ppermute | solution.py:63
  66.8 6.3 %collective-permute-done.6 = f32[8,128,128]{2,1,0:T(8,128)S(1)} collective-permute-done((f32[8,128,128]{2,1,0:T(8,128)S(1)}, f32[8,128,128]{2,1,0:T(8,128)S(1)}, u32[]{:S(2)}, u32[]{:S(2)}) %collective-permute-start.6) | collective-permute-done | bytes 524320 | tf_op jit(solution)/shard_map/ppermute | solution.py:63
  73.3 3.3 %collective-permute-start.8 = (f32[4,128,128]{2,1,0:T(8,128)S(1)}, f32[4,128,128]{2,1,0:T(8,128)S(1)}, u32[]{:S(2)}, u32[]{:S(2)}) collective-permute-start(f32[4,128,128]{2,1,0:T(8,128)S(1)} %pad_maximum_fusion.4), channel_id=1, source_target_pairs={{0,64},{4,68},{8,72},{12,76},{16,80},{20,84},{24,88},{28,92},{32,9... | collective-permute-start | bytes 786440 | tf_op jit(solution)/shard_map/ppermute | solution.py:63
  76.6 0.7 add_select_fusion.9.br_ref
  77.3 0.8 add_select_fusion.6.bi_ref
  78.1 0.7 add_select_fusion.3.ar_ref
  78.8 0.7 add_select_fusion.ai_ref
  79.6 3.6 %collective-permute-done.8.got_ref = f32[4,128,128]{2,1,0:T(8,128)S(1)} collective-permute-done((f32[4,128,128]{2,1,0:T(8,128)S(1)}, f32[4,128,128]{2,1,0:T(8,128)S(1)}, u32[]{:S(2)}, u32[]{:S(2)}) %collective-permute-start.8) | collective-permute-done | bytes 262176 | tf_op jit(solution)/shard_map/ppermute | solution.py:63
  83.9 3.2 %shard_map.82 = (f32[4,4,128,128]{3,2,1,0:T(8,128)}, f32[4,4,128]{2,1,0:T(4,128)}, f32[4,4,128]{2,1,0:T(4,128)}) custom-call(s32[3]{0:T(128)} %pad_add_fusion.flag_ref, f32[4,4,128,128]{3,2,1,0:T(8,128)} %copy-done, f32[4,128,128]{2,1,0:T(8,128)} %copy-done.2, f32[4,128,128]{2,1,0:T(8,128)} %copy-done.1, f32[2,128,128]{2,1,0:T(8,128)} %add_select_fusion.9.br_ref, ...), custom_call_target="tpu_custom_call" | custom-call | tf_op jit(solution)/shard_map/pallas_call | solution.py:292
  87.1 2.4 %collective-permute-start.9 = (f32[4,4,128]{2,1,0:T(4,128)}, f32[4,4,128]{2,1,0:T(4,128)S(1)}, u32[]{:S(2)}, u32[]{:S(2)}) collective-permute-start(f32[4,4,128]{2,1,0:T(4,128)} %get-tuple-element.9), channel_id=1, source_target_pairs={{0,2},{2,0},{1,3},{3,1},{4,6},{6,4},{5,7},{7,5},{8,10},{10,8},{9,1... | collective-permute-start | bytes 24584 | tf_op jit(solution)/shard_map/ppermute | solution.py:298
  89.5 6.5 %collective-permute-start.10 = (f32[4,4,128]{2,1,0:T(4,128)}, f32[4,4,128]{2,1,0:T(4,128)S(1)}, u32[]{:S(2)}, u32[]{:S(2)}) collective-permute-start(f32[4,4,128]{2,1,0:T(4,128)} %get-tuple-element.10), channel_id=1, source_target_pairs={{0,1},{1,0},{2,3},{3,2},{4,5},{5,4},{6,7},{7,6},{8,9},{9,8},{10,11... | collective-permute-start | bytes 24584 | tf_op jit(solution)/shard_map/ppermute | solution.py:299
  96.0 1.0 %collective-permute-done.10.gy_ref = f32[4,4,128]{2,1,0:T(4,128)S(1)} collective-permute-done((f32[4,4,128]{2,1,0:T(4,128)}, f32[4,4,128]{2,1,0:T(4,128)S(1)}, u32[]{:S(2)}, u32[]{:S(2)}) %collective-permute-start.10) | collective-permute-done | bytes 8224 | tf_op jit(solution)/shard_map/ppermute | solution.py:299
  97.7 3.4 %shard_map.83 = f32[4,4,128,128]{3,2,1,0:T(8,128)} custom-call(s32[3]{0:T(128)} %pad_add_fusion.flag_ref, f32[4,4,128,128]{3,2,1,0:T(8,128)} %get-tuple-element.8.c_ref, f32[4,4,128]{2,1,0:T(4,128)} %copy-done.4, f32[4,4,128]{2,1,0:T(4,128)} %copy-done.5), custom_call_target="tpu_custom_call" | custom-call | tf_op jit(solution)/shard_map/pallas_call | solution.py:300
  (68 shorter events, 10.3 us)
Async XLA Ops:
  6.4 17.0 %all-to-all-start = ((f32[32,1,320]{2,1,0:T(1,128)}), f32[32,1,320]{2,1,0:T(1,128)S(1)}, u32[]{:S(2)}, u32[]{:S(2)}) async-start(f32[32,1,320]{2,1,0:T(1,128)} %reshape.198), calls=%async_computation | async-start | bytes 98304 | tf_op jit(solution)/shard_map/all_to_all | solution.py:36
  19.0 10.7 %copy-start.1 = (f32[4,128,128]{2,1,0:T(8,128)}, f32[4,128,128]{2,1,0:T(8,128)S(1)}, u32[]{:S(2)}) copy-start(f32[4,128,128]{2,1,0:T(8,128)S(1)} %get-tuple-element.57.ri_ref) | copy-start | bytes 786436
  19.0 10.7 %copy-start.2 = (f32[4,128,128]{2,1,0:T(8,128)}, f32[4,128,128]{2,1,0:T(8,128)S(1)}, u32[]{:S(2)}) copy-start(f32[4,128,128]{2,1,0:T(8,128)S(1)} %get-tuple-element.58.rr_ref) | copy-start | bytes 786436
  19.2 13.5 %collective-permute-start.1 = (f32[2,128,128]{2,1,0:T(8,128)S(1)}, f32[2,128,128]{2,1,0:T(8,128)S(1)}, u32[]{:S(2)}, u32[]{:S(2)}) collective-permute-start(f32[2,128,128]{2,1,0:T(8,128)S(1)} %pad_maximum_fusion.5), channel_id=1, source_target_pairs={{0,4},{4,0},{8,12},{12,8},{16,20},{20,16},{24,28},{28,24},{32,36},... | collective-permute-start | bytes 393224 | tf_op jit(solution)/shard_map/ppermute | solution.py:63
  31.8 12.9 %copy-start = (f32[4,4,128,128]{3,2,1,0:T(8,128)}, f32[4,4,128,128]{3,2,1,0:T(8,128)S(1)}, u32[]{:S(2)}) copy-start(f32[4,4,128,128]{3,2,1,0:T(8,128)S(1)} %bitcast_add_fusion.f_ref) | copy-start | bytes 3145732
  32.1 11.4 %collective-permute-start = (f32[8,128,128]{2,1,0:T(8,128)S(1)}, f32[8,128,128]{2,1,0:T(8,128)S(1)}, u32[]{:S(2)}, u32[]{:S(2)}) collective-permute-start(f32[8,128,128]{2,1,0:T(8,128)S(1)} %pad_maximum_fusion), channel_id=1, source_target_pairs={{0,4},{4,0},{8,12},{12,8},{16,20},{20,16},{24,28},{28,24},{32,36},... | collective-permute-start | bytes 1572872 | tf_op jit(solution)/shard_map/ppermute | solution.py:63
  32.7 3.9 %collective-permute-start.3 = (f32[2,128,128]{2,1,0:T(8,128)S(1)}, f32[2,128,128]{2,1,0:T(8,128)S(1)}, u32[]{:S(2)}, u32[]{:S(2)}) collective-permute-start(f32[2,128,128]{2,1,0:T(8,128)S(1)} %pad_maximum_fusion.6), channel_id=1, source_target_pairs={{0,8},{4,12},{8,0},{12,4},{16,24},{20,28},{24,16},{28,20},{32,40},... | collective-permute-start | bytes 393224 | tf_op jit(solution)/shard_map/ppermute | solution.py:63
  36.7 7.9 %collective-permute-start.5 = (f32[2,128,128]{2,1,0:T(8,128)S(1)}, f32[2,128,128]{2,1,0:T(8,128)S(1)}, u32[]{:S(2)}, u32[]{:S(2)}) collective-permute-start(f32[2,128,128]{2,1,0:T(8,128)S(1)} %pad_maximum_fusion.7), channel_id=1, source_target_pairs={{0,16},{4,20},{8,24},{12,28},{16,0},{20,4},{24,8},{28,12},{32,48},... | collective-permute-start | bytes 393224 | tf_op jit(solution)/shard_map/ppermute | solution.py:63
  43.7 10.5 %collective-permute-start.2 = (f32[8,128,128]{2,1,0:T(8,128)S(1)}, f32[8,128,128]{2,1,0:T(8,128)S(1)}, u32[]{:S(2)}, u32[]{:S(2)}) collective-permute-start(f32[8,128,128]{2,1,0:T(8,128)S(1)} %pad_maximum_fusion.1), channel_id=1, source_target_pairs={{0,8},{4,12},{8,0},{12,4},{16,24},{20,28},{24,16},{28,20},{32,40},... | collective-permute-start | bytes 1572872 | tf_op jit(solution)/shard_map/ppermute | solution.py:63
  54.4 10.5 %collective-permute-start.4 = (f32[8,128,128]{2,1,0:T(8,128)S(1)}, f32[8,128,128]{2,1,0:T(8,128)S(1)}, u32[]{:S(2)}, u32[]{:S(2)}) collective-permute-start(f32[8,128,128]{2,1,0:T(8,128)S(1)} %pad_maximum_fusion.2), channel_id=1, source_target_pairs={{0,16},{4,20},{8,24},{12,28},{16,0},{20,4},{24,8},{28,12},{32,48},... | collective-permute-start | bytes 1572872 | tf_op jit(solution)/shard_map/ppermute | solution.py:63
  55.6 9.8 %collective-permute-start.7 = (f32[2,128,128]{2,1,0:T(8,128)S(1)}, f32[2,128,128]{2,1,0:T(8,128)S(1)}, u32[]{:S(2)}, u32[]{:S(2)}) collective-permute-start(f32[2,128,128]{2,1,0:T(8,128)S(1)} %pad_maximum_fusion.8), channel_id=1, source_target_pairs={{0,32},{4,36},{8,40},{12,44},{16,48},{20,52},{24,56},{28,60},{32,0... | collective-permute-start | bytes 393224 | tf_op jit(solution)/shard_map/ppermute | solution.py:63
  65.1 8.1 %collective-permute-start.6 = (f32[8,128,128]{2,1,0:T(8,128)S(1)}, f32[8,128,128]{2,1,0:T(8,128)S(1)}, u32[]{:S(2)}, u32[]{:S(2)}) collective-permute-start(f32[8,128,128]{2,1,0:T(8,128)S(1)} %pad_maximum_fusion.3), channel_id=1, source_target_pairs={{0,32},{4,36},{8,40},{12,44},{16,48},{20,52},{24,56},{28,60},{32,0... | collective-permute-start | bytes 1572872 | tf_op jit(solution)/shard_map/ppermute | solution.py:63
  73.3 9.8 %collective-permute-start.8 = (f32[4,128,128]{2,1,0:T(8,128)S(1)}, f32[4,128,128]{2,1,0:T(8,128)S(1)}, u32[]{:S(2)}, u32[]{:S(2)}) collective-permute-start(f32[4,128,128]{2,1,0:T(8,128)S(1)} %pad_maximum_fusion.4), channel_id=1, source_target_pairs={{0,64},{4,68},{8,72},{12,76},{16,80},{20,84},{24,88},{28,92},{32,9... | collective-permute-start | bytes 786440 | tf_op jit(solution)/shard_map/ppermute | solution.py:63
  83.2 0.7 copy-start.3
  87.1 9.0 %collective-permute-start.9 = (f32[4,4,128]{2,1,0:T(4,128)}, f32[4,4,128]{2,1,0:T(4,128)S(1)}, u32[]{:S(2)}, u32[]{:S(2)}) collective-permute-start(f32[4,4,128]{2,1,0:T(4,128)} %get-tuple-element.9), channel_id=1, source_target_pairs={{0,2},{2,0},{1,3},{3,1},{4,6},{6,4},{5,7},{7,5},{8,10},{10,8},{9,1... | collective-permute-start | bytes 24584 | tf_op jit(solution)/shard_map/ppermute | solution.py:298
  89.5 7.6 %collective-permute-start.10 = (f32[4,4,128]{2,1,0:T(4,128)}, f32[4,4,128]{2,1,0:T(4,128)S(1)}, u32[]{:S(2)}, u32[]{:S(2)}) collective-permute-start(f32[4,4,128]{2,1,0:T(4,128)} %get-tuple-element.10), channel_id=1, source_target_pairs={{0,1},{1,0},{2,3},{3,2},{4,5},{5,4},{6,7},{7,6},{8,9},{9,8},{10,11... | collective-permute-start | bytes 24584 | tf_op jit(solution)/shard_map/ppermute | solution.py:299
  96.0 1.0 %copy-start.4 = (f32[4,4,128]{2,1,0:T(4,128)}, f32[4,4,128]{2,1,0:T(4,128)S(1)}, u32[]{:S(2)}) copy-start(f32[4,4,128]{2,1,0:T(4,128)S(1)} %collective-permute-done.9.gx_ref) | copy-start | bytes 24580
  97.1 0.6 copy-start.5

commit v11 on v10

--- a/solution.py
+++ b/solution.py
@@ -43,17 +43,14 @@
     ).astype(jnp.bfloat16)
     pick_cols = col_of[:, None] == jnp.arange(width_y, dtype=jnp.int32)[None, :]
     high = lax.reduce_precision(inject_values, exponent_bits=8, mantissa_bits=7)
-    rest = inject_values - high
-    middle = lax.reduce_precision(rest, exponent_bits=8, mantissa_bits=7)
-    low = rest - middle
-    pieces = jnp.stack([high, middle, low], axis=0)
+    pieces = jnp.stack([high, inject_values - high], axis=0)
     spread = jnp.where(pick_cols[None, None, :, :], pieces[:, :, :, None], 0.0)
     spread = jnp.transpose(spread, (2, 0, 1, 3)).reshape(
-        slab_count * capacity, 3 * components * width_y
+        slab_count * capacity, 2 * components * width_y
     )
     added = jnp.dot(pick_rows, spread.astype(jnp.bfloat16), preferred_element_type=jnp.float32)
-    added = added.reshape(layers * width_x, 3, components * width_y)
-    added = (added[:, 0] + added[:, 1]) + added[:, 2]
+    added = added.reshape(layers * width_x, 2, components * width_y)
+    added = added[:, 0] + added[:, 1]
     added = jnp.transpose(added.reshape(layers, width_x, components, width_y), (0, 2, 1, 3))
     return source + added, levels
 
@@ -255,28 +252,23 @@
     layers, components, width_x, width_y = c_ref.shape
     rows = lax.broadcasted_iota(jnp.int32, (width_x, width_y), 0)
     cols = lax.broadcasted_iota(jnp.int32, (width_x, width_y), 1)
+    side_rows = lax.broadcasted_iota(jnp.int32, (width_y, width_x), 0)
     first_x = flag_ref[1] == 0
     first_y = flag_ref[2] == 0
     for k in range(layers):
         for c in range(components):
             plane = c_ref[k, c]
             edge_x = gx_ref[k, pl.ds(c, 1), :]
-            edge_y = gy_ref[k, pl.ds(c, 1), :]
+            edge_y = jnp.broadcast_to(gy_ref[k, pl.ds(c, 1), :], (width_y, width_x))
             none_x = jnp.zeros_like(edge_x)
-            none_y = jnp.zeros_like(edge_y)
             low_x = jnp.broadcast_to(jnp.where(first_x, none_x, edge_x), (width_x, width_y))
             high_x = jnp.broadcast_to(jnp.where(first_x, edge_x, none_x), (width_x, width_y))
-            low_y = jnp.transpose(
-                jnp.broadcast_to(jnp.where(first_y, none_y, edge_y), (width_y, width_x))
-            )
-            high_y = jnp.transpose(
-                jnp.broadcast_to(jnp.where(first_y, edge_y, none_y), (width_y, width_x))
-            )
+            side = jnp.where(side_rows == jnp.where(first_y, width_y - 1, 0), edge_y, 0.0)
             next_x = jnp.where(rows == width_x - 1, high_x, pltpu.roll(plane, width_x - 1, 0))
             prev_x = jnp.where(rows == 0, low_x, pltpu.roll(plane, 1, 0))
-            next_y = jnp.where(cols == width_y - 1, high_y, pltpu.roll(plane, width_y - 1, 1))
-            prev_y = jnp.where(cols == 0, low_y, pltpu.roll(plane, 1, 1))
-            neighbours = next_x + prev_x + next_y + prev_y
+            next_y = jnp.where(cols == width_y - 1, 0.0, pltpu.roll(plane, width_y - 1, 1))
+            prev_y = jnp.where(cols == 0, 0.0, pltpu.roll(plane, 1, 1))
+            neighbours = next_x + prev_x + next_y + prev_y + jnp.transpose(side)
             o_ref[k, c] = plane - 0.2 * (4.0 * plane - neighbours)
 
 

time: 103 us -> 101 us (0.981)
  matrix products: 3.53 us -> 2.36 us
    dot_general x1, matrix products: 3.53 us -> 2.36 us  [inject_receivers(): jnp.dot(pick_rows, spread.astype(jnp.bfloat16), preferred_element_type=jn...]
  transfers between devices with their start and end apart: 12 -> 12, of which waited for: 8 -> 8; matrix products, arithmetic and copies ran while one was open for 17% -> 16% of each run, Pallas kernels for 0% -> 0%
where the time goes in v11:
time: 101 us; the launch traced here: 99.4 us
  waiting for transfers between devices  40.2 us (40%)
  starting transfers between devices  28.9 us (29%)
  other arithmetic  15.4 us (15%)
  Pallas kernels  6.4 us (6%)
  local copies, waits for them, and re-layouts  5.71 us (6%)
  matrix products  2.36 us (2%)
    ppermute x9, waiting for transfers between devices, exchange(): return lax.ppermute(array, 'slab', [(i, i ^ step) for i in range(count)])  36.3 us
    ppermute x9, starting transfers between devices, exchange(): return lax.ppermute(array, 'slab', [(i, i ^ step) for i in range(count)])  10.1 us
    all_to_all x1, starting transfers between devices, inject_receivers(): lax.all_to_all(send_rows, 'slab', split_axis=1, concat_axis=1, tiled=True)  9.81 us
    ppermute x1, starting transfers between devices, finish_paired(): got_y = lax.ppermute(send_y, 'py', [(0, 1), (1, 0)])  6.58 us
    pallas_call x1, Pallas kernels, finish_paired(): pl.pallas_call(paired_stencil_kernel, in_specs=[smem, vmem, vmem, vmem],...  3.23 us
    pallas_call x1, Pallas kernels, finish_paired(): pl.pallas_call(last_sweep_kernel, in_specs=[smem] + [vmem] * 12, out_spec...  3.16 us
    all_to_all x1, waiting for transfers between devices, inject_receivers(): lax.all_to_all(send_rows, 'slab', split_axis=1, concat_axis=1, tiled=True)  2.86 us
    ppermute x1, starting transfers between devices, finish_paired(): got_x = lax.ppermute(send_x, 'px', [(0, 1), (1, 0)])  2.44 us
  transfers between devices with their start and end apart: 12, of which 8 were waited for; matrix products, arithmetic and copies ran while one was open for 16% of the time, Pallas kernels for 0%

profile of v11, /device:TPU:1, one launch (start us, length us, event | category | flops | bytes accessed | tf_op | source)
XLA Modules:
  0.0 99.4 jit_solution(7998143642216328104)
XLA Ops:
  0.0 1.0 %convert_reduce_fusion = s32[512]{0:T(512)S(1)} fusion(s32[512]{0:T(512)} %bitcast.319), kind=kLoop, calls=%fused_computation.9 | loop fusion | flops 1310208 | bytes 4096 | tf_op jit(solution)/shard_map/reduce_sum | solution.py:30
  3.3 2.0 %scatter_custom_fusion = f32[5,2048]{0,1:T(8,128)S(1)} fusion(s32[512]{0:T(512)S(1)} %bitcast.322, f32[512,5]{1,0:T(8,128)S(1)} %copy.45, f32[]{:T(128)} %constant.52.clone.1), kind=kCustom, calls=%fused_computation.16 | custom fusion | bytes 40964 | tf_op jit(solution)/shard_map/scatter | solution.py:34
  5.6 0.7 reshape.187
  6.4 9.8 %all-to-all-start = ((f32[32,1,320]{2,1,0:T(1,128)}), f32[32,1,320]{2,1,0:T(1,128)S(1)}, u32[]{:S(2)}, u32[]{:S(2)}) async-start(f32[32,1,320]{2,1,0:T(1,128)} %reshape.187), calls=%async_computation | async-start | bytes 98304 | tf_op jit(solution)/shard_map/all_to_all | solution.py:36
  16.2 0.8 convert_multiply_fusion
  17.0 2.0 %sine_multiply_fusion = (f32[4,128,128]{2,1,0:T(8,128)S(1)}, f32[4,128,128]{2,1,0:T(8,128)S(1)}) fusion(f32[4,128,128]{2,1,0:T(8,128)} %param.9, f32[4,128,128]{2,1,0:T(8,128)} %param.10, f32[128,128]{1,0:T(8,128)S(1)} %convert_multiply_fusion), kind=kLoop, calls=%fused_computation.19 | loop fusion | flops 262144 | bytes 1114112 | tf_op jit(solution)/shard_map/mul | solution.py:309
  19.2 1.3 %collective-permute-start.1 = (f32[2,128,128]{2,1,0:T(8,128)S(1)}, f32[2,128,128]{2,1,0:T(8,128)S(1)}, u32[]{:S(2)}, u32[]{:S(2)}) collective-permute-start(f32[2,128,128]{2,1,0:T(8,128)S(1)} %pad_maximum_fusion.5), channel_id=1, source_target_pairs={{0,4},{4,0},{8,12},{12,8},{16,20},{20,16},{24,28},{28,24},{32,36},... | collective-permute-start | bytes 393224 | tf_op jit(solution)/shard_map/ppermute | solution.py:60
  20.5 2.9 %all-to-all-done = f32[32,1,320]{2,1,0:T(1,128)S(1)} async-done(((f32[32,1,320]{2,1,0:T(1,128)}), f32[32,1,320]{2,1,0:T(1,128)S(1)}, u32[]{:S(2)}, u32[]{:S(2)}) %all-to-all-start) | async-done | bytes 40992 | tf_op jit(solution)/shard_map/all_to_all | solution.py:36
  23.9 0.8 reduce.4
  25.8 2.4 %fusion.1 = f32[512,2,512]{2,0,1:T(8,128)S(1)} fusion(bf16[2,512,2048]{2,1,0:T(8,128)(2,1)S(1)} %bitcast.306, s32[2048]{0:T(1024)S(1)} %get-tuple-element.116), kind=kOutput, calls=%fused_computation.4 | convolution fusion | flops 2148532224 | bytes 6299648 | tf_op jit(solution)/shard_map/dot_general | solution.py:51
  28.8 1.4 %bitcast_add_fusion.f_ref = f32[4,4,128,128]{3,2,1,0:T(8,128)S(1)} fusion(f32[4,4,128,128]{3,2,1,0:T(8,128)} %param.8, f32[4,128,4,128]{3,2,1,0:T(4,128)S(1)} %add.359), kind=kLoop, calls=%fused_computation.7 | loop fusion | flops 262144 | bytes 3145728 | tf_op jit(solution)/shard_map/add | solution.py:55
  32.1 2.9 %collective-permute-done.3 = f32[2,128,128]{2,1,0:T(8,128)S(1)} collective-permute-done((f32[2,128,128]{2,1,0:T(8,128)S(1)}, f32[2,128,128]{2,1,0:T(8,128)S(1)}, u32[]{:S(2)}, u32[]{:S(2)}) %collective-permute-start.3) | collective-permute-done | bytes 131104 | tf_op jit(solution)/shard_map/ppermute | solution.py:60
  35.0 0.9 collective-permute-start.5
  36.0 6.0 %collective-permute-done = f32[8,128,128]{2,1,0:T(8,128)S(1)} collective-permute-done((f32[8,128,128]{2,1,0:T(8,128)S(1)}, f32[8,128,128]{2,1,0:T(8,128)S(1)}, u32[]{:S(2)}, u32[]{:S(2)}) %collective-permute-start) | collective-permute-done | bytes 524320 | tf_op jit(solution)/shard_map/ppermute | solution.py:60
  42.1 0.8 collective-permute-start.2
  43.1 9.5 %collective-permute-done.2 = f32[8,128,128]{2,1,0:T(8,128)S(1)} collective-permute-done((f32[8,128,128]{2,1,0:T(8,128)S(1)}, f32[8,128,128]{2,1,0:T(8,128)S(1)}, u32[]{:S(2)}, u32[]{:S(2)}) %collective-permute-start.2) | collective-permute-done | bytes 524320 | tf_op jit(solution)/shard_map/ppermute | solution.py:60
  52.8 1.2 %collective-permute-start.4 = (f32[8,128,128]{2,1,0:T(8,128)S(1)}, f32[8,128,128]{2,1,0:T(8,128)S(1)}, u32[]{:S(2)}, u32[]{:S(2)}) collective-permute-start(f32[8,128,128]{2,1,0:T(8,128)S(1)} %pad_maximum_fusion.2), channel_id=1, source_target_pairs={{0,16},{4,20},{8,24},{12,28},{16,0},{20,4},{24,8},{28,12},{32,48},... | collective-permute-start | bytes 1572872 | tf_op jit(solution)/shard_map/ppermute | solution.py:60
  54.1 1.1 %collective-permute-start.7 = (f32[2,128,128]{2,1,0:T(8,128)S(1)}, f32[2,128,128]{2,1,0:T(8,128)S(1)}, u32[]{:S(2)}, u32[]{:S(2)}) collective-permute-start(f32[2,128,128]{2,1,0:T(8,128)S(1)} %pad_maximum_fusion.8), channel_id=1, source_target_pairs={{0,32},{4,36},{8,40},{12,44},{16,48},{20,52},{24,56},{28,60},{32,0... | collective-permute-start | bytes 393224 | tf_op jit(solution)/shard_map/ppermute | solution.py:60
  55.2 8.1 %collective-permute-done.4 = f32[8,128,128]{2,1,0:T(8,128)S(1)} collective-permute-done((f32[8,128,128]{2,1,0:T(8,128)S(1)}, f32[8,128,128]{2,1,0:T(8,128)S(1)}, u32[]{:S(2)}, u32[]{:S(2)}) %collective-permute-start.4) | collective-permute-done | bytes 524320 | tf_op jit(solution)/shard_map/ppermute | solution.py:60
  65.2 6.3 %collective-permute-done.6 = f32[8,128,128]{2,1,0:T(8,128)S(1)} collective-permute-done((f32[8,128,128]{2,1,0:T(8,128)S(1)}, f32[8,128,128]{2,1,0:T(8,128)S(1)}, u32[]{:S(2)}, u32[]{:S(2)}) %collective-permute-start.6) | collective-permute-done | bytes 524320 | tf_op jit(solution)/shard_map/ppermute | solution.py:60
  71.7 3.5 %collective-permute-start.8 = (f32[4,128,128]{2,1,0:T(8,128)S(1)}, f32[4,128,128]{2,1,0:T(8,128)S(1)}, u32[]{:S(2)}, u32[]{:S(2)}) collective-permute-start(f32[4,128,128]{2,1,0:T(8,128)S(1)} %pad_maximum_fusion.4), channel_id=1, source_target_pairs={{0,64},{4,68},{8,72},{12,76},{16,80},{20,84},{24,88},{28,92},{32,9... | collective-permute-start | bytes 786440 | tf_op jit(solution)/shard_map/ppermute | solution.py:60
  75.2 0.7 add_select_fusion.9.br_ref
  75.9 0.8 add_select_fusion.6.bi_ref
  76.7 0.7 add_select_fusion.3.ar_ref
  77.4 0.7 add_select_fusion.ai_ref
  78.1 3.4 %collective-permute-done.8.got_ref = f32[4,128,128]{2,1,0:T(8,128)S(1)} collective-permute-done((f32[4,128,128]{2,1,0:T(8,128)S(1)}, f32[4,128,128]{2,1,0:T(8,128)S(1)}, u32[]{:S(2)}, u32[]{:S(2)}) %collective-permute-start.8) | collective-permute-done | bytes 262176 | tf_op jit(solution)/shard_map/ppermute | solution.py:60
  81.6 0.7 copy-done.3
  82.3 3.2 %shard_map.82 = (f32[4,4,128,128]{3,2,1,0:T(8,128)}, f32[4,4,128]{2,1,0:T(4,128)}, f32[4,4,128]{2,1,0:T(4,128)}) custom-call(s32[3]{0:T(128)} %pad_add_fusion.flag_ref, f32[4,4,128,128]{3,2,1,0:T(8,128)} %copy-done, f32[4,128,128]{2,1,0:T(8,128)} %copy-done.2, f32[4,128,128]{2,1,0:T(8,128)} %copy-done.1, f32[2,128,128]{2,1,0:T(8,128)} %add_select_fusion.9.br_ref, ...), custom_call_target="tpu_custom_call" | custom-call | tf_op jit(solution)/shard_map/pallas_call | solution.py:284
  85.5 2.4 %collective-permute-start.9 = (f32[4,4,128]{2,1,0:T(4,128)}, f32[4,4,128]{2,1,0:T(4,128)S(1)}, u32[]{:S(2)}, u32[]{:S(2)}) collective-permute-start(f32[4,4,128]{2,1,0:T(4,128)} %get-tuple-element.9), channel_id=1, source_target_pairs={{0,2},{2,0},{1,3},{3,1},{4,6},{6,4},{5,7},{7,5},{8,10},{10,8},{9,1... | collective-permute-start | bytes 24584 | tf_op jit(solution)/shard_map/ppermute | solution.py:290
  87.9 6.6 %collective-permute-start.10 = (f32[4,4,128]{2,1,0:T(4,128)}, f32[4,4,128]{2,1,0:T(4,128)S(1)}, u32[]{:S(2)}, u32[]{:S(2)}) collective-permute-start(f32[4,4,128]{2,1,0:T(4,128)} %get-tuple-element.10), channel_id=1, source_target_pairs={{0,1},{1,0},{2,3},{3,2},{4,5},{5,4},{6,7},{7,6},{8,9},{9,8},{10,11... | collective-permute-start | bytes 24584 | tf_op jit(solution)/shard_map/ppermute | solution.py:291
  94.5 1.0 %collective-permute-done.10.gy_ref = f32[4,4,128]{2,1,0:T(4,128)S(1)} collective-permute-done((f32[4,4,128]{2,1,0:T(4,128)}, f32[4,4,128]{2,1,0:T(4,128)S(1)}, u32[]{:S(2)}, u32[]{:S(2)}) %collective-permute-start.10) | collective-permute-done | bytes 8224 | tf_op jit(solution)/shard_map/ppermute | solution.py:291
  96.1 3.2 %shard_map.83 = f32[4,4,128,128]{3,2,1,0:T(8,128)} custom-call(s32[3]{0:T(128)} %pad_add_fusion.flag_ref, f32[4,4,128,128]{3,2,1,0:T(8,128)} %get-tuple-element.8.c_ref, f32[4,4,128]{2,1,0:T(4,128)} %copy-done.4, f32[4,4,128]{2,1,0:T(4,128)} %copy-done.5), custom_call_target="tpu_custom_call" | custom-call | tf_op jit(solution)/shard_map/pallas_call | solution.py:292
  (68 shorter events, 10.0 us)
Async XLA Ops:
  6.4 17.0 %all-to-all-start = ((f32[32,1,320]{2,1,0:T(1,128)}), f32[32,1,320]{2,1,0:T(1,128)S(1)}, u32[]{:S(2)}, u32[]{:S(2)}) async-start(f32[32,1,320]{2,1,0:T(1,128)} %reshape.187), calls=%async_computation | async-start | bytes 98304 | tf_op jit(solution)/shard_map/all_to_all | solution.py:36
  19.0 9.2 %copy-start.1 = (f32[4,128,128]{2,1,0:T(8,128)}, f32[4,128,128]{2,1,0:T(8,128)S(1)}, u32[]{:S(2)}) copy-start(f32[4,128,128]{2,1,0:T(8,128)S(1)} %get-tuple-element.57.ri_ref) | copy-start | bytes 786436
  19.0 9.2 %copy-start.2 = (f32[4,128,128]{2,1,0:T(8,128)}, f32[4,128,128]{2,1,0:T(8,128)S(1)}, u32[]{:S(2)}) copy-start(f32[4,128,128]{2,1,0:T(8,128)S(1)} %get-tuple-element.58.rr_ref) | copy-start | bytes 786436
  19.2 11.9 %collective-permute-start.1 = (f32[2,128,128]{2,1,0:T(8,128)S(1)}, f32[2,128,128]{2,1,0:T(8,128)S(1)}, u32[]{:S(2)}, u32[]{:S(2)}) collective-permute-start(f32[2,128,128]{2,1,0:T(8,128)S(1)} %pad_maximum_fusion.5), channel_id=1, source_target_pairs={{0,4},{4,0},{8,12},{12,8},{16,20},{20,16},{24,28},{28,24},{32,36},... | collective-permute-start | bytes 393224 | tf_op jit(solution)/shard_map/ppermute | solution.py:60
  30.2 11.9 %copy-start = (f32[4,4,128,128]{3,2,1,0:T(8,128)}, f32[4,4,128,128]{3,2,1,0:T(8,128)S(1)}, u32[]{:S(2)}) copy-start(f32[4,4,128,128]{3,2,1,0:T(8,128)S(1)} %bitcast_add_fusion.f_ref) | copy-start | bytes 3145732
  30.5 11.4 %collective-permute-start = (f32[8,128,128]{2,1,0:T(8,128)S(1)}, f32[8,128,128]{2,1,0:T(8,128)S(1)}, u32[]{:S(2)}, u32[]{:S(2)}) collective-permute-start(f32[8,128,128]{2,1,0:T(8,128)S(1)} %pad_maximum_fusion), channel_id=1, source_target_pairs={{0,4},{4,0},{8,12},{12,8},{16,20},{20,16},{24,28},{28,24},{32,36},... | collective-permute-start | bytes 1572872 | tf_op jit(solution)/shard_map/ppermute | solution.py:60
  31.1 3.9 %collective-permute-start.3 = (f32[2,128,128]{2,1,0:T(8,128)S(1)}, f32[2,128,128]{2,1,0:T(8,128)S(1)}, u32[]{:S(2)}, u32[]{:S(2)}) collective-permute-start(f32[2,128,128]{2,1,0:T(8,128)S(1)} %pad_maximum_fusion.6), channel_id=1, source_target_pairs={{0,8},{4,12},{8,0},{12,4},{16,24},{20,28},{24,16},{28,20},{32,40},... | collective-permute-start | bytes 393224 | tf_op jit(solution)/shard_map/ppermute | solution.py:60
  35.0 8.0 %collective-permute-start.5 = (f32[2,128,128]{2,1,0:T(8,128)S(1)}, f32[2,128,128]{2,1,0:T(8,128)S(1)}, u32[]{:S(2)}, u32[]{:S(2)}) collective-permute-start(f32[2,128,128]{2,1,0:T(8,128)S(1)} %pad_maximum_fusion.7), channel_id=1, source_target_pairs={{0,16},{4,20},{8,24},{12,28},{16,0},{20,4},{24,8},{28,12},{32,48},... | collective-permute-start | bytes 393224 | tf_op jit(solution)/shard_map/ppermute | solution.py:60
  42.1 10.5 %collective-permute-start.2 = (f32[8,128,128]{2,1,0:T(8,128)S(1)}, f32[8,128,128]{2,1,0:T(8,128)S(1)}, u32[]{:S(2)}, u32[]{:S(2)}) collective-permute-start(f32[8,128,128]{2,1,0:T(8,128)S(1)} %pad_maximum_fusion.1), channel_id=1, source_target_pairs={{0,8},{4,12},{8,0},{12,4},{16,24},{20,28},{24,16},{28,20},{32,40},... | collective-permute-start | bytes 1572872 | tf_op jit(solution)/shard_map/ppermute | solution.py:60
  52.8 10.5 %collective-permute-start.4 = (f32[8,128,128]{2,1,0:T(8,128)S(1)}, f32[8,128,128]{2,1,0:T(8,128)S(1)}, u32[]{:S(2)}, u32[]{:S(2)}) collective-permute-start(f32[8,128,128]{2,1,0:T(8,128)S(1)} %pad_maximum_fusion.2), channel_id=1, source_target_pairs={{0,16},{4,20},{8,24},{12,28},{16,0},{20,4},{24,8},{28,12},{32,48},... | collective-permute-start | bytes 1572872 | tf_op jit(solution)/shard_map/ppermute | solution.py:60
  54.1 9.8 %collective-permute-start.7 = (f32[2,128,128]{2,1,0:T(8,128)S(1)}, f32[2,128,128]{2,1,0:T(8,128)S(1)}, u32[]{:S(2)}, u32[]{:S(2)}) collective-permute-start(f32[2,128,128]{2,1,0:T(8,128)S(1)} %pad_maximum_fusion.8), channel_id=1, source_target_pairs={{0,32},{4,36},{8,40},{12,44},{16,48},{20,52},{24,56},{28,60},{32,0... | collective-permute-start | bytes 393224 | tf_op jit(solution)/shard_map/ppermute | solution.py:60
  63.4 8.1 %collective-permute-start.6 = (f32[8,128,128]{2,1,0:T(8,128)S(1)}, f32[8,128,128]{2,1,0:T(8,128)S(1)}, u32[]{:S(2)}, u32[]{:S(2)}) collective-permute-start(f32[8,128,128]{2,1,0:T(8,128)S(1)} %pad_maximum_fusion.3), channel_id=1, source_target_pairs={{0,32},{4,36},{8,40},{12,44},{16,48},{20,52},{24,56},{28,60},{32,0... | collective-permute-start | bytes 1572872 | tf_op jit(solution)/shard_map/ppermute | solution.py:60
  71.7 9.9 %collective-permute-start.8 = (f32[4,128,128]{2,1,0:T(8,128)S(1)}, f32[4,128,128]{2,1,0:T(8,128)S(1)}, u32[]{:S(2)}, u32[]{:S(2)}) collective-permute-start(f32[4,128,128]{2,1,0:T(8,128)S(1)} %pad_maximum_fusion.4), channel_id=1, source_target_pairs={{0,64},{4,68},{8,72},{12,76},{16,80},{20,84},{24,88},{28,92},{32,9... | collective-permute-start | bytes 786440 | tf_op jit(solution)/shard_map/ppermute | solution.py:60
  81.6 0.7 copy-start.3
  85.5 9.0 %collective-permute-start.9 = (f32[4,4,128]{2,1,0:T(4,128)}, f32[4,4,128]{2,1,0:T(4,128)S(1)}, u32[]{:S(2)}, u32[]{:S(2)}) collective-permute-start(f32[4,4,128]{2,1,0:T(4,128)} %get-tuple-element.9), channel_id=1, source_target_pairs={{0,2},{2,0},{1,3},{3,1},{4,6},{6,4},{5,7},{7,5},{8,10},{10,8},{9,1... | collective-permute-start | bytes 24584 | tf_op jit(solution)/shard_map/ppermute | solution.py:290
  87.9 7.6 %collective-permute-start.10 = (f32[4,4,128]{2,1,0:T(4,128)}, f32[4,4,128]{2,1,0:T(4,128)S(1)}, u32[]{:S(2)}, u32[]{:S(2)}) collective-permute-start(f32[4,4,128]{2,1,0:T(4,128)} %get-tuple-element.10), channel_id=1, source_target_pairs={{0,1},{1,0},{2,3},{3,2},{4,5},{5,4},{6,7},{7,6},{8,9},{9,8},{10,11... | collective-permute-start | bytes 24584 | tf_op jit(solution)/shard_map/ppermute | solution.py:291
  94.5 1.0 %copy-start.4 = (f32[4,4,128]{2,1,0:T(4,128)}, f32[4,4,128]{2,1,0:T(4,128)S(1)}, u32[]{:S(2)}) copy-start(f32[4,4,128]{2,1,0:T(4,128)S(1)} %collective-permute-done.9.gx_ref) | copy-start | bytes 24580
  95.5 0.6 copy-start.5

commit v12 on v11

--- a/solution.py
+++ b/solution.py
@@ -215,61 +215,98 @@
     )(combined, from_low_x, from_high_x, from_low_y, from_high_y)
 
 
-def last_sweep_kernel(flag_ref, f_ref, rr_ref, ri_ref, br_ref, bi_ref, ar_ref, ai_ref,
-                      lr_ref, li_ref, hr_ref, hi_ref, got_ref, c_ref, sx_ref, sy_ref):
+def swept_values(flag_ref, f_ref, rr_ref, ri_ref, br_ref, bi_ref, ar_ref, ai_ref,
+                 lr_ref, li_ref, hr_ref, hi_ref, got_ref, cut, emit):
     layers = f_ref.shape[0]
     shots = br_ref.shape[0]
     lower = flag_ref[0] == 1
+    for s in range(shots):
+        p_re, p_im = cut(got_ref, s), cut(got_ref, shots + s)
+        g_re, g_im = complex_times(cut(lr_ref), cut(li_ref), p_re, p_im)
+        w_re = jnp.where(lower, cut(br_ref, s), g_re + cut(br_ref, s))
+        w_im = jnp.where(lower, cut(bi_ref, s), g_im + cut(bi_ref, s))
+        g_re, g_im = complex_times(cut(hr_ref), cut(hi_ref), p_re, p_im)
+        v_re = jnp.where(lower, g_re + cut(ar_ref, s), cut(ar_ref, s))
+        v_im = jnp.where(lower, g_im + cut(ai_ref, s), cut(ai_ref, s))
+        downs = []
+        for k in range(layers):
+            t_re, t_im = complex_times(cut(rr_ref, k), cut(ri_ref, k), w_re, w_im)
+            w_re, w_im = t_re + cut(f_ref, k, 2 * s), t_im + cut(f_ref, k, 2 * s + 1)
+            downs.append((w_re, w_im))
+        for k in range(layers - 1, -1, -1):
+            t_re, t_im = complex_times(cut(rr_ref, k), cut(ri_ref, k), v_re, v_im)
+            f_re, f_im = cut(f_ref, k, 2 * s), cut(f_ref, k, 2 * s + 1)
+            v_re, v_im = t_re + f_re, t_im + f_im
+            d_re, d_im = downs[k]
+            emit(k, 2 * s, d_re + v_re - f_re)
+            emit(k, 2 * s + 1, d_im + v_im - f_im)
+
+
+def edge_kernel(*refs):
+    ins, (sx_ref, sy_ref, side_ref) = refs[:13], refs[13:]
+    flag_ref = ins[0]
+    components = sx_ref.shape[1]
     first_x = flag_ref[1] == 0
     first_y = flag_ref[2] == 0
-    for s in range(shots):
-        p_re, p_im = got_ref[s], got_ref[shots + s]
-        g_re, g_im = complex_times(lr_ref[...], li_ref[...], p_re, p_im)
-        w_re = jnp.where(lower, br_ref[s], g_re + br_ref[s])
-        w_im = jnp.where(lower, bi_ref[s], g_im + bi_ref[s])
-        g_re, g_im = complex_times(hr_ref[...], hi_ref[...], p_re, p_im)
-        v_re = jnp.where(lower, g_re + ar_ref[s], ar_ref[s])
-        v_im = jnp.where(lower, g_im + ai_ref[s], ai_ref[s])
-        downs = []
-        for k in range(layers):
-            t_re, t_im = complex_times(rr_ref[k], ri_ref[k], w_re, w_im)
-            w_re, w_im = t_re + f_ref[k, 2 * s], t_im + f_ref[k, 2 * s + 1]
-            downs.append((w_re, w_im))
-        for k in range(layers - 1, -1, -1):
-            t_re, t_im = complex_times(rr_ref[k], ri_ref[k], v_re, v_im)
-            f_re, f_im = f_ref[k, 2 * s], f_ref[k, 2 * s + 1]
-            v_re, v_im = t_re + f_re, t_im + f_im
-            d_re, d_im = downs[k]
-            for part, plane in ((0, d_re + v_re - f_re), (1, d_im + v_im - f_im)):
-                c = 2 * s + part
-                c_ref[k, c] = plane
-                sx_ref[k, pl.ds(c, 1), :] = jnp.where(first_x, plane[-1:, :], plane[0:1, :])
-                flipped = jnp.transpose(plane)
-                sy_ref[k, pl.ds(c, 1), :] = jnp.where(first_y, flipped[-1:, :], flipped[0:1, :])
-
-
-def paired_stencil_kernel(flag_ref, c_ref, gx_ref, gy_ref, o_ref):
-    layers, components, width_x, width_y = c_ref.shape
+    found = {}
+
+    def keep(name):
+        def emit(k, c, value):
+            found[(name, k, c)] = value
+        return emit
+
+    for name, part in (("x0", (pl.ds(0, 1), slice(None))), ("x1", (pl.ds(-1 % 128, 1), slice(None))),
+                       ("y0", (slice(None), pl.ds(0, 1))), ("y1", (slice(None), pl.ds(-1 % 128, 1)))):
+        def cut(ref, *lead, part=part):
+            return ref[tuple(lead) + part]
+        swept_values(*ins, cut, keep(name))
+    side_ref[...] = jnp.zeros_like(side_ref)
+    layers = sx_ref.shape[0]
+    for k in range(layers):
+        for c in range(components):
+            sx_ref[k, pl.ds(c, 1), :] = jnp.where(first_x, found[("x1", k, c)], found[("x0", k, c)])
+            j = k * components + c
+            side_ref[:, pl.ds(j, 1)] = jnp.where(first_y, found[("y1", k, c)], found[("y0", k, c)])
+    flipped = jnp.transpose(side_ref[...])
+    for k in range(layers):
+        for c in range(components):
+            j = k * components + c
+            sy_ref[k, pl.ds(c, 1), :] = flipped[j : j + 1, :]
+
+
+def main_kernel(*refs):
+    ins, o_ref = refs[:13], refs[13]
+    width_x, width_y = o_ref.shape[2], o_ref.shape[3]
     rows = lax.broadcasted_iota(jnp.int32, (width_x, width_y), 0)
     cols = lax.broadcasted_iota(jnp.int32, (width_x, width_y), 1)
+
+    def cut(ref, *lead):
+        return ref[tuple(lead)]
+
+    def emit(k, c, plane):
+        next_x = jnp.where(rows == width_x - 1, 0.0, pltpu.roll(plane, width_x - 1, 0))
+        prev_x = jnp.where(rows == 0, 0.0, pltpu.roll(plane, 1, 0))
+        next_y = jnp.where(cols == width_y - 1, 0.0, pltpu.roll(plane, width_y - 1, 1))
+        prev_y = jnp.where(cols == 0, 0.0, pltpu.roll(plane, 1, 1))
+        neighbours = next_x + prev_x + next_y + prev_y
+        o_ref[k, c] = plane - 0.2 * (4.0 * plane - neighbours)
+
+    swept_values(*ins, cut, emit)
+
+
+def fix_kernel(flag_ref, base_ref, gx_ref, gy_ref, o_ref):
+    layers, components, width_x, width_y = base_ref.shape
+    rows = lax.broadcasted_iota(jnp.int32, (width_x, width_y), 0)
     side_rows = lax.broadcasted_iota(jnp.int32, (width_y, width_x), 0)
     first_x = flag_ref[1] == 0
     first_y = flag_ref[2] == 0
     for k in range(layers):
         for c in range(components):
-            plane = c_ref[k, c]
-            edge_x = gx_ref[k, pl.ds(c, 1), :]
+            edge_x = jnp.broadcast_to(gx_ref[k, pl.ds(c, 1), :], (width_x, width_y))
             edge_y = jnp.broadcast_to(gy_ref[k, pl.ds(c, 1), :], (width_y, width_x))
-            none_x = jnp.zeros_like(edge_x)
-            low_x = jnp.broadcast_to(jnp.where(first_x, none_x, edge_x), (width_x, width_y))
-            high_x = jnp.broadcast_to(jnp.where(first_x, edge_x, none_x), (width_x, width_y))
+            across = jnp.where(rows == jnp.where(first_x, width_x - 1, 0), edge_x, 0.0)
             side = jnp.where(side_rows == jnp.where(first_y, width_y - 1, 0), edge_y, 0.0)
-            next_x = jnp.where(rows == width_x - 1, high_x, pltpu.roll(plane, width_x - 1, 0))
-            prev_x = jnp.where(rows == 0, low_x, pltpu.roll(plane, 1, 0))
-            next_y = jnp.where(cols == width_y - 1, 0.0, pltpu.roll(plane, width_y - 1, 1))
-            prev_y = jnp.where(cols == 0, 0.0, pltpu.roll(plane, 1, 1))
-            neighbours = next_x + prev_x + next_y + prev_y + jnp.transpose(side)
-            o_ref[k, c] = plane - 0.2 * (4.0 * plane - neighbours)
+            o_ref[k, c] = base_ref[k, c] + 0.2 * (across + jnp.transpose(side))
 
 
 def finish_paired(fields, rate_re, rate_im, before, after, got, below, above, lower):
@@ -279,22 +316,31 @@
     ).astype(jnp.int32)
     smem = pl.BlockSpec(memory_space=pltpu.SMEM)
     vmem = pl.BlockSpec(memory_space=pltpu.VMEM)
+    operands = (flags, fields, rate_re, rate_im, *before, *after, *below, *above, got)
     edge_x = jax.ShapeDtypeStruct((layers, components, width_y), jnp.float32)
     edge_y = jax.ShapeDtypeStruct((layers, components, width_x), jnp.float32)
-    combined, send_x, send_y = pl.pallas_call(
-        last_sweep_kernel,
+    send_x, send_y = pl.pallas_call(
+        edge_kernel,
         in_specs=[smem] + [vmem] * 12,
-        out_specs=(vmem, vmem, vmem),
-        out_shape=(jax.ShapeDtypeStruct(fields.shape, jnp.float32), edge_x, edge_y),
-    )(flags, fields, rate_re, rate_im, *before, *after, *below, *above, got)
+        out_specs=(vmem, vmem),
+        out_shape=(edge_x, edge_y),
+        scratch_shapes=[pltpu.VMEM((width_x, width_y), jnp.float32)],
+    )(*operands)
     got_x = lax.ppermute(send_x, "px", [(0, 1), (1, 0)])
     got_y = lax.ppermute(send_y, "py", [(0, 1), (1, 0)])
+    base = pl.pallas_call(
+        main_kernel,
+        in_specs=[smem] + [vmem] * 12,
+        out_specs=vmem,
+        out_shape=jax.ShapeDtypeStruct(fields.shape, jnp.float32),
+    )(*operands)
     return pl.pallas_call(
-        paired_stencil_kernel,
+        fix_kernel,
         in_specs=[smem, vmem, vmem, vmem],
         out_specs=vmem,
         out_shape=jax.ShapeDtypeStruct(fields.shape, jnp.float32),
-    )(flags, combined, got_x, got_y)
+        input_output_aliases={1: 0},
+    )(flags, base, got_x, got_y)
 
 
 def shards(source, phase, attenuation, pml_level, recv_values, recv_slab, recv_lateral, recv_layer):

time: 101 us -> 105 us (1.040)
  waiting for transfers between devices: 40.2 us -> 35.9 us
  Pallas kernels: 6.4 us -> 9.96 us
  starting transfers between devices: 28.9 us -> 31.6 us
  other arithmetic: 15.4 us -> 16.9 us
  local copies, waits for them, and re-layouts: 5.71 us -> 6.96 us
    ppermute x9, starting transfers between devices: 10.1 us -> 14.9 us  [exchange(): return lax.ppermute(array, 'slab', [(i, i ^ step) for i in range(count)])]
    pallas_call x2 -> x3, Pallas kernels: 6.4 us -> 9.96 us  [the longest x1 3.78 us: finish_paired(): pl.pallas_call(edge_kernel, in_specs=[smem] + [vmem] * 12, out_specs=(vme...]
    ppermute x1, starting transfers between devices: 6.58 us -> 4.48 us  [finish_paired(): got_y = lax.ppermute(send_y, 'py', [(0, 1), (1, 0)])]
    ppermute x9, waiting for transfers between devices: 36.3 us -> 34.3 us  [exchange(): return lax.ppermute(array, 'slab', [(i, i ^ step) for i in range(count)])]
    all_to_all x1, waiting for transfers between devices: 2.86 us -> 1.5 us  [inject_receivers(): lax.all_to_all(send_rows, 'slab', split_axis=1, concat_axis=1, tiled=True)]
    add x4, other arithmetic: 0.25 us -> 1.5 us  [shards(): state = (t_re + f_re[k], t_im + f_im[k])]
    unnamed x14 -> x28, local copies, waits for them, and re-layouts: 2.16 us -> 3.36 us
    add x1, other arithmetic: 1.36 us -> 0.16 us  [inject_receivers(): return (source + added, levels)]
  transfers between devices with their start and end apart: 12 -> 12, of which waited for: 8 -> 7; matrix products, arithmetic and copies ran while one was open for 16% -> 16% of each run, Pallas kernels for 0% -> 3%
where the time goes in v12:
time: 105 us; the launch traced here: 104 us
  waiting for transfers between devices  35.9 us (34%)
  starting transfers between devices  31.6 us (30%)
  other arithmetic  16.9 us (16%)
  Pallas kernels  9.96 us (9%)
  local copies, waits for them, and re-layouts  6.96 us (7%)
  matrix products  2.36 us (2%)
    ppermute x9, waiting for transfers between devices, exchange(): return lax.ppermute(array, 'slab', [(i, i ^ step) for i in range(count)])  34.3 us
    ppermute x9, starting transfers between devices, exchange(): return lax.ppermute(array, 'slab', [(i, i ^ step) for i in range(count)])  14.9 us
    all_to_all x1, starting transfers between devices, inject_receivers(): lax.all_to_all(send_rows, 'slab', split_axis=1, concat_axis=1, tiled=True)  9.81 us
    ppermute x1, starting transfers between devices, finish_paired(): got_y = lax.ppermute(send_y, 'py', [(0, 1), (1, 0)])  4.48 us
    pallas_call x1, Pallas kernels, finish_paired(): pl.pallas_call(edge_kernel, in_specs=[smem] + [vmem] * 12, out_specs=(vme...  3.78 us
    pallas_call x1, Pallas kernels, finish_paired(): pl.pallas_call(main_kernel, in_specs=[smem] + [vmem] * 12, out_specs=vmem...  3.62 us
    unnamed x28, local copies, waits for them, and re-layouts  3.36 us
    pallas_call x1, Pallas kernels, finish_paired(): pl.pallas_call(fix_kernel, in_specs=[smem, vmem, vmem, vmem], out_specs=v...  2.57 us
  transfers between devices with their start and end apart: 12, of which 7 were waited for; matrix products, arithmetic and copies ran while one was open for 16% of the time, Pallas kernels for 3%

profile of v12, /device:TPU:1, one launch (start us, length us, event | category | flops | bytes accessed | tf_op | source)
XLA Modules:
  0.0 104.0 jit_solution(12107878671932958614)
XLA Ops:
  0.0 1.0 convert_reduce_fusion
  3.3 2.0 %scatter_custom_fusion = f32[5,2048]{0,1:T(8,128)S(1)} fusion(s32[512]{0:T(512)S(1)} %bitcast.322, f32[512,5]{1,0:T(8,128)S(1)} %copy.46, f32[]{:T(128)} %constant.52.clone.1), kind=kCustom, calls=%fused_computation.16 | custom fusion | bytes 40964 | tf_op jit(solution)/shard_map/scatter | solution.py:34
  5.6 0.7 reshape.187
  6.4 9.8 %all-to-all-start = ((f32[32,1,320]{2,1,0:T(1,128)}), f32[32,1,320]{2,1,0:T(1,128)S(1)}, u32[]{:S(2)}, u32[]{:S(2)}) async-start(f32[32,1,320]{2,1,0:T(1,128)} %reshape.187), calls=%async_computation | async-start | bytes 98304 | tf_op jit(solution)/shard_map/all_to_all | solution.py:36
  16.2 0.8 convert_multiply_fusion
  17.0 2.0 %sine_multiply_fusion = (f32[4,128,128]{2,1,0:T(8,128)S(1)}, f32[4,128,128]{2,1,0:T(8,128)S(1)}) fusion(f32[4,128,128]{2,1,0:T(8,128)} %param.9, f32[4,128,128]{2,1,0:T(8,128)} %param.10, f32[128,128]{1,0:T(8,128)S(1)} %convert_multiply_fusion), kind=kLoop, calls=%fused_computation.19 | loop fusion | flops 262144 | bytes 1114112 | tf_op jit(solution)/shard_map/mul | solution.py:355
  19.1 0.8 multiply_add_fusion.4
  20.6 1.2 %collective-permute-start.1 = (f32[2,128,128]{2,1,0:T(8,128)}, f32[2,128,128]{2,1,0:T(8,128)S(1)}, u32[]{:S(2)}, u32[]{:S(2)}) collective-permute-start(f32[2,128,128]{2,1,0:T(8,128)} %pad_maximum_fusion.5), channel_id=1, source_target_pairs={{0,4},{4,0},{8,12},{12,8},{16,20},{20,16},{24,28},{28,24},{32,36},... | collective-permute-start | bytes 393224 | tf_op jit(solution)/shard_map/ppermute | solution.py:60
  21.8 1.5 %all-to-all-done = f32[32,1,320]{2,1,0:T(1,128)S(1)} async-done(((f32[32,1,320]{2,1,0:T(1,128)}), f32[32,1,320]{2,1,0:T(1,128)S(1)}, u32[]{:S(2)}, u32[]{:S(2)}) %all-to-all-start) | async-done | bytes 40992 | tf_op jit(solution)/shard_map/all_to_all | solution.py:36
  23.9 0.7 reduce.4
  25.9 2.4 %fusion.1 = f32[512,2,512]{2,0,1:T(8,128)S(1)} fusion(bf16[2,512,2048]{2,1,0:T(8,128)(2,1)S(1)} %bitcast.306, s32[2048]{0:T(1024)S(1)} %get-tuple-element.114), kind=kOutput, calls=%fused_computation.4 | convolution fusion | flops 2148532224 | bytes 6299648 | tf_op jit(solution)/shard_map/dot_general | solution.py:51
  29.7 1.3 %subtract_add_fusion.3 = (f32[2,128,128]{2,1,0:T(8,128)S(1)}, f32[2,128,128]{2,1,0:T(8,128)S(1)}, f32[2,128,128]{2,1,0:T(8,128)S(1)}, f32[2,128,128]{2,1,0:T(8,128)S(1)}, f32[2,128,128]{2,1,0:T(8,128)S(1)}) fusion(f32[4,2,2,128,128]{4,3,2,1,0:T(8,128)S(1)} %bitcast.303, f32[128,128]{1,0:T(8,128)} %get-tuple-element.83, f32[128,128]{1,0:T(8,128)} %get-tuple-element.81, ...), kind=kLoop, calls=%fused_computation.67 | loop fusion | flops 655360 | bytes 1703936 | tf_op jit(solution)/shard_map/add | solution.py:374
  32.8 2.9 %collective-permute-done.3 = f32[2,128,128]{2,1,0:T(8,128)S(1)} collective-permute-done((f32[2,128,128]{2,1,0:T(8,128)S(1)}, f32[2,128,128]{2,1,0:T(8,128)S(1)}, u32[]{:S(2)}, u32[]{:S(2)}) %collective-permute-start.3) | collective-permute-done | bytes 131104 | tf_op jit(solution)/shard_map/ppermute | solution.py:60
  35.8 1.1 %collective-permute-start.5 = (f32[2,128,128]{2,1,0:T(8,128)S(1)}, f32[2,128,128]{2,1,0:T(8,128)S(1)}, u32[]{:S(2)}, u32[]{:S(2)}) collective-permute-start(f32[2,128,128]{2,1,0:T(8,128)S(1)} %pad_maximum_fusion.7), channel_id=1, source_target_pairs={{0,16},{4,20},{8,24},{12,28},{16,0},{20,4},{24,8},{28,12},{32,48},... | collective-permute-start | bytes 393224 | tf_op jit(solution)/shard_map/ppermute | solution.py:60
  36.9 5.8 %collective-permute-done = f32[8,128,128]{2,1,0:T(8,128)S(1)} collective-permute-done((f32[8,128,128]{2,1,0:T(8,128)S(1)}, f32[8,128,128]{2,1,0:T(8,128)S(1)}, u32[]{:S(2)}, u32[]{:S(2)}) %collective-permute-start) | collective-permute-done | bytes 524320 | tf_op jit(solution)/shard_map/ppermute | solution.py:60
  42.9 0.8 collective-permute-start.2
  43.8 9.5 %collective-permute-done.2 = f32[8,128,128]{2,1,0:T(8,128)S(1)} collective-permute-done((f32[8,128,128]{2,1,0:T(8,128)S(1)}, f32[8,128,128]{2,1,0:T(8,128)S(1)}, u32[]{:S(2)}, u32[]{:S(2)}) %collective-permute-start.2) | collective-permute-done | bytes 524320 | tf_op jit(solution)/shard_map/ppermute | solution.py:60
  53.5 1.5 %collective-permute-start.4 = (f32[8,128,128]{2,1,0:T(8,128)S(1)}, f32[8,128,128]{2,1,0:T(8,128)S(1)}, u32[]{:S(2)}, u32[]{:S(2)}) collective-permute-start(f32[8,128,128]{2,1,0:T(8,128)S(1)} %pad_maximum_fusion.2), channel_id=1, source_target_pairs={{0,16},{4,20},{8,24},{12,28},{16,0},{20,4},{24,8},{28,12},{32,48},... | collective-permute-start | bytes 1572872 | tf_op jit(solution)/shard_map/ppermute | solution.py:60
  55.1 2.2 %collective-permute-start.7 = (f32[2,128,128]{2,1,0:T(8,128)S(1)}, f32[2,128,128]{2,1,0:T(8,128)S(1)}, u32[]{:S(2)}, u32[]{:S(2)}) collective-permute-start(f32[2,128,128]{2,1,0:T(8,128)S(1)} %pad_maximum_fusion.8), channel_id=1, source_target_pairs={{0,32},{4,36},{8,40},{12,44},{16,48},{20,52},{24,56},{28,60},{32,0... | collective-permute-start | bytes 393224 | tf_op jit(solution)/shard_map/ppermute | solution.py:60
  57.3 6.8 %collective-permute-done.4 = f32[8,128,128]{2,1,0:T(8,128)S(1)} collective-permute-done((f32[8,128,128]{2,1,0:T(8,128)S(1)}, f32[8,128,128]{2,1,0:T(8,128)S(1)}, u32[]{:S(2)}, u32[]{:S(2)}) %collective-permute-start.4) | collective-permute-done | bytes 524320 | tf_op jit(solution)/shard_map/ppermute | solution.py:60
  64.3 3.1 %collective-permute-start.6 = (f32[8,128,128]{2,1,0:T(8,128)S(1)}, f32[8,128,128]{2,1,0:T(8,128)S(1)}, u32[]{:S(2)}, u32[]{:S(2)}) collective-permute-start(f32[8,128,128]{2,1,0:T(8,128)S(1)} %pad_maximum_fusion.3), channel_id=1, source_target_pairs={{0,32},{4,36},{8,40},{12,44},{16,48},{20,52},{24,56},{28,60},{32,0... | collective-permute-start | bytes 1572872 | tf_op jit(solution)/shard_map/ppermute | solution.py:60
  68.9 6.8 %collective-permute-done.6 = f32[8,128,128]{2,1,0:T(8,128)S(1)} collective-permute-done((f32[8,128,128]{2,1,0:T(8,128)S(1)}, f32[8,128,128]{2,1,0:T(8,128)S(1)}, u32[]{:S(2)}, u32[]{:S(2)}) %collective-permute-start.6) | collective-permute-done | bytes 524320 | tf_op jit(solution)/shard_map/ppermute | solution.py:60
  75.8 4.0 %collective-permute-start.8 = (f32[4,128,128]{2,1,0:T(8,128)S(1)}, f32[4,128,128]{2,1,0:T(8,128)S(1)}, u32[]{:S(2)}, u32[]{:S(2)}) collective-permute-start(f32[4,128,128]{2,1,0:T(8,128)S(1)} %pad_maximum_fusion.4), channel_id=1, source_target_pairs={{0,64},{4,68},{8,72},{12,76},{16,80},{20,84},{24,88},{28,92},{32,9... | collective-permute-start | bytes 786440 | tf_op jit(solution)/shard_map/ppermute | solution.py:60
  79.8 0.8 add_select_fusion.9.refs_4_
  80.5 0.7 add_select_fusion.6.refs_5_
  81.3 0.7 add_select_fusion.3.refs_6_
  82.7 2.5 %collective-permute-done.8.refs_12_ = f32[4,128,128]{2,1,0:T(8,128)S(1)} collective-permute-done((f32[4,128,128]{2,1,0:T(8,128)S(1)}, f32[4,128,128]{2,1,0:T(8,128)S(1)}, u32[]{:S(2)}, u32[]{:S(2)}) %collective-permute-start.8) | collective-permute-done | bytes 262176 | tf_op jit(solution)/shard_map/ppermute | solution.py:60
  85.9 3.8 %shard_map.83 = (f32[4,4,128]{2,1,0:T(4,128)}, f32[4,4,128]{2,1,0:T(4,128)}) custom-call(s32[3]{0:T(128)} %pad_add_fusion.refs_0_.flag_ref, f32[4,4,128,128]{3,2,1,0:T(8,128)} %copy-done, f32[4,128,128]{2,1,0:T(8,128)} %copy-done.2, f32[4,128,128]{2,1,0:T(8,128)} %copy-done.1, f32[2,128,128]{2,1,0:T(8,128)} %add_select_fusion.9.refs_4_, ...), custom_call_target="tpu_custom_call" | custom-call | tf_op jit(solution)/shard_map/pallas_call | solution.py:322
  89.7 2.4 %collective-permute-start.9 = (f32[4,4,128]{2,1,0:T(4,128)}, f32[4,4,128]{2,1,0:T(4,128)S(1)}, u32[]{:S(2)}, u32[]{:S(2)}) collective-permute-start(f32[4,4,128]{2,1,0:T(4,128)} %get-tuple-element.7), channel_id=1, source_target_pairs={{0,2},{2,0},{1,3},{3,1},{4,6},{6,4},{5,7},{7,5},{8,10},{10,8},{9,1... | collective-permute-start | bytes 24584 | tf_op jit(solution)/shard_map/ppermute | solution.py:329
  92.2 4.5 %collective-permute-start.10 = (f32[4,4,128]{2,1,0:T(4,128)}, f32[4,4,128]{2,1,0:T(4,128)S(1)}, u32[]{:S(2)}, u32[]{:S(2)}) collective-permute-start(f32[4,4,128]{2,1,0:T(4,128)} %get-tuple-element.8), channel_id=1, source_target_pairs={{0,1},{1,0},{2,3},{3,2},{4,5},{5,4},{6,7},{7,6},{8,9},{9,8},{10,11... | collective-permute-start | bytes 24584 | tf_op jit(solution)/shard_map/ppermute | solution.py:330
  96.6 3.6 %shard_map.82.base_ref = f32[4,4,128,128]{3,2,1,0:T(8,128)} custom-call(s32[3]{0:T(128)} %pad_add_fusion.refs_0_.flag_ref, f32[4,4,128,128]{3,2,1,0:T(8,128)} %copy-done, f32[4,128,128]{2,1,0:T(8,128)} %copy-done.2, f32[4,128,128]{2,1,0:T(8,128)} %copy-done.1, f32[2,128,128]{2,1,0:T(8,128)} %add_select_fusion.9.refs_4_, ...), custom_call_target="tpu_custom_call" | custom-call | tf_op jit(solution)/shard_map/pallas_call | solution.py:331
  101.5 2.6 %shard_map.84 = f32[4,4,128,128]{3,2,1,0:T(8,128)} custom-call(s32[3]{0:T(128)} %pad_add_fusion.refs_0_.flag_ref, f32[4,4,128,128]{3,2,1,0:T(8,128)} %shard_map.82.base_ref, f32[4,4,128]{2,1,0:T(4,128)} %copy-done.11, f32[4,4,128]{2,1,0:T(4,128)} %copy-done.12), custom_call_target="tpu_custom_call", output_to_operand_aliasing={{}: (1, {})} | custom-call | tf_op jit(solution)/shard_map/pallas_call | solution.py:337
  (83 shorter events, 13.1 us)
Async XLA Ops:
  6.4 17.0 %all-to-all-start = ((f32[32,1,320]{2,1,0:T(1,128)}), f32[32,1,320]{2,1,0:T(1,128)S(1)}, u32[]{:S(2)}, u32[]{:S(2)}) async-start(f32[32,1,320]{2,1,0:T(1,128)} %reshape.187), calls=%async_computation | async-start | bytes 98304 | tf_op jit(solution)/shard_map/all_to_all | solution.py:36
  19.0 9.2 %copy-start.1 = (f32[4,128,128]{2,1,0:T(8,128)}, f32[4,128,128]{2,1,0:T(8,128)S(1)}, u32[]{:S(2)}) copy-start(f32[4,128,128]{2,1,0:T(8,128)S(1)} %get-tuple-element.55.refs_3_) | copy-start | bytes 786436
  19.0 9.2 %copy-start.2 = (f32[4,128,128]{2,1,0:T(8,128)}, f32[4,128,128]{2,1,0:T(8,128)S(1)}, u32[]{:S(2)}) copy-start(f32[4,128,128]{2,1,0:T(8,128)S(1)} %get-tuple-element.56.refs_2_) | copy-start | bytes 786436
  19.1 5.9 %copy-start.5 = (f32[1,128,128]{2,1,0:T(8,128)}, f32[1,128,128]{2,1,0:T(8,128)S(1)}, u32[]{:S(2)}) copy-start(f32[1,128,128]{2,1,0:T(8,128)S(1)} %get-tuple-element.26) | copy-start | bytes 196612
  19.9 5.1 %copy-start.7 = (f32[1,128,128]{2,1,0:T(8,128)}, f32[1,128,128]{2,1,0:T(8,128)S(1)}, u32[]{:S(2)}) copy-start(f32[1,128,128]{2,1,0:T(8,128)S(1)} %get-tuple-element.77) | copy-start | bytes 196612
  20.6 11.2 %collective-permute-start.1 = (f32[2,128,128]{2,1,0:T(8,128)}, f32[2,128,128]{2,1,0:T(8,128)S(1)}, u32[]{:S(2)}, u32[]{:S(2)}) collective-permute-start(f32[2,128,128]{2,1,0:T(8,128)} %pad_maximum_fusion.5), channel_id=1, source_target_pairs={{0,4},{4,0},{8,12},{12,8},{16,20},{20,16},{24,28},{28,24},{32,36},... | collective-permute-start | bytes 393224 | tf_op jit(solution)/shard_map/ppermute | solution.py:60
  28.3 1.2 %copy-start.3 = (f32[4,4,128,128]{3,2,1,0:T(8,128)S(1)}, f32[4,4,128,128]{3,2,1,0:T(8,128)}, u32[]{:S(2)}) copy-start(f32[4,4,128,128]{3,2,1,0:T(8,128)} %param.8) | copy-start | bytes 3145732
  29.5 1.7 %copy-start.9 = (f32[128,128]{1,0:T(8,128)S(1)}, f32[128,128]{1,0:T(8,128)}, u32[]{:S(2)}) copy-start(f32[128,128]{1,0:T(8,128)} %get-tuple-element.81) | copy-start | bytes 196612
  29.5 1.7 %copy-start.10 = (f32[128,128]{1,0:T(8,128)S(1)}, f32[128,128]{1,0:T(8,128)}, u32[]{:S(2)}) copy-start(f32[128,128]{1,0:T(8,128)} %get-tuple-element.83) | copy-start | bytes 196612
  29.5 2.3 %copy-start.6 = (f32[1,128,128]{2,1,0:T(8,128)S(1)}, f32[1,128,128]{2,1,0:T(8,128)}, u32[]{:S(2)}) copy-start(f32[1,128,128]{2,1,0:T(8,128)} %copy-done.5) | copy-start | bytes 196612
  29.5 2.3 %copy-start.8 = (f32[1,128,128]{2,1,0:T(8,128)S(1)}, f32[1,128,128]{2,1,0:T(8,128)}, u32[]{:S(2)}) copy-start(f32[1,128,128]{2,1,0:T(8,128)} %copy-done.7) | copy-start | bytes 196612
  29.7 13.1 %copy-start = (f32[4,4,128,128]{3,2,1,0:T(8,128)}, f32[4,4,128,128]{3,2,1,0:T(8,128)S(1)}, u32[]{:S(2)}) copy-start(f32[4,4,128,128]{3,2,1,0:T(8,128)S(1)} %bitcast_add_fusion.refs_1_) | copy-start | bytes 3145732
  31.3 11.4 %collective-permute-start = (f32[8,128,128]{2,1,0:T(8,128)S(1)}, f32[8,128,128]{2,1,0:T(8,128)S(1)}, u32[]{:S(2)}, u32[]{:S(2)}) collective-permute-start(f32[8,128,128]{2,1,0:T(8,128)S(1)} %pad_maximum_fusion), channel_id=1, source_target_pairs={{0,4},{4,0},{8,12},{12,8},{16,20},{20,16},{24,28},{28,24},{32,36},... | collective-permute-start | bytes 1572872 | tf_op jit(solution)/shard_map/ppermute | solution.py:60
  31.9 3.9 %collective-permute-start.3 = (f32[2,128,128]{2,1,0:T(8,128)S(1)}, f32[2,128,128]{2,1,0:T(8,128)S(1)}, u32[]{:S(2)}, u32[]{:S(2)}) collective-permute-start(f32[2,128,128]{2,1,0:T(8,128)S(1)} %pad_maximum_fusion.6), channel_id=1, source_target_pairs={{0,8},{4,12},{8,0},{12,4},{16,24},{20,28},{24,16},{28,20},{32,40},... | collective-permute-start | bytes 393224 | tf_op jit(solution)/shard_map/ppermute | solution.py:60
  35.8 7.9 %collective-permute-start.5 = (f32[2,128,128]{2,1,0:T(8,128)S(1)}, f32[2,128,128]{2,1,0:T(8,128)S(1)}, u32[]{:S(2)}, u32[]{:S(2)}) collective-permute-start(f32[2,128,128]{2,1,0:T(8,128)S(1)} %pad_maximum_fusion.7), channel_id=1, source_target_pairs={{0,16},{4,20},{8,24},{12,28},{16,0},{20,4},{24,8},{28,12},{32,48},... | collective-permute-start | bytes 393224 | tf_op jit(solution)/shard_map/ppermute | solution.py:60
  42.9 10.5 %collective-permute-start.2 = (f32[8,128,128]{2,1,0:T(8,128)S(1)}, f32[8,128,128]{2,1,0:T(8,128)S(1)}, u32[]{:S(2)}, u32[]{:S(2)}) collective-permute-start(f32[8,128,128]{2,1,0:T(8,128)S(1)} %pad_maximum_fusion.1), channel_id=1, source_target_pairs={{0,8},{4,12},{8,0},{12,4},{16,24},{20,28},{24,16},{28,20},{32,40},... | collective-permute-start | bytes 1572872 | tf_op jit(solution)/shard_map/ppermute | solution.py:60
  53.5 10.6 %collective-permute-start.4 = (f32[8,128,128]{2,1,0:T(8,128)S(1)}, f32[8,128,128]{2,1,0:T(8,128)S(1)}, u32[]{:S(2)}, u32[]{:S(2)}) collective-permute-start(f32[8,128,128]{2,1,0:T(8,128)S(1)} %pad_maximum_fusion.2), channel_id=1, source_target_pairs={{0,16},{4,20},{8,24},{12,28},{16,0},{20,4},{24,8},{28,12},{32,48},... | collective-permute-start | bytes 1572872 | tf_op jit(solution)/shard_map/ppermute | solution.py:60
  55.1 12.3 %collective-permute-start.7 = (f32[2,128,128]{2,1,0:T(8,128)S(1)}, f32[2,128,128]{2,1,0:T(8,128)S(1)}, u32[]{:S(2)}, u32[]{:S(2)}) collective-permute-start(f32[2,128,128]{2,1,0:T(8,128)S(1)} %pad_maximum_fusion.8), channel_id=1, source_target_pairs={{0,32},{4,36},{8,40},{12,44},{16,48},{20,52},{24,56},{28,60},{32,0... | collective-permute-start | bytes 393224 | tf_op jit(solution)/shard_map/ppermute | solution.py:60
  64.3 11.4 %collective-permute-start.6 = (f32[8,128,128]{2,1,0:T(8,128)S(1)}, f32[8,128,128]{2,1,0:T(8,128)S(1)}, u32[]{:S(2)}, u32[]{:S(2)}) collective-permute-start(f32[8,128,128]{2,1,0:T(8,128)S(1)} %pad_maximum_fusion.3), channel_id=1, source_target_pairs={{0,32},{4,36},{8,40},{12,44},{16,48},{20,52},{24,56},{28,60},{32,0... | collective-permute-start | bytes 1572872 | tf_op jit(solution)/shard_map/ppermute | solution.py:60
  75.8 9.4 %collective-permute-start.8 = (f32[4,128,128]{2,1,0:T(8,128)S(1)}, f32[4,128,128]{2,1,0:T(8,128)S(1)}, u32[]{:S(2)}, u32[]{:S(2)}) collective-permute-start(f32[4,128,128]{2,1,0:T(8,128)S(1)} %pad_maximum_fusion.4), channel_id=1, source_target_pairs={{0,64},{4,68},{8,72},{12,76},{16,80},{20,84},{24,88},{28,92},{32,9... | collective-permute-start | bytes 786440 | tf_op jit(solution)/shard_map/ppermute | solution.py:60
  85.2 0.7 copy-start.4
  89.7 10.5 %collective-permute-start.9 = (f32[4,4,128]{2,1,0:T(4,128)}, f32[4,4,128]{2,1,0:T(4,128)S(1)}, u32[]{:S(2)}, u32[]{:S(2)}) collective-permute-start(f32[4,4,128]{2,1,0:T(4,128)} %get-tuple-element.7), channel_id=1, source_target_pairs={{0,2},{2,0},{1,3},{3,1},{4,6},{6,4},{5,7},{7,5},{8,10},{10,8},{9,1... | collective-permute-start | bytes 24584 | tf_op jit(solution)/shard_map/ppermute | solution.py:329
  92.2 8.1 %collective-permute-start.10 = (f32[4,4,128]{2,1,0:T(4,128)}, f32[4,4,128]{2,1,0:T(4,128)S(1)}, u32[]{:S(2)}, u32[]{:S(2)}) collective-permute-start(f32[4,4,128]{2,1,0:T(4,128)} %get-tuple-element.8), channel_id=1, source_target_pairs={{0,1},{1,0},{2,3},{3,2},{4,5},{5,4},{6,7},{7,6},{8,9},{9,8},{10,11... | collective-permute-start | bytes 24584 | tf_op jit(solution)/shard_map/ppermute | solution.py:330
  100.3 0.6 copy-start.11
  100.9 0.6 copy-start.12

commit v13 on v11

--- a/solution.py
+++ b/solution.py
@@ -244,31 +244,32 @@
                 c = 2 * s + part
                 c_ref[k, c] = plane
                 sx_ref[k, pl.ds(c, 1), :] = jnp.where(first_x, plane[-1:, :], plane[0:1, :])
-                flipped = jnp.transpose(plane)
-                sy_ref[k, pl.ds(c, 1), :] = jnp.where(first_y, flipped[-1:, :], flipped[0:1, :])
+                j = k * c_ref.shape[1] + c
+                sy_ref[:, pl.ds(j, 1)] = jnp.where(first_y, plane[:, -1:], plane[:, 0:1])
 
 
 def paired_stencil_kernel(flag_ref, c_ref, gx_ref, gy_ref, o_ref):
     layers, components, width_x, width_y = c_ref.shape
     rows = lax.broadcasted_iota(jnp.int32, (width_x, width_y), 0)
     cols = lax.broadcasted_iota(jnp.int32, (width_x, width_y), 1)
-    side_rows = lax.broadcasted_iota(jnp.int32, (width_y, width_x), 0)
     first_x = flag_ref[1] == 0
     first_y = flag_ref[2] == 0
     for k in range(layers):
         for c in range(components):
             plane = c_ref[k, c]
             edge_x = gx_ref[k, pl.ds(c, 1), :]
-            edge_y = jnp.broadcast_to(gy_ref[k, pl.ds(c, 1), :], (width_y, width_x))
+            edge_y = gy_ref[:, pl.ds(k * components + c, 1)]
             none_x = jnp.zeros_like(edge_x)
+            none_y = jnp.zeros_like(edge_y)
             low_x = jnp.broadcast_to(jnp.where(first_x, none_x, edge_x), (width_x, width_y))
             high_x = jnp.broadcast_to(jnp.where(first_x, edge_x, none_x), (width_x, width_y))
-            side = jnp.where(side_rows == jnp.where(first_y, width_y - 1, 0), edge_y, 0.0)
+            low_y = jnp.broadcast_to(jnp.where(first_y, none_y, edge_y), (width_x, width_y))
+            high_y = jnp.broadcast_to(jnp.where(first_y, edge_y, none_y), (width_x, width_y))
             next_x = jnp.where(rows == width_x - 1, high_x, pltpu.roll(plane, width_x - 1, 0))
             prev_x = jnp.where(rows == 0, low_x, pltpu.roll(plane, 1, 0))
-            next_y = jnp.where(cols == width_y - 1, 0.0, pltpu.roll(plane, width_y - 1, 1))
-            prev_y = jnp.where(cols == 0, 0.0, pltpu.roll(plane, 1, 1))
-            neighbours = next_x + prev_x + next_y + prev_y + jnp.transpose(side)
+            next_y = jnp.where(cols == width_y - 1, high_y, pltpu.roll(plane, width_y - 1, 1))
+            prev_y = jnp.where(cols == 0, low_y, pltpu.roll(plane, 1, 1))
+            neighbours = next_x + prev_x + next_y + prev_y
             o_ref[k, c] = plane - 0.2 * (4.0 * plane - neighbours)
 
 
@@ -280,7 +281,7 @@
     smem = pl.BlockSpec(memory_space=pltpu.SMEM)
     vmem = pl.BlockSpec(memory_space=pltpu.VMEM)
     edge_x = jax.ShapeDtypeStruct((layers, components, width_y), jnp.float32)
-    edge_y = jax.ShapeDtypeStruct((layers, components, width_x), jnp.float32)
+    edge_y = jax.ShapeDtypeStruct((width_x, layers * components), jnp.float32)
     combined, send_x, send_y = pl.pallas_call(
         last_sweep_kernel,
         in_specs=[smem] + [vmem] * 12,

time: 101 us -> 102 us (level)
  transfers between devices with their start and end apart: 12 -> 12, of which waited for: 8 -> 8; matrix products, arithmetic and copies ran while one was open for 16% -> 15% of each run, Pallas kernels for 0% -> 0%
where the time goes in v13:
time: 102 us; the launch traced here: 100 us
  waiting for transfers between devices  40.2 us (39%)
  starting transfers between devices  28.9 us (28%)
  other arithmetic  15.4 us (15%)
  Pallas kernels  7.36 us (7%)
  local copies, waits for them, and re-layouts  5.73 us (6%)
  matrix products  2.36 us (2%)
    ppermute x9, waiting for transfers between devices, exchange(): return lax.ppermute(array, 'slab', [(i, i ^ step) for i in range(count)])  36.3 us
    ppermute x9, starting transfers between devices, exchange(): return lax.ppermute(array, 'slab', [(i, i ^ step) for i in range(count)])  10.1 us
    all_to_all x1, starting transfers between devices, inject_receivers(): lax.all_to_all(send_rows, 'slab', split_axis=1, concat_axis=1, tiled=True)  9.81 us
    ppermute x1, starting transfers between devices, finish_paired(): got_y = lax.ppermute(send_y, 'py', [(0, 1), (1, 0)])  6.58 us
    pallas_call x1, Pallas kernels, finish_paired(): pl.pallas_call(last_sweep_kernel, in_specs=[smem] + [vmem] * 12, out_spec...  3.92 us
    pallas_call x1, Pallas kernels, finish_paired(): pl.pallas_call(paired_stencil_kernel, in_specs=[smem, vmem, vmem, vmem],...  3.44 us
    all_to_all x1, waiting for transfers between devices, inject_receivers(): lax.all_to_all(send_rows, 'slab', split_axis=1, concat_axis=1, tiled=True)  2.86 us
    ppermute x1, starting transfers between devices, finish_paired(): got_x = lax.ppermute(send_x, 'px', [(0, 1), (1, 0)])  2.44 us
  transfers between devices with their start and end apart: 12, of which 8 were waited for; matrix products, arithmetic and copies ran while one was open for 15% of the time, Pallas kernels for 0%

profile of v13, /device:TPU:1, one launch (start us, length us, event | category | flops | bytes accessed | tf_op | source)
XLA Modules:
  0.0 100.4 jit_solution(4903386268441599794)
XLA Ops:
  0.0 1.0 convert_reduce_fusion
  3.3 2.0 %scatter_custom_fusion = f32[5,2048]{0,1:T(8,128)S(1)} fusion(s32[512]{0:T(512)S(1)} %bitcast.322, f32[512,5]{1,0:T(8,128)S(1)} %copy.45, f32[]{:T(128)} %constant.52.clone.1), kind=kCustom, calls=%fused_computation.16 | custom fusion | bytes 40964 | tf_op jit(solution)/shard_map/scatter | solution.py:34
  5.6 0.7 reshape.187
  6.4 9.8 %all-to-all-start = ((f32[32,1,320]{2,1,0:T(1,128)}), f32[32,1,320]{2,1,0:T(1,128)S(1)}, u32[]{:S(2)}, u32[]{:S(2)}) async-start(f32[32,1,320]{2,1,0:T(1,128)} %reshape.187), calls=%async_computation | async-start | bytes 98304 | tf_op jit(solution)/shard_map/all_to_all | solution.py:36
  16.2 0.8 convert_multiply_fusion
  17.0 2.0 %sine_multiply_fusion = (f32[4,128,128]{2,1,0:T(8,128)S(1)}, f32[4,128,128]{2,1,0:T(8,128)S(1)}) fusion(f32[4,128,128]{2,1,0:T(8,128)} %param.9, f32[4,128,128]{2,1,0:T(8,128)} %param.10, f32[128,128]{1,0:T(8,128)S(1)} %convert_multiply_fusion), kind=kLoop, calls=%fused_computation.19 | loop fusion | flops 262144 | bytes 1114112 | tf_op jit(solution)/shard_map/mul | solution.py:310
  19.2 1.3 %collective-permute-start.1 = (f32[2,128,128]{2,1,0:T(8,128)S(1)}, f32[2,128,128]{2,1,0:T(8,128)S(1)}, u32[]{:S(2)}, u32[]{:S(2)}) collective-permute-start(f32[2,128,128]{2,1,0:T(8,128)S(1)} %pad_maximum_fusion.5), channel_id=1, source_target_pairs={{0,4},{4,0},{8,12},{12,8},{16,20},{20,16},{24,28},{28,24},{32,36},... | collective-permute-start | bytes 393224 | tf_op jit(solution)/shard_map/ppermute | solution.py:60
  20.5 2.9 %all-to-all-done = f32[32,1,320]{2,1,0:T(1,128)S(1)} async-done(((f32[32,1,320]{2,1,0:T(1,128)}), f32[32,1,320]{2,1,0:T(1,128)S(1)}, u32[]{:S(2)}, u32[]{:S(2)}) %all-to-all-start) | async-done | bytes 40992 | tf_op jit(solution)/shard_map/all_to_all | solution.py:36
  23.9 0.8 reduce.4
  25.8 2.4 %fusion.1 = f32[512,2,512]{2,0,1:T(8,128)S(1)} fusion(bf16[2,512,2048]{2,1,0:T(8,128)(2,1)S(1)} %bitcast.306, s32[2048]{0:T(1024)S(1)} %get-tuple-element.116), kind=kOutput, calls=%fused_computation.4 | convolution fusion | flops 2148532224 | bytes 6299648 | tf_op jit(solution)/shard_map/dot_general | solution.py:51
  28.8 1.4 %bitcast_add_fusion.f_ref = f32[4,4,128,128]{3,2,1,0:T(8,128)S(1)} fusion(f32[4,4,128,128]{3,2,1,0:T(8,128)} %param.8, f32[4,128,4,128]{3,2,1,0:T(4,128)S(1)} %add.359), kind=kLoop, calls=%fused_computation.7 | loop fusion | flops 262144 | bytes 3145728 | tf_op jit(solution)/shard_map/add | solution.py:55
  32.1 2.9 %collective-permute-done.3 = f32[2,128,128]{2,1,0:T(8,128)S(1)} collective-permute-done((f32[2,128,128]{2,1,0:T(8,128)S(1)}, f32[2,128,128]{2,1,0:T(8,128)S(1)}, u32[]{:S(2)}, u32[]{:S(2)}) %collective-permute-start.3) | collective-permute-done | bytes 131104 | tf_op jit(solution)/shard_map/ppermute | solution.py:60
  35.0 0.9 collective-permute-start.5
  36.0 6.0 %collective-permute-done = f32[8,128,128]{2,1,0:T(8,128)S(1)} collective-permute-done((f32[8,128,128]{2,1,0:T(8,128)S(1)}, f32[8,128,128]{2,1,0:T(8,128)S(1)}, u32[]{:S(2)}, u32[]{:S(2)}) %collective-permute-start) | collective-permute-done | bytes 524320 | tf_op jit(solution)/shard_map/ppermute | solution.py:60
  42.1 0.8 collective-permute-start.2
  43.1 9.5 %collective-permute-done.2 = f32[8,128,128]{2,1,0:T(8,128)S(1)} collective-permute-done((f32[8,128,128]{2,1,0:T(8,128)S(1)}, f32[8,128,128]{2,1,0:T(8,128)S(1)}, u32[]{:S(2)}, u32[]{:S(2)}) %collective-permute-start.2) | collective-permute-done | bytes 524320 | tf_op jit(solution)/shard_map/ppermute | solution.py:60
  52.8 1.2 %collective-permute-start.4 = (f32[8,128,128]{2,1,0:T(8,128)S(1)}, f32[8,128,128]{2,1,0:T(8,128)S(1)}, u32[]{:S(2)}, u32[]{:S(2)}) collective-permute-start(f32[8,128,128]{2,1,0:T(8,128)S(1)} %pad_maximum_fusion.2), channel_id=1, source_target_pairs={{0,16},{4,20},{8,24},{12,28},{16,0},{20,4},{24,8},{28,12},{32,48},... | collective-permute-start | bytes 1572872 | tf_op jit(solution)/shard_map/ppermute | solution.py:60
  54.1 1.1 %collective-permute-start.7 = (f32[2,128,128]{2,1,0:T(8,128)S(1)}, f32[2,128,128]{2,1,0:T(8,128)S(1)}, u32[]{:S(2)}, u32[]{:S(2)}) collective-permute-start(f32[2,128,128]{2,1,0:T(8,128)S(1)} %pad_maximum_fusion.8), channel_id=1, source_target_pairs={{0,32},{4,36},{8,40},{12,44},{16,48},{20,52},{24,56},{28,60},{32,0... | collective-permute-start | bytes 393224 | tf_op jit(solution)/shard_map/ppermute | solution.py:60
  55.2 8.1 %collective-permute-done.4 = f32[8,128,128]{2,1,0:T(8,128)S(1)} collective-permute-done((f32[8,128,128]{2,1,0:T(8,128)S(1)}, f32[8,128,128]{2,1,0:T(8,128)S(1)}, u32[]{:S(2)}, u32[]{:S(2)}) %collective-permute-start.4) | collective-permute-done | bytes 524320 | tf_op jit(solution)/shard_map/ppermute | solution.py:60
  65.2 6.3 %collective-permute-done.6 = f32[8,128,128]{2,1,0:T(8,128)S(1)} collective-permute-done((f32[8,128,128]{2,1,0:T(8,128)S(1)}, f32[8,128,128]{2,1,0:T(8,128)S(1)}, u32[]{:S(2)}, u32[]{:S(2)}) %collective-permute-start.6) | collective-permute-done | bytes 524320 | tf_op jit(solution)/shard_map/ppermute | solution.py:60
  71.7 3.5 %collective-permute-start.8 = (f32[4,128,128]{2,1,0:T(8,128)S(1)}, f32[4,128,128]{2,1,0:T(8,128)S(1)}, u32[]{:S(2)}, u32[]{:S(2)}) collective-permute-start(f32[4,128,128]{2,1,0:T(8,128)S(1)} %pad_maximum_fusion.4), channel_id=1, source_target_pairs={{0,64},{4,68},{8,72},{12,76},{16,80},{20,84},{24,88},{28,92},{32,9... | collective-permute-start | bytes 786440 | tf_op jit(solution)/shard_map/ppermute | solution.py:60
  75.2 0.7 add_select_fusion.9.br_ref
  75.9 0.8 add_select_fusion.6.bi_ref
  76.7 0.7 add_select_fusion.3.ar_ref
  77.4 0.7 add_select_fusion.ai_ref
  78.1 3.4 %collective-permute-done.8.got_ref = f32[4,128,128]{2,1,0:T(8,128)S(1)} collective-permute-done((f32[4,128,128]{2,1,0:T(8,128)S(1)}, f32[4,128,128]{2,1,0:T(8,128)S(1)}, u32[]{:S(2)}, u32[]{:S(2)}) %collective-permute-start.8) | collective-permute-done | bytes 262176 | tf_op jit(solution)/shard_map/ppermute | solution.py:60
  81.6 0.7 copy-done.3
  82.3 3.9 %shard_map.82 = (f32[4,4,128,128]{3,2,1,0:T(8,128)}, f32[4,4,128]{2,1,0:T(4,128)}, f32[128,16]{1,0:T(8,128)}) custom-call(s32[3]{0:T(128)} %pad_add_fusion.flag_ref, f32[4,4,128,128]{3,2,1,0:T(8,128)} %copy-done, f32[4,128,128]{2,1,0:T(8,128)} %copy-done.2, f32[4,128,128]{2,1,0:T(8,128)} %copy-done.1, f32[2,128,128]{2,1,0:T(8,128)} %add_select_fusion.9.br_ref, ...), custom_call_target="tpu_custom_call" | custom-call | tf_op jit(solution)/shard_map/pallas_call | solution.py:285
  86.2 2.4 %collective-permute-start.9 = (f32[4,4,128]{2,1,0:T(4,128)}, f32[4,4,128]{2,1,0:T(4,128)S(1)}, u32[]{:S(2)}, u32[]{:S(2)}) collective-permute-start(f32[4,4,128]{2,1,0:T(4,128)} %get-tuple-element.9), channel_id=1, source_target_pairs={{0,2},{2,0},{1,3},{3,1},{4,6},{6,4},{5,7},{7,5},{8,10},{10,8},{9,1... | collective-permute-start | bytes 24584 | tf_op jit(solution)/shard_map/ppermute | solution.py:291
  88.7 6.6 %collective-permute-start.10 = (f32[128,16]{1,0:T(8,128)}, f32[128,16]{1,0:T(8,128)S(1)}, u32[]{:S(2)}, u32[]{:S(2)}) collective-permute-start(f32[128,16]{1,0:T(8,128)} %get-tuple-element.10), channel_id=1, source_target_pairs={{0,1},{1,0},{2,3},{3,2},{4,5},{5,4},{6,7},{7,6},{8,9},{9,8},{10,11... | collective-permute-start | bytes 24584 | tf_op jit(solution)/shard_map/ppermute | solution.py:292
  95.3 1.1 %collective-permute-done.10.gy_ref = f32[128,16]{1,0:T(8,128)S(1)} collective-permute-done((f32[128,16]{1,0:T(8,128)}, f32[128,16]{1,0:T(8,128)S(1)}, u32[]{:S(2)}, u32[]{:S(2)}) %collective-permute-start.10) | collective-permute-done | bytes 8224 | tf_op jit(solution)/shard_map/ppermute | solution.py:292
  97.0 3.4 %shard_map.83 = f32[4,4,128,128]{3,2,1,0:T(8,128)} custom-call(s32[3]{0:T(128)} %pad_add_fusion.flag_ref, f32[4,4,128,128]{3,2,1,0:T(8,128)} %get-tuple-element.8.c_ref, f32[4,4,128]{2,1,0:T(4,128)} %copy-done.5, f32[128,16]{1,0:T(8,128)} %copy-done.4), custom_call_target="tpu_custom_call" | custom-call | tf_op jit(solution)/shard_map/pallas_call | solution.py:293
  (68 shorter events, 10.1 us)
Async XLA Ops:
  6.4 17.0 %all-to-all-start = ((f32[32,1,320]{2,1,0:T(1,128)}), f32[32,1,320]{2,1,0:T(1,128)S(1)}, u32[]{:S(2)}, u32[]{:S(2)}) async-start(f32[32,1,320]{2,1,0:T(1,128)} %reshape.187), calls=%async_computation | async-start | bytes 98304 | tf_op jit(solution)/shard_map/all_to_all | solution.py:36
  19.0 9.2 %copy-start.1 = (f32[4,128,128]{2,1,0:T(8,128)}, f32[4,128,128]{2,1,0:T(8,128)S(1)}, u32[]{:S(2)}) copy-start(f32[4,128,128]{2,1,0:T(8,128)S(1)} %get-tuple-element.57.ri_ref) | copy-start | bytes 786436
  19.0 9.2 %copy-start.2 = (f32[4,128,128]{2,1,0:T(8,128)}, f32[4,128,128]{2,1,0:T(8,128)S(1)}, u32[]{:S(2)}) copy-start(f32[4,128,128]{2,1,0:T(8,128)S(1)} %get-tuple-element.58.rr_ref) | copy-start | bytes 786436
  19.2 11.9 %collective-permute-start.1 = (f32[2,128,128]{2,1,0:T(8,128)S(1)}, f32[2,128,128]{2,1,0:T(8,128)S(1)}, u32[]{:S(2)}, u32[]{:S(2)}) collective-permute-start(f32[2,128,128]{2,1,0:T(8,128)S(1)} %pad_maximum_fusion.5), channel_id=1, source_target_pairs={{0,4},{4,0},{8,12},{12,8},{16,20},{20,16},{24,28},{28,24},{32,36},... | collective-permute-start | bytes 393224 | tf_op jit(solution)/shard_map/ppermute | solution.py:60
  30.2 11.9 %copy-start = (f32[4,4,128,128]{3,2,1,0:T(8,128)}, f32[4,4,128,128]{3,2,1,0:T(8,128)S(1)}, u32[]{:S(2)}) copy-start(f32[4,4,128,128]{3,2,1,0:T(8,128)S(1)} %bitcast_add_fusion.f_ref) | copy-start | bytes 3145732
  30.5 11.4 %collective-permute-start = (f32[8,128,128]{2,1,0:T(8,128)S(1)}, f32[8,128,128]{2,1,0:T(8,128)S(1)}, u32[]{:S(2)}, u32[]{:S(2)}) collective-permute-start(f32[8,128,128]{2,1,0:T(8,128)S(1)} %pad_maximum_fusion), channel_id=1, source_target_pairs={{0,4},{4,0},{8,12},{12,8},{16,20},{20,16},{24,28},{28,24},{32,36},... | collective-permute-start | bytes 1572872 | tf_op jit(solution)/shard_map/ppermute | solution.py:60
  31.1 3.9 %collective-permute-start.3 = (f32[2,128,128]{2,1,0:T(8,128)S(1)}, f32[2,128,128]{2,1,0:T(8,128)S(1)}, u32[]{:S(2)}, u32[]{:S(2)}) collective-permute-start(f32[2,128,128]{2,1,0:T(8,128)S(1)} %pad_maximum_fusion.6), channel_id=1, source_target_pairs={{0,8},{4,12},{8,0},{12,4},{16,24},{20,28},{24,16},{28,20},{32,40},... | collective-permute-start | bytes 393224 | tf_op jit(solution)/shard_map/ppermute | solution.py:60
  35.0 8.0 %collective-permute-start.5 = (f32[2,128,128]{2,1,0:T(8,128)S(1)}, f32[2,128,128]{2,1,0:T(8,128)S(1)}, u32[]{:S(2)}, u32[]{:S(2)}) collective-permute-start(f32[2,128,128]{2,1,0:T(8,128)S(1)} %pad_maximum_fusion.7), channel_id=1, source_target_pairs={{0,16},{4,20},{8,24},{12,28},{16,0},{20,4},{24,8},{28,12},{32,48},... | collective-permute-start | bytes 393224 | tf_op jit(solution)/shard_map/ppermute | solution.py:60
  42.1 10.5 %collective-permute-start.2 = (f32[8,128,128]{2,1,0:T(8,128)S(1)}, f32[8,128,128]{2,1,0:T(8,128)S(1)}, u32[]{:S(2)}, u32[]{:S(2)}) collective-permute-start(f32[8,128,128]{2,1,0:T(8,128)S(1)} %pad_maximum_fusion.1), channel_id=1, source_target_pairs={{0,8},{4,12},{8,0},{12,4},{16,24},{20,28},{24,16},{28,20},{32,40},... | collective-permute-start | bytes 1572872 | tf_op jit(solution)/shard_map/ppermute | solution.py:60
  52.8 10.5 %collective-permute-start.4 = (f32[8,128,128]{2,1,0:T(8,128)S(1)}, f32[8,128,128]{2,1,0:T(8,128)S(1)}, u32[]{:S(2)}, u32[]{:S(2)}) collective-permute-start(f32[8,128,128]{2,1,0:T(8,128)S(1)} %pad_maximum_fusion.2), channel_id=1, source_target_pairs={{0,16},{4,20},{8,24},{12,28},{16,0},{20,4},{24,8},{28,12},{32,48},... | collective-permute-start | bytes 1572872 | tf_op jit(solution)/shard_map/ppermute | solution.py:60
  54.1 9.8 %collective-permute-start.7 = (f32[2,128,128]{2,1,0:T(8,128)S(1)}, f32[2,128,128]{2,1,0:T(8,128)S(1)}, u32[]{:S(2)}, u32[]{:S(2)}) collective-permute-start(f32[2,128,128]{2,1,0:T(8,128)S(1)} %pad_maximum_fusion.8), channel_id=1, source_target_pairs={{0,32},{4,36},{8,40},{12,44},{16,48},{20,52},{24,56},{28,60},{32,0... | collective-permute-start | bytes 393224 | tf_op jit(solution)/shard_map/ppermute | solution.py:60
  63.4 8.1 %collective-permute-start.6 = (f32[8,128,128]{2,1,0:T(8,128)S(1)}, f32[8,128,128]{2,1,0:T(8,128)S(1)}, u32[]{:S(2)}, u32[]{:S(2)}) collective-permute-start(f32[8,128,128]{2,1,0:T(8,128)S(1)} %pad_maximum_fusion.3), channel_id=1, source_target_pairs={{0,32},{4,36},{8,40},{12,44},{16,48},{20,52},{24,56},{28,60},{32,0... | collective-permute-start | bytes 1572872 | tf_op jit(solution)/shard_map/ppermute | solution.py:60
  71.7 9.9 %collective-permute-start.8 = (f32[4,128,128]{2,1,0:T(8,128)S(1)}, f32[4,128,128]{2,1,0:T(8,128)S(1)}, u32[]{:S(2)}, u32[]{:S(2)}) collective-permute-start(f32[4,128,128]{2,1,0:T(8,128)S(1)} %pad_maximum_fusion.4), channel_id=1, source_target_pairs={{0,64},{4,68},{8,72},{12,76},{16,80},{20,84},{24,88},{28,92},{32,9... | collective-permute-start | bytes 786440 | tf_op jit(solution)/shard_map/ppermute | solution.py:60
  81.6 0.7 copy-start.3
  86.2 9.0 %collective-permute-start.9 = (f32[4,4,128]{2,1,0:T(4,128)}, f32[4,4,128]{2,1,0:T(4,128)S(1)}, u32[]{:S(2)}, u32[]{:S(2)}) collective-permute-start(f32[4,4,128]{2,1,0:T(4,128)} %get-tuple-element.9), channel_id=1, source_target_pairs={{0,2},{2,0},{1,3},{3,1},{4,6},{6,4},{5,7},{7,5},{8,10},{10,8},{9,1... | collective-permute-start | bytes 24584 | tf_op jit(solution)/shard_map/ppermute | solution.py:291
  88.7 7.7 %collective-permute-start.10 = (f32[128,16]{1,0:T(8,128)}, f32[128,16]{1,0:T(8,128)S(1)}, u32[]{:S(2)}, u32[]{:S(2)}) collective-permute-start(f32[128,16]{1,0:T(8,128)} %get-tuple-element.10), channel_id=1, source_target_pairs={{0,1},{1,0},{2,3},{3,2},{4,5},{5,4},{6,7},{7,6},{8,9},{9,8},{10,11... | collective-permute-start | bytes 24584 | tf_op jit(solution)/shard_map/ppermute | solution.py:292
  95.3 1.1 %copy-start.5 = (f32[4,4,128]{2,1,0:T(4,128)}, f32[4,4,128]{2,1,0:T(4,128)S(1)}, u32[]{:S(2)}) copy-start(f32[4,4,128]{2,1,0:T(4,128)S(1)} %collective-permute-done.9.gx_ref) | copy-start | bytes 24580
  96.4 0.6 copy-start.4

commit v14 on v11

--- a/solution.py
+++ b/solution.py
@@ -30,9 +30,17 @@
     ranking = jnp.sum(same_before.astype(jnp.int32), axis=1)
     target_slot = target_slab * capacity + ranking
     rows = jnp.concatenate([values, position.astype(jnp.float32)[None, :]], axis=0)
-    send_rows = (
-        jnp.zeros((components + 1, slab_count * capacity), jnp.float32).at[:, target_slot].set(rows)
-    )
+    high = lax.reduce_precision(rows, exponent_bits=8, mantissa_bits=7)
+    rest = rows - high
+    middle = lax.reduce_precision(rest, exponent_bits=8, mantissa_bits=7)
+    parts = jnp.stack([high, middle, rest - middle], axis=0).astype(jnp.bfloat16)
+    spots = (
+        target_slot[:, None] == jnp.arange(slab_count * capacity, dtype=jnp.int32)[None, :]
+    ).astype(jnp.bfloat16)
+    placed = jnp.dot(
+        parts.reshape(3 * (components + 1), rows_here), spots, preferred_element_type=jnp.float32
+    ).reshape(3, components + 1, slab_count * capacity)
+    send_rows = (placed[0] + placed[1]) + placed[2]
     got_rows = lax.all_to_all(send_rows, "slab", split_axis=1, concat_axis=1, tiled=True)
     inject_values = got_rows[:components]
     inject_places = got_rows[components].astype(jnp.int32)

time: 101 us -> 99.6 us (0.986)
  local copies, waits for them, and re-layouts: 5.71 us -> 3.32 us
    scatter x1 -> x0, local copies, waits for them, and re-layouts: 1.97 us -> none  [inject_receivers(): jnp.zeros((components + 1, slab_count * capacity), jnp.float32)]
where the time goes in v14:
time: 99.6 us; the launch traced here: 97.9 us
  waiting for transfers between devices  40.4 us (41%)
  starting transfers between devices  28.7 us (29%)
  other arithmetic  15.4 us (15%)
  Pallas kernels  6.42 us (6%)
  local copies, waits for them, and re-layouts  3.32 us (3%)
  matrix products  3.22 us (3%)
    ppermute x9, waiting for transfers between devices, exchange(): return lax.ppermute(array, 'slab', [(i, i ^ step) for i in range(count)])  36.5 us
    ppermute x9, starting transfers between devices, exchange(): return lax.ppermute(array, 'slab', [(i, i ^ step) for i in range(count)])  9.85 us
    all_to_all x1, starting transfers between devices, inject_receivers(): lax.all_to_all(send_rows, 'slab', split_axis=1, concat_axis=1, tiled=True)  9.81 us
    ppermute x1, starting transfers between devices, finish_paired(): got_y = lax.ppermute(send_y, 'py', [(0, 1), (1, 0)])  6.57 us
    pallas_call x1, Pallas kernels, finish_paired(): pl.pallas_call(paired_stencil_kernel, in_specs=[smem, vmem, vmem, vmem],...  3.23 us
    pallas_call x1, Pallas kernels, finish_paired(): pl.pallas_call(last_sweep_kernel, in_specs=[smem] + [vmem] * 12, out_spec...  3.18 us
    all_to_all x1, waiting for transfers between devices, inject_receivers(): lax.all_to_all(send_rows, 'slab', split_axis=1, concat_axis=1, tiled=True)  2.86 us
    ppermute x1, starting transfers between devices, finish_paired(): got_x = lax.ppermute(send_x, 'px', [(0, 1), (1, 0)])  2.47 us
  transfers between devices with their start and end apart: 12, of which 8 were waited for; matrix products, arithmetic and copies ran while one was open for 16% of the time, Pallas kernels for 0%

profile of v14, /device:TPU:1, one launch (start us, length us, event | category | flops | bytes accessed | tf_op | source)
XLA Modules:
  0.0 97.9 jit_solution(4630565564725873899)
XLA Ops:
  1.5 1.0 %convert_reduce_fusion = s32[512]{0:T(512)S(1)} fusion(s32[512]{0:T(512)} %bitcast.310), kind=kLoop, calls=%fused_computation.11 | loop fusion | flops 1310208 | bytes 4096 | tf_op jit(solution)/shard_map/reduce_sum | solution.py:30
  3.1 0.9 fusion.3
  4.2 0.7 reshape.253
  4.9 9.8 %all-to-all-start = ((f32[32,1,320]{2,1,0:T(1,128)}), f32[32,1,320]{2,1,0:T(1,128)S(1)}, u32[]{:S(2)}, u32[]{:S(2)}) async-start(f32[32,1,320]{2,1,0:T(1,128)} %reshape.253), calls=%async_computation | async-start | bytes 98304 | tf_op jit(solution)/shard_map/all_to_all | solution.py:44
  14.7 0.8 convert_multiply_fusion
  15.6 2.0 %sine_multiply_fusion = (f32[4,128,128]{2,1,0:T(8,128)S(1)}, f32[4,128,128]{2,1,0:T(8,128)S(1)}) fusion(f32[4,128,128]{2,1,0:T(8,128)} %param.9, f32[4,128,128]{2,1,0:T(8,128)} %param.10, f32[128,128]{1,0:T(8,128)S(1)} %convert_multiply_fusion), kind=kLoop, calls=%fused_computation.19 | loop fusion | flops 262144 | bytes 1114112 | tf_op jit(solution)/shard_map/mul | solution.py:317
  17.7 1.3 %collective-permute-start.1 = (f32[2,128,128]{2,1,0:T(8,128)S(1)}, f32[2,128,128]{2,1,0:T(8,128)S(1)}, u32[]{:S(2)}, u32[]{:S(2)}) collective-permute-start(f32[2,128,128]{2,1,0:T(8,128)S(1)} %pad_maximum_fusion.5), channel_id=1, source_target_pairs={{0,4},{4,0},{8,12},{12,8},{16,20},{20,16},{24,28},{28,24},{32,36},... | collective-permute-start | bytes 393224 | tf_op jit(solution)/shard_map/ppermute | solution.py:68
  19.0 2.9 %all-to-all-done = f32[32,1,320]{2,1,0:T(1,128)S(1)} async-done(((f32[32,1,320]{2,1,0:T(1,128)}), f32[32,1,320]{2,1,0:T(1,128)S(1)}, u32[]{:S(2)}, u32[]{:S(2)}) %all-to-all-start) | async-done | bytes 40992 | tf_op jit(solution)/shard_map/all_to_all | solution.py:44
  22.4 0.8 reduce.4
  24.4 2.4 %fusion.1 = f32[512,2,512]{2,0,1:T(8,128)S(1)} fusion(bf16[2,512,2048]{2,1,0:T(8,128)(2,1)S(1)} %bitcast.298, s32[2048]{0:T(1024)S(1)} %get-tuple-element.119), kind=kOutput, calls=%fused_computation.4 | convolution fusion | flops 2148532224 | bytes 6299648 | tf_op jit(solution)/shard_map/dot_general | solution.py:59
  27.3 1.4 %bitcast_add_fusion.f_ref = f32[4,4,128,128]{3,2,1,0:T(8,128)S(1)} fusion(f32[4,4,128,128]{3,2,1,0:T(8,128)} %param.8, f32[4,128,4,128]{3,2,1,0:T(4,128)S(1)} %add.352), kind=kLoop, calls=%fused_computation.9 | loop fusion | flops 262144 | bytes 3145728 | tf_op jit(solution)/shard_map/add | solution.py:63
  30.6 2.9 %collective-permute-done.3 = f32[2,128,128]{2,1,0:T(8,128)S(1)} collective-permute-done((f32[2,128,128]{2,1,0:T(8,128)S(1)}, f32[2,128,128]{2,1,0:T(8,128)S(1)}, u32[]{:S(2)}, u32[]{:S(2)}) %collective-permute-start.3) | collective-permute-done | bytes 131104 | tf_op jit(solution)/shard_map/ppermute | solution.py:68
  33.6 0.9 collective-permute-start.5
  34.5 6.0 %collective-permute-done = f32[8,128,128]{2,1,0:T(8,128)S(1)} collective-permute-done((f32[8,128,128]{2,1,0:T(8,128)S(1)}, f32[8,128,128]{2,1,0:T(8,128)S(1)}, u32[]{:S(2)}, u32[]{:S(2)}) %collective-permute-start) | collective-permute-done | bytes 524320 | tf_op jit(solution)/shard_map/ppermute | solution.py:68
  40.6 0.8 collective-permute-start.2
  41.6 9.5 %collective-permute-done.2 = f32[8,128,128]{2,1,0:T(8,128)S(1)} collective-permute-done((f32[8,128,128]{2,1,0:T(8,128)S(1)}, f32[8,128,128]{2,1,0:T(8,128)S(1)}, u32[]{:S(2)}, u32[]{:S(2)}) %collective-permute-start.2) | collective-permute-done | bytes 524320 | tf_op jit(solution)/shard_map/ppermute | solution.py:68
  51.3 1.2 %collective-permute-start.4 = (f32[8,128,128]{2,1,0:T(8,128)S(1)}, f32[8,128,128]{2,1,0:T(8,128)S(1)}, u32[]{:S(2)}, u32[]{:S(2)}) collective-permute-start(f32[8,128,128]{2,1,0:T(8,128)S(1)} %pad_maximum_fusion.2), channel_id=1, source_target_pairs={{0,16},{4,20},{8,24},{12,28},{16,0},{20,4},{24,8},{28,12},{32,48},... | collective-permute-start | bytes 1572872 | tf_op jit(solution)/shard_map/ppermute | solution.py:68
  52.6 1.1 %collective-permute-start.7 = (f32[2,128,128]{2,1,0:T(8,128)S(1)}, f32[2,128,128]{2,1,0:T(8,128)S(1)}, u32[]{:S(2)}, u32[]{:S(2)}) collective-permute-start(f32[2,128,128]{2,1,0:T(8,128)S(1)} %pad_maximum_fusion.8), channel_id=1, source_target_pairs={{0,32},{4,36},{8,40},{12,44},{16,48},{20,52},{24,56},{28,60},{32,0... | collective-permute-start | bytes 393224 | tf_op jit(solution)/shard_map/ppermute | solution.py:68
  53.7 8.1 %collective-permute-done.4 = f32[8,128,128]{2,1,0:T(8,128)S(1)} collective-permute-done((f32[8,128,128]{2,1,0:T(8,128)S(1)}, f32[8,128,128]{2,1,0:T(8,128)S(1)}, u32[]{:S(2)}, u32[]{:S(2)}) %collective-permute-start.4) | collective-permute-done | bytes 524320 | tf_op jit(solution)/shard_map/ppermute | solution.py:68
  62.4 0.7 fusion.14
  63.8 6.3 %collective-permute-done.6 = f32[8,128,128]{2,1,0:T(8,128)S(1)} collective-permute-done((f32[8,128,128]{2,1,0:T(8,128)S(1)}, f32[8,128,128]{2,1,0:T(8,128)S(1)}, u32[]{:S(2)}, u32[]{:S(2)}) %collective-permute-start.6) | collective-permute-done | bytes 524320 | tf_op jit(solution)/shard_map/ppermute | solution.py:68
  70.3 3.2 %collective-permute-start.8 = (f32[4,128,128]{2,1,0:T(8,128)S(1)}, f32[4,128,128]{2,1,0:T(8,128)S(1)}, u32[]{:S(2)}, u32[]{:S(2)}) collective-permute-start(f32[4,128,128]{2,1,0:T(8,128)S(1)} %pad_maximum_fusion.4), channel_id=1, source_target_pairs={{0,64},{4,68},{8,72},{12,76},{16,80},{20,84},{24,88},{28,92},{32,9... | collective-permute-start | bytes 786440 | tf_op jit(solution)/shard_map/ppermute | solution.py:68
  73.5 0.7 add_select_fusion.9.br_ref
  74.2 0.7 add_select_fusion.6.bi_ref
  74.9 0.7 add_select_fusion.3.ar_ref
  75.7 0.7 add_select_fusion.ai_ref
  76.4 3.7 %collective-permute-done.8.got_ref = f32[4,128,128]{2,1,0:T(8,128)S(1)} collective-permute-done((f32[4,128,128]{2,1,0:T(8,128)S(1)}, f32[4,128,128]{2,1,0:T(8,128)S(1)}, u32[]{:S(2)}, u32[]{:S(2)}) %collective-permute-start.8) | collective-permute-done | bytes 262176 | tf_op jit(solution)/shard_map/ppermute | solution.py:68
  80.8 3.2 %shard_map.82 = (f32[4,4,128,128]{3,2,1,0:T(8,128)}, f32[4,4,128]{2,1,0:T(4,128)}, f32[4,4,128]{2,1,0:T(4,128)}) custom-call(s32[3]{0:T(128)} %pad_add_fusion.flag_ref, f32[4,4,128,128]{3,2,1,0:T(8,128)} %copy-done, f32[4,128,128]{2,1,0:T(8,128)} %copy-done.2, f32[4,128,128]{2,1,0:T(8,128)} %copy-done.1, f32[2,128,128]{2,1,0:T(8,128)} %add_select_fusion.9.br_ref, ...), custom_call_target="tpu_custom_call" | custom-call | tf_op jit(solution)/shard_map/pallas_call | solution.py:292
  84.0 2.5 %collective-permute-start.9 = (f32[4,4,128]{2,1,0:T(4,128)}, f32[4,4,128]{2,1,0:T(4,128)S(1)}, u32[]{:S(2)}, u32[]{:S(2)}) collective-permute-start(f32[4,4,128]{2,1,0:T(4,128)} %get-tuple-element.9), channel_id=1, source_target_pairs={{0,2},{2,0},{1,3},{3,1},{4,6},{6,4},{5,7},{7,5},{8,10},{10,8},{9,1... | collective-permute-start | bytes 24584 | tf_op jit(solution)/shard_map/ppermute | solution.py:298
  86.4 6.6 %collective-permute-start.10 = (f32[4,4,128]{2,1,0:T(4,128)}, f32[4,4,128]{2,1,0:T(4,128)S(1)}, u32[]{:S(2)}, u32[]{:S(2)}) collective-permute-start(f32[4,4,128]{2,1,0:T(4,128)} %get-tuple-element.10), channel_id=1, source_target_pairs={{0,1},{1,0},{2,3},{3,2},{4,5},{5,4},{6,7},{7,6},{8,9},{9,8},{10,11... | collective-permute-start | bytes 24584 | tf_op jit(solution)/shard_map/ppermute | solution.py:299
  93.0 1.0 %collective-permute-done.10.gy_ref = f32[4,4,128]{2,1,0:T(4,128)S(1)} collective-permute-done((f32[4,4,128]{2,1,0:T(4,128)}, f32[4,4,128]{2,1,0:T(4,128)S(1)}, u32[]{:S(2)}, u32[]{:S(2)}) %collective-permute-start.10) | collective-permute-done | bytes 8224 | tf_op jit(solution)/shard_map/ppermute | solution.py:299
  94.7 3.2 %shard_map.83 = f32[4,4,128,128]{3,2,1,0:T(8,128)} custom-call(s32[3]{0:T(128)} %pad_add_fusion.flag_ref, f32[4,4,128,128]{3,2,1,0:T(8,128)} %get-tuple-element.8.c_ref, f32[4,4,128]{2,1,0:T(4,128)} %copy-done.4, f32[4,4,128]{2,1,0:T(4,128)} %copy-done.5), custom_call_target="tpu_custom_call" | custom-call | tf_op jit(solution)/shard_map/pallas_call | solution.py:300
  (71 shorter events, 9.7 us)
Async XLA Ops:
  4.9 17.0 %all-to-all-start = ((f32[32,1,320]{2,1,0:T(1,128)}), f32[32,1,320]{2,1,0:T(1,128)S(1)}, u32[]{:S(2)}, u32[]{:S(2)}) async-start(f32[32,1,320]{2,1,0:T(1,128)} %reshape.253), calls=%async_computation | async-start | bytes 98304 | tf_op jit(solution)/shard_map/all_to_all | solution.py:44
  17.6 9.2 %copy-start.1 = (f32[4,128,128]{2,1,0:T(8,128)}, f32[4,128,128]{2,1,0:T(8,128)S(1)}, u32[]{:S(2)}) copy-start(f32[4,128,128]{2,1,0:T(8,128)S(1)} %get-tuple-element.57.ri_ref) | copy-start | bytes 786436
  17.6 9.2 %copy-start.2 = (f32[4,128,128]{2,1,0:T(8,128)}, f32[4,128,128]{2,1,0:T(8,128)S(1)}, u32[]{:S(2)}) copy-start(f32[4,128,128]{2,1,0:T(8,128)S(1)} %get-tuple-element.58.rr_ref) | copy-start | bytes 786436
  17.7 11.9 %collective-permute-start.1 = (f32[2,128,128]{2,1,0:T(8,128)S(1)}, f32[2,128,128]{2,1,0:T(8,128)S(1)}, u32[]{:S(2)}, u32[]{:S(2)}) collective-permute-start(f32[2,128,128]{2,1,0:T(8,128)S(1)} %pad_maximum_fusion.5), channel_id=1, source_target_pairs={{0,4},{4,0},{8,12},{12,8},{16,20},{20,16},{24,28},{28,24},{32,36},... | collective-permute-start | bytes 393224 | tf_op jit(solution)/shard_map/ppermute | solution.py:68
  28.7 11.9 %copy-start = (f32[4,4,128,128]{3,2,1,0:T(8,128)}, f32[4,4,128,128]{3,2,1,0:T(8,128)S(1)}, u32[]{:S(2)}) copy-start(f32[4,4,128,128]{3,2,1,0:T(8,128)S(1)} %bitcast_add_fusion.f_ref) | copy-start | bytes 3145732
  29.0 11.4 %collective-permute-start = (f32[8,128,128]{2,1,0:T(8,128)S(1)}, f32[8,128,128]{2,1,0:T(8,128)S(1)}, u32[]{:S(2)}, u32[]{:S(2)}) collective-permute-start(f32[8,128,128]{2,1,0:T(8,128)S(1)} %pad_maximum_fusion), channel_id=1, source_target_pairs={{0,4},{4,0},{8,12},{12,8},{16,20},{20,16},{24,28},{28,24},{32,36},... | collective-permute-start | bytes 1572872 | tf_op jit(solution)/shard_map/ppermute | solution.py:68
  29.6 3.9 %collective-permute-start.3 = (f32[2,128,128]{2,1,0:T(8,128)S(1)}, f32[2,128,128]{2,1,0:T(8,128)S(1)}, u32[]{:S(2)}, u32[]{:S(2)}) collective-permute-start(f32[2,128,128]{2,1,0:T(8,128)S(1)} %pad_maximum_fusion.6), channel_id=1, source_target_pairs={{0,8},{4,12},{8,0},{12,4},{16,24},{20,28},{24,16},{28,20},{32,40},... | collective-permute-start | bytes 393224 | tf_op jit(solution)/shard_map/ppermute | solution.py:68
  33.6 8.0 %collective-permute-start.5 = (f32[2,128,128]{2,1,0:T(8,128)S(1)}, f32[2,128,128]{2,1,0:T(8,128)S(1)}, u32[]{:S(2)}, u32[]{:S(2)}) collective-permute-start(f32[2,128,128]{2,1,0:T(8,128)S(1)} %pad_maximum_fusion.7), channel_id=1, source_target_pairs={{0,16},{4,20},{8,24},{12,28},{16,0},{20,4},{24,8},{28,12},{32,48},... | collective-permute-start | bytes 393224 | tf_op jit(solution)/shard_map/ppermute | solution.py:68
  40.6 10.5 %collective-permute-start.2 = (f32[8,128,128]{2,1,0:T(8,128)S(1)}, f32[8,128,128]{2,1,0:T(8,128)S(1)}, u32[]{:S(2)}, u32[]{:S(2)}) collective-permute-start(f32[8,128,128]{2,1,0:T(8,128)S(1)} %pad_maximum_fusion.1), channel_id=1, source_target_pairs={{0,8},{4,12},{8,0},{12,4},{16,24},{20,28},{24,16},{28,20},{32,40},... | collective-permute-start | bytes 1572872 | tf_op jit(solution)/shard_map/ppermute | solution.py:68
  51.3 10.6 %collective-permute-start.4 = (f32[8,128,128]{2,1,0:T(8,128)S(1)}, f32[8,128,128]{2,1,0:T(8,128)S(1)}, u32[]{:S(2)}, u32[]{:S(2)}) collective-permute-start(f32[8,128,128]{2,1,0:T(8,128)S(1)} %pad_maximum_fusion.2), channel_id=1, source_target_pairs={{0,16},{4,20},{8,24},{12,28},{16,0},{20,4},{24,8},{28,12},{32,48},... | collective-permute-start | bytes 1572872 | tf_op jit(solution)/shard_map/ppermute | solution.py:68
  52.6 9.8 %collective-permute-start.7 = (f32[2,128,128]{2,1,0:T(8,128)S(1)}, f32[2,128,128]{2,1,0:T(8,128)S(1)}, u32[]{:S(2)}, u32[]{:S(2)}) collective-permute-start(f32[2,128,128]{2,1,0:T(8,128)S(1)} %pad_maximum_fusion.8), channel_id=1, source_target_pairs={{0,32},{4,36},{8,40},{12,44},{16,48},{20,52},{24,56},{28,60},{32,0... | collective-permute-start | bytes 393224 | tf_op jit(solution)/shard_map/ppermute | solution.py:68
  62.0 8.1 %collective-permute-start.6 = (f32[8,128,128]{2,1,0:T(8,128)S(1)}, f32[8,128,128]{2,1,0:T(8,128)S(1)}, u32[]{:S(2)}, u32[]{:S(2)}) collective-permute-start(f32[8,128,128]{2,1,0:T(8,128)S(1)} %pad_maximum_fusion.3), channel_id=1, source_target_pairs={{0,32},{4,36},{8,40},{12,44},{16,48},{20,52},{24,56},{28,60},{32,0... | collective-permute-start | bytes 1572872 | tf_op jit(solution)/shard_map/ppermute | solution.py:68
  70.3 9.8 %collective-permute-start.8 = (f32[4,128,128]{2,1,0:T(8,128)S(1)}, f32[4,128,128]{2,1,0:T(8,128)S(1)}, u32[]{:S(2)}, u32[]{:S(2)}) collective-permute-start(f32[4,128,128]{2,1,0:T(8,128)S(1)} %pad_maximum_fusion.4), channel_id=1, source_target_pairs={{0,64},{4,68},{8,72},{12,76},{16,80},{20,84},{24,88},{28,92},{32,9... | collective-permute-start | bytes 786440 | tf_op jit(solution)/shard_map/ppermute | solution.py:68
  80.1 0.7 copy-start.3
  84.0 9.0 %collective-permute-start.9 = (f32[4,4,128]{2,1,0:T(4,128)}, f32[4,4,128]{2,1,0:T(4,128)S(1)}, u32[]{:S(2)}, u32[]{:S(2)}) collective-permute-start(f32[4,4,128]{2,1,0:T(4,128)} %get-tuple-element.9), channel_id=1, source_target_pairs={{0,2},{2,0},{1,3},{3,1},{4,6},{6,4},{5,7},{7,5},{8,10},{10,8},{9,1... | collective-permute-start | bytes 24584 | tf_op jit(solution)/shard_map/ppermute | solution.py:298
  86.4 7.6 %collective-permute-start.10 = (f32[4,4,128]{2,1,0:T(4,128)}, f32[4,4,128]{2,1,0:T(4,128)S(1)}, u32[]{:S(2)}, u32[]{:S(2)}) collective-permute-start(f32[4,4,128]{2,1,0:T(4,128)} %get-tuple-element.10), channel_id=1, source_target_pairs={{0,1},{1,0},{2,3},{3,2},{4,5},{5,4},{6,7},{7,6},{8,9},{9,8},{10,11... | collective-permute-start | bytes 24584 | tf_op jit(solution)/shard_map/ppermute | solution.py:299
  93.0 1.0 %copy-start.4 = (f32[4,4,128]{2,1,0:T(4,128)}, f32[4,4,128]{2,1,0:T(4,128)S(1)}, u32[]{:S(2)}) copy-start(f32[4,4,128]{2,1,0:T(4,128)S(1)} %collective-permute-done.9.gx_ref) | copy-start | bytes 24580
  94.1 0.6 copy-start.5

commit v15 on v14

--- a/solution.py
+++ b/solution.py
@@ -297,10 +297,13 @@
     )(flags, fields, rate_re, rate_im, *before, *after, *below, *above, got)
     got_x = lax.ppermute(send_x, "px", [(0, 1), (1, 0)])
     got_y = lax.ppermute(send_y, "py", [(0, 1), (1, 0)])
+    plane_block = pl.BlockSpec((1, components, width_x, width_y), lambda k: (k, 0, 0, 0))
+    edge_block = pl.BlockSpec((1, components, width_y), lambda k: (k, 0, 0))
     return pl.pallas_call(
         paired_stencil_kernel,
-        in_specs=[smem, vmem, vmem, vmem],
-        out_specs=vmem,
+        grid=(layers,),
+        in_specs=[smem, plane_block, edge_block, edge_block],
+        out_specs=plane_block,
         out_shape=jax.ShapeDtypeStruct(fields.shape, jnp.float32),
     )(flags, combined, got_x, got_y)
 

time: 99.6 us -> 100 us (level)
  no operation moved by 1% of the time
where the time goes in v15:
time: 100 us; the launch traced here: 98.7 us
  waiting for transfers between devices  40.4 us (40%)
  starting transfers between devices  28.7 us (29%)
  other arithmetic  15.4 us (15%)
  Pallas kernels  7.19 us (7%)
  local copies, waits for them, and re-layouts  3.32 us (3%)
  matrix products  3.22 us (3%)
    ppermute x9, waiting for transfers between devices, exchange(): return lax.ppermute(array, 'slab', [(i, i ^ step) for i in range(count)])  36.5 us
    ppermute x9, starting transfers between devices, exchange(): return lax.ppermute(array, 'slab', [(i, i ^ step) for i in range(count)])  9.85 us
    all_to_all x1, starting transfers between devices, inject_receivers(): lax.all_to_all(send_rows, 'slab', split_axis=1, concat_axis=1, tiled=True)  9.81 us
    ppermute x1, starting transfers between devices, finish_paired(): got_y = lax.ppermute(send_y, 'py', [(0, 1), (1, 0)])  6.57 us
    pallas_call x1, Pallas kernels, finish_paired(): pl.pallas_call(paired_stencil_kernel, grid=(layers,), in_specs=[smem, pla...  4.01 us
    pallas_call x1, Pallas kernels, finish_paired(): pl.pallas_call(last_sweep_kernel, in_specs=[smem] + [vmem] * 12, out_spec...  3.18 us
    all_to_all x1, waiting for transfers between devices, inject_receivers(): lax.all_to_all(send_rows, 'slab', split_axis=1, concat_axis=1, tiled=True)  2.86 us
    ppermute x1, starting transfers between devices, finish_paired(): got_x = lax.ppermute(send_x, 'px', [(0, 1), (1, 0)])  2.47 us
  transfers between devices with their start and end apart: 12, of which 8 were waited for; matrix products, arithmetic and copies ran while one was open for 16% of the time, Pallas kernels for 0%

profile of v15, /device:TPU:1, one launch (start us, length us, event | category | flops | bytes accessed | tf_op | source)
XLA Modules:
  0.0 98.7 jit_solution(12003892543659160045)
XLA Ops:
  1.5 1.0 %convert_reduce_fusion = s32[512]{0:T(512)S(1)} fusion(s32[512]{0:T(512)} %bitcast.310), kind=kLoop, calls=%fused_computation.11 | loop fusion | flops 1310208 | bytes 4096 | tf_op jit(solution)/shard_map/reduce_sum | solution.py:30
  3.1 0.9 fusion.3
  4.2 0.7 reshape.253
  4.9 9.8 %all-to-all-start = ((f32[32,1,320]{2,1,0:T(1,128)}), f32[32,1,320]{2,1,0:T(1,128)S(1)}, u32[]{:S(2)}, u32[]{:S(2)}) async-start(f32[32,1,320]{2,1,0:T(1,128)} %reshape.253), calls=%async_computation | async-start | bytes 98304 | tf_op jit(solution)/shard_map/all_to_all | solution.py:44
  14.7 0.8 convert_multiply_fusion
  15.6 2.0 %sine_multiply_fusion = (f32[4,128,128]{2,1,0:T(8,128)S(1)}, f32[4,128,128]{2,1,0:T(8,128)S(1)}) fusion(f32[4,128,128]{2,1,0:T(8,128)} %param.9, f32[4,128,128]{2,1,0:T(8,128)} %param.10, f32[128,128]{1,0:T(8,128)S(1)} %convert_multiply_fusion), kind=kLoop, calls=%fused_computation.19 | loop fusion | flops 262144 | bytes 1114112 | tf_op jit(solution)/shard_map/mul | solution.py:320
  17.7 1.3 %collective-permute-start.1 = (f32[2,128,128]{2,1,0:T(8,128)S(1)}, f32[2,128,128]{2,1,0:T(8,128)S(1)}, u32[]{:S(2)}, u32[]{:S(2)}) collective-permute-start(f32[2,128,128]{2,1,0:T(8,128)S(1)} %pad_maximum_fusion.5), channel_id=1, source_target_pairs={{0,4},{4,0},{8,12},{12,8},{16,20},{20,16},{24,28},{28,24},{32,36},... | collective-permute-start | bytes 393224 | tf_op jit(solution)/shard_map/ppermute | solution.py:68
  19.0 2.9 %all-to-all-done = f32[32,1,320]{2,1,0:T(1,128)S(1)} async-done(((f32[32,1,320]{2,1,0:T(1,128)}), f32[32,1,320]{2,1,0:T(1,128)S(1)}, u32[]{:S(2)}, u32[]{:S(2)}) %all-to-all-start) | async-done | bytes 40992 | tf_op jit(solution)/shard_map/all_to_all | solution.py:44
  22.4 0.8 reduce.4
  24.4 2.4 %fusion.1 = f32[512,2,512]{2,0,1:T(8,128)S(1)} fusion(bf16[2,512,2048]{2,1,0:T(8,128)(2,1)S(1)} %bitcast.298, s32[2048]{0:T(1024)S(1)} %get-tuple-element.119), kind=kOutput, calls=%fused_computation.4 | convolution fusion | flops 2148532224 | bytes 6299648 | tf_op jit(solution)/shard_map/dot_general | solution.py:59
  27.3 1.4 %bitcast_add_fusion.f_ref = f32[4,4,128,128]{3,2,1,0:T(8,128)S(1)} fusion(f32[4,4,128,128]{3,2,1,0:T(8,128)} %param.8, f32[4,128,4,128]{3,2,1,0:T(4,128)S(1)} %add.352), kind=kLoop, calls=%fused_computation.9 | loop fusion | flops 262144 | bytes 3145728 | tf_op jit(solution)/shard_map/add | solution.py:63
  30.6 2.9 %collective-permute-done.3 = f32[2,128,128]{2,1,0:T(8,128)S(1)} collective-permute-done((f32[2,128,128]{2,1,0:T(8,128)S(1)}, f32[2,128,128]{2,1,0:T(8,128)S(1)}, u32[]{:S(2)}, u32[]{:S(2)}) %collective-permute-start.3) | collective-permute-done | bytes 131104 | tf_op jit(solution)/shard_map/ppermute | solution.py:68
  33.6 0.9 collective-permute-start.5
  34.5 6.0 %collective-permute-done = f32[8,128,128]{2,1,0:T(8,128)S(1)} collective-permute-done((f32[8,128,128]{2,1,0:T(8,128)S(1)}, f32[8,128,128]{2,1,0:T(8,128)S(1)}, u32[]{:S(2)}, u32[]{:S(2)}) %collective-permute-start) | collective-permute-done | bytes 524320 | tf_op jit(solution)/shard_map/ppermute | solution.py:68
  40.6 0.8 collective-permute-start.2
  41.6 9.5 %collective-permute-done.2 = f32[8,128,128]{2,1,0:T(8,128)S(1)} collective-permute-done((f32[8,128,128]{2,1,0:T(8,128)S(1)}, f32[8,128,128]{2,1,0:T(8,128)S(1)}, u32[]{:S(2)}, u32[]{:S(2)}) %collective-permute-start.2) | collective-permute-done | bytes 524320 | tf_op jit(solution)/shard_map/ppermute | solution.py:68
  51.3 1.2 %collective-permute-start.4 = (f32[8,128,128]{2,1,0:T(8,128)S(1)}, f32[8,128,128]{2,1,0:T(8,128)S(1)}, u32[]{:S(2)}, u32[]{:S(2)}) collective-permute-start(f32[8,128,128]{2,1,0:T(8,128)S(1)} %pad_maximum_fusion.2), channel_id=1, source_target_pairs={{0,16},{4,20},{8,24},{12,28},{16,0},{20,4},{24,8},{28,12},{32,48},... | collective-permute-start | bytes 1572872 | tf_op jit(solution)/shard_map/ppermute | solution.py:68
  52.6 1.1 %collective-permute-start.7 = (f32[2,128,128]{2,1,0:T(8,128)S(1)}, f32[2,128,128]{2,1,0:T(8,128)S(1)}, u32[]{:S(2)}, u32[]{:S(2)}) collective-permute-start(f32[2,128,128]{2,1,0:T(8,128)S(1)} %pad_maximum_fusion.8), channel_id=1, source_target_pairs={{0,32},{4,36},{8,40},{12,44},{16,48},{20,52},{24,56},{28,60},{32,0... | collective-permute-start | bytes 393224 | tf_op jit(solution)/shard_map/ppermute | solution.py:68
  53.7 8.1 %collective-permute-done.4 = f32[8,128,128]{2,1,0:T(8,128)S(1)} collective-permute-done((f32[8,128,128]{2,1,0:T(8,128)S(1)}, f32[8,128,128]{2,1,0:T(8,128)S(1)}, u32[]{:S(2)}, u32[]{:S(2)}) %collective-permute-start.4) | collective-permute-done | bytes 524320 | tf_op jit(solution)/shard_map/ppermute | solution.py:68
  62.4 0.7 fusion.14
  63.8 6.3 %collective-permute-done.6 = f32[8,128,128]{2,1,0:T(8,128)S(1)} collective-permute-done((f32[8,128,128]{2,1,0:T(8,128)S(1)}, f32[8,128,128]{2,1,0:T(8,128)S(1)}, u32[]{:S(2)}, u32[]{:S(2)}) %collective-permute-start.6) | collective-permute-done | bytes 524320 | tf_op jit(solution)/shard_map/ppermute | solution.py:68
  70.3 3.2 %collective-permute-start.8 = (f32[4,128,128]{2,1,0:T(8,128)S(1)}, f32[4,128,128]{2,1,0:T(8,128)S(1)}, u32[]{:S(2)}, u32[]{:S(2)}) collective-permute-start(f32[4,128,128]{2,1,0:T(8,128)S(1)} %pad_maximum_fusion.4), channel_id=1, source_target_pairs={{0,64},{4,68},{8,72},{12,76},{16,80},{20,84},{24,88},{28,92},{32,9... | collective-permute-start | bytes 786440 | tf_op jit(solution)/shard_map/ppermute | solution.py:68
  73.5 0.7 add_select_fusion.9.br_ref
  74.2 0.7 add_select_fusion.6.bi_ref
  74.9 0.7 add_select_fusion.3.ar_ref
  75.7 0.7 add_select_fusion.ai_ref
  76.4 3.7 %collective-permute-done.8.got_ref = f32[4,128,128]{2,1,0:T(8,128)S(1)} collective-permute-done((f32[4,128,128]{2,1,0:T(8,128)S(1)}, f32[4,128,128]{2,1,0:T(8,128)S(1)}, u32[]{:S(2)}, u32[]{:S(2)}) %collective-permute-start.8) | collective-permute-done | bytes 262176 | tf_op jit(solution)/shard_map/ppermute | solution.py:68
  80.8 3.2 %shard_map.82 = (f32[4,4,128,128]{3,2,1,0:T(8,128)}, f32[4,4,128]{2,1,0:T(4,128)}, f32[4,4,128]{2,1,0:T(4,128)}) custom-call(s32[3]{0:T(128)} %pad_add_fusion.flag_ref, f32[4,4,128,128]{3,2,1,0:T(8,128)} %copy-done, f32[4,128,128]{2,1,0:T(8,128)} %copy-done.2, f32[4,128,128]{2,1,0:T(8,128)} %copy-done.1, f32[2,128,128]{2,1,0:T(8,128)} %add_select_fusion.9.br_ref, ...), custom_call_target="tpu_custom_call" | custom-call | tf_op jit(solution)/shard_map/pallas_call | solution.py:292
  84.0 2.5 %collective-permute-start.9 = (f32[4,4,128]{2,1,0:T(4,128)}, f32[4,4,128]{2,1,0:T(4,128)S(1)}, u32[]{:S(2)}, u32[]{:S(2)}) collective-permute-start(f32[4,4,128]{2,1,0:T(4,128)} %get-tuple-element.9), channel_id=1, source_target_pairs={{0,2},{2,0},{1,3},{3,1},{4,6},{6,4},{5,7},{7,5},{8,10},{10,8},{9,1... | collective-permute-start | bytes 24584 | tf_op jit(solution)/shard_map/ppermute | solution.py:298
  86.4 6.6 %collective-permute-start.10 = (f32[4,4,128]{2,1,0:T(4,128)}, f32[4,4,128]{2,1,0:T(4,128)S(1)}, u32[]{:S(2)}, u32[]{:S(2)}) collective-permute-start(f32[4,4,128]{2,1,0:T(4,128)} %get-tuple-element.10), channel_id=1, source_target_pairs={{0,1},{1,0},{2,3},{3,2},{4,5},{5,4},{6,7},{7,6},{8,9},{9,8},{10,11... | collective-permute-start | bytes 24584 | tf_op jit(solution)/shard_map/ppermute | solution.py:299
  93.0 1.0 %collective-permute-done.10.gy_ref = f32[4,4,128]{2,1,0:T(4,128)S(1)} collective-permute-done((f32[4,4,128]{2,1,0:T(4,128)}, f32[4,4,128]{2,1,0:T(4,128)S(1)}, u32[]{:S(2)}, u32[]{:S(2)}) %collective-permute-start.10) | collective-permute-done | bytes 8224 | tf_op jit(solution)/shard_map/ppermute | solution.py:299
  94.7 4.0 %shard_map.83 = f32[4,4,128,128]{3,2,1,0:T(8,128)} custom-call(s32[3]{0:T(128)} %pad_add_fusion.flag_ref, f32[4,4,128,128]{3,2,1,0:T(8,128)} %get-tuple-element.8.c_ref, f32[4,4,128]{2,1,0:T(4,128)} %copy-done.4, f32[4,4,128]{2,1,0:T(4,128)} %copy-done.5), custom_call_target="tpu_custom_call" | custom-call | tf_op jit(solution)/shard_map/pallas_call | solution.py:302
  (71 shorter events, 9.7 us)
Async XLA Ops:
  4.9 17.0 %all-to-all-start = ((f32[32,1,320]{2,1,0:T(1,128)}), f32[32,1,320]{2,1,0:T(1,128)S(1)}, u32[]{:S(2)}, u32[]{:S(2)}) async-start(f32[32,1,320]{2,1,0:T(1,128)} %reshape.253), calls=%async_computation | async-start | bytes 98304 | tf_op jit(solution)/shard_map/all_to_all | solution.py:44
  17.6 9.2 %copy-start.1 = (f32[4,128,128]{2,1,0:T(8,128)}, f32[4,128,128]{2,1,0:T(8,128)S(1)}, u32[]{:S(2)}) copy-start(f32[4,128,128]{2,1,0:T(8,128)S(1)} %get-tuple-element.57.ri_ref) | copy-start | bytes 786436
  17.6 9.2 %copy-start.2 = (f32[4,128,128]{2,1,0:T(8,128)}, f32[4,128,128]{2,1,0:T(8,128)S(1)}, u32[]{:S(2)}) copy-start(f32[4,128,128]{2,1,0:T(8,128)S(1)} %get-tuple-element.58.rr_ref) | copy-start | bytes 786436
  17.7 11.9 %collective-permute-start.1 = (f32[2,128,128]{2,1,0:T(8,128)S(1)}, f32[2,128,128]{2,1,0:T(8,128)S(1)}, u32[]{:S(2)}, u32[]{:S(2)}) collective-permute-start(f32[2,128,128]{2,1,0:T(8,128)S(1)} %pad_maximum_fusion.5), channel_id=1, source_target_pairs={{0,4},{4,0},{8,12},{12,8},{16,20},{20,16},{24,28},{28,24},{32,36},... | collective-permute-start | bytes 393224 | tf_op jit(solution)/shard_map/ppermute | solution.py:68
  28.7 11.9 %copy-start = (f32[4,4,128,128]{3,2,1,0:T(8,128)}, f32[4,4,128,128]{3,2,1,0:T(8,128)S(1)}, u32[]{:S(2)}) copy-start(f32[4,4,128,128]{3,2,1,0:T(8,128)S(1)} %bitcast_add_fusion.f_ref) | copy-start | bytes 3145732
  29.0 11.4 %collective-permute-start = (f32[8,128,128]{2,1,0:T(8,128)S(1)}, f32[8,128,128]{2,1,0:T(8,128)S(1)}, u32[]{:S(2)}, u32[]{:S(2)}) collective-permute-start(f32[8,128,128]{2,1,0:T(8,128)S(1)} %pad_maximum_fusion), channel_id=1, source_target_pairs={{0,4},{4,0},{8,12},{12,8},{16,20},{20,16},{24,28},{28,24},{32,36},... | collective-permute-start | bytes 1572872 | tf_op jit(solution)/shard_map/ppermute | solution.py:68
  29.6 3.9 %collective-permute-start.3 = (f32[2,128,128]{2,1,0:T(8,128)S(1)}, f32[2,128,128]{2,1,0:T(8,128)S(1)}, u32[]{:S(2)}, u32[]{:S(2)}) collective-permute-start(f32[2,128,128]{2,1,0:T(8,128)S(1)} %pad_maximum_fusion.6), channel_id=1, source_target_pairs={{0,8},{4,12},{8,0},{12,4},{16,24},{20,28},{24,16},{28,20},{32,40},... | collective-permute-start | bytes 393224 | tf_op jit(solution)/shard_map/ppermute | solution.py:68
  33.6 8.0 %collective-permute-start.5 = (f32[2,128,128]{2,1,0:T(8,128)S(1)}, f32[2,128,128]{2,1,0:T(8,128)S(1)}, u32[]{:S(2)}, u32[]{:S(2)}) collective-permute-start(f32[2,128,128]{2,1,0:T(8,128)S(1)} %pad_maximum_fusion.7), channel_id=1, source_target_pairs={{0,16},{4,20},{8,24},{12,28},{16,0},{20,4},{24,8},{28,12},{32,48},... | collective-permute-start | bytes 393224 | tf_op jit(solution)/shard_map/ppermute | solution.py:68
  40.6 10.5 %collective-permute-start.2 = (f32[8,128,128]{2,1,0:T(8,128)S(1)}, f32[8,128,128]{2,1,0:T(8,128)S(1)}, u32[]{:S(2)}, u32[]{:S(2)}) collective-permute-start(f32[8,128,128]{2,1,0:T(8,128)S(1)} %pad_maximum_fusion.1), channel_id=1, source_target_pairs={{0,8},{4,12},{8,0},{12,4},{16,24},{20,28},{24,16},{28,20},{32,40},... | collective-permute-start | bytes 1572872 | tf_op jit(solution)/shard_map/ppermute | solution.py:68
  51.3 10.6 %collective-permute-start.4 = (f32[8,128,128]{2,1,0:T(8,128)S(1)}, f32[8,128,128]{2,1,0:T(8,128)S(1)}, u32[]{:S(2)}, u32[]{:S(2)}) collective-permute-start(f32[8,128,128]{2,1,0:T(8,128)S(1)} %pad_maximum_fusion.2), channel_id=1, source_target_pairs={{0,16},{4,20},{8,24},{12,28},{16,0},{20,4},{24,8},{28,12},{32,48},... | collective-permute-start | bytes 1572872 | tf_op jit(solution)/shard_map/ppermute | solution.py:68
  52.6 9.8 %collective-permute-start.7 = (f32[2,128,128]{2,1,0:T(8,128)S(1)}, f32[2,128,128]{2,1,0:T(8,128)S(1)}, u32[]{:S(2)}, u32[]{:S(2)}) collective-permute-start(f32[2,128,128]{2,1,0:T(8,128)S(1)} %pad_maximum_fusion.8), channel_id=1, source_target_pairs={{0,32},{4,36},{8,40},{12,44},{16,48},{20,52},{24,56},{28,60},{32,0... | collective-permute-start | bytes 393224 | tf_op jit(solution)/shard_map/ppermute | solution.py:68
  62.0 8.1 %collective-permute-start.6 = (f32[8,128,128]{2,1,0:T(8,128)S(1)}, f32[8,128,128]{2,1,0:T(8,128)S(1)}, u32[]{:S(2)}, u32[]{:S(2)}) collective-permute-start(f32[8,128,128]{2,1,0:T(8,128)S(1)} %pad_maximum_fusion.3), channel_id=1, source_target_pairs={{0,32},{4,36},{8,40},{12,44},{16,48},{20,52},{24,56},{28,60},{32,0... | collective-permute-start | bytes 1572872 | tf_op jit(solution)/shard_map/ppermute | solution.py:68
  70.3 9.8 %collective-permute-start.8 = (f32[4,128,128]{2,1,0:T(8,128)S(1)}, f32[4,128,128]{2,1,0:T(8,128)S(1)}, u32[]{:S(2)}, u32[]{:S(2)}) collective-permute-start(f32[4,128,128]{2,1,0:T(8,128)S(1)} %pad_maximum_fusion.4), channel_id=1, source_target_pairs={{0,64},{4,68},{8,72},{12,76},{16,80},{20,84},{24,88},{28,92},{32,9... | collective-permute-start | bytes 786440 | tf_op jit(solution)/shard_map/ppermute | solution.py:68
  80.1 0.7 copy-start.3
  84.0 9.0 %collective-permute-start.9 = (f32[4,4,128]{2,1,0:T(4,128)}, f32[4,4,128]{2,1,0:T(4,128)S(1)}, u32[]{:S(2)}, u32[]{:S(2)}) collective-permute-start(f32[4,4,128]{2,1,0:T(4,128)} %get-tuple-element.9), channel_id=1, source_target_pairs={{0,2},{2,0},{1,3},{3,1},{4,6},{6,4},{5,7},{7,5},{8,10},{10,8},{9,1... | collective-permute-start | bytes 24584 | tf_op jit(solution)/shard_map/ppermute | solution.py:298
  86.4 7.6 %collective-permute-start.10 = (f32[4,4,128]{2,1,0:T(4,128)}, f32[4,4,128]{2,1,0:T(4,128)S(1)}, u32[]{:S(2)}, u32[]{:S(2)}) collective-permute-start(f32[4,4,128]{2,1,0:T(4,128)} %get-tuple-element.10), channel_id=1, source_target_pairs={{0,1},{1,0},{2,3},{3,2},{4,5},{5,4},{6,7},{7,6},{8,9},{9,8},{10,11... | collective-permute-start | bytes 24584 | tf_op jit(solution)/shard_map/ppermute | solution.py:299
  93.0 1.0 %copy-start.4 = (f32[4,4,128]{2,1,0:T(4,128)}, f32[4,4,128]{2,1,0:T(4,128)S(1)}, u32[]{:S(2)}) copy-start(f32[4,4,128]{2,1,0:T(4,128)S(1)} %collective-permute-done.9.gx_ref) | copy-start | bytes 24580
  94.1 0.6 copy-start.5

commit v16 on v14

--- a/solution.py
+++ b/solution.py
@@ -230,6 +230,10 @@
     lower = flag_ref[0] == 1
     first_x = flag_ref[1] == 0
     first_y = flag_ref[2] == 0
+    components = c_ref.shape[1]
+    width_x, width_y = c_ref.shape[2], c_ref.shape[3]
+    lanes = lax.broadcasted_iota(jnp.int32, (width_x, width_y), 1)
+    gathered = jnp.zeros((width_x, width_y), jnp.float32)
     for s in range(shots):
         p_re, p_im = got_ref[s], got_ref[shots + s]
         g_re, g_im = complex_times(lr_ref[...], li_ref[...], p_re, p_im)
@@ -252,8 +256,15 @@
                 c = 2 * s + part
                 c_ref[k, c] = plane
                 sx_ref[k, pl.ds(c, 1), :] = jnp.where(first_x, plane[-1:, :], plane[0:1, :])
-                flipped = jnp.transpose(plane)
-                sy_ref[k, pl.ds(c, 1), :] = jnp.where(first_y, flipped[-1:, :], flipped[0:1, :])
+                j = k * components + c
+                last_col = pltpu.roll(plane, (j + 1) % width_y, 1)
+                first_col = pltpu.roll(plane, j, 1) if j else plane
+                gathered = jnp.where(lanes == j, jnp.where(first_y, last_col, first_col), gathered)
+    flipped = jnp.transpose(gathered)
+    for k in range(layers):
+        for c in range(components):
+            j = k * components + c
+            sy_ref[k, pl.ds(c, 1), :] = flipped[j : j + 1, :]
 
 
 def paired_stencil_kernel(flag_ref, c_ref, gx_ref, gy_ref, o_ref):

time: 99.6 us -> 100 us (level)
  no operation moved by 1% of the time
where the time goes in v16:
time: 100 us; the launch traced here: 98 us
  waiting for transfers between devices  40.2 us (40%)
  starting transfers between devices  28.8 us (29%)
  other arithmetic  15.4 us (15%)
  Pallas kernels  6.58 us (7%)
  local copies, waits for them, and re-layouts  3.32 us (3%)
  matrix products  3.22 us (3%)
    ppermute x9, waiting for transfers between devices, exchange(): return lax.ppermute(array, 'slab', [(i, i ^ step) for i in range(count)])  36.3 us
    ppermute x9, starting transfers between devices, exchange(): return lax.ppermute(array, 'slab', [(i, i ^ step) for i in range(count)])  10.1 us
    all_to_all x1, starting transfers between devices, inject_receivers(): lax.all_to_all(send_rows, 'slab', split_axis=1, concat_axis=1, tiled=True)  9.81 us
    ppermute x1, starting transfers between devices, finish_paired(): got_y = lax.ppermute(send_y, 'py', [(0, 1), (1, 0)])  6.53 us
    pallas_call x1, Pallas kernels, finish_paired(): pl.pallas_call(last_sweep_kernel, in_specs=[smem] + [vmem] * 12, out_spec...  3.34 us
    pallas_call x1, Pallas kernels, finish_paired(): pl.pallas_call(paired_stencil_kernel, in_specs=[smem, vmem, vmem, vmem],...  3.23 us
    all_to_all x1, waiting for transfers between devices, inject_receivers(): lax.all_to_all(send_rows, 'slab', split_axis=1, concat_axis=1, tiled=True)  2.86 us
    ppermute x1, starting transfers between devices, finish_paired(): got_x = lax.ppermute(send_x, 'px', [(0, 1), (1, 0)])  2.43 us
  transfers between devices with their start and end apart: 12, of which 8 were waited for; matrix products, arithmetic and copies ran while one was open for 16% of the time, Pallas kernels for 0%

profile of v16, /device:TPU:1, one launch (start us, length us, event | category | flops | bytes accessed | tf_op | source)
XLA Modules:
  0.0 98.0 jit_solution(14775750255330237868)
XLA Ops:
  1.5 1.0 %convert_reduce_fusion = s32[512]{0:T(512)S(1)} fusion(s32[512]{0:T(512)} %bitcast.310), kind=kLoop, calls=%fused_computation.11 | loop fusion | flops 1310208 | bytes 4096 | tf_op jit(solution)/shard_map/reduce_sum | solution.py:30
  3.1 0.9 fusion.3
  4.2 0.7 reshape.253
  4.9 9.8 %all-to-all-start = ((f32[32,1,320]{2,1,0:T(1,128)}), f32[32,1,320]{2,1,0:T(1,128)S(1)}, u32[]{:S(2)}, u32[]{:S(2)}) async-start(f32[32,1,320]{2,1,0:T(1,128)} %reshape.253), calls=%async_computation | async-start | bytes 98304 | tf_op jit(solution)/shard_map/all_to_all | solution.py:44
  14.7 0.8 convert_multiply_fusion
  15.6 2.0 %sine_multiply_fusion = (f32[4,128,128]{2,1,0:T(8,128)S(1)}, f32[4,128,128]{2,1,0:T(8,128)S(1)}) fusion(f32[4,128,128]{2,1,0:T(8,128)} %param.9, f32[4,128,128]{2,1,0:T(8,128)} %param.10, f32[128,128]{1,0:T(8,128)S(1)} %convert_multiply_fusion), kind=kLoop, calls=%fused_computation.19 | loop fusion | flops 262144 | bytes 1114112 | tf_op jit(solution)/shard_map/mul | solution.py:328
  17.7 1.3 %collective-permute-start.1 = (f32[2,128,128]{2,1,0:T(8,128)S(1)}, f32[2,128,128]{2,1,0:T(8,128)S(1)}, u32[]{:S(2)}, u32[]{:S(2)}) collective-permute-start(f32[2,128,128]{2,1,0:T(8,128)S(1)} %pad_maximum_fusion.5), channel_id=1, source_target_pairs={{0,4},{4,0},{8,12},{12,8},{16,20},{20,16},{24,28},{28,24},{32,36},... | collective-permute-start | bytes 393224 | tf_op jit(solution)/shard_map/ppermute | solution.py:68
  19.0 2.9 %all-to-all-done = f32[32,1,320]{2,1,0:T(1,128)S(1)} async-done(((f32[32,1,320]{2,1,0:T(1,128)}), f32[32,1,320]{2,1,0:T(1,128)S(1)}, u32[]{:S(2)}, u32[]{:S(2)}) %all-to-all-start) | async-done | bytes 40992 | tf_op jit(solution)/shard_map/all_to_all | solution.py:44
  22.4 0.8 reduce.4
  24.4 2.4 %fusion.1 = f32[512,2,512]{2,0,1:T(8,128)S(1)} fusion(bf16[2,512,2048]{2,1,0:T(8,128)(2,1)S(1)} %bitcast.298, s32[2048]{0:T(1024)S(1)} %get-tuple-element.119), kind=kOutput, calls=%fused_computation.4 | convolution fusion | flops 2148532224 | bytes 6299648 | tf_op jit(solution)/shard_map/dot_general | solution.py:59
  27.3 1.4 %bitcast_add_fusion.f_ref = f32[4,4,128,128]{3,2,1,0:T(8,128)S(1)} fusion(f32[4,4,128,128]{3,2,1,0:T(8,128)} %param.8, f32[4,128,4,128]{3,2,1,0:T(4,128)S(1)} %add.352), kind=kLoop, calls=%fused_computation.9 | loop fusion | flops 262144 | bytes 3145728 | tf_op jit(solution)/shard_map/add | solution.py:63
  30.6 2.9 %collective-permute-done.3 = f32[2,128,128]{2,1,0:T(8,128)S(1)} collective-permute-done((f32[2,128,128]{2,1,0:T(8,128)S(1)}, f32[2,128,128]{2,1,0:T(8,128)S(1)}, u32[]{:S(2)}, u32[]{:S(2)}) %collective-permute-start.3) | collective-permute-done | bytes 131104 | tf_op jit(solution)/shard_map/ppermute | solution.py:68
  33.6 0.9 collective-permute-start.5
  34.5 6.0 %collective-permute-done = f32[8,128,128]{2,1,0:T(8,128)S(1)} collective-permute-done((f32[8,128,128]{2,1,0:T(8,128)S(1)}, f32[8,128,128]{2,1,0:T(8,128)S(1)}, u32[]{:S(2)}, u32[]{:S(2)}) %collective-permute-start) | collective-permute-done | bytes 524320 | tf_op jit(solution)/shard_map/ppermute | solution.py:68
  40.6 0.8 collective-permute-start.2
  41.6 9.5 %collective-permute-done.2 = f32[8,128,128]{2,1,0:T(8,128)S(1)} collective-permute-done((f32[8,128,128]{2,1,0:T(8,128)S(1)}, f32[8,128,128]{2,1,0:T(8,128)S(1)}, u32[]{:S(2)}, u32[]{:S(2)}) %collective-permute-start.2) | collective-permute-done | bytes 524320 | tf_op jit(solution)/shard_map/ppermute | solution.py:68
  51.3 1.2 %collective-permute-start.4 = (f32[8,128,128]{2,1,0:T(8,128)S(1)}, f32[8,128,128]{2,1,0:T(8,128)S(1)}, u32[]{:S(2)}, u32[]{:S(2)}) collective-permute-start(f32[8,128,128]{2,1,0:T(8,128)S(1)} %pad_maximum_fusion.2), channel_id=1, source_target_pairs={{0,16},{4,20},{8,24},{12,28},{16,0},{20,4},{24,8},{28,12},{32,48},... | collective-permute-start | bytes 1572872 | tf_op jit(solution)/shard_map/ppermute | solution.py:68
  52.6 1.2 %collective-permute-start.7 = (f32[2,128,128]{2,1,0:T(8,128)S(1)}, f32[2,128,128]{2,1,0:T(8,128)S(1)}, u32[]{:S(2)}, u32[]{:S(2)}) collective-permute-start(f32[2,128,128]{2,1,0:T(8,128)S(1)} %pad_maximum_fusion.8), channel_id=1, source_target_pairs={{0,32},{4,36},{8,40},{12,44},{16,48},{20,52},{24,56},{28,60},{32,0... | collective-permute-start | bytes 393224 | tf_op jit(solution)/shard_map/ppermute | solution.py:68
  53.7 8.1 %collective-permute-done.4 = f32[8,128,128]{2,1,0:T(8,128)S(1)} collective-permute-done((f32[8,128,128]{2,1,0:T(8,128)S(1)}, f32[8,128,128]{2,1,0:T(8,128)S(1)}, u32[]{:S(2)}, u32[]{:S(2)}) %collective-permute-start.4) | collective-permute-done | bytes 524320 | tf_op jit(solution)/shard_map/ppermute | solution.py:68
  62.4 0.7 fusion.14
  63.8 6.3 %collective-permute-done.6 = f32[8,128,128]{2,1,0:T(8,128)S(1)} collective-permute-done((f32[8,128,128]{2,1,0:T(8,128)S(1)}, f32[8,128,128]{2,1,0:T(8,128)S(1)}, u32[]{:S(2)}, u32[]{:S(2)}) %collective-permute-start.6) | collective-permute-done | bytes 524320 | tf_op jit(solution)/shard_map/ppermute | solution.py:68
  70.2 3.4 %collective-permute-start.8 = (f32[4,128,128]{2,1,0:T(8,128)S(1)}, f32[4,128,128]{2,1,0:T(8,128)S(1)}, u32[]{:S(2)}, u32[]{:S(2)}) collective-permute-start(f32[4,128,128]{2,1,0:T(8,128)S(1)} %pad_maximum_fusion.4), channel_id=1, source_target_pairs={{0,64},{4,68},{8,72},{12,76},{16,80},{20,84},{24,88},{28,92},{32,9... | collective-permute-start | bytes 786440 | tf_op jit(solution)/shard_map/ppermute | solution.py:68
  73.7 0.7 add_select_fusion.9.br_ref
  74.4 0.7 add_select_fusion.6.bi_ref
  75.1 0.7 add_select_fusion.3.ar_ref
  75.9 0.7 add_select_fusion.ai_ref
  76.6 3.5 %collective-permute-done.8.got_ref = f32[4,128,128]{2,1,0:T(8,128)S(1)} collective-permute-done((f32[4,128,128]{2,1,0:T(8,128)S(1)}, f32[4,128,128]{2,1,0:T(8,128)S(1)}, u32[]{:S(2)}, u32[]{:S(2)}) %collective-permute-start.8) | collective-permute-done | bytes 262176 | tf_op jit(solution)/shard_map/ppermute | solution.py:68
  80.8 3.3 %shard_map.82 = (f32[4,4,128,128]{3,2,1,0:T(8,128)}, f32[4,4,128]{2,1,0:T(4,128)}, f32[4,4,128]{2,1,0:T(4,128)}) custom-call(s32[3]{0:T(128)} %pad_add_fusion.flag_ref, f32[4,4,128,128]{3,2,1,0:T(8,128)} %copy-done, f32[4,128,128]{2,1,0:T(8,128)} %copy-done.2, f32[4,128,128]{2,1,0:T(8,128)} %copy-done.1, f32[2,128,128]{2,1,0:T(8,128)} %add_select_fusion.9.br_ref, ...), custom_call_target="tpu_custom_call" | custom-call | tf_op jit(solution)/shard_map/pallas_call | solution.py:303
  84.2 2.4 %collective-permute-start.9 = (f32[4,4,128]{2,1,0:T(4,128)}, f32[4,4,128]{2,1,0:T(4,128)S(1)}, u32[]{:S(2)}, u32[]{:S(2)}) collective-permute-start(f32[4,4,128]{2,1,0:T(4,128)} %get-tuple-element.9), channel_id=1, source_target_pairs={{0,2},{2,0},{1,3},{3,1},{4,6},{6,4},{5,7},{7,5},{8,10},{10,8},{9,1... | collective-permute-start | bytes 24584 | tf_op jit(solution)/shard_map/ppermute | solution.py:309
  86.6 6.5 %collective-permute-start.10 = (f32[4,4,128]{2,1,0:T(4,128)}, f32[4,4,128]{2,1,0:T(4,128)S(1)}, u32[]{:S(2)}, u32[]{:S(2)}) collective-permute-start(f32[4,4,128]{2,1,0:T(4,128)} %get-tuple-element.10), channel_id=1, source_target_pairs={{0,1},{1,0},{2,3},{3,2},{4,5},{5,4},{6,7},{7,6},{8,9},{9,8},{10,11... | collective-permute-start | bytes 24584 | tf_op jit(solution)/shard_map/ppermute | solution.py:310
  93.1 1.0 %collective-permute-done.10.gy_ref = f32[4,4,128]{2,1,0:T(4,128)S(1)} collective-permute-done((f32[4,4,128]{2,1,0:T(4,128)}, f32[4,4,128]{2,1,0:T(4,128)S(1)}, u32[]{:S(2)}, u32[]{:S(2)}) %collective-permute-start.10) | collective-permute-done | bytes 8224 | tf_op jit(solution)/shard_map/ppermute | solution.py:310
  94.8 3.2 %shard_map.83 = f32[4,4,128,128]{3,2,1,0:T(8,128)} custom-call(s32[3]{0:T(128)} %pad_add_fusion.flag_ref, f32[4,4,128,128]{3,2,1,0:T(8,128)} %get-tuple-element.8.c_ref, f32[4,4,128]{2,1,0:T(4,128)} %copy-done.4, f32[4,4,128]{2,1,0:T(4,128)} %copy-done.5), custom_call_target="tpu_custom_call" | custom-call | tf_op jit(solution)/shard_map/pallas_call | solution.py:311
  (71 shorter events, 9.7 us)
Async XLA Ops:
  4.9 17.0 %all-to-all-start = ((f32[32,1,320]{2,1,0:T(1,128)}), f32[32,1,320]{2,1,0:T(1,128)S(1)}, u32[]{:S(2)}, u32[]{:S(2)}) async-start(f32[32,1,320]{2,1,0:T(1,128)} %reshape.253), calls=%async_computation | async-start | bytes 98304 | tf_op jit(solution)/shard_map/all_to_all | solution.py:44
  17.6 9.2 %copy-start.1 = (f32[4,128,128]{2,1,0:T(8,128)}, f32[4,128,128]{2,1,0:T(8,128)S(1)}, u32[]{:S(2)}) copy-start(f32[4,128,128]{2,1,0:T(8,128)S(1)} %get-tuple-element.57.ri_ref) | copy-start | bytes 786436
  17.6 9.2 %copy-start.2 = (f32[4,128,128]{2,1,0:T(8,128)}, f32[4,128,128]{2,1,0:T(8,128)S(1)}, u32[]{:S(2)}) copy-start(f32[4,128,128]{2,1,0:T(8,128)S(1)} %get-tuple-element.58.rr_ref) | copy-start | bytes 786436
  17.7 11.9 %collective-permute-start.1 = (f32[2,128,128]{2,1,0:T(8,128)S(1)}, f32[2,128,128]{2,1,0:T(8,128)S(1)}, u32[]{:S(2)}, u32[]{:S(2)}) collective-permute-start(f32[2,128,128]{2,1,0:T(8,128)S(1)} %pad_maximum_fusion.5), channel_id=1, source_target_pairs={{0,4},{4,0},{8,12},{12,8},{16,20},{20,16},{24,28},{28,24},{32,36},... | collective-permute-start | bytes 393224 | tf_op jit(solution)/shard_map/ppermute | solution.py:68
  28.7 11.9 %copy-start = (f32[4,4,128,128]{3,2,1,0:T(8,128)}, f32[4,4,128,128]{3,2,1,0:T(8,128)S(1)}, u32[]{:S(2)}) copy-start(f32[4,4,128,128]{3,2,1,0:T(8,128)S(1)} %bitcast_add_fusion.f_ref) | copy-start | bytes 3145732
  29.0 11.4 %collective-permute-start = (f32[8,128,128]{2,1,0:T(8,128)S(1)}, f32[8,128,128]{2,1,0:T(8,128)S(1)}, u32[]{:S(2)}, u32[]{:S(2)}) collective-permute-start(f32[8,128,128]{2,1,0:T(8,128)S(1)} %pad_maximum_fusion), channel_id=1, source_target_pairs={{0,4},{4,0},{8,12},{12,8},{16,20},{20,16},{24,28},{28,24},{32,36},... | collective-permute-start | bytes 1572872 | tf_op jit(solution)/shard_map/ppermute | solution.py:68
  29.6 3.9 %collective-permute-start.3 = (f32[2,128,128]{2,1,0:T(8,128)S(1)}, f32[2,128,128]{2,1,0:T(8,128)S(1)}, u32[]{:S(2)}, u32[]{:S(2)}) collective-permute-start(f32[2,128,128]{2,1,0:T(8,128)S(1)} %pad_maximum_fusion.6), channel_id=1, source_target_pairs={{0,8},{4,12},{8,0},{12,4},{16,24},{20,28},{24,16},{28,20},{32,40},... | collective-permute-start | bytes 393224 | tf_op jit(solution)/shard_map/ppermute | solution.py:68
  33.6 8.0 %collective-permute-start.5 = (f32[2,128,128]{2,1,0:T(8,128)S(1)}, f32[2,128,128]{2,1,0:T(8,128)S(1)}, u32[]{:S(2)}, u32[]{:S(2)}) collective-permute-start(f32[2,128,128]{2,1,0:T(8,128)S(1)} %pad_maximum_fusion.7), channel_id=1, source_target_pairs={{0,16},{4,20},{8,24},{12,28},{16,0},{20,4},{24,8},{28,12},{32,48},... | collective-permute-start | bytes 393224 | tf_op jit(solution)/shard_map/ppermute | solution.py:68
  40.6 10.5 %collective-permute-start.2 = (f32[8,128,128]{2,1,0:T(8,128)S(1)}, f32[8,128,128]{2,1,0:T(8,128)S(1)}, u32[]{:S(2)}, u32[]{:S(2)}) collective-permute-start(f32[8,128,128]{2,1,0:T(8,128)S(1)} %pad_maximum_fusion.1), channel_id=1, source_target_pairs={{0,8},{4,12},{8,0},{12,4},{16,24},{20,28},{24,16},{28,20},{32,40},... | collective-permute-start | bytes 1572872 | tf_op jit(solution)/shard_map/ppermute | solution.py:68
  51.3 10.5 %collective-permute-start.4 = (f32[8,128,128]{2,1,0:T(8,128)S(1)}, f32[8,128,128]{2,1,0:T(8,128)S(1)}, u32[]{:S(2)}, u32[]{:S(2)}) collective-permute-start(f32[8,128,128]{2,1,0:T(8,128)S(1)} %pad_maximum_fusion.2), channel_id=1, source_target_pairs={{0,16},{4,20},{8,24},{12,28},{16,0},{20,4},{24,8},{28,12},{32,48},... | collective-permute-start | bytes 1572872 | tf_op jit(solution)/shard_map/ppermute | solution.py:68
  52.6 9.8 %collective-permute-start.7 = (f32[2,128,128]{2,1,0:T(8,128)S(1)}, f32[2,128,128]{2,1,0:T(8,128)S(1)}, u32[]{:S(2)}, u32[]{:S(2)}) collective-permute-start(f32[2,128,128]{2,1,0:T(8,128)S(1)} %pad_maximum_fusion.8), channel_id=1, source_target_pairs={{0,32},{4,36},{8,40},{12,44},{16,48},{20,52},{24,56},{28,60},{32,0... | collective-permute-start | bytes 393224 | tf_op jit(solution)/shard_map/ppermute | solution.py:68
  62.0 8.1 %collective-permute-start.6 = (f32[8,128,128]{2,1,0:T(8,128)S(1)}, f32[8,128,128]{2,1,0:T(8,128)S(1)}, u32[]{:S(2)}, u32[]{:S(2)}) collective-permute-start(f32[8,128,128]{2,1,0:T(8,128)S(1)} %pad_maximum_fusion.3), channel_id=1, source_target_pairs={{0,32},{4,36},{8,40},{12,44},{16,48},{20,52},{24,56},{28,60},{32,0... | collective-permute-start | bytes 1572872 | tf_op jit(solution)/shard_map/ppermute | solution.py:68
  70.2 9.8 %collective-permute-start.8 = (f32[4,128,128]{2,1,0:T(8,128)S(1)}, f32[4,128,128]{2,1,0:T(8,128)S(1)}, u32[]{:S(2)}, u32[]{:S(2)}) collective-permute-start(f32[4,128,128]{2,1,0:T(8,128)S(1)} %pad_maximum_fusion.4), channel_id=1, source_target_pairs={{0,64},{4,68},{8,72},{12,76},{16,80},{20,84},{24,88},{28,92},{32,9... | collective-permute-start | bytes 786440 | tf_op jit(solution)/shard_map/ppermute | solution.py:68
  80.1 0.7 copy-start.3
  84.2 9.0 %collective-permute-start.9 = (f32[4,4,128]{2,1,0:T(4,128)}, f32[4,4,128]{2,1,0:T(4,128)S(1)}, u32[]{:S(2)}, u32[]{:S(2)}) collective-permute-start(f32[4,4,128]{2,1,0:T(4,128)} %get-tuple-element.9), channel_id=1, source_target_pairs={{0,2},{2,0},{1,3},{3,1},{4,6},{6,4},{5,7},{7,5},{8,10},{10,8},{9,1... | collective-permute-start | bytes 24584 | tf_op jit(solution)/shard_map/ppermute | solution.py:309
  86.6 7.6 %collective-permute-start.10 = (f32[4,4,128]{2,1,0:T(4,128)}, f32[4,4,128]{2,1,0:T(4,128)S(1)}, u32[]{:S(2)}, u32[]{:S(2)}) collective-permute-start(f32[4,4,128]{2,1,0:T(4,128)} %get-tuple-element.10), channel_id=1, source_target_pairs={{0,1},{1,0},{2,3},{3,2},{4,5},{5,4},{6,7},{7,6},{8,9},{9,8},{10,11... | collective-permute-start | bytes 24584 | tf_op jit(solution)/shard_map/ppermute | solution.py:310
  93.1 1.0 %copy-start.4 = (f32[4,4,128]{2,1,0:T(4,128)}, f32[4,4,128]{2,1,0:T(4,128)S(1)}, u32[]{:S(2)}) copy-start(f32[4,4,128]{2,1,0:T(4,128)S(1)} %collective-permute-done.9.gx_ref) | copy-start | bytes 24580
  94.2 0.6 copy-start.5

commit v17 on v16

--- a/solution.py
+++ b/solution.py
@@ -267,27 +267,31 @@
             sy_ref[k, pl.ds(c, 1), :] = flipped[j : j + 1, :]
 
 
-def paired_stencil_kernel(flag_ref, c_ref, gx_ref, gy_ref, o_ref):
+def paired_stencil_kernel(flag_ref, c_ref, gx_ref, gy_ref, o_ref, pack_ref):
     layers, components, width_x, width_y = c_ref.shape
     rows = lax.broadcasted_iota(jnp.int32, (width_x, width_y), 0)
     cols = lax.broadcasted_iota(jnp.int32, (width_x, width_y), 1)
-    side_rows = lax.broadcasted_iota(jnp.int32, (width_y, width_x), 0)
     first_x = flag_ref[1] == 0
     first_y = flag_ref[2] == 0
+    pack_ref[...] = jnp.zeros_like(pack_ref)
+    for k in range(layers):
+        pack_ref[pl.ds(k * components, components), :] = gy_ref[k]
+    columns = jnp.transpose(pack_ref[...])
     for k in range(layers):
         for c in range(components):
+            j = k * components + c
             plane = c_ref[k, c]
             edge_x = gx_ref[k, pl.ds(c, 1), :]
-            edge_y = jnp.broadcast_to(gy_ref[k, pl.ds(c, 1), :], (width_y, width_x))
             none_x = jnp.zeros_like(edge_x)
             low_x = jnp.broadcast_to(jnp.where(first_x, none_x, edge_x), (width_x, width_y))
             high_x = jnp.broadcast_to(jnp.where(first_x, edge_x, none_x), (width_x, width_y))
-            side = jnp.where(side_rows == jnp.where(first_y, width_y - 1, 0), edge_y, 0.0)
+            edge_y = jnp.broadcast_to(columns[:, j : j + 1], (width_x, width_y))
+            side = jnp.where(cols == jnp.where(first_y, width_y - 1, 0), edge_y, 0.0)
             next_x = jnp.where(rows == width_x - 1, high_x, pltpu.roll(plane, width_x - 1, 0))
             prev_x = jnp.where(rows == 0, low_x, pltpu.roll(plane, 1, 0))
             next_y = jnp.where(cols == width_y - 1, 0.0, pltpu.roll(plane, width_y - 1, 1))
             prev_y = jnp.where(cols == 0, 0.0, pltpu.roll(plane, 1, 1))
-            neighbours = next_x + prev_x + next_y + prev_y + jnp.transpose(side)
+            neighbours = next_x + prev_x + next_y + prev_y + side
             o_ref[k, c] = plane - 0.2 * (4.0 * plane - neighbours)
 
 
@@ -313,6 +317,7 @@
         in_specs=[smem, vmem, vmem, vmem],
         out_specs=vmem,
         out_shape=jax.ShapeDtypeStruct(fields.shape, jnp.float32),
+        scratch_shapes=[pltpu.VMEM((width_y, width_x), jnp.float32)],
     )(flags, combined, got_x, got_y)
 
 

time: 100 us -> 100 us (level)
  no operation moved by 1% of the time
where the time goes in v17:
time: 100 us; the launch traced here: 98 us
  waiting for transfers between devices  40.2 us (40%)
  starting transfers between devices  28.8 us (29%)
  other arithmetic  15.4 us (15%)
  Pallas kernels  6.57 us (7%)
  local copies, waits for them, and re-layouts  3.32 us (3%)
  matrix products  3.22 us (3%)
    ppermute x9, waiting for transfers between devices, exchange(): return lax.ppermute(array, 'slab', [(i, i ^ step) for i in range(count)])  36.3 us
    ppermute x9, starting transfers between devices, exchange(): return lax.ppermute(array, 'slab', [(i, i ^ step) for i in range(count)])  10.1 us
    all_to_all x1, starting transfers between devices, inject_receivers(): lax.all_to_all(send_rows, 'slab', split_axis=1, concat_axis=1, tiled=True)  9.81 us
    ppermute x1, starting transfers between devices, finish_paired(): got_y = lax.ppermute(send_y, 'py', [(0, 1), (1, 0)])  6.53 us
    pallas_call x1, Pallas kernels, finish_paired(): pl.pallas_call(last_sweep_kernel, in_specs=[smem] + [vmem] * 12, out_spec...  3.34 us
    pallas_call x1, Pallas kernels, finish_paired(): pl.pallas_call(paired_stencil_kernel, in_specs=[smem, vmem, vmem, vmem],...  3.23 us
    all_to_all x1, waiting for transfers between devices, inject_receivers(): lax.all_to_all(send_rows, 'slab', split_axis=1, concat_axis=1, tiled=True)  2.86 us
    ppermute x1, starting transfers between devices, finish_paired(): got_x = lax.ppermute(send_x, 'px', [(0, 1), (1, 0)])  2.43 us
  transfers between devices with their start and end apart: 12, of which 8 were waited for; matrix products, arithmetic and copies ran while one was open for 16% of the time, Pallas kernels for 0%

profile of v17, /device:TPU:1, one launch (start us, length us, event | category | flops | bytes accessed | tf_op | source)
XLA Modules:
  0.0 98.0 jit_solution(5435673320821250925)
XLA Ops:
  1.5 1.0 %convert_reduce_fusion = s32[512]{0:T(512)S(1)} fusion(s32[512]{0:T(512)} %bitcast.310), kind=kLoop, calls=%fused_computation.11 | loop fusion | flops 1310208 | bytes 4096 | tf_op jit(solution)/shard_map/reduce_sum | solution.py:30
  3.1 0.9 fusion.3
  4.2 0.7 reshape.253
  4.9 9.8 %all-to-all-start = ((f32[32,1,320]{2,1,0:T(1,128)}), f32[32,1,320]{2,1,0:T(1,128)S(1)}, u32[]{:S(2)}, u32[]{:S(2)}) async-start(f32[32,1,320]{2,1,0:T(1,128)} %reshape.253), calls=%async_computation | async-start | bytes 98304 | tf_op jit(solution)/shard_map/all_to_all | solution.py:44
  14.7 0.8 convert_multiply_fusion
  15.6 2.0 %sine_multiply_fusion = (f32[4,128,128]{2,1,0:T(8,128)S(1)}, f32[4,128,128]{2,1,0:T(8,128)S(1)}) fusion(f32[4,128,128]{2,1,0:T(8,128)} %param.9, f32[4,128,128]{2,1,0:T(8,128)} %param.10, f32[128,128]{1,0:T(8,128)S(1)} %convert_multiply_fusion), kind=kLoop, calls=%fused_computation.19 | loop fusion | flops 262144 | bytes 1114112 | tf_op jit(solution)/shard_map/mul | solution.py:333
  17.7 1.3 %collective-permute-start.1 = (f32[2,128,128]{2,1,0:T(8,128)S(1)}, f32[2,128,128]{2,1,0:T(8,128)S(1)}, u32[]{:S(2)}, u32[]{:S(2)}) collective-permute-start(f32[2,128,128]{2,1,0:T(8,128)S(1)} %pad_maximum_fusion.5), channel_id=1, source_target_pairs={{0,4},{4,0},{8,12},{12,8},{16,20},{20,16},{24,28},{28,24},{32,36},... | collective-permute-start | bytes 393224 | tf_op jit(solution)/shard_map/ppermute | solution.py:68
  19.0 2.9 %all-to-all-done = f32[32,1,320]{2,1,0:T(1,128)S(1)} async-done(((f32[32,1,320]{2,1,0:T(1,128)}), f32[32,1,320]{2,1,0:T(1,128)S(1)}, u32[]{:S(2)}, u32[]{:S(2)}) %all-to-all-start) | async-done | bytes 40992 | tf_op jit(solution)/shard_map/all_to_all | solution.py:44
  22.4 0.8 reduce.4
  24.4 2.4 %fusion.1 = f32[512,2,512]{2,0,1:T(8,128)S(1)} fusion(bf16[2,512,2048]{2,1,0:T(8,128)(2,1)S(1)} %bitcast.298, s32[2048]{0:T(1024)S(1)} %get-tuple-element.119), kind=kOutput, calls=%fused_computation.4 | convolution fusion | flops 2148532224 | bytes 6299648 | tf_op jit(solution)/shard_map/dot_general | solution.py:59
  27.3 1.4 %bitcast_add_fusion.f_ref = f32[4,4,128,128]{3,2,1,0:T(8,128)S(1)} fusion(f32[4,4,128,128]{3,2,1,0:T(8,128)} %param.8, f32[4,128,4,128]{3,2,1,0:T(4,128)S(1)} %add.352), kind=kLoop, calls=%fused_computation.9 | loop fusion | flops 262144 | bytes 3145728 | tf_op jit(solution)/shard_map/add | solution.py:63
  30.6 2.9 %collective-permute-done.3 = f32[2,128,128]{2,1,0:T(8,128)S(1)} collective-permute-done((f32[2,128,128]{2,1,0:T(8,128)S(1)}, f32[2,128,128]{2,1,0:T(8,128)S(1)}, u32[]{:S(2)}, u32[]{:S(2)}) %collective-permute-start.3) | collective-permute-done | bytes 131104 | tf_op jit(solution)/shard_map/ppermute | solution.py:68
  33.6 0.9 collective-permute-start.5
  34.5 6.0 %collective-permute-done = f32[8,128,128]{2,1,0:T(8,128)S(1)} collective-permute-done((f32[8,128,128]{2,1,0:T(8,128)S(1)}, f32[8,128,128]{2,1,0:T(8,128)S(1)}, u32[]{:S(2)}, u32[]{:S(2)}) %collective-permute-start) | collective-permute-done | bytes 524320 | tf_op jit(solution)/shard_map/ppermute | solution.py:68
  40.6 0.8 collective-permute-start.2
  41.6 9.5 %collective-permute-done.2 = f32[8,128,128]{2,1,0:T(8,128)S(1)} collective-permute-done((f32[8,128,128]{2,1,0:T(8,128)S(1)}, f32[8,128,128]{2,1,0:T(8,128)S(1)}, u32[]{:S(2)}, u32[]{:S(2)}) %collective-permute-start.2) | collective-permute-done | bytes 524320 | tf_op jit(solution)/shard_map/ppermute | solution.py:68
  51.3 1.2 %collective-permute-start.4 = (f32[8,128,128]{2,1,0:T(8,128)S(1)}, f32[8,128,128]{2,1,0:T(8,128)S(1)}, u32[]{:S(2)}, u32[]{:S(2)}) collective-permute-start(f32[8,128,128]{2,1,0:T(8,128)S(1)} %pad_maximum_fusion.2), channel_id=1, source_target_pairs={{0,16},{4,20},{8,24},{12,28},{16,0},{20,4},{24,8},{28,12},{32,48},... | collective-permute-start | bytes 1572872 | tf_op jit(solution)/shard_map/ppermute | solution.py:68
  52.6 1.2 %collective-permute-start.7 = (f32[2,128,128]{2,1,0:T(8,128)S(1)}, f32[2,128,128]{2,1,0:T(8,128)S(1)}, u32[]{:S(2)}, u32[]{:S(2)}) collective-permute-start(f32[2,128,128]{2,1,0:T(8,128)S(1)} %pad_maximum_fusion.8), channel_id=1, source_target_pairs={{0,32},{4,36},{8,40},{12,44},{16,48},{20,52},{24,56},{28,60},{32,0... | collective-permute-start | bytes 393224 | tf_op jit(solution)/shard_map/ppermute | solution.py:68
  53.7 8.1 %collective-permute-done.4 = f32[8,128,128]{2,1,0:T(8,128)S(1)} collective-permute-done((f32[8,128,128]{2,1,0:T(8,128)S(1)}, f32[8,128,128]{2,1,0:T(8,128)S(1)}, u32[]{:S(2)}, u32[]{:S(2)}) %collective-permute-start.4) | collective-permute-done | bytes 524320 | tf_op jit(solution)/shard_map/ppermute | solution.py:68
  62.4 0.7 fusion.14
  63.8 6.3 %collective-permute-done.6 = f32[8,128,128]{2,1,0:T(8,128)S(1)} collective-permute-done((f32[8,128,128]{2,1,0:T(8,128)S(1)}, f32[8,128,128]{2,1,0:T(8,128)S(1)}, u32[]{:S(2)}, u32[]{:S(2)}) %collective-permute-start.6) | collective-permute-done | bytes 524320 | tf_op jit(solution)/shard_map/ppermute | solution.py:68
  70.2 3.4 %collective-permute-start.8 = (f32[4,128,128]{2,1,0:T(8,128)S(1)}, f32[4,128,128]{2,1,0:T(8,128)S(1)}, u32[]{:S(2)}, u32[]{:S(2)}) collective-permute-start(f32[4,128,128]{2,1,0:T(8,128)S(1)} %pad_maximum_fusion.4), channel_id=1, source_target_pairs={{0,64},{4,68},{8,72},{12,76},{16,80},{20,84},{24,88},{28,92},{32,9... | collective-permute-start | bytes 786440 | tf_op jit(solution)/shard_map/ppermute | solution.py:68
  73.7 0.7 add_select_fusion.9.br_ref
  74.4 0.7 add_select_fusion.6.bi_ref
  75.1 0.7 add_select_fusion.3.ar_ref
  75.9 0.7 add_select_fusion.ai_ref
  76.6 3.5 %collective-permute-done.8.got_ref = f32[4,128,128]{2,1,0:T(8,128)S(1)} collective-permute-done((f32[4,128,128]{2,1,0:T(8,128)S(1)}, f32[4,128,128]{2,1,0:T(8,128)S(1)}, u32[]{:S(2)}, u32[]{:S(2)}) %collective-permute-start.8) | collective-permute-done | bytes 262176 | tf_op jit(solution)/shard_map/ppermute | solution.py:68
  80.8 3.3 %shard_map.82 = (f32[4,4,128,128]{3,2,1,0:T(8,128)}, f32[4,4,128]{2,1,0:T(4,128)}, f32[4,4,128]{2,1,0:T(4,128)}) custom-call(s32[3]{0:T(128)} %pad_add_fusion.flag_ref, f32[4,4,128,128]{3,2,1,0:T(8,128)} %copy-done, f32[4,128,128]{2,1,0:T(8,128)} %copy-done.2, f32[4,128,128]{2,1,0:T(8,128)} %copy-done.1, f32[2,128,128]{2,1,0:T(8,128)} %add_select_fusion.9.br_ref, ...), custom_call_target="tpu_custom_call" | custom-call | tf_op jit(solution)/shard_map/pallas_call | solution.py:307
  84.2 2.4 %collective-permute-start.9 = (f32[4,4,128]{2,1,0:T(4,128)}, f32[4,4,128]{2,1,0:T(4,128)S(1)}, u32[]{:S(2)}, u32[]{:S(2)}) collective-permute-start(f32[4,4,128]{2,1,0:T(4,128)} %get-tuple-element.9), channel_id=1, source_target_pairs={{0,2},{2,0},{1,3},{3,1},{4,6},{6,4},{5,7},{7,5},{8,10},{10,8},{9,1... | collective-permute-start | bytes 24584 | tf_op jit(solution)/shard_map/ppermute | solution.py:313
  86.6 6.5 %collective-permute-start.10 = (f32[4,4,128]{2,1,0:T(4,128)}, f32[4,4,128]{2,1,0:T(4,128)S(1)}, u32[]{:S(2)}, u32[]{:S(2)}) collective-permute-start(f32[4,4,128]{2,1,0:T(4,128)} %get-tuple-element.10), channel_id=1, source_target_pairs={{0,1},{1,0},{2,3},{3,2},{4,5},{5,4},{6,7},{7,6},{8,9},{9,8},{10,11... | collective-permute-start | bytes 24584 | tf_op jit(solution)/shard_map/ppermute | solution.py:314
  93.1 1.0 %collective-permute-done.10.gy_ref = f32[4,4,128]{2,1,0:T(4,128)S(1)} collective-permute-done((f32[4,4,128]{2,1,0:T(4,128)}, f32[4,4,128]{2,1,0:T(4,128)S(1)}, u32[]{:S(2)}, u32[]{:S(2)}) %collective-permute-start.10) | collective-permute-done | bytes 8224 | tf_op jit(solution)/shard_map/ppermute | solution.py:314
  94.8 3.2 %shard_map.83 = f32[4,4,128,128]{3,2,1,0:T(8,128)} custom-call(s32[3]{0:T(128)} %pad_add_fusion.flag_ref, f32[4,4,128,128]{3,2,1,0:T(8,128)} %get-tuple-element.8.c_ref, f32[4,4,128]{2,1,0:T(4,128)} %copy-done.4, f32[4,4,128]{2,1,0:T(4,128)} %copy-done.5), custom_call_target="tpu_custom_call" | custom-call | tf_op jit(solution)/shard_map/pallas_call | solution.py:315
  (71 shorter events, 9.7 us)
Async XLA Ops:
  4.9 17.0 %all-to-all-start = ((f32[32,1,320]{2,1,0:T(1,128)}), f32[32,1,320]{2,1,0:T(1,128)S(1)}, u32[]{:S(2)}, u32[]{:S(2)}) async-start(f32[32,1,320]{2,1,0:T(1,128)} %reshape.253), calls=%async_computation | async-start | bytes 98304 | tf_op jit(solution)/shard_map/all_to_all | solution.py:44
  17.6 9.2 %copy-start.1 = (f32[4,128,128]{2,1,0:T(8,128)}, f32[4,128,128]{2,1,0:T(8,128)S(1)}, u32[]{:S(2)}) copy-start(f32[4,128,128]{2,1,0:T(8,128)S(1)} %get-tuple-element.57.ri_ref) | copy-start | bytes 786436
  17.6 9.2 %copy-start.2 = (f32[4,128,128]{2,1,0:T(8,128)}, f32[4,128,128]{2,1,0:T(8,128)S(1)}, u32[]{:S(2)}) copy-start(f32[4,128,128]{2,1,0:T(8,128)S(1)} %get-tuple-element.58.rr_ref) | copy-start | bytes 786436
  17.7 11.9 %collective-permute-start.1 = (f32[2,128,128]{2,1,0:T(8,128)S(1)}, f32[2,128,128]{2,1,0:T(8,128)S(1)}, u32[]{:S(2)}, u32[]{:S(2)}) collective-permute-start(f32[2,128,128]{2,1,0:T(8,128)S(1)} %pad_maximum_fusion.5), channel_id=1, source_target_pairs={{0,4},{4,0},{8,12},{12,8},{16,20},{20,16},{24,28},{28,24},{32,36},... | collective-permute-start | bytes 393224 | tf_op jit(solution)/shard_map/ppermute | solution.py:68
  28.7 11.9 %copy-start = (f32[4,4,128,128]{3,2,1,0:T(8,128)}, f32[4,4,128,128]{3,2,1,0:T(8,128)S(1)}, u32[]{:S(2)}) copy-start(f32[4,4,128,128]{3,2,1,0:T(8,128)S(1)} %bitcast_add_fusion.f_ref) | copy-start | bytes 3145732
  29.0 11.4 %collective-permute-start = (f32[8,128,128]{2,1,0:T(8,128)S(1)}, f32[8,128,128]{2,1,0:T(8,128)S(1)}, u32[]{:S(2)}, u32[]{:S(2)}) collective-permute-start(f32[8,128,128]{2,1,0:T(8,128)S(1)} %pad_maximum_fusion), channel_id=1, source_target_pairs={{0,4},{4,0},{8,12},{12,8},{16,20},{20,16},{24,28},{28,24},{32,36},... | collective-permute-start | bytes 1572872 | tf_op jit(solution)/shard_map/ppermute | solution.py:68
  29.6 3.9 %collective-permute-start.3 = (f32[2,128,128]{2,1,0:T(8,128)S(1)}, f32[2,128,128]{2,1,0:T(8,128)S(1)}, u32[]{:S(2)}, u32[]{:S(2)}) collective-permute-start(f32[2,128,128]{2,1,0:T(8,128)S(1)} %pad_maximum_fusion.6), channel_id=1, source_target_pairs={{0,8},{4,12},{8,0},{12,4},{16,24},{20,28},{24,16},{28,20},{32,40},... | collective-permute-start | bytes 393224 | tf_op jit(solution)/shard_map/ppermute | solution.py:68
  33.6 8.0 %collective-permute-start.5 = (f32[2,128,128]{2,1,0:T(8,128)S(1)}, f32[2,128,128]{2,1,0:T(8,128)S(1)}, u32[]{:S(2)}, u32[]{:S(2)}) collective-permute-start(f32[2,128,128]{2,1,0:T(8,128)S(1)} %pad_maximum_fusion.7), channel_id=1, source_target_pairs={{0,16},{4,20},{8,24},{12,28},{16,0},{20,4},{24,8},{28,12},{32,48},... | collective-permute-start | bytes 393224 | tf_op jit(solution)/shard_map/ppermute | solution.py:68
  40.6 10.5 %collective-permute-start.2 = (f32[8,128,128]{2,1,0:T(8,128)S(1)}, f32[8,128,128]{2,1,0:T(8,128)S(1)}, u32[]{:S(2)}, u32[]{:S(2)}) collective-permute-start(f32[8,128,128]{2,1,0:T(8,128)S(1)} %pad_maximum_fusion.1), channel_id=1, source_target_pairs={{0,8},{4,12},{8,0},{12,4},{16,24},{20,28},{24,16},{28,20},{32,40},... | collective-permute-start | bytes 1572872 | tf_op jit(solution)/shard_map/ppermute | solution.py:68
  51.3 10.5 %collective-permute-start.4 = (f32[8,128,128]{2,1,0:T(8,128)S(1)}, f32[8,128,128]{2,1,0:T(8,128)S(1)}, u32[]{:S(2)}, u32[]{:S(2)}) collective-permute-start(f32[8,128,128]{2,1,0:T(8,128)S(1)} %pad_maximum_fusion.2), channel_id=1, source_target_pairs={{0,16},{4,20},{8,24},{12,28},{16,0},{20,4},{24,8},{28,12},{32,48},... | collective-permute-start | bytes 1572872 | tf_op jit(solution)/shard_map/ppermute | solution.py:68
  52.6 9.8 %collective-permute-start.7 = (f32[2,128,128]{2,1,0:T(8,128)S(1)}, f32[2,128,128]{2,1,0:T(8,128)S(1)}, u32[]{:S(2)}, u32[]{:S(2)}) collective-permute-start(f32[2,128,128]{2,1,0:T(8,128)S(1)} %pad_maximum_fusion.8), channel_id=1, source_target_pairs={{0,32},{4,36},{8,40},{12,44},{16,48},{20,52},{24,56},{28,60},{32,0... | collective-permute-start | bytes 393224 | tf_op jit(solution)/shard_map/ppermute | solution.py:68
  62.0 8.1 %collective-permute-start.6 = (f32[8,128,128]{2,1,0:T(8,128)S(1)}, f32[8,128,128]{2,1,0:T(8,128)S(1)}, u32[]{:S(2)}, u32[]{:S(2)}) collective-permute-start(f32[8,128,128]{2,1,0:T(8,128)S(1)} %pad_maximum_fusion.3), channel_id=1, source_target_pairs={{0,32},{4,36},{8,40},{12,44},{16,48},{20,52},{24,56},{28,60},{32,0... | collective-permute-start | bytes 1572872 | tf_op jit(solution)/shard_map/ppermute | solution.py:68
  70.2 9.8 %collective-permute-start.8 = (f32[4,128,128]{2,1,0:T(8,128)S(1)}, f32[4,128,128]{2,1,0:T(8,128)S(1)}, u32[]{:S(2)}, u32[]{:S(2)}) collective-permute-start(f32[4,128,128]{2,1,0:T(8,128)S(1)} %pad_maximum_fusion.4), channel_id=1, source_target_pairs={{0,64},{4,68},{8,72},{12,76},{16,80},{20,84},{24,88},{28,92},{32,9... | collective-permute-start | bytes 786440 | tf_op jit(solution)/shard_map/ppermute | solution.py:68
  80.1 0.7 copy-start.3
  84.2 9.0 %collective-permute-start.9 = (f32[4,4,128]{2,1,0:T(4,128)}, f32[4,4,128]{2,1,0:T(4,128)S(1)}, u32[]{:S(2)}, u32[]{:S(2)}) collective-permute-start(f32[4,4,128]{2,1,0:T(4,128)} %get-tuple-element.9), channel_id=1, source_target_pairs={{0,2},{2,0},{1,3},{3,1},{4,6},{6,4},{5,7},{7,5},{8,10},{10,8},{9,1... | collective-permute-start | bytes 24584 | tf_op jit(solution)/shard_map/ppermute | solution.py:313
  86.6 7.6 %collective-permute-start.10 = (f32[4,4,128]{2,1,0:T(4,128)}, f32[4,4,128]{2,1,0:T(4,128)S(1)}, u32[]{:S(2)}, u32[]{:S(2)}) collective-permute-start(f32[4,4,128]{2,1,0:T(4,128)} %get-tuple-element.10), channel_id=1, source_target_pairs={{0,1},{1,0},{2,3},{3,2},{4,5},{5,4},{6,7},{7,6},{8,9},{9,8},{10,11... | collective-permute-start | bytes 24584 | tf_op jit(solution)/shard_map/ppermute | solution.py:314
  93.1 1.0 %copy-start.4 = (f32[4,4,128]{2,1,0:T(4,128)}, f32[4,4,128]{2,1,0:T(4,128)S(1)}, u32[]{:S(2)}) copy-start(f32[4,4,128]{2,1,0:T(4,128)S(1)} %collective-permute-done.9.gx_ref) | copy-start | bytes 24580
  94.2 0.6 copy-start.5

commit v18 on v17

--- a/solution.py
+++ b/solution.py
@@ -60,7 +60,7 @@
     added = added.reshape(layers * width_x, 2, components * width_y)
     added = added[:, 0] + added[:, 1]
     added = jnp.transpose(added.reshape(layers, width_x, components, width_y), (0, 2, 1, 3))
-    return source + added, levels
+    return source + added, levels, added
 
 
 def exchange(array, step):
@@ -337,27 +337,33 @@
         prod_down.append(complex_times(rate_re[k], rate_im[k], *prod_down[-1]))
     levels = block_products(*prod_down[-1])
 
-    forcing, levels = inject_receivers(
+    forcing, levels, added = inject_receivers(
         source, recv_values, recv_slab, recv_lateral, recv_layer, levels
     )
     fields = forcing.reshape(layers, shot_count, 2, width_x, width_y)
     f_re = fields[:, :, 0]
     f_im = fields[:, :, 1]
 
+    def local_ends(planes):
+        p = planes.reshape(layers, shot_count, 2, width_x, width_y)
+        p_re, p_im = p[:, :, 0], p[:, :, 1]
+        state = (p_re[0], p_im[0])
+        for k in range(1, layers):
+            t_re, t_im = complex_times(rate_re[k][None], rate_im[k][None], *state)
+            state = (t_re + p_re[k], t_im + p_im[k])
+        last_down = state
+        state = (p_re[layers - 1], p_im[layers - 1])
+        for k in range(layers - 2, -1, -1):
+            t_re, t_im = complex_times(rate_re[k][None], rate_im[k][None], *state)
+            state = (t_re + p_re[k], t_im + p_im[k])
+        return last_down, state
+
+    src_down, src_up = local_ends(source)
+    add_down, add_up = local_ends(added)
     down = [None] * layers
-    state = (f_re[0], f_im[0])
-    down[0] = state
-    for k in range(1, layers):
-        t_re, t_im = complex_times(rate_re[k][None], rate_im[k][None], *state)
-        state = (t_re + f_re[k], t_im + f_im[k])
-        down[k] = state
     up = [None] * layers
-    state = (f_re[layers - 1], f_im[layers - 1])
-    up[layers - 1] = state
-    for k in range(layers - 2, -1, -1):
-        t_re, t_im = complex_times(rate_re[k][None], rate_im[k][None], *state)
-        state = (t_re + f_re[k], t_im + f_im[k])
-        up[k] = state
+    down[layers - 1] = (src_down[0] + add_down[0], src_down[1] + add_down[1])
+    up[0] = (src_up[0] + add_up[0], src_up[1] + add_up[1])
 
     if lax.axis_size("px") == 2 and lax.axis_size("py") == 2 and slab_count > 1:
         parts = entering_states(down[layers - 1], up[0], levels, defer_last=True)

time: 100 us -> 102 us (1.020)
  waiting for transfers between devices: 40.2 us -> 35.7 us
  other arithmetic: 15.4 us -> 18.7 us
  starting transfers between devices: 28.8 us -> 31.8 us
  local copies, waits for them, and re-layouts: 3.32 us -> 4.42 us
    ppermute x9, starting transfers between devices: 10.1 us -> 15.2 us  [exchange(): return lax.ppermute(array, 'slab', [(i, i ^ step) for i in range(count)])]
    all_to_all x1, waiting for transfers between devices: 2.86 us -> 0.01 us  [inject_receivers(): lax.all_to_all(send_rows, 'slab', split_axis=1, concat_axis=1, tiled=True)]
    ppermute x1, starting transfers between devices: 6.53 us -> 4.25 us  [finish_paired(): got_y = lax.ppermute(send_y, 'py', [(0, 1), (1, 0)])]
    add x5 -> x6, other arithmetic: 1.61 us -> 3.43 us  [the longest x2 1.32 us: shards(): down[layers - 1] = (src_down[0] + add_down[0], src_down[1] + add_down[1])]
    ppermute x9, waiting for transfers between devices: 36.3 us -> 34.7 us  [exchange(): return lax.ppermute(array, 'slab', [(i, i ^ step) for i in range(count)])]
    unnamed x14 -> x50, local copies, waits for them, and re-layouts: 2.12 us -> 3.09 us
  transfers between devices with their start and end apart: 12 -> 12, of which waited for: 8 -> 7; matrix products, arithmetic and copies ran while one was open for 16% -> 19% of each run, Pallas kernels for 0% -> 0%
where the time goes in v18:
time: 102 us; the launch traced here: 101 us
  waiting for transfers between devices  35.7 us (35%)
  starting transfers between devices  31.8 us (31%)
  other arithmetic  18.7 us (18%)
  Pallas kernels  6.58 us (6%)
  local copies, waits for them, and re-layouts  4.42 us (4%)
  matrix products  3.22 us (3%)
    ppermute x9, waiting for transfers between devices, exchange(): return lax.ppermute(array, 'slab', [(i, i ^ step) for i in range(count)])  34.7 us
    ppermute x9, starting transfers between devices, exchange(): return lax.ppermute(array, 'slab', [(i, i ^ step) for i in range(count)])  15.2 us
    all_to_all x1, starting transfers between devices, inject_receivers(): lax.all_to_all(send_rows, 'slab', split_axis=1, concat_axis=1, tiled=True)  9.81 us
    ppermute x1, starting transfers between devices, finish_paired(): got_y = lax.ppermute(send_y, 'py', [(0, 1), (1, 0)])  4.25 us
    pallas_call x1, Pallas kernels, finish_paired(): pl.pallas_call(last_sweep_kernel, in_specs=[smem] + [vmem] * 12, out_spec...  3.36 us
    pallas_call x1, Pallas kernels, finish_paired(): pl.pallas_call(paired_stencil_kernel, in_specs=[smem, vmem, vmem, vmem],...  3.23 us
    unnamed x50, local copies, waits for them, and re-layouts  3.09 us
    ppermute x1, starting transfers between devices, finish_paired(): got_x = lax.ppermute(send_x, 'px', [(0, 1), (1, 0)])  2.45 us
  transfers between devices with their start and end apart: 12, of which 7 were waited for; matrix products, arithmetic and copies ran while one was open for 19% of the time, Pallas kernels for 0%

profile of v18, /device:TPU:1, one launch (start us, length us, event | category | flops | bytes accessed | tf_op | source)
XLA Modules:
  0.0 101.0 jit_solution(6864683130122945455)
XLA Ops:
  0.0 0.8 add_convert_fusion
  1.5 1.0 convert_reduce_fusion
  3.2 0.9 fusion.3
  5.0 9.8 %all-to-all-start = ((f32[32,1,320]{2,1,0:T(1,128)}), f32[32,1,320]{2,1,0:T(1,128)S(1)}, u32[]{:S(2)}, u32[]{:S(2)}) async-start(f32[32,1,320]{2,1,0:T(1,128)} %reshape.273), calls=%async_computation | async-start | bytes 98304 | tf_op jit(solution)/shard_map/all_to_all | solution.py:44
  14.8 0.8 convert_multiply_fusion
  15.6 2.0 %sine_multiply_fusion = (f32[4,128,128]{2,1,0:T(8,128)S(1)}, f32[4,128,128]{2,1,0:T(8,128)S(1)}) fusion(f32[4,128,128]{2,1,0:T(8,128)} %param.9, f32[4,128,128]{2,1,0:T(8,128)} %param.10, f32[128,128]{1,0:T(8,128)S(1)} %convert_multiply_fusion), kind=kLoop, calls=%fused_computation.19 | loop fusion | flops 262144 | bytes 1114112 | tf_op jit(solution)/shard_map/mul | solution.py:333
  17.7 0.9 multiply_add_fusion.4
  19.9 1.2 %collective-permute-start.1 = (f32[2,128,128]{2,1,0:T(8,128)}, f32[2,128,128]{2,1,0:T(8,128)S(1)}, u32[]{:S(2)}, u32[]{:S(2)}) collective-permute-start(f32[2,128,128]{2,1,0:T(8,128)} %pad_maximum_fusion.5), channel_id=1, source_target_pairs={{0,4},{4,0},{8,12},{12,8},{16,20},{20,16},{24,28},{28,24},{32,36},... | collective-permute-start | bytes 393224 | tf_op jit(solution)/shard_map/ppermute | solution.py:68
  21.1 0.8 add_add_fusion.11
  25.0 2.4 %fusion.1 = f32[512,2,512]{2,0,1:T(8,128)S(1)} fusion(bf16[2,512,2048]{2,1,0:T(8,128)(2,1)S(1)} %bitcast.380, s32[2048]{0:T(1024)S(1)} %get-tuple-element.129), kind=kOutput, calls=%fused_computation.4 | convolution fusion | flops 2148532224 | bytes 6299648 | tf_op jit(solution)/shard_map/dot_general | solution.py:59
  28.6 1.2 %add_add_fusion.7 = (f32[2,128,128]{2,1,0:T(8,128)S(1)}, f32[2,128,128]{2,1,0:T(8,128)S(1)}, f32[2,128,128]{2,1,0:T(8,128)S(1)}, f32[2,128,128]{2,1,0:T(8,128)S(...) fusion(f32[4,2,2,128,128]{4,3,2,1,0:T(8,128)S(1)} %bitcast.373, f32[4,2,2,128,128]{4,3,2,1,0:T(8,128)S(1)} %bitcast.377, ...), kind=kLoop, calls=%fused_computation.79 | loop fusion | flops 950272 | bytes 2490368 | tf_op jit(solution)/shard_map/add | solution.py:365
  30.6 1.3 %collective-permute-start.3 = (f32[2,128,128]{2,1,0:T(8,128)S(1)}, f32[2,128,128]{2,1,0:T(8,128)S(1)}, u32[]{:S(2)}, u32[]{:S(2)}) collective-permute-start(f32[2,128,128]{2,1,0:T(8,128)S(1)} %pad_maximum_fusion.6), channel_id=1, source_target_pairs={{0,8},{4,12},{8,0},{12,4},{16,24},{20,28},{24,16},{28,20},{32,40},... | collective-permute-start | bytes 393224 | tf_op jit(solution)/shard_map/ppermute | solution.py:68
  31.9 1.1 %bitcast_add_fusion.f_ref = f32[4,4,128,128]{3,2,1,0:T(8,128)} fusion(f32[4,4,128,128]{3,2,1,0:T(8,128)S(1)} %copy-done, f32[4,128,4,128]{3,2,1,0:T(4,128)S(1)} %add.418), kind=kLoop, calls=%fused_computation.9 | loop fusion | flops 262144 | bytes 3145728 | tf_op jit(solution)/shard_map/add | solution.py:63
  33.0 1.5 %collective-permute-done.3 = f32[2,128,128]{2,1,0:T(8,128)S(1)} collective-permute-done((f32[2,128,128]{2,1,0:T(8,128)S(1)}, f32[2,128,128]{2,1,0:T(8,128)S(1)}, u32[]{:S(2)}, u32[]{:S(2)}) %collective-permute-start.3) | collective-permute-done | bytes 131104 | tf_op jit(solution)/shard_map/ppermute | solution.py:68
  34.5 2.8 %collective-permute-start.5 = (f32[2,128,128]{2,1,0:T(8,128)S(1)}, f32[2,128,128]{2,1,0:T(8,128)S(1)}, u32[]{:S(2)}, u32[]{:S(2)}) collective-permute-start(f32[2,128,128]{2,1,0:T(8,128)S(1)} %pad_maximum_fusion.7), channel_id=1, source_target_pairs={{0,16},{4,20},{8,24},{12,28},{16,0},{20,4},{24,8},{28,12},{32,48},... | collective-permute-start | bytes 393224 | tf_op jit(solution)/shard_map/ppermute | solution.py:68
  37.3 4.8 %collective-permute-done = f32[8,128,128]{2,1,0:T(8,128)S(1)} collective-permute-done((f32[8,128,128]{2,1,0:T(8,128)S(1)}, f32[8,128,128]{2,1,0:T(8,128)S(1)}, u32[]{:S(2)}, u32[]{:S(2)}) %collective-permute-start) | collective-permute-done | bytes 524320 | tf_op jit(solution)/shard_map/ppermute | solution.py:68
  42.3 1.3 %collective-permute-start.2 = (f32[8,128,128]{2,1,0:T(8,128)S(1)}, f32[8,128,128]{2,1,0:T(8,128)S(1)}, u32[]{:S(2)}, u32[]{:S(2)}) collective-permute-start(f32[8,128,128]{2,1,0:T(8,128)S(1)} %pad_maximum_fusion.1), channel_id=1, source_target_pairs={{0,8},{4,12},{8,0},{12,4},{16,24},{20,28},{24,16},{28,20},{32,40},... | collective-permute-start | bytes 1572872 | tf_op jit(solution)/shard_map/ppermute | solution.py:68
  43.7 9.6 %collective-permute-done.2 = f32[8,128,128]{2,1,0:T(8,128)S(1)} collective-permute-done((f32[8,128,128]{2,1,0:T(8,128)S(1)}, f32[8,128,128]{2,1,0:T(8,128)S(1)}, u32[]{:S(2)}, u32[]{:S(2)}) %collective-permute-start.2) | collective-permute-done | bytes 524320 | tf_op jit(solution)/shard_map/ppermute | solution.py:68
  53.5 2.8 %collective-permute-start.4 = (f32[8,128,128]{2,1,0:T(8,128)S(1)}, f32[8,128,128]{2,1,0:T(8,128)S(1)}, u32[]{:S(2)}, u32[]{:S(2)}) collective-permute-start(f32[8,128,128]{2,1,0:T(8,128)S(1)} %pad_maximum_fusion.2), channel_id=1, source_target_pairs={{0,16},{4,20},{8,24},{12,28},{16,0},{20,4},{24,8},{28,12},{32,48},... | collective-permute-start | bytes 1572872 | tf_op jit(solution)/shard_map/ppermute | solution.py:68
  56.4 1.3 %collective-permute-start.7 = (f32[2,128,128]{2,1,0:T(8,128)S(1)}, f32[2,128,128]{2,1,0:T(8,128)S(1)}, u32[]{:S(2)}, u32[]{:S(2)}) collective-permute-start(f32[2,128,128]{2,1,0:T(8,128)S(1)} %pad_maximum_fusion.8), channel_id=1, source_target_pairs={{0,32},{4,36},{8,40},{12,44},{16,48},{20,52},{24,56},{28,60},{32,0... | collective-permute-start | bytes 393224 | tf_op jit(solution)/shard_map/ppermute | solution.py:68
  57.7 8.8 %collective-permute-done.4 = f32[8,128,128]{2,1,0:T(8,128)S(1)} collective-permute-done((f32[8,128,128]{2,1,0:T(8,128)S(1)}, f32[8,128,128]{2,1,0:T(8,128)S(1)}, u32[]{:S(2)}, u32[]{:S(2)}) %collective-permute-start.4) | collective-permute-done | bytes 524320 | tf_op jit(solution)/shard_map/ppermute | solution.py:68
  66.6 1.2 %collective-permute-start.6 = (f32[8,128,128]{2,1,0:T(8,128)S(1)}, f32[8,128,128]{2,1,0:T(8,128)S(1)}, u32[]{:S(2)}, u32[]{:S(2)}) collective-permute-start(f32[8,128,128]{2,1,0:T(8,128)S(1)} %pad_maximum_fusion.3), channel_id=1, source_target_pairs={{0,32},{4,36},{8,40},{12,44},{16,48},{20,52},{24,56},{28,60},{32,0... | collective-permute-start | bytes 1572872 | tf_op jit(solution)/shard_map/ppermute | solution.py:68
  69.3 7.2 %collective-permute-done.6 = f32[8,128,128]{2,1,0:T(8,128)S(1)} collective-permute-done((f32[8,128,128]{2,1,0:T(8,128)S(1)}, f32[8,128,128]{2,1,0:T(8,128)S(1)}, u32[]{:S(2)}, u32[]{:S(2)}) %collective-permute-start.6) | collective-permute-done | bytes 524320 | tf_op jit(solution)/shard_map/ppermute | solution.py:68
  76.6 3.0 %collective-permute-start.8 = (f32[4,128,128]{2,1,0:T(8,128)S(1)}, f32[4,128,128]{2,1,0:T(8,128)S(1)}, u32[]{:S(2)}, u32[]{:S(2)}) collective-permute-start(f32[4,128,128]{2,1,0:T(8,128)S(1)} %pad_maximum_fusion.4), channel_id=1, source_target_pairs={{0,64},{4,68},{8,72},{12,76},{16,80},{20,84},{24,88},{28,92},{32,9... | collective-permute-start | bytes 786440 | tf_op jit(solution)/shard_map/ppermute | solution.py:68
  79.6 0.7 add_select_fusion.9.br_ref
  81.1 0.7 add_select_fusion.3.ar_ref
  82.6 2.8 %collective-permute-done.8.got_ref = f32[4,128,128]{2,1,0:T(8,128)S(1)} collective-permute-done((f32[4,128,128]{2,1,0:T(8,128)S(1)}, f32[4,128,128]{2,1,0:T(8,128)S(1)}, u32[]{:S(2)}, u32[]{:S(2)}) %collective-permute-start.8) | collective-permute-done | bytes 262176 | tf_op jit(solution)/shard_map/ppermute | solution.py:68
  86.1 3.4 %shard_map.82 = (f32[4,4,128,128]{3,2,1,0:T(8,128)}, f32[4,4,128]{2,1,0:T(4,128)}, f32[4,4,128]{2,1,0:T(4,128)}) custom-call(s32[3]{0:T(128)} %pad_add_fusion.flag_ref, f32[4,4,128,128]{3,2,1,0:T(8,128)} %bitcast_add_fusion.f_ref, f32[4,128,128]{2,1,0:T(8,128)} %copy-done.2, f32[4,128,128]{2,1,0:T(8,128)} %copy-done.1, ...), custom_call_target="tpu_custom_call" | custom-call | tf_op jit(solution)/shard_map/pallas_call | solution.py:307
  89.4 2.4 %collective-permute-start.9 = (f32[4,4,128]{2,1,0:T(4,128)}, f32[4,4,128]{2,1,0:T(4,128)S(1)}, u32[]{:S(2)}, u32[]{:S(2)}) collective-permute-start(f32[4,4,128]{2,1,0:T(4,128)} %get-tuple-element.9), channel_id=1, source_target_pairs={{0,2},{2,0},{1,3},{3,1},{4,6},{6,4},{5,7},{7,5},{8,10},{10,8},{9,1... | collective-permute-start | bytes 24584 | tf_op jit(solution)/shard_map/ppermute | solution.py:313
  91.9 4.2 %collective-permute-start.10 = (f32[4,4,128]{2,1,0:T(4,128)}, f32[4,4,128]{2,1,0:T(4,128)S(1)}, u32[]{:S(2)}, u32[]{:S(2)}) collective-permute-start(f32[4,4,128]{2,1,0:T(4,128)} %get-tuple-element.10), channel_id=1, source_target_pairs={{0,1},{1,0},{2,3},{3,2},{4,5},{5,4},{6,7},{7,6},{8,9},{9,8},{10,11... | collective-permute-start | bytes 24584 | tf_op jit(solution)/shard_map/ppermute | solution.py:314
  96.1 1.0 %collective-permute-done.10.gy_ref = f32[4,4,128]{2,1,0:T(4,128)S(1)} collective-permute-done((f32[4,4,128]{2,1,0:T(4,128)}, f32[4,4,128]{2,1,0:T(4,128)S(1)}, u32[]{:S(2)}, u32[]{:S(2)}) %collective-permute-start.10) | collective-permute-done | bytes 8224 | tf_op jit(solution)/shard_map/ppermute | solution.py:314
  97.8 3.2 %shard_map.83 = f32[4,4,128,128]{3,2,1,0:T(8,128)} custom-call(s32[3]{0:T(128)} %pad_add_fusion.flag_ref, f32[4,4,128,128]{3,2,1,0:T(8,128)} %get-tuple-element.8.c_ref, f32[4,4,128]{2,1,0:T(4,128)} %copy-done.22, f32[4,4,128]{2,1,0:T(4,128)} %copy-done.23), custom_call_target="tpu_custom_call" | custom-call | tf_op jit(solution)/shard_map/pallas_call | solution.py:315
  (109 shorter events, 13.4 us)
Async XLA Ops:
  0.0 21.1 %copy-start = (f32[4,4,128,128]{3,2,1,0:T(8,128)S(1)}, f32[4,4,128,128]{3,2,1,0:T(8,128)}, u32[]{:S(2)}) copy-start(f32[4,4,128,128]{3,2,1,0:T(8,128)} %param.8) | copy-start | bytes 3145732
  5.0 17.5 %all-to-all-start = ((f32[32,1,320]{2,1,0:T(1,128)}), f32[32,1,320]{2,1,0:T(1,128)S(1)}, u32[]{:S(2)}, u32[]{:S(2)}) async-start(f32[32,1,320]{2,1,0:T(1,128)} %reshape.273), calls=%async_computation | async-start | bytes 98304 | tf_op jit(solution)/shard_map/all_to_all | solution.py:44
  17.6 7.3 %copy-start.1 = (f32[4,128,128]{2,1,0:T(8,128)}, f32[4,128,128]{2,1,0:T(8,128)S(1)}, u32[]{:S(2)}) copy-start(f32[4,128,128]{2,1,0:T(8,128)S(1)} %get-tuple-element.67.ri_ref) | copy-start | bytes 786436
  17.6 7.3 %copy-start.2 = (f32[4,128,128]{2,1,0:T(8,128)}, f32[4,128,128]{2,1,0:T(8,128)S(1)}, u32[]{:S(2)}) copy-start(f32[4,128,128]{2,1,0:T(8,128)S(1)} %get-tuple-element.68.rr_ref) | copy-start | bytes 786436
  17.7 0.9 copy-start.15
  18.6 8.8 %copy-start.3 = (f32[128,128]{1,0:T(8,128)}, f32[128,128]{1,0:T(8,128)S(1)}, u32[]{:S(2)}) copy-start(f32[128,128]{1,0:T(8,128)S(1)} %get-tuple-element.91) | copy-start | bytes 196612
  18.6 8.8 %copy-start.5 = (f32[128,128]{1,0:T(8,128)}, f32[128,128]{1,0:T(8,128)S(1)}, u32[]{:S(2)}) copy-start(f32[128,128]{1,0:T(8,128)S(1)} %get-tuple-element.97) | copy-start | bytes 196612
  18.6 8.8 %copy-start.7 = (f32[128,128]{1,0:T(8,128)}, f32[128,128]{1,0:T(8,128)S(1)}, u32[]{:S(2)}) copy-start(f32[128,128]{1,0:T(8,128)S(1)} %get-tuple-element.92) | copy-start | bytes 196612
  18.6 8.8 %copy-start.9 = (f32[128,128]{1,0:T(8,128)}, f32[128,128]{1,0:T(8,128)S(1)}, u32[]{:S(2)}) copy-start(f32[128,128]{1,0:T(8,128)S(1)} %get-tuple-element.96) | copy-start | bytes 196612
  19.9 10.6 %collective-permute-start.1 = (f32[2,128,128]{2,1,0:T(8,128)}, f32[2,128,128]{2,1,0:T(8,128)S(1)}, u32[]{:S(2)}, u32[]{:S(2)}) collective-permute-start(f32[2,128,128]{2,1,0:T(8,128)} %pad_maximum_fusion.5), channel_id=1, source_target_pairs={{0,4},{4,0},{8,12},{12,8},{16,20},{20,16},{24,28},{28,24},{32,36},... | collective-permute-start | bytes 393224 | tf_op jit(solution)/shard_map/ppermute | solution.py:68
  27.6 0.9 copy-start.6
  27.6 0.9 copy-start.8
  27.6 0.9 copy-start.10
  28.0 1.8 %copy-start.11 = (f32[128,128]{1,0:T(8,128)S(1)}, f32[128,128]{1,0:T(8,128)}, u32[]{:S(2)}) copy-start(f32[128,128]{1,0:T(8,128)} %get-tuple-element.90) | copy-start | bytes 196612
  28.0 1.8 %copy-start.13 = (f32[128,128]{1,0:T(8,128)S(1)}, f32[128,128]{1,0:T(8,128)}, u32[]{:S(2)}) copy-start(f32[128,128]{1,0:T(8,128)} %get-tuple-element.94) | copy-start | bytes 196612
  28.0 1.8 %copy-start.19 = (f32[2,128,128]{2,1,0:T(8,128)S(1)}, f32[2,128,128]{2,1,0:T(8,128)}, u32[]{:S(2)}) copy-start(f32[2,128,128]{2,1,0:T(8,128)} %get-tuple-element.53) | copy-start | bytes 393220
  28.0 1.8 %copy-start.20 = (f32[2,128,128]{2,1,0:T(8,128)S(1)}, f32[2,128,128]{2,1,0:T(8,128)}, u32[]{:S(2)}) copy-start(f32[2,128,128]{2,1,0:T(8,128)} %get-tuple-element.54) | copy-start | bytes 393220
  28.0 2.0 %copy-start.12 = (f32[128,128]{1,0:T(8,128)S(1)}, f32[128,128]{1,0:T(8,128)}, u32[]{:S(2)}) copy-start(f32[128,128]{1,0:T(8,128)} %get-tuple-element.93) | copy-start | bytes 196612
  28.1 2.0 %copy-start.14 = (f32[128,128]{1,0:T(8,128)S(1)}, f32[128,128]{1,0:T(8,128)}, u32[]{:S(2)}) copy-start(f32[128,128]{1,0:T(8,128)} %get-tuple-element.95) | copy-start | bytes 196612
  28.6 1.9 %copy-start.16 = (f32[1,128,128]{2,1,0:T(8,128)S(1)}, f32[1,128,128]{2,1,0:T(8,128)}, u32[]{:S(2)}) copy-start(f32[1,128,128]{2,1,0:T(8,128)} %copy-done.15) | copy-start | bytes 196612
  28.6 1.9 %copy-start.18 = (f32[1,128,128]{2,1,0:T(8,128)S(1)}, f32[1,128,128]{2,1,0:T(8,128)}, u32[]{:S(2)}) copy-start(f32[1,128,128]{2,1,0:T(8,128)} %copy-done.17) | copy-start | bytes 196612
  30.2 11.9 %collective-permute-start = (f32[8,128,128]{2,1,0:T(8,128)S(1)}, f32[8,128,128]{2,1,0:T(8,128)S(1)}, u32[]{:S(2)}, u32[]{:S(2)}) collective-permute-start(f32[8,128,128]{2,1,0:T(8,128)S(1)} %pad_maximum_fusion), channel_id=1, source_target_pairs={{0,4},{4,0},{8,12},{12,8},{16,20},{20,16},{24,28},{28,24},{32,36},... | collective-permute-start | bytes 1572872 | tf_op jit(solution)/shard_map/ppermute | solution.py:68
  30.6 3.9 %collective-permute-start.3 = (f32[2,128,128]{2,1,0:T(8,128)S(1)}, f32[2,128,128]{2,1,0:T(8,128)S(1)}, u32[]{:S(2)}, u32[]{:S(2)}) collective-permute-start(f32[2,128,128]{2,1,0:T(8,128)S(1)} %pad_maximum_fusion.6), channel_id=1, source_target_pairs={{0,8},{4,12},{8,0},{12,4},{16,24},{20,28},{24,16},{28,20},{32,40},... | collective-permute-start | bytes 393224 | tf_op jit(solution)/shard_map/ppermute | solution.py:68
  34.5 9.1 %collective-permute-start.5 = (f32[2,128,128]{2,1,0:T(8,128)S(1)}, f32[2,128,128]{2,1,0:T(8,128)S(1)}, u32[]{:S(2)}, u32[]{:S(2)}) collective-permute-start(f32[2,128,128]{2,1,0:T(8,128)S(1)} %pad_maximum_fusion.7), channel_id=1, source_target_pairs={{0,16},{4,20},{8,24},{12,28},{16,0},{20,4},{24,8},{28,12},{32,48},... | collective-permute-start | bytes 393224 | tf_op jit(solution)/shard_map/ppermute | solution.py:68
  42.3 11.0 %collective-permute-start.2 = (f32[8,128,128]{2,1,0:T(8,128)S(1)}, f32[8,128,128]{2,1,0:T(8,128)S(1)}, u32[]{:S(2)}, u32[]{:S(2)}) collective-permute-start(f32[8,128,128]{2,1,0:T(8,128)S(1)} %pad_maximum_fusion.1), channel_id=1, source_target_pairs={{0,8},{4,12},{8,0},{12,4},{16,24},{20,28},{24,16},{28,20},{32,40},... | collective-permute-start | bytes 1572872 | tf_op jit(solution)/shard_map/ppermute | solution.py:68
  53.5 13.0 %collective-permute-start.4 = (f32[8,128,128]{2,1,0:T(8,128)S(1)}, f32[8,128,128]{2,1,0:T(8,128)S(1)}, u32[]{:S(2)}, u32[]{:S(2)}) collective-permute-start(f32[8,128,128]{2,1,0:T(8,128)S(1)} %pad_maximum_fusion.2), channel_id=1, source_target_pairs={{0,16},{4,20},{8,24},{12,28},{16,0},{20,4},{24,8},{28,12},{32,48},... | collective-permute-start | bytes 1572872 | tf_op jit(solution)/shard_map/ppermute | solution.py:68
  56.4 11.4 %collective-permute-start.7 = (f32[2,128,128]{2,1,0:T(8,128)S(1)}, f32[2,128,128]{2,1,0:T(8,128)S(1)}, u32[]{:S(2)}, u32[]{:S(2)}) collective-permute-start(f32[2,128,128]{2,1,0:T(8,128)S(1)} %pad_maximum_fusion.8), channel_id=1, source_target_pairs={{0,32},{4,36},{8,40},{12,44},{16,48},{20,52},{24,56},{28,60},{32,0... | collective-permute-start | bytes 393224 | tf_op jit(solution)/shard_map/ppermute | solution.py:68
  66.6 9.9 %collective-permute-start.6 = (f32[8,128,128]{2,1,0:T(8,128)S(1)}, f32[8,128,128]{2,1,0:T(8,128)S(1)}, u32[]{:S(2)}, u32[]{:S(2)}) collective-permute-start(f32[8,128,128]{2,1,0:T(8,128)S(1)} %pad_maximum_fusion.3), channel_id=1, source_target_pairs={{0,32},{4,36},{8,40},{12,44},{16,48},{20,52},{24,56},{28,60},{32,0... | collective-permute-start | bytes 1572872 | tf_op jit(solution)/shard_map/ppermute | solution.py:68
  76.6 8.7 %collective-permute-start.8 = (f32[4,128,128]{2,1,0:T(8,128)S(1)}, f32[4,128,128]{2,1,0:T(8,128)S(1)}, u32[]{:S(2)}, u32[]{:S(2)}) collective-permute-start(f32[4,128,128]{2,1,0:T(8,128)S(1)} %pad_maximum_fusion.4), channel_id=1, source_target_pairs={{0,64},{4,68},{8,72},{12,76},{16,80},{20,84},{24,88},{28,92},{32,9... | collective-permute-start | bytes 786440 | tf_op jit(solution)/shard_map/ppermute | solution.py:68
  89.4 6.7 %collective-permute-start.9 = (f32[4,4,128]{2,1,0:T(4,128)}, f32[4,4,128]{2,1,0:T(4,128)S(1)}, u32[]{:S(2)}, u32[]{:S(2)}) collective-permute-start(f32[4,4,128]{2,1,0:T(4,128)} %get-tuple-element.9), channel_id=1, source_target_pairs={{0,2},{2,0},{1,3},{3,1},{4,6},{6,4},{5,7},{7,5},{8,10},{10,8},{9,1... | collective-permute-start | bytes 24584 | tf_op jit(solution)/shard_map/ppermute | solution.py:313
  91.9 5.3 %collective-permute-start.10 = (f32[4,4,128]{2,1,0:T(4,128)}, f32[4,4,128]{2,1,0:T(4,128)S(1)}, u32[]{:S(2)}, u32[]{:S(2)}) collective-permute-start(f32[4,4,128]{2,1,0:T(4,128)} %get-tuple-element.10), channel_id=1, source_target_pairs={{0,1},{1,0},{2,3},{3,2},{4,5},{5,4},{6,7},{7,6},{8,9},{9,8},{10,11... | collective-permute-start | bytes 24584 | tf_op jit(solution)/shard_map/ppermute | solution.py:314
  96.1 1.0 %copy-start.22 = (f32[4,4,128]{2,1,0:T(4,128)}, f32[4,4,128]{2,1,0:T(4,128)S(1)}, u32[]{:S(2)}) copy-start(f32[4,4,128]{2,1,0:T(4,128)S(1)} %collective-permute-done.9.gx_ref) | copy-start | bytes 24580
  (4 other events, 2.8 us)
